TPU v7x, 32 devices: a whole 2x2x4 slice. The times are simulated.
32 devices in a mesh: gz: 4 (over x, core), yx: 8 (over z, y).
Axes of the slice: x: 2, y: 2, z: 4, core: 2. Of those that a mesh axis runs over, the one named last changes fastest.
Arguments:
- features: bfloat16 [16, 64, 128, 128], P(None, 'gz', 'yx'), may hold values from -19 to 19
- conv_weight: bfloat16 [3, 16, 3, 3, 3], replicated, may hold values from -0.3125 to 0.3125
- conv_bias: float32 [3], replicated, may hold values from -3 to 3
- labels: int32 [64, 128, 128], P('gz', 'yx'), may hold values from 0 to 8, as said below
Outputs:
- probabilities: float32 [8, 64, 128, 128], P(None, 'gz', 'yx')
- affinities: float32 [3, 64, 128, 128], P(None, 'gz', 'yx')
Inputs may be any that keep to these rules, and one draw needn't show every extreme that they name: `labels`: 0 marks an unseeded voxel, k marks a seed of colour k.
All inputs are finite; a program needn't handle non-finite values.
Results may differ from a plain program's by a relative error of at most 0.0012.
Values may be sent and summed in bfloat16 or wider, within the bound.
No kernel may reach another device: no remote copies, remote signals or barrier semaphores. Data moves between devices by JAX's collectives and lax.ppermute only.
A program may use at most 64 MiB of HBM per device.

v0:
```python
import jax
import jax.numpy as jnp
from jax import lax
from jax.sharding import PartitionSpec as P

FIELDS = 8
ITERS = 3


RIDGE_WEIGHT = 0.5


def padded_2(cells, sides, width):
    for axis, dim in sides:
        count = lax.axis_size(axis)
        ends = count - 1
        head = lax.slice_in_dim(cells, 0, width, axis=dim)
        tail = lax.slice_in_dim(cells, cells.shape[dim] - width, cells.shape[dim], axis=dim)
        cells = jnp.concatenate(
            [
                lax.ppermute(tail, axis, [(i, (i + 1) % count) for i in range(ends)]),
                cells,
                lax.ppermute(head, axis, [((i + 1) % count, i) for i in range(ends)]),
            ],
            axis=dim,
        )
    return cells


def from_behind(value, axis, by):
    devices = lax.axis_size(axis)
    pairs = [(i, i + by) for i in range(devices) if 0 <= i + by < devices]
    return lax.ppermute(value, axis, pairs)


def conv_region(padded, conv_weight, count_z, count_y):
    col_cells = padded.shape[3] - 2
    summed = jnp.zeros((3, count_z, count_y, col_cells), jnp.float32)
    for offset_z in range(3):
        for offset_y in range(3):
            for offset_x in range(3):
                window = padded[
                    :,
                    offset_z : offset_z + count_z,
                    offset_y : offset_y + count_y,
                    offset_x : offset_x + col_cells,
                ]
                summed = summed + jnp.einsum(
                    "oc,czyx->ozyx",
                    conv_weight[:, :, offset_z, offset_y, offset_x],
                    window,
                    preferred_element_type=jnp.float32,
                )
    return summed


def stencil(field, padded, weights, seeded):
    weight_zup, weight_zdown, weight_yup, weight_ydown, weight_xup, weight_xdown = weights
    padded = jnp.pad(padded, ((0, 0), (0, 0), (0, 0), (1, 1)))
    laplace = weight_zup * (field - padded[:, 2:, 1:-1, 1:-1]) + weight_zdown * (
        field - padded[:, :-2, 1:-1, 1:-1]
    )
    laplace = (
        laplace
        + weight_yup * (field - padded[:, 1:-1, 2:, 1:-1])
        + weight_ydown * (field - padded[:, 1:-1, :-2, 1:-1])
    )
    laplace = (
        laplace
        + weight_xup * (field - padded[:, 1:-1, 1:-1, 2:])
        + weight_xdown * (field - padded[:, 1:-1, 1:-1, :-2])
    )
    return (1.0 - seeded) * (laplace + RIDGE_WEIGHT * field) + seeded * field


def operate(field, weights, seeded):
    padded = padded_2(field.astype(jnp.bfloat16), (("gz", 1), ("yx", 2)), 1).astype(field.dtype)
    return stencil(field, padded, weights, seeded)


def field_sums(left, right):
    return jnp.sum(left * right, axis=(1, 2, 3))


def spread_out(values):
    return values[:, None, None, None]


def squares(residual):
    return lax.psum(field_sums(residual, residual), ("gz", "yx"))


def body(features, conv_weight, conv_bias, labels):
    depth_cells = features.shape[1]
    row_cells = features.shape[2]
    col_cells = features.shape[3]
    global_z = lax.axis_index("gz") * depth_cells + jnp.arange(depth_cells, dtype=jnp.int32)
    global_y = lax.axis_index("yx") * row_cells + jnp.arange(row_cells, dtype=jnp.int32)
    keep_z = (global_z < depth_cells * lax.axis_size("gz") - 1).astype(jnp.float32)[:, None, None]
    keep_y = (global_y < row_cells * lax.axis_size("yx") - 1).astype(jnp.float32)[None, :, None]
    keep_x = (jnp.arange(col_cells, dtype=jnp.int32) < col_cells - 1).astype(jnp.float32)[
        None, None, :
    ]
    bias_column = conv_bias[:, None, None, None]
    padded = padded_2(features, (("gz", 1), ("yx", 2)), 1)
    padded = jnp.pad(padded, ((0, 0), (0, 0), (0, 0), (1, 1)))
    affinities = jax.nn.sigmoid(
        conv_region(padded, conv_weight, depth_cells, row_cells) + bias_column
    )
    below_plane = from_behind(affinities[0, -1], "gz", 1)
    below_row = from_behind(affinities[1, :, -1], "yx", 1)
    weight_zdown = jnp.concatenate([below_plane[None], affinities[0, :-1]], axis=0)
    weight_ydown = jnp.concatenate([below_row[:, None, :], affinities[1, :, :-1]], axis=1)
    weight_zup = affinities[0] * keep_z
    weight_yup = affinities[1] * keep_y
    weight_xup = affinities[2] * keep_x
    weight_xdown = jnp.pad(weight_xup, ((0, 0), (0, 0), (1, 0)))[:, :, :-1]
    weights = (
        weight_zup[None],
        weight_zdown[None],
        weight_yup[None],
        weight_ydown[None],
        weight_xup[None],
        weight_xdown[None],
    )
    seeded = (labels > 0).astype(jnp.float32)[None]
    colours = jnp.arange(1, FIELDS + 1, dtype=jnp.int32)[:, None, None, None]
    seed_field = (labels[None] == colours).astype(jnp.float32)
    right_side = seed_field - operate(seed_field, weights, seeded)
    solution = jnp.zeros_like(right_side)
    residual = right_side
    direction = right_side
    norm_now = squares(residual)
    for iteration in range(ITERS):
        applied = operate(direction, weights, seeded)
        curve = lax.psum(field_sums(direction, applied), ("gz", "yx"))
        step_size = norm_now / curve
        solution = solution + spread_out(step_size) * direction
        residual = residual - spread_out(step_size) * applied
        norm_next = squares(residual)
        direction = residual + spread_out(norm_next / norm_now) * direction
        norm_now = norm_next
    return (seed_field + solution, affinities)


def solution(mesh):
    in_specs = (P(None, "gz", "yx", None), P(), P(), P("gz", "yx", None))
    out_specs = (P(None, "gz", "yx", None), P(None, "gz", "yx", None))
    return jax.shard_map(body, mesh=mesh, in_specs=in_specs, out_specs=out_specs, check_vma=False)
```

profile of v0, /device:TPU:0, one launch (start us, length us, event | category | flops | bytes accessed | tf_op | source)
XLA Modules:
  0.0 327.7 jit_solution(10682856943272510199)
XLA Ops:
  0.7 3.0 copy.15
  3.6 0.9 fusion.207
  4.5 2.4 collective-permute-start
  6.9 1.3 collective-permute-start.1
  8.4 5.1 %collective-permute-start.4 = (bf16[8,1,16,128]{3,2,1,0:T(8,128)(2,1)S(1)}, bf16[8,1,16,128]{3,2,1,0:T(8,128)(2,1)S(1)}, u32[]{:S(2)}, u32[]{:S(2)}) collective-permute-start(bf16[8,1,16,128]{3,2,1,0:T(8,128)(2,1)S(1)} %get-tuple-element.43), channel_id=1, source_target_pairs={{0,8},{8,16},{16,24},{1,9},{9,17},{17,25},{2,10},{10,18},{18,26},{... | collective-permute-start | bytes 98312 | tf_op jit(solution)/shard_map/ppermute | solution.py:21
  13.6 1.3 collective-permute-start.5
  15.0 0.7 fusion.150
  15.7 2.2 collective-permute-done.5
  18.0 3.4 %collective-permute-start.6 = (bf16[8,18,1,128]{3,2,1,0:T(2,128)(2,1)S(1)}, bf16[8,18,1,128]{3,2,1,0:T(2,128)(2,1)S(1)}, u32[]{:S(2)}, u32[]{:S(2)}) collective-permute-start(bf16[8,18,1,128]{3,2,1,0:T(2,128)(2,1)S(1)} %get-tuple-element.31), channel_id=1, source_target_pairs={{0,1},{1,2},{2,3},{3,4},{4,5},{5,6},{6,7},{8,9},{9,10},{10,11},{11... | collective-permute-start | bytes 110600 | tf_op jit(solution)/shard_map/ppermute | solution.py:21
  21.5 1.3 collective-permute-start.7
  22.8 0.7 constant_dynamic-update-slice_fusion.1
  23.6 4.5 %collective-permute-start.2 = (bf16[16,18,1,128]{3,0,2,1:T(8,128)(2,1)S(1)}, bf16[16,18,1,128]{3,0,2,1:T(8,128)(2,1)S(1)}, u32[]{:S(2)}, u32[]{:S(2)}) collective-permute-start(bf16[16,18,1,128]{3,0,2,1:T(8,128)(2,1)S(1)} %get-tuple-element.21), channel_id=1, source_target_pairs={{0,1},{1,2},{2,3},{3,4},{4,5},{5,6},{6,7},{8,9},{9,10},{10,11},{11... | collective-permute-start | bytes 221192 | tf_op jit(solution)/shard_map/ppermute | solution.py:21
  28.2 1.5 collective-permute-start.3
  29.6 1.5 fusion.37
  31.1 1.5 convolution_bitcast_fusion.1
  33.1 1.7 collective-permute-done.3
  34.8 1.8 fusion.5
  36.9 0.5 fusion.118
  37.7 0.5 fusion.122
  38.5 0.5 fusion.126
  39.3 0.5 fusion.130
  39.8 0.5 convolution_bitcast_fusion.10
  41.7 0.5 convolution_bitcast_fusion.8
  42.5 0.5 convolution_bitcast_fusion.4
  43.8 1.0 fusion.29
  45.8 1.0 fusion.36
  46.9 2.8 collective-permute-start.8
  49.7 4.7 %collective-permute-start.9 = (f32[16,128]{1,0:T(8,128)S(1)}, f32[16,128]{1,0:T(8,128)S(1)}, u32[]{:S(2)}, u32[]{:S(2)}) collective-permute-start(f32[16,128]{1,0:T(8,128)S(1)} %bitcast.231), channel_id=1, source_target_pairs={{0,1},{1,2},{2,3},{3,4},{4,5},{5,6},{6,7},{8,9},{9,10},{10,11},{11... | collective-permute-start | bytes 24584 | tf_op jit(solution)/shard_map/ppermute | solution.py:33
  55.7 1.4 fusion.205
  57.1 3.4 %collective-permute-start.10 = (bf16[8,1,16,128]{3,2,1,0:T(8,128)(2,1)S(1)}, bf16[8,1,16,128]{3,2,1,0:T(8,128)(2,1)S(1)}, u32[]{:S(2)}, u32[]{:S(2)}) collective-permute-start(bf16[8,1,16,128]{3,2,1,0:T(8,128)(2,1)S(1)} %get-tuple-element.37), channel_id=1, source_target_pairs={{0,8},{8,16},{16,24},{1,9},{9,17},{17,25},{2,10},{10,18},{18,26},{... | collective-permute-start | bytes 98312 | tf_op jit(solution)/shard_map/ppermute | solution.py:21
  60.5 1.3 collective-permute-start.11
  61.8 1.8 collective-permute-done.11
  63.8 4.2 %collective-permute-start.12 = (bf16[8,18,1,128]{3,2,1,0:T(2,128)(2,1)S(1)}, bf16[8,18,1,128]{3,2,1,0:T(2,128)(2,1)S(1)}, u32[]{:S(2)}, u32[]{:S(2)}) collective-permute-start(bf16[8,18,1,128]{3,2,1,0:T(2,128)(2,1)S(1)} %get-tuple-element.29), channel_id=1, source_target_pairs={{0,1},{1,2},{2,3},{3,4},{4,5},{5,6},{6,7},{8,9},{9,10},{10,11},{11... | collective-permute-start | bytes 110600 | tf_op jit(solution)/shard_map/ppermute | solution.py:21
  68.0 1.3 collective-permute-start.13
  69.3 0.7 collective-permute-done.12
  69.9 4.5 %collective-permute-done.13 = bf16[8,18,1,128]{3,2,1,0:T(2,128)(2,1)S(1)} collective-permute-done((bf16[8,18,1,128]{3,2,1,0:T(2,128)(2,1)S(1)}, bf16[8,18,1,128]{3,2,1,0:T(2,128)(2,1)S(1)}, u32[]{:S(2)}, u32[]{:S(2)}) %collective-permute-start.13) | collective-permute-done | bytes 36896 | tf_op jit(solution)/shard_map/ppermute | solution.py:23
  74.9 1.5 multiply_reduce_fusion.3
  76.5 42.8 %all-reduce.6 = (f32[8]{0:T(128)S(1)}, f32[8]{0:T(128)S(1)}) all-reduce(f32[8]{0:T(128)S(1)} %get-tuple-element.7, f32[8]{0:T(128)S(1)} %get-tuple-element.6), channel_id=1, replica_groups=mesh['gz'=4,'yx'=8] {'gz','yx'}, use_global_device_ids=true, to_apply=%region_1.2 | all-reduce | flops 16 | bytes 128 | tf_op jit(solution)/shard_map/psum | solution.py:90
  119.3 0.5 copy-done.24
  120.2 38.3 %psum.44 = f32[8]{0:T(128)S(1)} all-reduce(f32[8]{0:T(128)S(1)} %get-tuple-element.16), channel_id=1, replica_groups=mesh['gz'=4,'yx'=8] {'gz','yx'}, use_global_device_ids=true, to_apply=%region_5.6 | all-reduce | flops 8 | bytes 64 | tf_op jit(solution)/shard_map/psum | solution.py:90
  158.4 0.7 div.20
  159.4 1.4 collective-permute-start.14
  160.9 1.3 collective-permute-start.15
  162.2 4.3 %collective-permute-done.15 = bf16[8,1,16,128]{3,2,1,0:T(8,128)(2,1)S(1)} collective-permute-done((bf16[8,1,16,128]{3,2,1,0:T(8,128)(2,1)S(1)}, bf16[8,1,16,128]{3,2,1,0:T(8,128)(2,1)S(1)}, u32[]{:S(2)}, u32[]{:S(2)}) %collective-permute-start.15) | collective-permute-done | bytes 32800 | tf_op jit(solution)/shard_map/ppermute | solution.py:23
  166.6 3.8 %collective-permute-start.16 = (bf16[8,18,1,128]{3,2,1,0:T(2,128)(2,1)S(1)}, bf16[8,18,1,128]{3,2,1,0:T(2,128)(2,1)S(1)}, u32[]{:S(2)}, u32[]{:S(2)}) collective-permute-start(bf16[8,18,1,128]{3,2,1,0:T(2,128)(2,1)S(1)} %get-tuple-element.27), channel_id=1, source_target_pairs={{0,1},{1,2},{2,3},{3,4},{4,5},{5,6},{6,7},{8,9},{9,10},{10,11},{11... | collective-permute-start | bytes 110600 | tf_op jit(solution)/shard_map/ppermute | solution.py:21
  170.4 1.3 collective-permute-start.17
  171.7 0.7 collective-permute-done.16
  172.4 4.3 %collective-permute-done.17 = bf16[8,18,1,128]{3,2,1,0:T(2,128)(2,1)S(1)} collective-permute-done((bf16[8,18,1,128]{3,2,1,0:T(2,128)(2,1)S(1)}, bf16[8,18,1,128]{3,2,1,0:T(2,128)(2,1)S(1)}, u32[]{:S(2)}, u32[]{:S(2)}) %collective-permute-start.17) | collective-permute-done | bytes 36896 | tf_op jit(solution)/shard_map/ppermute | solution.py:23
  177.2 2.3 multiply_reduce_fusion.1
  179.5 41.7 %psum.45 = f32[8]{0:T(128)} all-reduce(f32[8]{0:T(128)S(1)} %get-tuple-element.12), channel_id=1, replica_groups=mesh['gz'=4,'yx'=8] {'gz','yx'}, use_global_device_ids=true, to_apply=%region_7.8 | all-reduce | flops 8 | bytes 64 | tf_op jit(solution)/shard_map/psum | solution.py:136
  221.2 0.6 div.21
  221.8 1.5 multiply_reduce_fusion
  223.3 38.9 %psum.46 = f32[8]{0:T(128)} all-reduce(f32[8]{0:T(128)S(1)} %multiply_reduce_fusion), channel_id=1, replica_groups=mesh['gz'=4,'yx'=8] {'gz','yx'}, use_global_device_ids=true, to_apply=%region_9.10 | all-reduce | flops 8 | bytes 64 | tf_op jit(solution)/shard_map/psum | solution.py:90
  262.2 0.7 div.22
  262.9 1.5 fusion.201
  264.5 1.4 collective-permute-start.18
  266.0 1.3 collective-permute-start.19
  267.3 4.3 %collective-permute-done.19 = bf16[8,1,16,128]{3,2,1,0:T(8,128)(2,1)S(1)} collective-permute-done((bf16[8,1,16,128]{3,2,1,0:T(8,128)(2,1)S(1)}, bf16[8,1,16,128]{3,2,1,0:T(8,128)(2,1)S(1)}, u32[]{:S(2)}, u32[]{:S(2)}) %collective-permute-start.19) | collective-permute-done | bytes 32800 | tf_op jit(solution)/shard_map/ppermute | solution.py:23
  271.7 3.9 %collective-permute-start.20 = (bf16[8,18,1,128]{3,2,1,0:T(2,128)(2,1)S(1)}, bf16[8,18,1,128]{3,2,1,0:T(2,128)(2,1)S(1)}, u32[]{:S(2)}, u32[]{:S(2)}) collective-permute-start(bf16[8,18,1,128]{3,2,1,0:T(2,128)(2,1)S(1)} %get-tuple-element.25), channel_id=1, source_target_pairs={{0,1},{1,2},{2,3},{3,4},{4,5},{5,6},{6,7},{8,9},{9,10},{10,11},{11... | collective-permute-start | bytes 110600 | tf_op jit(solution)/shard_map/ppermute | solution.py:21
  275.6 1.6 collective-permute-start.21
  277.6 4.3 %collective-permute-done.21 = bf16[8,18,1,128]{3,2,1,0:T(2,128)(2,1)S(1)} collective-permute-done((bf16[8,18,1,128]{3,2,1,0:T(2,128)(2,1)S(1)}, bf16[8,18,1,128]{3,2,1,0:T(2,128)(2,1)S(1)}, u32[]{:S(2)}, u32[]{:S(2)}) %collective-permute-start.21) | collective-permute-done | bytes 36896 | tf_op jit(solution)/shard_map/ppermute | solution.py:23
  282.4 1.5 fusion.133
  283.9 41.3 %psum.47 = f32[8]{0:T(128)S(1)} all-reduce(f32[8]{0:T(128)S(1)} %fusion.133), channel_id=1, replica_groups=mesh['gz'=4,'yx'=8] {'gz','yx'}, use_global_device_ids=true, to_apply=%region_11.12 | all-reduce | flops 8 | bytes 64 | tf_op jit(solution)/shard_map/psum | solution.py:136
  325.2 2.5 convert_add_fusion
  (115 shorter events, 9.4 us)
Async XLA Ops:
  0.6 14.4 %copy-start.1 = (bf16[16,16,16,128]{3,2,1,0:T(8,128)(2,1)S(1)}, bf16[16,16,16,128]{3,2,1,0:T(8,128)(2,1)}, u32[]{:S(2)}) copy-start(bf16[16,16,16,128]{3,2,1,0:T(8,128)(2,1)} %param.4) | copy-start | bytes 3145732
  0.6 7.6 %copy-start.17 = (s32[16,16,128]{2,1,0:T(8,128)S(1)}, s32[16,16,128]{2,1,0:T(8,128)}, u32[]{:S(2)}) copy-start(s32[16,16,128]{2,1,0:T(8,128)} %param.7) | copy-start | bytes 393220
  0.7 14.2 %copy-start.20 = (bf16[3,16,3,3,3]{1,4,3,2,0:T(4,128)(2,1)S(1)}, bf16[3,16,3,3,3]{1,4,3,2,0:T(4,128)(2,1)}, u32[]{:S(2)}) copy-start(bf16[3,16,3,3,3]{1,4,3,2,0:T(4,128)(2,1)} %param.5) | copy-start | bytes 7780
  4.5 18.3 %collective-permute-start = (bf16[16,1,16,128]{3,0,2,1:T(8,128)(2,1)S(1)}, bf16[16,1,16,128]{3,0,2,1:T(8,128)(2,1)S(1)}, u32[]{:S(2)}, u32[]{:S(2)}) collective-permute-start(bf16[16,1,16,128]{3,0,2,1:T(8,128)(2,1)S(1)} %get-tuple-element.24), channel_id=1, source_target_pairs={{0,8},{8,16},{16,24},{1,9},{9,17},{17,25},{2,10},{10,18},{18,26},{... | collective-permute-start | bytes 196616 | tf_op jit(solution)/shard_map/ppermute | solution.py:21
  6.9 16.6 %collective-permute-start.1 = (bf16[16,1,16,128]{3,0,2,1:T(8,128)(2,1)S(1)}, bf16[16,1,16,128]{3,0,2,1:T(8,128)(2,1)S(1)}, u32[]{:S(2)}, u32[]{:S(2)}) collective-permute-start(bf16[16,1,16,128]{3,0,2,1:T(8,128)(2,1)S(1)} %get-tuple-element.23), channel_id=1, source_target_pairs={{8,0},{16,8},{24,16},{9,1},{17,9},{25,17},{10,2},{18,10},{26,18},{... | collective-permute-start | bytes 196616 | tf_op jit(solution)/shard_map/ppermute | solution.py:23
  8.4 7.3 %collective-permute-start.4 = (bf16[8,1,16,128]{3,2,1,0:T(8,128)(2,1)S(1)}, bf16[8,1,16,128]{3,2,1,0:T(8,128)(2,1)S(1)}, u32[]{:S(2)}, u32[]{:S(2)}) collective-permute-start(bf16[8,1,16,128]{3,2,1,0:T(8,128)(2,1)S(1)} %get-tuple-element.43), channel_id=1, source_target_pairs={{0,8},{8,16},{16,24},{1,9},{9,17},{17,25},{2,10},{10,18},{18,26},{... | collective-permute-start | bytes 98312 | tf_op jit(solution)/shard_map/ppermute | solution.py:21
  13.6 4.3 %collective-permute-start.5 = (bf16[8,1,16,128]{3,2,1,0:T(8,128)(2,1)S(1)}, bf16[8,1,16,128]{3,2,1,0:T(8,128)(2,1)S(1)}, u32[]{:S(2)}, u32[]{:S(2)}) collective-permute-start(bf16[8,1,16,128]{3,2,1,0:T(8,128)(2,1)S(1)} %get-tuple-element.44), channel_id=1, source_target_pairs={{8,0},{16,8},{24,16},{9,1},{17,9},{25,17},{10,2},{18,10},{26,18},{... | collective-permute-start | bytes 98312 | tf_op jit(solution)/shard_map/ppermute | solution.py:23
  18.0 14.6 %collective-permute-start.6 = (bf16[8,18,1,128]{3,2,1,0:T(2,128)(2,1)S(1)}, bf16[8,18,1,128]{3,2,1,0:T(2,128)(2,1)S(1)}, u32[]{:S(2)}, u32[]{:S(2)}) collective-permute-start(bf16[8,18,1,128]{3,2,1,0:T(2,128)(2,1)S(1)} %get-tuple-element.31), channel_id=1, source_target_pairs={{0,1},{1,2},{2,3},{3,4},{4,5},{5,6},{6,7},{8,9},{9,10},{10,11},{11... | collective-permute-start | bytes 110600 | tf_op jit(solution)/shard_map/ppermute | solution.py:21
  21.5 11.2 %collective-permute-start.7 = (bf16[8,18,1,128]{3,2,1,0:T(2,128)(2,1)S(1)}, bf16[8,18,1,128]{3,2,1,0:T(2,128)(2,1)S(1)}, u32[]{:S(2)}, u32[]{:S(2)}) collective-permute-start(bf16[8,18,1,128]{3,2,1,0:T(2,128)(2,1)S(1)} %get-tuple-element.32), channel_id=1, source_target_pairs={{1,0},{2,1},{3,2},{4,3},{5,4},{6,5},{7,6},{9,8},{10,9},{11,10},{12... | collective-permute-start | bytes 110600 | tf_op jit(solution)/shard_map/ppermute | solution.py:23
  23.6 9.5 %collective-permute-start.2 = (bf16[16,18,1,128]{3,0,2,1:T(8,128)(2,1)S(1)}, bf16[16,18,1,128]{3,0,2,1:T(8,128)(2,1)S(1)}, u32[]{:S(2)}, u32[]{:S(2)}) collective-permute-start(bf16[16,18,1,128]{3,0,2,1:T(8,128)(2,1)S(1)} %get-tuple-element.21), channel_id=1, source_target_pairs={{0,1},{1,2},{2,3},{3,4},{4,5},{5,6},{6,7},{8,9},{9,10},{10,11},{11... | collective-permute-start | bytes 221192 | tf_op jit(solution)/shard_map/ppermute | solution.py:21
  28.2 6.7 %collective-permute-start.3 = (bf16[16,18,1,128]{3,0,2,1:T(8,128)(2,1)S(1)}, bf16[16,18,1,128]{3,0,2,1:T(8,128)(2,1)S(1)}, u32[]{:S(2)}, u32[]{:S(2)}) collective-permute-start(bf16[16,18,1,128]{3,0,2,1:T(8,128)(2,1)S(1)} %get-tuple-element.22), channel_id=1, source_target_pairs={{1,0},{2,1},{3,2},{4,3},{5,4},{6,5},{7,6},{9,8},{10,9},{11,10},{12... | collective-permute-start | bytes 221192 | tf_op jit(solution)/shard_map/ppermute | solution.py:23
  45.1 0.7 copy-start.21
  46.8 8.2 %copy-start.19 = (f32[3,16,16,128]{3,2,1,0:T(8,128)}, f32[3,16,16,128]{3,2,1,0:T(8,128)S(1)}, u32[]{:S(2)}) copy-start(f32[3,16,16,128]{3,2,1,0:T(8,128)S(1)} %copy.21) | copy-start | bytes 1179652
  46.9 8.8 %collective-permute-start.8 = (f32[16,128]{1,0:T(8,128)S(1)}, f32[16,128]{1,0:T(8,128)S(1)}, u32[]{:S(2)}, u32[]{:S(2)}) collective-permute-start(f32[16,128]{1,0:T(8,128)S(1)} %slice_bitcast_fusion), channel_id=1, source_target_pairs={{0,8},{8,16},{16,24},{1,9},{9,17},{17,25},{2,10},{10,18},{18,26},{... | collective-permute-start | bytes 24584 | tf_op jit(solution)/shard_map/ppermute | solution.py:33
  49.7 5.9 %collective-permute-start.9 = (f32[16,128]{1,0:T(8,128)S(1)}, f32[16,128]{1,0:T(8,128)S(1)}, u32[]{:S(2)}, u32[]{:S(2)}) collective-permute-start(f32[16,128]{1,0:T(8,128)S(1)} %bitcast.231), channel_id=1, source_target_pairs={{0,1},{1,2},{2,3},{3,4},{4,5},{5,6},{6,7},{8,9},{9,10},{10,11},{11... | collective-permute-start | bytes 24584 | tf_op jit(solution)/shard_map/ppermute | solution.py:33
  54.9 20.0 %copy-start.8 = (f32[1,16,16,128]{3,0,2,1:T(1,128)}, f32[1,16,16,128]{3,0,2,1:T(1,128)S(1)}, u32[]{:S(2)}) copy-start(f32[1,16,16,128]{3,0,2,1:T(1,128)S(1)} %get-tuple-element.39) | copy-start | bytes 393220
  54.9 20.0 %copy-start.11 = (f32[1,16,16,128]{3,0,2,1:T(1,128)}, f32[1,16,16,128]{3,0,2,1:T(1,128)S(1)}, u32[]{:S(2)}) copy-start(f32[1,16,16,128]{3,0,2,1:T(1,128)S(1)} %get-tuple-element.40) | copy-start | bytes 393220
  54.9 20.0 %copy-start.14 = (f32[1,16,16,128]{3,0,2,1:T(1,128)}, f32[1,16,16,128]{3,0,2,1:T(1,128)S(1)}, u32[]{:S(2)}) copy-start(f32[1,16,16,128]{3,0,2,1:T(1,128)S(1)} %get-tuple-element.42) | copy-start | bytes 393220
  55.6 19.3 %copy-start.2 = (f32[16,16,128]{2,1,0:T(8,128)}, f32[16,16,128]{2,1,0:T(8,128)S(1)}, u32[]{:S(2)}) copy-start(f32[16,16,128]{2,1,0:T(8,128)S(1)} %copy.23) | copy-start | bytes 393220
  55.7 19.3 %copy-start.5 = (f32[16,16,128]{2,1,0:T(8,128)}, f32[16,16,128]{2,1,0:T(8,128)S(1)}, u32[]{:S(2)}) copy-start(f32[16,16,128]{2,1,0:T(8,128)S(1)} %pad_maximum_fusion.8) | copy-start | bytes 393220
  57.1 4.7 %collective-permute-start.10 = (bf16[8,1,16,128]{3,2,1,0:T(8,128)(2,1)S(1)}, bf16[8,1,16,128]{3,2,1,0:T(8,128)(2,1)S(1)}, u32[]{:S(2)}, u32[]{:S(2)}) collective-permute-start(bf16[8,1,16,128]{3,2,1,0:T(8,128)(2,1)S(1)} %get-tuple-element.37), channel_id=1, source_target_pairs={{0,8},{8,16},{16,24},{1,9},{9,17},{17,25},{2,10},{10,18},{18,26},{... | collective-permute-start | bytes 98312 | tf_op jit(solution)/shard_map/ppermute | solution.py:21
  60.5 3.1 collective-permute-start.11
  63.8 6.2 %collective-permute-start.12 = (bf16[8,18,1,128]{3,2,1,0:T(2,128)(2,1)S(1)}, bf16[8,18,1,128]{3,2,1,0:T(2,128)(2,1)S(1)}, u32[]{:S(2)}, u32[]{:S(2)}) collective-permute-start(bf16[8,18,1,128]{3,2,1,0:T(2,128)(2,1)S(1)} %get-tuple-element.29), channel_id=1, source_target_pairs={{0,1},{1,2},{2,3},{3,4},{4,5},{5,6},{6,7},{8,9},{9,10},{10,11},{11... | collective-permute-start | bytes 110600 | tf_op jit(solution)/shard_map/ppermute | solution.py:21
  68.0 6.5 %collective-permute-start.13 = (bf16[8,18,1,128]{3,2,1,0:T(2,128)(2,1)S(1)}, bf16[8,18,1,128]{3,2,1,0:T(2,128)(2,1)S(1)}, u32[]{:S(2)}, u32[]{:S(2)}) collective-permute-start(bf16[8,18,1,128]{3,2,1,0:T(2,128)(2,1)S(1)} %get-tuple-element.30), channel_id=1, source_target_pairs={{1,0},{2,1},{3,2},{4,3},{5,4},{6,5},{7,6},{9,8},{10,9},{11,10},{12... | collective-permute-start | bytes 110600 | tf_op jit(solution)/shard_map/ppermute | solution.py:23
  119.3 0.5 copy-start.24
  158.4 62.7 %copy-start.23 = (f32[8]{0:T(128)}, f32[8]{0:T(128)S(1)}, u32[]{:S(2)}) copy-start(f32[8]{0:T(128)S(1)} %psum.44) | copy-start | bytes 100
  159.4 17.8 %copy-start.3 = (f32[16,16,128]{2,1,0:T(8,128)S(1)}, f32[16,16,128]{2,1,0:T(8,128)}, u32[]{:S(2)}) copy-start(f32[16,16,128]{2,1,0:T(8,128)} %copy-done.2) | copy-start | bytes 393220
  159.4 17.8 %copy-start.6 = (f32[16,16,128]{2,1,0:T(8,128)S(1)}, f32[16,16,128]{2,1,0:T(8,128)}, u32[]{:S(2)}) copy-start(f32[16,16,128]{2,1,0:T(8,128)} %copy-done.5) | copy-start | bytes 393220
  159.4 17.8 %copy-start.9 = (f32[1,16,16,128]{3,0,2,1:T(1,128)S(1)}, f32[1,16,16,128]{3,0,2,1:T(1,128)}, u32[]{:S(2)}) copy-start(f32[1,16,16,128]{3,0,2,1:T(1,128)} %copy-done.8) | copy-start | bytes 393220
  159.4 17.8 %copy-start.12 = (f32[1,16,16,128]{3,0,2,1:T(1,128)S(1)}, f32[1,16,16,128]{3,0,2,1:T(1,128)}, u32[]{:S(2)}) copy-start(f32[1,16,16,128]{3,0,2,1:T(1,128)} %copy-done.11) | copy-start | bytes 393220
  159.4 17.8 %copy-start.15 = (f32[1,16,16,128]{3,0,2,1:T(1,128)S(1)}, f32[1,16,16,128]{3,0,2,1:T(1,128)}, u32[]{:S(2)}) copy-start(f32[1,16,16,128]{3,0,2,1:T(1,128)} %copy-done.14) | copy-start | bytes 393220
  159.4 2.7 collective-permute-start.14
  160.9 5.6 %collective-permute-start.15 = (bf16[8,1,16,128]{3,2,1,0:T(8,128)(2,1)S(1)}, bf16[8,1,16,128]{3,2,1,0:T(8,128)(2,1)S(1)}, u32[]{:S(2)}, u32[]{:S(2)}) collective-permute-start(bf16[8,1,16,128]{3,2,1,0:T(8,128)(2,1)S(1)} %get-tuple-element.36), channel_id=1, source_target_pairs={{8,0},{16,8},{24,16},{9,1},{17,9},{25,17},{10,2},{18,10},{26,18},{... | collective-permute-start | bytes 98312 | tf_op jit(solution)/shard_map/ppermute | solution.py:23
  166.6 5.8 %collective-permute-start.16 = (bf16[8,18,1,128]{3,2,1,0:T(2,128)(2,1)S(1)}, bf16[8,18,1,128]{3,2,1,0:T(2,128)(2,1)S(1)}, u32[]{:S(2)}, u32[]{:S(2)}) collective-permute-start(bf16[8,18,1,128]{3,2,1,0:T(2,128)(2,1)S(1)} %get-tuple-element.27), channel_id=1, source_target_pairs={{0,1},{1,2},{2,3},{3,4},{4,5},{5,6},{6,7},{8,9},{9,10},{10,11},{11... | collective-permute-start | bytes 110600 | tf_op jit(solution)/shard_map/ppermute | solution.py:21
  170.4 6.2 %collective-permute-start.17 = (bf16[8,18,1,128]{3,2,1,0:T(2,128)(2,1)S(1)}, bf16[8,18,1,128]{3,2,1,0:T(2,128)(2,1)S(1)}, u32[]{:S(2)}, u32[]{:S(2)}) collective-permute-start(bf16[8,18,1,128]{3,2,1,0:T(2,128)(2,1)S(1)} %get-tuple-element.28), channel_id=1, source_target_pairs={{1,0},{2,1},{3,2},{4,3},{5,4},{6,5},{7,6},{9,8},{10,9},{11,10},{12... | collective-permute-start | bytes 110600 | tf_op jit(solution)/shard_map/ppermute | solution.py:23
  264.4 17.9 %copy-start = (f32[8,16,16,128]{3,2,1,0:T(8,128)}, f32[8,16,16,128]{3,2,1,0:T(8,128)S(1)}, u32[]{:S(2)}) copy-start(f32[8,16,16,128]{3,2,1,0:T(8,128)S(1)} %get-tuple-element.11) | copy-start | bytes 3145732
  264.5 17.9 %copy-start.4 = (f32[16,16,128]{2,1,0:T(8,128)S(1)}, f32[16,16,128]{2,1,0:T(8,128)}, u32[]{:S(2)}) copy-start(f32[16,16,128]{2,1,0:T(8,128)} %copy-done.2) | copy-start | bytes 393220
  264.5 17.9 %copy-start.7 = (f32[16,16,128]{2,1,0:T(8,128)S(1)}, f32[16,16,128]{2,1,0:T(8,128)}, u32[]{:S(2)}) copy-start(f32[16,16,128]{2,1,0:T(8,128)} %copy-done.5) | copy-start | bytes 393220
  264.5 17.9 %copy-start.10 = (f32[1,16,16,128]{3,0,2,1:T(1,128)S(1)}, f32[1,16,16,128]{3,0,2,1:T(1,128)}, u32[]{:S(2)}) copy-start(f32[1,16,16,128]{3,0,2,1:T(1,128)} %copy-done.8) | copy-start | bytes 393220
  264.5 17.9 %copy-start.13 = (f32[1,16,16,128]{3,0,2,1:T(1,128)S(1)}, f32[1,16,16,128]{3,0,2,1:T(1,128)}, u32[]{:S(2)}) copy-start(f32[1,16,16,128]{3,0,2,1:T(1,128)} %copy-done.11) | copy-start | bytes 393220
  264.5 17.9 %copy-start.16 = (f32[1,16,16,128]{3,0,2,1:T(1,128)S(1)}, f32[1,16,16,128]{3,0,2,1:T(1,128)}, u32[]{:S(2)}) copy-start(f32[1,16,16,128]{3,0,2,1:T(1,128)} %copy-done.14) | copy-start | bytes 393220
  264.5 2.7 collective-permute-start.18
  266.0 5.6 %collective-permute-start.19 = (bf16[8,1,16,128]{3,2,1,0:T(8,128)(2,1)S(1)}, bf16[8,1,16,128]{3,2,1,0:T(8,128)(2,1)S(1)}, u32[]{:S(2)}, u32[]{:S(2)}) collective-permute-start(bf16[8,1,16,128]{3,2,1,0:T(8,128)(2,1)S(1)} %get-tuple-element.34), channel_id=1, source_target_pairs={{8,0},{16,8},{24,16},{9,1},{17,9},{25,17},{10,2},{18,10},{26,18},{... | collective-permute-start | bytes 98312 | tf_op jit(solution)/shard_map/ppermute | solution.py:23
  271.7 5.9 %collective-permute-start.20 = (bf16[8,18,1,128]{3,2,1,0:T(2,128)(2,1)S(1)}, bf16[8,18,1,128]{3,2,1,0:T(2,128)(2,1)S(1)}, u32[]{:S(2)}, u32[]{:S(2)}) collective-permute-start(bf16[8,18,1,128]{3,2,1,0:T(2,128)(2,1)S(1)} %get-tuple-element.25), channel_id=1, source_target_pairs={{0,1},{1,2},{2,3},{3,4},{4,5},{5,6},{6,7},{8,9},{9,10},{10,11},{11... | collective-permute-start | bytes 110600 | tf_op jit(solution)/shard_map/ppermute | solution.py:21
  275.6 6.2 %collective-permute-start.21 = (bf16[8,18,1,128]{3,2,1,0:T(2,128)(2,1)S(1)}, bf16[8,18,1,128]{3,2,1,0:T(2,128)(2,1)S(1)}, u32[]{:S(2)}, u32[]{:S(2)}) collective-permute-start(bf16[8,18,1,128]{3,2,1,0:T(2,128)(2,1)S(1)} %get-tuple-element.26), channel_id=1, source_target_pairs={{1,0},{2,1},{3,2},{4,3},{5,4},{6,5},{7,6},{9,8},{10,9},{11,10},{12... | collective-permute-start | bytes 110600 | tf_op jit(solution)/shard_map/ppermute | solution.py:23
  282.4 42.8 %copy-start.22 = (f32[8]{0:T(128)S(1)}, f32[8]{0:T(128)}, u32[]{:S(2)}) copy-start(f32[8]{0:T(128)} %psum.46) | copy-start | bytes 100
  282.4 42.8 %copy-start.18 = (s32[16,16,128]{2,1,0:T(8,128)S(1)}, s32[16,16,128]{2,1,0:T(8,128)}, u32[]{:S(2)}) copy-start(s32[16,16,128]{2,1,0:T(8,128)} %param.7) | copy-start | bytes 393220
where the time goes:
time: 329 us; the launch traced here: 328 us
  blocking collectives  203 us (62%)
  starting transfers between devices  54.6 us (17%)
  waiting for transfers between devices  29.5 us (9%)
  other arithmetic  19.6 us (6%)
  matrix products  13.6 us (4%)
  local copies, waits for them, and re-layouts  5.8 us (2%)
    psum x3, blocking collectives, squares(): return lax.psum(field_sums(residual, residual), ('gz', 'yx'))  120 us
    psum x2, blocking collectives, body(): curve = lax.psum(field_sums(direction, applied), ('gz', 'yx'))  83 us
    ppermute x10, starting transfers between devices, padded_2(): lax.ppermute(tail, axis, [(i, (i + 1) % count) for i in range(ends)])  33.7 us
    ppermute x10, waiting for transfers between devices, padded_2(): lax.ppermute(head, axis, [((i + 1) % count, i) for i in range(ends)])  27.5 us
    dot_general x27, matrix products, conv_region(): jnp.einsum('oc,czyx->ozyx', conv_weight[:, :, offset_z, offset_y, offset_...  13.6 us
    ppermute x10, starting transfers between devices, padded_2(): lax.ppermute(head, axis, [((i + 1) % count, i) for i in range(ends)])  13.4 us
    ppermute x2, starting transfers between devices, from_behind(): return lax.ppermute(value, axis, pairs)  7.57 us
    reduce_sum x5, other arithmetic, field_sums(): return jnp.sum(left * right, axis=(1, 2, 3))  7.21 us
  transfers between devices with their start and end apart: 22, of which 12 were waited for; matrix products, arithmetic and copies ran while one was open for 2% of the time, Pallas kernels for 0%

commit v1 on v0

--- a/solution.py
+++ b/solution.py
@@ -54,40 +54,32 @@
     return summed
 
 
-def stencil(field, padded, weights, seeded):
-    weight_zup, weight_zdown, weight_yup, weight_ydown, weight_xup, weight_xdown = weights
-    padded = jnp.pad(padded, ((0, 0), (0, 0), (0, 0), (1, 1)))
-    laplace = weight_zup * (field - padded[:, 2:, 1:-1, 1:-1]) + weight_zdown * (
-        field - padded[:, :-2, 1:-1, 1:-1]
-    )
-    laplace = (
-        laplace
-        + weight_yup * (field - padded[:, 1:-1, 2:, 1:-1])
-        + weight_ydown * (field - padded[:, 1:-1, :-2, 1:-1])
-    )
-    laplace = (
-        laplace
-        + weight_xup * (field - padded[:, 1:-1, 1:-1, 2:])
-        + weight_xdown * (field - padded[:, 1:-1, 1:-1, :-2])
-    )
-    return (1.0 - seeded) * (laplace + RIDGE_WEIGHT * field) + seeded * field
+def neighbours(field):
+    below_z = from_behind(field[:, -1], "gz", 1)
+    above_z = from_behind(field[:, 0], "gz", -1)
+    below_y = from_behind(field[:, :, -1], "yx", 1)
+    above_y = from_behind(field[:, :, 0], "yx", -1)
+    up_z = jnp.concatenate([field[:, 1:], above_z[:, None]], axis=1)
+    down_z = jnp.concatenate([below_z[:, None], field[:, :-1]], axis=1)
+    up_y = jnp.concatenate([field[:, :, 1:], above_y[:, :, None]], axis=2)
+    down_y = jnp.concatenate([below_y[:, :, None], field[:, :, :-1]], axis=2)
+    zero_col = jnp.zeros_like(field[..., :1])
+    up_x = jnp.concatenate([field[..., 1:], zero_col], axis=3)
+    down_x = jnp.concatenate([zero_col, field[..., :-1]], axis=3)
+    return up_z, down_z, up_y, down_y, up_x, down_x
 
 
 def operate(field, weights, seeded):
-    padded = padded_2(field.astype(jnp.bfloat16), (("gz", 1), ("yx", 2)), 1).astype(field.dtype)
-    return stencil(field, padded, weights, seeded)
+    weight_zup, weight_zdown, weight_yup, weight_ydown, weight_xup, weight_xdown = weights
+    up_z, down_z, up_y, down_y, up_x, down_x = neighbours(field)
+    laplace = weight_zup * (field - up_z) + weight_zdown * (field - down_z)
+    laplace = laplace + weight_yup * (field - up_y) + weight_ydown * (field - down_y)
+    laplace = laplace + weight_xup * (field - up_x) + weight_xdown * (field - down_x)
+    return (1.0 - seeded) * (laplace + RIDGE_WEIGHT * field) + seeded * field
 
 
 def field_sums(left, right):
     return jnp.sum(left * right, axis=(1, 2, 3))
-
-
-def spread_out(values):
-    return values[:, None, None, None]
-
-
-def squares(residual):
-    return lax.psum(field_sums(residual, residual), ("gz", "yx"))
 
 
 def body(features, conv_weight, conv_bias, labels):
@@ -126,21 +118,66 @@
     seeded = (labels > 0).astype(jnp.float32)[None]
     colours = jnp.arange(1, FIELDS + 1, dtype=jnp.int32)[:, None, None, None]
     seed_field = (labels[None] == colours).astype(jnp.float32)
-    right_side = seed_field - operate(seed_field, weights, seeded)
-    solution = jnp.zeros_like(right_side)
-    residual = right_side
-    direction = right_side
-    norm_now = squares(residual)
+
+    basis = [seed_field - operate(seed_field, weights, seeded)]
+    for power in range(ITERS):
+        basis.append(operate(basis[-1], weights, seeded))
+    size = ITERS + 1
+    pairs = [(i, j) for i in range(size) for j in range(i, size) if i < size - 1]
+    local = jnp.stack([field_sums(basis[i], basis[j]) for i, j in pairs])
+    total = lax.psum(local, ("gz", "yx"))
+    gram = {}
+    for index, (i, j) in enumerate(pairs):
+        gram[i, j] = total[index]
+        gram[j, i] = total[index]
+
+    zero = jnp.zeros((FIELDS,), jnp.float32)
+    one = jnp.ones((FIELDS,), jnp.float32)
+
+    def inner(left, right):
+        acc = zero
+        for i in range(size):
+            for j in range(size):
+                if (i, j) in gram and not (
+                    isinstance(left[i], float) or isinstance(right[j], float)
+                ):
+                    acc = acc + left[i] * gram[i, j] * right[j]
+        return acc
+
+    def shift(coeffs):
+        return [0.0] + coeffs[:-1]
+
+    def axpy(scale, left, right):
+        out = []
+        for a, b in zip(left, right):
+            if isinstance(b, float):
+                out.append(a)
+            elif isinstance(a, float):
+                out.append(scale * b)
+            else:
+                out.append(a + scale * b)
+        return out
+
+    residual = [one] + [0.0] * (size - 1)
+    direction = list(residual)
+    solution = [0.0] * size
+    norm_now = inner(residual, residual)
     for iteration in range(ITERS):
-        applied = operate(direction, weights, seeded)
-        curve = lax.psum(field_sums(direction, applied), ("gz", "yx"))
-        step_size = norm_now / curve
-        solution = solution + spread_out(step_size) * direction
-        residual = residual - spread_out(step_size) * applied
-        norm_next = squares(residual)
-        direction = residual + spread_out(norm_next / norm_now) * direction
+        applied = shift(direction)
+        step_size = norm_now / inner(direction, applied)
+        solution = axpy(step_size, solution, direction)
+        if iteration == ITERS - 1:
+            break
+        residual = axpy(-step_size, residual, applied)
+        norm_next = inner(residual, residual)
+        direction = axpy(norm_next / norm_now, residual, direction)
         norm_now = norm_next
-    return (seed_field + solution, affinities)
+
+    probabilities = seed_field
+    for coeff, vector in zip(solution, basis):
+        if not isinstance(coeff, float):
+            probabilities = probabilities + coeff[:, None, None, None] * vector
+    return (probabilities, affinities)
 
 
 def solution(mesh):

time: 329 us -> 160 us (0.49)
  blocking collectives: 203 us -> 42.8 us
  waiting for transfers between devices: 29.5 us -> 8.7 us
  starting transfers between devices: 54.6 us -> 64.9 us
  local copies, waits for them, and re-layouts: 5.8 us -> 15.3 us
  other arithmetic: 19.6 us -> 12.1 us
    psum x5 -> x1, blocking collectives: 203 us -> 42.8 us  [body(): total = lax.psum(local, ('gz', 'yx'))]
    ppermute x2 -> x18, starting transfers between devices: 7.57 us -> 54.8 us  [from_behind(): return lax.ppermute(value, axis, pairs)]
    ppermute x10 -> x2, waiting for transfers between devices: 27.5 us -> 0.01 us  [padded_2(): lax.ppermute(head, axis, [((i + 1) % count, i) for i in range(ends)])]
    ppermute x10 -> x2, starting transfers between devices: 33.7 us -> 7.56 us  [padded_2(): lax.ppermute(tail, axis, [(i, (i + 1) % count) for i in range(ends)])]
    ppermute x10 -> x2, starting transfers between devices: 13.4 us -> 2.57 us  [padded_2(): lax.ppermute(head, axis, [((i + 1) % count, i) for i in range(ends)])]
    ppermute x2 -> x18, waiting for transfers between devices: 0.26 us -> 8.69 us  [from_behind(): return lax.ppermute(value, axis, pairs)]
    slice x0 -> x16, local copies, waits for them, and re-layouts: none -> 6.38 us  [the longest x4 2.09 us: neighbours(): down_y = jnp.concatenate([below_y[:, :, None], field[:, :, :-1]], axis=2)]
    reduce_sum x5 -> x1, other arithmetic: 7.21 us -> 3.02 us  [field_sums(): return jnp.sum(left * right, axis=(1, 2, 3))]
  transfers between devices with their start and end apart: 22 -> 22, of which waited for: 12 -> 8; matrix products, arithmetic and copies ran while one was open for 2% -> 17% of each run, Pallas kernels for 0% -> 0%
where the time goes in v1:
time: 160 us; the launch traced here: 159 us
  starting transfers between devices  64.9 us (41%)
  blocking collectives  42.8 us (27%)
  local copies, waits for them, and re-layouts  15.3 us (10%)
  matrix products  13.7 us (9%)
  other arithmetic  12.1 us (8%)
  waiting for transfers between devices  8.7 us (5%)
  between operations  1.71 us (1%)
    ppermute x18, starting transfers between devices, from_behind(): return lax.ppermute(value, axis, pairs)  54.8 us
    psum x1, blocking collectives, body(): total = lax.psum(local, ('gz', 'yx'))  42.8 us
    dot_general x27, matrix products, conv_region(): jnp.einsum('oc,czyx->ozyx', conv_weight[:, :, offset_z, offset_y, offset_...  13.7 us
    ppermute x18, waiting for transfers between devices, from_behind(): return lax.ppermute(value, axis, pairs)  8.69 us
    ppermute x2, starting transfers between devices, padded_2(): lax.ppermute(tail, axis, [(i, (i + 1) % count) for i in range(ends)])  7.56 us
    unnamed x71, local copies, waits for them, and re-layouts  4.2 us
  transfers between devices with their start and end apart: 22, of which 8 were waited for; matrix products, arithmetic and copies ran while one was open for 17% of the time, Pallas kernels for 0%

profile of v1, /device:TPU:0, one launch (start us, length us, event | category | flops | bytes accessed | tf_op | source)
XLA Modules:
  0.0 159.2 jit_solution(2098768814768198746)
XLA Ops:
  0.6 1.9 %copy.31 = bf16[16,16,16,128]{3,0,2,1:T(8,128)(2,1)S(1)} copy(bf16[16,16,16,128]{3,2,1,0:T(8,128)(2,1)} %param.4) | data formatting | bytes 2097152 | tf_op args[0]
  2.6 0.7 fusion.225
  3.3 3.0 %collective-permute-start = (bf16[16,1,16,128]{3,0,2,1:T(8,128)(2,1)}, bf16[16,1,16,128]{3,0,2,1:T(8,128)(2,1)}, u32[]{:S(2)}, u32[]{:S(2)}) collective-permute-start(bf16[16,1,16,128]{3,0,2,1:T(8,128)(2,1)} %get-tuple-element.56), channel_id=1, source_target_pairs={{0,8},{8,16},{16,24},{1,9},{9,17},{17,25},{2,10},{10,18},{18,26},{... | collective-permute-start | bytes 196616 | tf_op jit(solution)/shard_map/ppermute | solution.py:21
  6.3 1.3 collective-permute-start.1
  7.6 1.1 compare_convert_fusion
  8.7 0.7 slice_bitcast_fusion.6
  9.3 1.3 collective-permute-start.4
  10.6 5.8 %collective-permute-start.6 = (f32[8,16,128]{2,1,0:T(8,128)}, f32[8,16,128]{2,1,0:T(8,128)}, u32[]{:S(2)}, u32[]{:S(2)}) collective-permute-start(f32[8,16,128]{2,1,0:T(8,128)} %get-tuple-element.63), channel_id=1, source_target_pairs={{0,8},{8,16},{16,24},{1,9},{9,17},{17,25},{2,10},{10,18},{18,26},{... | collective-permute-start | bytes 196616 | tf_op jit(solution)/shard_map/ppermute | solution.py:33
  16.4 0.7 fusion.227
  17.2 1.3 collective-permute-start.7
  18.5 0.7 fusion.230
  19.1 0.6 fusion.231
  19.7 0.3 fusion.226
  20.1 1.5 fusion.228
  21.6 1.4 fusion.229
  23.4 1.5 fusion.138
  24.9 0.9 constant_dynamic-update-slice_fusion.2
  25.9 0.7 constant_dynamic-update-slice_fusion.1
  26.6 0.9 constant_dynamic-update-slice_fusion
  27.5 4.6 %collective-permute-start.2 = (bf16[16,18,1,128]{3,0,2,1:T(8,128)(2,1)S(1)}, bf16[16,18,1,128]{3,0,2,1:T(8,128)(2,1)S(1)}, u32[]{:S(2)}, u32[]{:S(2)}) collective-permute-start(bf16[16,18,1,128]{3,0,2,1:T(8,128)(2,1)S(1)} %get-tuple-element.23), channel_id=1, source_target_pairs={{0,1},{1,2},{2,3},{3,4},{4,5},{5,6},{6,7},{8,9},{9,10},{10,11},{11... | collective-permute-start | bytes 221192 | tf_op jit(solution)/shard_map/ppermute | solution.py:21
  32.1 1.3 collective-permute-start.3
  33.4 1.1 fusion.37
  34.5 1.1 convolution_bitcast_fusion.1
  35.7 5.1 %collective-permute-start.9 = (f32[8,16,128]{2,1,0:T(8,128)S(1)}, f32[8,16,128]{2,1,0:T(8,128)S(1)}, u32[]{:S(2)}, u32[]{:S(2)}) collective-permute-start(f32[8,16,128]{2,1,0:T(8,128)S(1)} %bitcast.421), channel_id=1, source_target_pairs={{0,1},{1,2},{2,3},{3,4},{4,5},{5,6},{6,7},{8,9},{9,10},{10,11},{11... | collective-permute-start | bytes 196616 | tf_op jit(solution)/shard_map/ppermute | solution.py:33
  40.9 1.8 %fusion.5 = bf16[16,18,18,130]{3,0,2,1:T(8,128)(2,1)S(1)} fusion(bf16[16,18,1,128]{3,0,2,1:T(8,128)(2,1)S(1)} %collective-permute-done.3, bf16[16,18,16,128]{3,0,2,1:T(8,128)(2,1)S(1)} %constant_dynamic-update-slice_fusion, bf16[16,18,1,128]{3,0,2,1:T(8,128)(2,1)S(1)} %collective-permute-done.2), kind=kLoop, calls=%fused_computation.18 | loop fusion | flops 8087040 | bytes 2674944 | tf_op jit(solution)/shard_map/concatenate | solution.py:19
  43.0 0.5 fusion.71
  43.9 0.5 fusion.75
  44.7 0.5 fusion.79
  45.5 0.5 fusion.83
  46.0 0.5 convolution_bitcast_fusion.10
  47.1 0.5 convolution_bitcast_fusion.6
  47.9 0.5 convolution_bitcast_fusion.8
  48.7 0.5 convolution_bitcast_fusion.4
  50.3 0.9 fusion.29
  52.2 1.1 fusion.36
  53.4 5.1 %collective-permute-start.8 = (f32[16,128]{1,0:T(8,128)S(1)}, f32[16,128]{1,0:T(8,128)S(1)}, u32[]{:S(2)}, u32[]{:S(2)}) collective-permute-start(f32[16,128]{1,0:T(8,128)S(1)} %bitcast.430), channel_id=1, source_target_pairs={{0,1},{1,2},{2,3},{3,4},{4,5},{5,6},{6,7},{8,9},{9,10},{10,11},{11... | collective-permute-start | bytes 24584 | tf_op jit(solution)/shard_map/ppermute | solution.py:33
  58.5 0.5 slice_multiply_fusion.1
  59.3 0.5 collective-permute-done.8
  59.8 1.5 collective-permute-start.5
  61.4 0.5 collective-permute-done.5
  62.0 2.1 %convert_subtract_fusion.3 = f32[8,16,16,128]{3,2,1,0:T(8,128)S(1)} fusion(f32[8,1,16,128]{3,2,1,0:T(8,128)} %bitcast.43, f32[8,15,16,128]{3,2,1,0:T(8,128)S(1)} %copy-done.4, f32[8,15,16,128]{3,2,1,0:T(8,128)S(1)} %copy-done.3, f32[8,1,16,128]{3,2,1,0:T(8,128)} %bitcast.48, f32[8,16,1,128]{3,2,1,0:T(1,128)} %bitcast.51, f32[8,16,15,128]{3,2,1,0:T(8,128)S(1)} %copy-done.2, ...), kind=kLoop, calls=%fused_computation.6 | loop fusion | flops 7602176 | bytes 8503328 | tf_op jit(solution)/shard_map/sub | solution.py:122
  64.2 0.4 fusion.221
  64.8 1.3 collective-permute-start.10
  66.1 5.3 %collective-permute-start.11 = (f32[8,16,128]{2,1,0:T(8,128)S(1)}, f32[8,16,128]{2,1,0:T(8,128)S(1)}, u32[]{:S(2)}, u32[]{:S(2)}) collective-permute-start(f32[8,16,128]{2,1,0:T(8,128)S(1)} %get-tuple-element.51), channel_id=1, source_target_pairs={{0,8},{8,16},{16,24},{1,9},{9,17},{17,25},{2,10},{10,18},{18,26},{... | collective-permute-start | bytes 196616 | tf_op jit(solution)/shard_map/ppermute | solution.py:33
  71.4 1.3 collective-permute-start.12
  72.7 4.8 %collective-permute-start.13 = (f32[8,16,128]{2,1,0:T(8,128)S(1)}, f32[8,16,128]{2,1,0:T(8,128)S(1)}, u32[]{:S(2)}, u32[]{:S(2)}) collective-permute-start(f32[8,16,128]{2,1,0:T(8,128)S(1)} %bitcast.422), channel_id=1, source_target_pairs={{0,1},{1,2},{2,3},{3,4},{4,5},{5,6},{6,7},{8,9},{9,10},{10,11},{11... | collective-permute-start | bytes 196616 | tf_op jit(solution)/shard_map/ppermute | solution.py:33
  77.8 2.2 %collective-permute-done.13 = f32[8,16,128]{2,1,0:T(8,128)S(1)} collective-permute-done((f32[8,16,128]{2,1,0:T(8,128)S(1)}, f32[8,16,128]{2,1,0:T(8,128)S(1)}, u32[]{:S(2)}, u32[]{:S(2)}) %collective-permute-start.13) | collective-permute-done | bytes 65568 | tf_op jit(solution)/shard_map/ppermute | solution.py:33
  80.0 1.1 fusion.94
  81.8 1.3 collective-permute-start.14
  83.1 3.4 %collective-permute-start.15 = (f32[8,16,128]{2,1,0:T(8,128)S(1)}, f32[8,16,128]{2,1,0:T(8,128)S(1)}, u32[]{:S(2)}, u32[]{:S(2)}) collective-permute-start(f32[8,16,128]{2,1,0:T(8,128)S(1)} %get-tuple-element.41), channel_id=1, source_target_pairs={{0,8},{8,16},{16,24},{1,9},{9,17},{17,25},{2,10},{10,18},{18,26},{... | collective-permute-start | bytes 196616 | tf_op jit(solution)/shard_map/ppermute | solution.py:33
  86.5 1.3 collective-permute-start.16
  87.8 5.2 %collective-permute-start.17 = (f32[8,16,128]{2,1,0:T(8,128)S(1)}, f32[8,16,128]{2,1,0:T(8,128)S(1)}, u32[]{:S(2)}, u32[]{:S(2)}) collective-permute-start(f32[8,16,128]{2,1,0:T(8,128)S(1)} %bitcast.423), channel_id=1, source_target_pairs={{0,1},{1,2},{2,3},{3,4},{4,5},{5,6},{6,7},{8,9},{9,10},{10,11},{11... | collective-permute-start | bytes 196616 | tf_op jit(solution)/shard_map/ppermute | solution.py:33
  93.2 2.4 %collective-permute-done.17 = f32[8,16,128]{2,1,0:T(8,128)S(1)} collective-permute-done((f32[8,16,128]{2,1,0:T(8,128)S(1)}, f32[8,16,128]{2,1,0:T(8,128)S(1)}, u32[]{:S(2)}, u32[]{:S(2)}) %collective-permute-start.17) | collective-permute-done | bytes 65568 | tf_op jit(solution)/shard_map/ppermute | solution.py:33
  95.6 1.1 fusion.106
  96.7 0.3 fusion.213
  97.3 1.3 collective-permute-start.18
  98.6 3.2 %collective-permute-start.19 = (f32[8,16,128]{2,1,0:T(8,128)S(1)}, f32[8,16,128]{2,1,0:T(8,128)S(1)}, u32[]{:S(2)}, u32[]{:S(2)}) collective-permute-start(f32[8,16,128]{2,1,0:T(8,128)S(1)} %get-tuple-element.31), channel_id=1, source_target_pairs={{0,8},{8,16},{16,24},{1,9},{9,17},{17,25},{2,10},{10,18},{18,26},{... | collective-permute-start | bytes 196616 | tf_op jit(solution)/shard_map/ppermute | solution.py:33
  101.8 1.3 collective-permute-start.20
  103.1 5.2 %collective-permute-start.21 = (f32[8,16,128]{2,1,0:T(8,128)S(1)}, f32[8,16,128]{2,1,0:T(8,128)S(1)}, u32[]{:S(2)}, u32[]{:S(2)}) collective-permute-start(f32[8,16,128]{2,1,0:T(8,128)S(1)} %bitcast.424), channel_id=1, source_target_pairs={{0,1},{1,2},{2,3},{3,4},{4,5},{5,6},{6,7},{8,9},{9,10},{10,11},{11... | collective-permute-start | bytes 196616 | tf_op jit(solution)/shard_map/ppermute | solution.py:33
  108.6 2.7 %collective-permute-done.21 = f32[8,16,128]{2,1,0:T(8,128)S(1)} collective-permute-done((f32[8,16,128]{2,1,0:T(8,128)S(1)}, f32[8,16,128]{2,1,0:T(8,128)S(1)}, u32[]{:S(2)}, u32[]{:S(2)}) %collective-permute-start.21) | collective-permute-done | bytes 65568 | tf_op jit(solution)/shard_map/ppermute | solution.py:33
  111.3 3.0 %multiply_reduce_fusion = (f32[8]{0:T(128)S(1)}, f32[8]{0:T(128)S(1)}, f32[8]{0:T(128)S(1)}, f32[8]{0:T(128)}, f32[8]{0:T(128)}, /*index=5*/f32[8]{0:T(128)}, f32[8]{0:T(128)}, f32[8]{0:T(128)}, f32[8]{0:T(128)}) fusion(f32[8,16,16,128]{3,2,1,0:T(8,128)S(1)} %fusion.106, f32[8,16,16,128]{3,2,1,0:T(8,128)S(1)} %fusion.94, ...), kind=kLoop, calls=%fused_computation.163 | loop fusion | flops 11534264 | bytes 10469664 | tf_op jit(solution)/shard_map/reduce_sum | solution.py:82
  114.3 0.7 stack.39
  115.0 42.8 %psum.7 = f32[9,8]{1,0:T(8,128)S(1)} all-reduce(f32[9,8]{1,0:T(8,128)S(1)} %stack.39), channel_id=1, replica_groups=mesh['gz'=4,'yx'=8] {'gz','yx'}, use_global_device_ids=true, to_apply=%region_9.10 | all-reduce | flops 72 | bytes 576 | tf_op jit(solution)/shard_map/psum | solution.py:128
  157.9 1.3 fusion.54
  (132 shorter events, 7.2 us)
Async XLA Ops:
  0.6 17.8 %copy-start.11 = (bf16[3,16,3,3,3]{1,4,3,2,0:T(4,128)(2,1)S(1)}, bf16[3,16,3,3,3]{1,4,3,2,0:T(4,128)(2,1)}, u32[]{:S(2)}) copy-start(bf16[3,16,3,3,3]{1,4,3,2,0:T(4,128)(2,1)} %param.5) | copy-start | bytes 7780
  2.6 17.2 %copy-start.7 = (bf16[16,16,16,128]{3,0,2,1:T(8,128)(2,1)}, bf16[16,16,16,128]{3,0,2,1:T(8,128)(2,1)S(1)}, u32[]{:S(2)}) copy-start(bf16[16,16,16,128]{3,0,2,1:T(8,128)(2,1)S(1)} %copy.31) | copy-start | bytes 3145732
  3.3 21.6 %collective-permute-start = (bf16[16,1,16,128]{3,0,2,1:T(8,128)(2,1)}, bf16[16,1,16,128]{3,0,2,1:T(8,128)(2,1)}, u32[]{:S(2)}, u32[]{:S(2)}) collective-permute-start(bf16[16,1,16,128]{3,0,2,1:T(8,128)(2,1)} %get-tuple-element.56), channel_id=1, source_target_pairs={{0,8},{8,16},{16,24},{1,9},{9,17},{17,25},{2,10},{10,18},{18,26},{... | collective-permute-start | bytes 196616 | tf_op jit(solution)/shard_map/ppermute | solution.py:21
  6.3 20.3 %collective-permute-start.1 = (bf16[16,1,16,128]{3,0,2,1:T(8,128)(2,1)}, bf16[16,1,16,128]{3,0,2,1:T(8,128)(2,1)}, u32[]{:S(2)}, u32[]{:S(2)}) collective-permute-start(bf16[16,1,16,128]{3,0,2,1:T(8,128)(2,1)} %get-tuple-element.55), channel_id=1, source_target_pairs={{8,0},{16,8},{24,16},{9,1},{17,9},{25,17},{10,2},{18,10},{26,18},{... | collective-permute-start | bytes 196616 | tf_op jit(solution)/shard_map/ppermute | solution.py:23
  9.3 52.6 %collective-permute-start.4 = (f32[8,16,128]{2,1,0:T(8,128)}, f32[8,16,128]{2,1,0:T(8,128)}, u32[]{:S(2)}, u32[]{:S(2)}) collective-permute-start(f32[8,16,128]{2,1,0:T(8,128)} %get-tuple-element.64), channel_id=1, source_target_pairs={{8,0},{16,8},{24,16},{9,1},{17,9},{25,17},{10,2},{18,10},{26,18},{... | collective-permute-start | bytes 196616 | tf_op jit(solution)/shard_map/ppermute | solution.py:33
  10.6 51.4 %collective-permute-start.6 = (f32[8,16,128]{2,1,0:T(8,128)}, f32[8,16,128]{2,1,0:T(8,128)}, u32[]{:S(2)}, u32[]{:S(2)}) collective-permute-start(f32[8,16,128]{2,1,0:T(8,128)} %get-tuple-element.63), channel_id=1, source_target_pairs={{0,8},{8,16},{16,24},{1,9},{9,17},{17,25},{2,10},{10,18},{18,26},{... | collective-permute-start | bytes 196616 | tf_op jit(solution)/shard_map/ppermute | solution.py:33
  17.2 44.8 %collective-permute-start.7 = (f32[8,16,128]{2,1,0:T(8,128)}, f32[8,16,128]{2,1,0:T(8,128)}, u32[]{:S(2)}, u32[]{:S(2)}) collective-permute-start(f32[8,16,128]{2,1,0:T(8,128)} %bitcast.50), channel_id=1, source_target_pairs={{1,0},{2,1},{3,2},{4,3},{5,4},{6,5},{7,6},{9,8},{10,9},{11,10},{12... | collective-permute-start | bytes 196616 | tf_op jit(solution)/shard_map/ppermute | solution.py:33
  21.6 1.5 copy-start.5
  21.6 1.8 %copy-start = (bf16[16,16,16,128]{3,2,1,0:T(8,128)(2,1)S(1)}, bf16[16,16,16,128]{3,2,1,0:T(8,128)(2,1)}, u32[]{:S(2)}) copy-start(bf16[16,16,16,128]{3,2,1,0:T(8,128)(2,1)} %param.4) | copy-start | bytes 3145732
  24.9 8.5 %copy-start.8 = (bf16[16,16,16,128]{3,0,2,1:T(8,128)(2,1)S(1)}, bf16[16,16,16,128]{3,0,2,1:T(8,128)(2,1)}, u32[]{:S(2)}) copy-start(bf16[16,16,16,128]{3,0,2,1:T(8,128)(2,1)} %copy-done.7) | copy-start | bytes 3145732
  26.6 9.1 %copy-start.10 = (f32[8,16,1,128]{3,2,1,0:T(1,128)S(1)}, f32[8,16,1,128]{3,2,1,0:T(1,128)}, u32[]{:S(2)}) copy-start(f32[8,16,1,128]{3,2,1,0:T(1,128)} %get-tuple-element.59) | copy-start | bytes 196612
  27.5 8.1 %collective-permute-start.2 = (bf16[16,18,1,128]{3,0,2,1:T(8,128)(2,1)S(1)}, bf16[16,18,1,128]{3,0,2,1:T(8,128)(2,1)S(1)}, u32[]{:S(2)}, u32[]{:S(2)}) collective-permute-start(bf16[16,18,1,128]{3,0,2,1:T(8,128)(2,1)S(1)} %get-tuple-element.23), channel_id=1, source_target_pairs={{0,1},{1,2},{2,3},{3,4},{4,5},{5,6},{6,7},{8,9},{9,10},{10,11},{11... | collective-permute-start | bytes 221192 | tf_op jit(solution)/shard_map/ppermute | solution.py:21
  32.1 8.8 %collective-permute-start.3 = (bf16[16,18,1,128]{3,0,2,1:T(8,128)(2,1)S(1)}, bf16[16,18,1,128]{3,0,2,1:T(8,128)(2,1)S(1)}, u32[]{:S(2)}, u32[]{:S(2)}) collective-permute-start(bf16[16,18,1,128]{3,0,2,1:T(8,128)(2,1)S(1)} %get-tuple-element.24), channel_id=1, source_target_pairs={{1,0},{2,1},{3,2},{4,3},{5,4},{6,5},{7,6},{9,8},{10,9},{11,10},{12... | collective-permute-start | bytes 221192 | tf_op jit(solution)/shard_map/ppermute | solution.py:23
  34.5 8.2 %copy-start.25 = (bf16[3,16,1,1,1]{1,4,3,2,0:T(2,128)(2,1)S(1)}, bf16[3,16,1,1,1]{1,4,3,2,0:T(2,128)(2,1)}, u32[]{:S(2)}) copy-start(bf16[3,16,1,1,1]{1,4,3,2,0:T(2,128)(2,1)} %get-tuple-element.83) | copy-start | bytes 292
  35.7 7.3 %copy-start.24 = (bf16[3,16,1,1,1]{1,4,3,2,0:T(2,128)(2,1)S(1)}, bf16[3,16,1,1,1]{1,4,3,2,0:T(2,128)(2,1)}, u32[]{:S(2)}) copy-start(bf16[3,16,1,1,1]{1,4,3,2,0:T(2,128)(2,1)} %get-tuple-element.84) | copy-start | bytes 292
  35.7 26.3 %collective-permute-start.9 = (f32[8,16,128]{2,1,0:T(8,128)S(1)}, f32[8,16,128]{2,1,0:T(8,128)S(1)}, u32[]{:S(2)}, u32[]{:S(2)}) collective-permute-start(f32[8,16,128]{2,1,0:T(8,128)S(1)} %bitcast.421), channel_id=1, source_target_pairs={{0,1},{1,2},{2,3},{3,4},{4,5},{5,6},{6,7},{8,9},{9,10},{10,11},{11... | collective-permute-start | bytes 196616 | tf_op jit(solution)/shard_map/ppermute | solution.py:33
  42.7 0.8 copy-start.23
  42.7 1.1 copy-start.22
  43.0 1.3 copy-start.21
  43.5 1.1 copy-start.13
  43.8 1.3 copy-start.12
  44.7 1.3 copy-start.20
  45.2 1.3 copy-start.19
  45.5 1.3 copy-start.18
  46.0 1.1 copy-start.17
  46.5 1.1 copy-start.16
  46.8 1.1 copy-start.15
  47.1 1.3 copy-start.14
  47.9 1.3 copy-start.32
  48.4 1.1 copy-start.31
  48.7 1.1 copy-start.27
  49.3 1.0 copy-start.6
  50.3 0.9 copy-start.30
  50.3 1.3 copy-start.29
  51.2 0.6 copy-start.26
  51.3 0.9 copy-start.28
  51.3 0.9 copy-start.33
  52.2 9.8 %copy-start.4 = (f32[8,15,16,128]{3,2,1,0:T(8,128)S(1)}, f32[8,15,16,128]{3,2,1,0:T(8,128)}, u32[]{:S(2)}) copy-start(f32[8,15,16,128]{3,2,1,0:T(8,128)} %get-tuple-element.66) | copy-start | bytes 2949124
  53.3 8.7 %copy-start.1 = (f32[8,16,15,128]{3,2,1,0:T(8,128)S(1)}, f32[8,16,15,128]{3,2,1,0:T(8,128)}, u32[]{:S(2)}) copy-start(f32[8,16,15,128]{3,2,1,0:T(8,128)} %get-tuple-element.61) | copy-start | bytes 2949124
  53.3 8.7 %copy-start.2 = (f32[8,16,15,128]{3,2,1,0:T(8,128)S(1)}, f32[8,16,15,128]{3,2,1,0:T(8,128)}, u32[]{:S(2)}) copy-start(f32[8,16,15,128]{3,2,1,0:T(8,128)} %get-tuple-element.62) | copy-start | bytes 2949124
  53.3 8.7 %copy-start.3 = (f32[8,15,16,128]{3,2,1,0:T(8,128)S(1)}, f32[8,15,16,128]{3,2,1,0:T(8,128)}, u32[]{:S(2)}) copy-start(f32[8,15,16,128]{3,2,1,0:T(8,128)} %get-tuple-element.65) | copy-start | bytes 2949124
  53.4 5.1 %copy-start.9 = (f32[3,16,16,128]{3,2,1,0:T(8,128)}, f32[3,16,16,128]{3,2,1,0:T(8,128)S(1)}, u32[]{:S(2)}) copy-start(f32[3,16,16,128]{3,2,1,0:T(8,128)S(1)} %copy.38) | copy-start | bytes 1179652
  53.4 6.4 %collective-permute-start.8 = (f32[16,128]{1,0:T(8,128)S(1)}, f32[16,128]{1,0:T(8,128)S(1)}, u32[]{:S(2)}, u32[]{:S(2)}) collective-permute-start(f32[16,128]{1,0:T(8,128)S(1)} %bitcast.430), channel_id=1, source_target_pairs={{0,1},{1,2},{2,3},{3,4},{4,5},{5,6},{6,7},{8,9},{9,10},{10,11},{11... | collective-permute-start | bytes 24584 | tf_op jit(solution)/shard_map/ppermute | solution.py:33
  59.8 2.1 %collective-permute-start.5 = (f32[16,128]{1,0:T(8,128)S(1)}, f32[16,128]{1,0:T(8,128)S(1)}, u32[]{:S(2)}, u32[]{:S(2)}) collective-permute-start(f32[16,128]{1,0:T(8,128)S(1)} %slice_bitcast_fusion.8), channel_id=1, source_target_pairs={{0,8},{8,16},{16,24},{1,9},{9,17},{17,25},{2,10},{10,18},{18,26},{... | collective-permute-start | bytes 24584 | tf_op jit(solution)/shard_map/ppermute | solution.py:33
  64.8 12.9 %collective-permute-start.10 = (f32[8,16,128]{2,1,0:T(8,128)S(1)}, f32[8,16,128]{2,1,0:T(8,128)S(1)}, u32[]{:S(2)}, u32[]{:S(2)}) collective-permute-start(f32[8,16,128]{2,1,0:T(8,128)S(1)} %get-tuple-element.52), channel_id=1, source_target_pairs={{8,0},{16,8},{24,16},{9,1},{17,9},{25,17},{10,2},{18,10},{26,18},{... | collective-permute-start | bytes 196616 | tf_op jit(solution)/shard_map/ppermute | solution.py:33
  66.1 11.6 %collective-permute-start.11 = (f32[8,16,128]{2,1,0:T(8,128)S(1)}, f32[8,16,128]{2,1,0:T(8,128)S(1)}, u32[]{:S(2)}, u32[]{:S(2)}) collective-permute-start(f32[8,16,128]{2,1,0:T(8,128)S(1)} %get-tuple-element.51), channel_id=1, source_target_pairs={{0,8},{8,16},{16,24},{1,9},{9,17},{17,25},{2,10},{10,18},{18,26},{... | collective-permute-start | bytes 196616 | tf_op jit(solution)/shard_map/ppermute | solution.py:33
  71.4 6.4 %collective-permute-start.12 = (f32[8,16,128]{2,1,0:T(8,128)S(1)}, f32[8,16,128]{2,1,0:T(8,128)S(1)}, u32[]{:S(2)}, u32[]{:S(2)}) collective-permute-start(f32[8,16,128]{2,1,0:T(8,128)S(1)} %bitcast.425), channel_id=1, source_target_pairs={{1,0},{2,1},{3,2},{4,3},{5,4},{6,5},{7,6},{9,8},{10,9},{11,10},{12... | collective-permute-start | bytes 196616 | tf_op jit(solution)/shard_map/ppermute | solution.py:33
  72.7 7.3 %collective-permute-start.13 = (f32[8,16,128]{2,1,0:T(8,128)S(1)}, f32[8,16,128]{2,1,0:T(8,128)S(1)}, u32[]{:S(2)}, u32[]{:S(2)}) collective-permute-start(f32[8,16,128]{2,1,0:T(8,128)S(1)} %bitcast.422), channel_id=1, source_target_pairs={{0,1},{1,2},{2,3},{3,4},{4,5},{5,6},{6,7},{8,9},{9,10},{10,11},{11... | collective-permute-start | bytes 196616 | tf_op jit(solution)/shard_map/ppermute | solution.py:33
  81.8 11.3 %collective-permute-start.14 = (f32[8,16,128]{2,1,0:T(8,128)S(1)}, f32[8,16,128]{2,1,0:T(8,128)S(1)}, u32[]{:S(2)}, u32[]{:S(2)}) collective-permute-start(f32[8,16,128]{2,1,0:T(8,128)S(1)} %get-tuple-element.42), channel_id=1, source_target_pairs={{8,0},{16,8},{24,16},{9,1},{17,9},{25,17},{10,2},{18,10},{26,18},{... | collective-permute-start | bytes 196616 | tf_op jit(solution)/shard_map/ppermute | solution.py:33
  83.1 10.0 %collective-permute-start.15 = (f32[8,16,128]{2,1,0:T(8,128)S(1)}, f32[8,16,128]{2,1,0:T(8,128)S(1)}, u32[]{:S(2)}, u32[]{:S(2)}) collective-permute-start(f32[8,16,128]{2,1,0:T(8,128)S(1)} %get-tuple-element.41), channel_id=1, source_target_pairs={{0,8},{8,16},{16,24},{1,9},{9,17},{17,25},{2,10},{10,18},{18,26},{... | collective-permute-start | bytes 196616 | tf_op jit(solution)/shard_map/ppermute | solution.py:33
  86.5 6.8 %collective-permute-start.16 = (f32[8,16,128]{2,1,0:T(8,128)S(1)}, f32[8,16,128]{2,1,0:T(8,128)S(1)}, u32[]{:S(2)}, u32[]{:S(2)}) collective-permute-start(f32[8,16,128]{2,1,0:T(8,128)S(1)} %bitcast.426), channel_id=1, source_target_pairs={{1,0},{2,1},{3,2},{4,3},{5,4},{6,5},{7,6},{9,8},{10,9},{11,10},{12... | collective-permute-start | bytes 196616 | tf_op jit(solution)/shard_map/ppermute | solution.py:33
  87.8 7.8 %collective-permute-start.17 = (f32[8,16,128]{2,1,0:T(8,128)S(1)}, f32[8,16,128]{2,1,0:T(8,128)S(1)}, u32[]{:S(2)}, u32[]{:S(2)}) collective-permute-start(f32[8,16,128]{2,1,0:T(8,128)S(1)} %bitcast.423), channel_id=1, source_target_pairs={{0,1},{1,2},{2,3},{3,4},{4,5},{5,6},{6,7},{8,9},{9,10},{10,11},{11... | collective-permute-start | bytes 196616 | tf_op jit(solution)/shard_map/ppermute | solution.py:33
  97.3 11.1 %collective-permute-start.18 = (f32[8,16,128]{2,1,0:T(8,128)S(1)}, f32[8,16,128]{2,1,0:T(8,128)S(1)}, u32[]{:S(2)}, u32[]{:S(2)}) collective-permute-start(f32[8,16,128]{2,1,0:T(8,128)S(1)} %get-tuple-element.32), channel_id=1, source_target_pairs={{8,0},{16,8},{24,16},{9,1},{17,9},{25,17},{10,2},{18,10},{26,18},{... | collective-permute-start | bytes 196616 | tf_op jit(solution)/shard_map/ppermute | solution.py:33
  98.6 9.8 %collective-permute-start.19 = (f32[8,16,128]{2,1,0:T(8,128)S(1)}, f32[8,16,128]{2,1,0:T(8,128)S(1)}, u32[]{:S(2)}, u32[]{:S(2)}) collective-permute-start(f32[8,16,128]{2,1,0:T(8,128)S(1)} %get-tuple-element.31), channel_id=1, source_target_pairs={{0,8},{8,16},{16,24},{1,9},{9,17},{17,25},{2,10},{10,18},{18,26},{... | collective-permute-start | bytes 196616 | tf_op jit(solution)/shard_map/ppermute | solution.py:33
  101.8 6.8 %collective-permute-start.20 = (f32[8,16,128]{2,1,0:T(8,128)S(1)}, f32[8,16,128]{2,1,0:T(8,128)S(1)}, u32[]{:S(2)}, u32[]{:S(2)}) collective-permute-start(f32[8,16,128]{2,1,0:T(8,128)S(1)} %bitcast.427), channel_id=1, source_target_pairs={{1,0},{2,1},{3,2},{4,3},{5,4},{6,5},{7,6},{9,8},{10,9},{11,10},{12... | collective-permute-start | bytes 196616 | tf_op jit(solution)/shard_map/ppermute | solution.py:33
  103.1 8.2 %collective-permute-start.21 = (f32[8,16,128]{2,1,0:T(8,128)S(1)}, f32[8,16,128]{2,1,0:T(8,128)S(1)}, u32[]{:S(2)}, u32[]{:S(2)}) collective-permute-start(f32[8,16,128]{2,1,0:T(8,128)S(1)} %bitcast.424), channel_id=1, source_target_pairs={{0,1},{1,2},{2,3},{3,4},{4,5},{5,6},{6,7},{8,9},{9,10},{10,11},{11... | collective-permute-start | bytes 196616 | tf_op jit(solution)/shard_map/ppermute | solution.py:33

commit v2 on v1

--- a/solution.py
+++ b/solution.py
@@ -78,6 +78,19 @@
     return (1.0 - seeded) * (laplace + RIDGE_WEIGHT * field) + seeded * field
 
 
+def all_sum(value, axes):
+    for axis in axes:
+        devices = lax.axis_size(axis)
+        if devices & (devices - 1):
+            value = lax.psum(value, axis)
+            continue
+        hop = 1
+        while hop < devices:
+            value = value + lax.ppermute(value, axis, [(i, i ^ hop) for i in range(devices)])
+            hop *= 2
+    return value
+
+
 def field_sums(left, right):
     return jnp.sum(left * right, axis=(1, 2, 3))
 
@@ -125,7 +138,7 @@
     size = ITERS + 1
     pairs = [(i, j) for i in range(size) for j in range(i, size) if i < size - 1]
     local = jnp.stack([field_sums(basis[i], basis[j]) for i, j in pairs])
-    total = lax.psum(local, ("gz", "yx"))
+    total = all_sum(local, ("gz", "yx"))
     gram = {}
     for index, (i, j) in enumerate(pairs):
         gram[i, j] = total[index]

time: 160 us -> 137 us (0.86)
  blocking collectives: 42.8 us -> 0 us
  starting transfers between devices: 64.9 us -> 75.6 us
  waiting for transfers between devices: 8.7 us -> 17.5 us
    psum x1 -> x0, blocking collectives: 42.8 us -> none  [body(): total = lax.psum(local, ('gz', 'yx'))]
    ppermute x0 -> x5, starting transfers between devices: none -> 10.7 us  [all_sum(): lax.ppermute(value, axis, [(i, i ^ hop) for i in range(devices)])]
    ppermute x0 -> x5, waiting for transfers between devices: none -> 8.77 us  [all_sum(): lax.ppermute(value, axis, [(i, i ^ hop) for i in range(devices)])]
  transfers between devices with their start and end apart: 22 -> 27, of which waited for: 8 -> 13; matrix products, arithmetic and copies ran while one was open for 17% -> 20% of each run, Pallas kernels for 0% -> 0%
where the time goes in v2:
time: 137 us; the launch traced here: 136 us
  starting transfers between devices  75.6 us (55%)
  waiting for transfers between devices  17.5 us (13%)
  local copies, waits for them, and re-layouts  15.3 us (11%)
  matrix products  13.7 us (10%)
  other arithmetic  12.1 us (9%)
  between operations  1.72 us (1%)
    ppermute x18, starting transfers between devices, from_behind(): return lax.ppermute(value, axis, pairs)  54.8 us
    dot_general x27, matrix products, conv_region(): jnp.einsum('oc,czyx->ozyx', conv_weight[:, :, offset_z, offset_y, offset_...  13.7 us
    ppermute x5, starting transfers between devices, all_sum(): lax.ppermute(value, axis, [(i, i ^ hop) for i in range(devices)])  10.7 us
    ppermute x5, waiting for transfers between devices, all_sum(): lax.ppermute(value, axis, [(i, i ^ hop) for i in range(devices)])  8.77 us
    ppermute x18, waiting for transfers between devices, from_behind(): return lax.ppermute(value, axis, pairs)  8.69 us
    ppermute x2, starting transfers between devices, padded_2(): lax.ppermute(tail, axis, [(i, (i + 1) % count) for i in range(ends)])  7.57 us
    unnamed x71, local copies, waits for them, and re-layouts  4.2 us
    reduce_sum x1, other arithmetic, field_sums(): return jnp.sum(left * right, axis=(1, 2, 3))  2.99 us
  transfers between devices with their start and end apart: 27, of which 13 were waited for; matrix products, arithmetic and copies ran while one was open for 20% of the time, Pallas kernels for 0%

profile of v2, /device:TPU:0, one launch (start us, length us, event | category | flops | bytes accessed | tf_op | source)
XLA Modules:
  0.0 135.9 jit_solution(1386635695457217874)
XLA Ops:
  0.6 1.9 %copy.31 = bf16[16,16,16,128]{3,0,2,1:T(8,128)(2,1)S(1)} copy(bf16[16,16,16,128]{3,2,1,0:T(8,128)(2,1)} %param.4) | data formatting | bytes 2097152 | tf_op args[0]
  2.6 0.7 fusion.225
  3.3 3.0 %collective-permute-start = (bf16[16,1,16,128]{3,0,2,1:T(8,128)(2,1)}, bf16[16,1,16,128]{3,0,2,1:T(8,128)(2,1)}, u32[]{:S(2)}, u32[]{:S(2)}) collective-permute-start(bf16[16,1,16,128]{3,0,2,1:T(8,128)(2,1)} %get-tuple-element.56), channel_id=1, source_target_pairs={{0,8},{8,16},{16,24},{1,9},{9,17},{17,25},{2,10},{10,18},{18,26},{... | collective-permute-start | bytes 196616 | tf_op jit(solution)/shard_map/ppermute | solution.py:21
  6.3 1.3 collective-permute-start.1
  7.6 1.1 compare_convert_fusion
  8.7 0.7 slice_bitcast_fusion.6
  9.3 1.3 collective-permute-start.4
  10.6 5.8 %collective-permute-start.6 = (f32[8,16,128]{2,1,0:T(8,128)}, f32[8,16,128]{2,1,0:T(8,128)}, u32[]{:S(2)}, u32[]{:S(2)}) collective-permute-start(f32[8,16,128]{2,1,0:T(8,128)} %get-tuple-element.63), channel_id=1, source_target_pairs={{0,8},{8,16},{16,24},{1,9},{9,17},{17,25},{2,10},{10,18},{18,26},{... | collective-permute-start | bytes 196616 | tf_op jit(solution)/shard_map/ppermute | solution.py:33
  16.4 0.7 fusion.227
  17.1 1.3 collective-permute-start.7
  18.4 0.7 fusion.230
  19.1 0.6 fusion.231
  20.1 1.5 %fusion.228 = (f32[8,16,15,128]{3,2,1,0:T(8,128)}, f32[8,16,15,128]{3,2,1,0:T(8,128)}) fusion(f32[8,16,16,128]{3,2,1,0:T(8,128)S(1)} %compare_convert_fusion), kind=kLoop, calls=%fused_computation.324 | loop fusion | bytes 3932160 | tf_op jit(solution)/shard_map/slice | solution.py:65
  21.6 1.4 %fusion.229 = (f32[8,15,16,128]{3,2,1,0:T(8,128)}, f32[8,15,16,128]{3,2,1,0:T(8,128)}) fusion(f32[8,16,16,128]{3,2,1,0:T(8,128)S(1)} %compare_convert_fusion), kind=kLoop, calls=%fused_computation.325 | loop fusion | bytes 3932160 | tf_op jit(solution)/shard_map/slice | solution.py:63
  23.4 1.5 %fusion.138 = f32[3,16,16,128]{3,0,2,1:T(4,128)} fusion(bf16[3,16,1,1,1]{1,4,3,2,0:T(2,128)(2,1)S(1)} %get-tuple-element.82, bf16[16,16,16,128]{3,2,1,0:T(8,128)(2,1)S(1)} %copy-done), kind=kOutput, calls=%fused_computation.213 | convolution fusion | flops 3145728 | bytes 1441888 | tf_op jit(solution)/shard_map/oc,czyx->ozyx/dot_general | solution.py:48
  25.0 0.9 constant_dynamic-update-slice_fusion.2
  25.9 0.7 constant_dynamic-update-slice_fusion.1
  26.7 0.9 constant_dynamic-update-slice_fusion
  27.6 4.6 %collective-permute-start.2 = (bf16[16,18,1,128]{3,0,2,1:T(8,128)(2,1)S(1)}, bf16[16,18,1,128]{3,0,2,1:T(8,128)(2,1)S(1)}, u32[]{:S(2)}, u32[]{:S(2)}) collective-permute-start(bf16[16,18,1,128]{3,0,2,1:T(8,128)(2,1)S(1)} %get-tuple-element.23), channel_id=1, source_target_pairs={{0,1},{1,2},{2,3},{3,4},{4,5},{5,6},{6,7},{8,9},{9,10},{10,11},{11... | collective-permute-start | bytes 221192 | tf_op jit(solution)/shard_map/ppermute | solution.py:21
  32.1 1.3 collective-permute-start.3
  33.4 1.1 fusion.37
  34.6 1.1 convolution_bitcast_fusion.1
  35.7 5.1 %collective-permute-start.9 = (f32[8,16,128]{2,1,0:T(8,128)S(1)}, f32[8,16,128]{2,1,0:T(8,128)S(1)}, u32[]{:S(2)}, u32[]{:S(2)}) collective-permute-start(f32[8,16,128]{2,1,0:T(8,128)S(1)} %bitcast.421), channel_id=1, source_target_pairs={{0,1},{1,2},{2,3},{3,4},{4,5},{5,6},{6,7},{8,9},{9,10},{10,11},{11... | collective-permute-start | bytes 196616 | tf_op jit(solution)/shard_map/ppermute | solution.py:33
  40.9 1.8 %fusion.5 = bf16[16,18,18,130]{3,0,2,1:T(8,128)(2,1)S(1)} fusion(bf16[16,18,1,128]{3,0,2,1:T(8,128)(2,1)S(1)} %collective-permute-done.3, bf16[16,18,16,128]{3,0,2,1:T(8,128)(2,1)S(1)} %constant_dynamic-update-slice_fusion, bf16[16,18,1,128]{3,0,2,1:T(8,128)(2,1)S(1)} %collective-permute-done.2), kind=kLoop, calls=%fused_computation.18 | loop fusion | flops 8087040 | bytes 2674944 | tf_op jit(solution)/shard_map/concatenate | solution.py:19
  43.1 0.5 fusion.71
  43.9 0.5 fusion.75
  44.7 0.5 fusion.79
  46.0 0.5 convolution_bitcast_fusion.10
  50.3 0.8 fusion.29
  52.1 1.2 fusion.36
  53.4 5.1 %collective-permute-start.8 = (f32[16,128]{1,0:T(8,128)S(1)}, f32[16,128]{1,0:T(8,128)S(1)}, u32[]{:S(2)}, u32[]{:S(2)}) collective-permute-start(f32[16,128]{1,0:T(8,128)S(1)} %bitcast.430), channel_id=1, source_target_pairs={{0,1},{1,2},{2,3},{3,4},{4,5},{5,6},{6,7},{8,9},{9,10},{10,11},{11... | collective-permute-start | bytes 24584 | tf_op jit(solution)/shard_map/ppermute | solution.py:33
  59.3 0.5 collective-permute-done.8
  59.8 1.5 %collective-permute-start.5 = (f32[16,128]{1,0:T(8,128)S(1)}, f32[16,128]{1,0:T(8,128)S(1)}, u32[]{:S(2)}, u32[]{:S(2)}) collective-permute-start(f32[16,128]{1,0:T(8,128)S(1)} %slice_bitcast_fusion.8), channel_id=1, source_target_pairs={{0,8},{8,16},{16,24},{1,9},{9,17},{17,25},{2,10},{10,18},{18,26},{... | collective-permute-start | bytes 24584 | tf_op jit(solution)/shard_map/ppermute | solution.py:33
  61.4 0.5 collective-permute-done.5
  62.0 2.1 %convert_subtract_fusion.3 = f32[8,16,16,128]{3,2,1,0:T(8,128)S(1)} fusion(f32[8,1,16,128]{3,2,1,0:T(8,128)} %bitcast.43, f32[8,15,16,128]{3,2,1,0:T(8,128)S(1)} %copy-done.4, f32[8,15,16,128]{3,2,1,0:T(8,128)S(1)} %copy-done.3, f32[8,1,16,128]{3,2,1,0:T(8,128)} %bitcast.48, f32[8,16,1,128]{3,2,1,0:T(1,128)} %bitcast.51, f32[8,16,15,128]{3,2,1,0:T(8,128)S(1)} %copy-done.2, ...), kind=kLoop, calls=%fused_computation.6 | loop fusion | flops 7602176 | bytes 8503328 | tf_op jit(solution)/shard_map/sub | solution.py:135
  64.8 1.3 collective-permute-start.10
  66.1 5.3 %collective-permute-start.11 = (f32[8,16,128]{2,1,0:T(8,128)S(1)}, f32[8,16,128]{2,1,0:T(8,128)S(1)}, u32[]{:S(2)}, u32[]{:S(2)}) collective-permute-start(f32[8,16,128]{2,1,0:T(8,128)S(1)} %get-tuple-element.51), channel_id=1, source_target_pairs={{0,8},{8,16},{16,24},{1,9},{9,17},{17,25},{2,10},{10,18},{18,26},{... | collective-permute-start | bytes 196616 | tf_op jit(solution)/shard_map/ppermute | solution.py:33
  71.4 1.3 collective-permute-start.12
  72.7 4.8 %collective-permute-start.13 = (f32[8,16,128]{2,1,0:T(8,128)S(1)}, f32[8,16,128]{2,1,0:T(8,128)S(1)}, u32[]{:S(2)}, u32[]{:S(2)}) collective-permute-start(f32[8,16,128]{2,1,0:T(8,128)S(1)} %bitcast.422), channel_id=1, source_target_pairs={{0,1},{1,2},{2,3},{3,4},{4,5},{5,6},{6,7},{8,9},{9,10},{10,11},{11... | collective-permute-start | bytes 196616 | tf_op jit(solution)/shard_map/ppermute | solution.py:33
  77.9 2.2 %collective-permute-done.13 = f32[8,16,128]{2,1,0:T(8,128)S(1)} collective-permute-done((f32[8,16,128]{2,1,0:T(8,128)S(1)}, f32[8,16,128]{2,1,0:T(8,128)S(1)}, u32[]{:S(2)}, u32[]{:S(2)}) %collective-permute-start.13) | collective-permute-done | bytes 65568 | tf_op jit(solution)/shard_map/ppermute | solution.py:33
  80.1 1.1 fusion.94
  81.8 1.3 collective-permute-start.14
  83.1 3.4 %collective-permute-start.15 = (f32[8,16,128]{2,1,0:T(8,128)S(1)}, f32[8,16,128]{2,1,0:T(8,128)S(1)}, u32[]{:S(2)}, u32[]{:S(2)}) collective-permute-start(f32[8,16,128]{2,1,0:T(8,128)S(1)} %get-tuple-element.41), channel_id=1, source_target_pairs={{0,8},{8,16},{16,24},{1,9},{9,17},{17,25},{2,10},{10,18},{18,26},{... | collective-permute-start | bytes 196616 | tf_op jit(solution)/shard_map/ppermute | solution.py:33
  86.5 1.3 collective-permute-start.16
  87.8 5.2 %collective-permute-start.17 = (f32[8,16,128]{2,1,0:T(8,128)S(1)}, f32[8,16,128]{2,1,0:T(8,128)S(1)}, u32[]{:S(2)}, u32[]{:S(2)}) collective-permute-start(f32[8,16,128]{2,1,0:T(8,128)S(1)} %bitcast.423), channel_id=1, source_target_pairs={{0,1},{1,2},{2,3},{3,4},{4,5},{5,6},{6,7},{8,9},{9,10},{10,11},{11... | collective-permute-start | bytes 196616 | tf_op jit(solution)/shard_map/ppermute | solution.py:33
  93.3 2.4 %collective-permute-done.17 = f32[8,16,128]{2,1,0:T(8,128)S(1)} collective-permute-done((f32[8,16,128]{2,1,0:T(8,128)S(1)}, f32[8,16,128]{2,1,0:T(8,128)S(1)}, u32[]{:S(2)}, u32[]{:S(2)}) %collective-permute-start.17) | collective-permute-done | bytes 65568 | tf_op jit(solution)/shard_map/ppermute | solution.py:33
  95.6 1.1 fusion.106
  97.4 1.3 collective-permute-start.18
  98.7 3.2 %collective-permute-start.19 = (f32[8,16,128]{2,1,0:T(8,128)S(1)}, f32[8,16,128]{2,1,0:T(8,128)S(1)}, u32[]{:S(2)}, u32[]{:S(2)}) collective-permute-start(f32[8,16,128]{2,1,0:T(8,128)S(1)} %get-tuple-element.31), channel_id=1, source_target_pairs={{0,8},{8,16},{16,24},{1,9},{9,17},{17,25},{2,10},{10,18},{18,26},{... | collective-permute-start | bytes 196616 | tf_op jit(solution)/shard_map/ppermute | solution.py:33
  101.9 1.3 collective-permute-start.20
  103.2 5.2 %collective-permute-start.21 = (f32[8,16,128]{2,1,0:T(8,128)S(1)}, f32[8,16,128]{2,1,0:T(8,128)S(1)}, u32[]{:S(2)}, u32[]{:S(2)}) collective-permute-start(f32[8,16,128]{2,1,0:T(8,128)S(1)} %bitcast.424), channel_id=1, source_target_pairs={{0,1},{1,2},{2,3},{3,4},{4,5},{5,6},{6,7},{8,9},{9,10},{10,11},{11... | collective-permute-start | bytes 196616 | tf_op jit(solution)/shard_map/ppermute | solution.py:33
  108.6 2.7 %collective-permute-done.21 = f32[8,16,128]{2,1,0:T(8,128)S(1)} collective-permute-done((f32[8,16,128]{2,1,0:T(8,128)S(1)}, f32[8,16,128]{2,1,0:T(8,128)S(1)}, u32[]{:S(2)}, u32[]{:S(2)}) %collective-permute-start.21) | collective-permute-done | bytes 65568 | tf_op jit(solution)/shard_map/ppermute | solution.py:33
  111.3 3.0 %multiply_reduce_fusion = (f32[8]{0:T(128)S(1)}, f32[8]{0:T(128)S(1)}, f32[8]{0:T(128)S(1)}, f32[8]{0:T(128)}, f32[8]{0:T(128)}, /*index=5*/f32[8]{0:T(128)}, f32[8]{0:T(128)}, f32[8]{0:T(128)}, f32[8]{0:T(128)}) fusion(f32[8,16,16,128]{3,2,1,0:T(8,128)S(1)} %fusion.106, f32[8,16,16,128]{3,2,1,0:T(8,128)S(1)} %fusion.94, ...), kind=kLoop, calls=%fused_computation.163 | loop fusion | flops 11534264 | bytes 10469664 | tf_op jit(solution)/shard_map/reduce_sum | solution.py:95
  114.3 0.7 stack.39
  115.4 0.9 collective-permute-done.22
  116.3 0.6 collective-permute-start.23
  116.9 3.0 %collective-permute-done.23 = f32[9,8]{1,0:T(8,128)S(1)} collective-permute-done((f32[9,8]{1,0:T(8,128)S(1)}, f32[9,8]{1,0:T(8,128)S(1)}, u32[]{:S(2)}, u32[]{:S(2)}) %collective-permute-start.23) | collective-permute-done | bytes 320 | tf_op jit(solution)/shard_map/ppermute | solution.py:89
  119.9 2.5 %collective-permute-start.24 = (f32[9,8]{1,0:T(8,128)S(1)}, f32[9,8]{1,0:T(8,128)S(1)}, u32[]{:S(2)}, u32[]{:S(2)}) collective-permute-start(f32[9,8]{1,0:T(8,128)S(1)} %add.647), channel_id=1, source_target_pairs={{0,1},{1,0},{2,3},{3,2},{4,5},{5,4},{6,7},{7,6},{8,9},{9,8},{10,11... | collective-permute-start | bytes 872 | tf_op jit(solution)/shard_map/ppermute | solution.py:89
  122.4 1.6 %collective-permute-done.24 = f32[9,8]{1,0:T(8,128)S(1)} collective-permute-done((f32[9,8]{1,0:T(8,128)S(1)}, f32[9,8]{1,0:T(8,128)S(1)}, u32[]{:S(2)}, u32[]{:S(2)}) %collective-permute-start.24) | collective-permute-done | bytes 320 | tf_op jit(solution)/shard_map/ppermute | solution.py:89
  124.1 3.4 %collective-permute-start.25 = (f32[9,8]{1,0:T(8,128)S(1)}, f32[9,8]{1,0:T(8,128)S(1)}, u32[]{:S(2)}, u32[]{:S(2)}) collective-permute-start(f32[9,8]{1,0:T(8,128)S(1)} %add.648), channel_id=1, source_target_pairs={{0,2},{1,3},{2,0},{3,1},{4,6},{5,7},{6,4},{7,5},{8,10},{9,11},{10,... | collective-permute-start | bytes 872 | tf_op jit(solution)/shard_map/ppermute | solution.py:89
  127.5 1.6 %collective-permute-done.25 = f32[9,8]{1,0:T(8,128)S(1)} collective-permute-done((f32[9,8]{1,0:T(8,128)S(1)}, f32[9,8]{1,0:T(8,128)S(1)}, u32[]{:S(2)}, u32[]{:S(2)}) %collective-permute-start.25) | collective-permute-done | bytes 320 | tf_op jit(solution)/shard_map/ppermute | solution.py:89
  129.1 3.8 %collective-permute-start.26 = (f32[9,8]{1,0:T(8,128)S(1)}, f32[9,8]{1,0:T(8,128)S(1)}, u32[]{:S(2)}, u32[]{:S(2)}) collective-permute-start(f32[9,8]{1,0:T(8,128)S(1)} %add.649), channel_id=1, source_target_pairs={{0,4},{1,5},{2,6},{3,7},{4,0},{5,1},{6,2},{7,3},{8,12},{9,13},{10,... | collective-permute-start | bytes 872 | tf_op jit(solution)/shard_map/ppermute | solution.py:89
  132.9 1.6 %collective-permute-done.26 = f32[9,8]{1,0:T(8,128)S(1)} collective-permute-done((f32[9,8]{1,0:T(8,128)S(1)}, f32[9,8]{1,0:T(8,128)S(1)}, u32[]{:S(2)}, u32[]{:S(2)}) %collective-permute-start.26) | collective-permute-done | bytes 320 | tf_op jit(solution)/shard_map/ppermute | solution.py:89
  134.6 1.3 fusion.54
  (146 shorter events, 11.1 us)
Async XLA Ops:
  0.6 17.8 %copy-start.11 = (bf16[3,16,3,3,3]{1,4,3,2,0:T(4,128)(2,1)S(1)}, bf16[3,16,3,3,3]{1,4,3,2,0:T(4,128)(2,1)}, u32[]{:S(2)}) copy-start(bf16[3,16,3,3,3]{1,4,3,2,0:T(4,128)(2,1)} %param.5) | copy-start | bytes 7780
  2.6 17.2 %copy-start.7 = (bf16[16,16,16,128]{3,0,2,1:T(8,128)(2,1)}, bf16[16,16,16,128]{3,0,2,1:T(8,128)(2,1)S(1)}, u32[]{:S(2)}) copy-start(bf16[16,16,16,128]{3,0,2,1:T(8,128)(2,1)S(1)} %copy.31) | copy-start | bytes 3145732
  3.3 21.7 %collective-permute-start = (bf16[16,1,16,128]{3,0,2,1:T(8,128)(2,1)}, bf16[16,1,16,128]{3,0,2,1:T(8,128)(2,1)}, u32[]{:S(2)}, u32[]{:S(2)}) collective-permute-start(bf16[16,1,16,128]{3,0,2,1:T(8,128)(2,1)} %get-tuple-element.56), channel_id=1, source_target_pairs={{0,8},{8,16},{16,24},{1,9},{9,17},{17,25},{2,10},{10,18},{18,26},{... | collective-permute-start | bytes 196616 | tf_op jit(solution)/shard_map/ppermute | solution.py:21
  6.3 20.3 %collective-permute-start.1 = (bf16[16,1,16,128]{3,0,2,1:T(8,128)(2,1)}, bf16[16,1,16,128]{3,0,2,1:T(8,128)(2,1)}, u32[]{:S(2)}, u32[]{:S(2)}) collective-permute-start(bf16[16,1,16,128]{3,0,2,1:T(8,128)(2,1)} %get-tuple-element.55), channel_id=1, source_target_pairs={{8,0},{16,8},{24,16},{9,1},{17,9},{25,17},{10,2},{18,10},{26,18},{... | collective-permute-start | bytes 196616 | tf_op jit(solution)/shard_map/ppermute | solution.py:23
  9.3 52.6 %collective-permute-start.4 = (f32[8,16,128]{2,1,0:T(8,128)}, f32[8,16,128]{2,1,0:T(8,128)}, u32[]{:S(2)}, u32[]{:S(2)}) collective-permute-start(f32[8,16,128]{2,1,0:T(8,128)} %get-tuple-element.64), channel_id=1, source_target_pairs={{8,0},{16,8},{24,16},{9,1},{17,9},{25,17},{10,2},{18,10},{26,18},{... | collective-permute-start | bytes 196616 | tf_op jit(solution)/shard_map/ppermute | solution.py:33
  10.6 51.3 %collective-permute-start.6 = (f32[8,16,128]{2,1,0:T(8,128)}, f32[8,16,128]{2,1,0:T(8,128)}, u32[]{:S(2)}, u32[]{:S(2)}) collective-permute-start(f32[8,16,128]{2,1,0:T(8,128)} %get-tuple-element.63), channel_id=1, source_target_pairs={{0,8},{8,16},{16,24},{1,9},{9,17},{17,25},{2,10},{10,18},{18,26},{... | collective-permute-start | bytes 196616 | tf_op jit(solution)/shard_map/ppermute | solution.py:33
  17.1 44.8 %collective-permute-start.7 = (f32[8,16,128]{2,1,0:T(8,128)}, f32[8,16,128]{2,1,0:T(8,128)}, u32[]{:S(2)}, u32[]{:S(2)}) collective-permute-start(f32[8,16,128]{2,1,0:T(8,128)} %bitcast.50), channel_id=1, source_target_pairs={{1,0},{2,1},{3,2},{4,3},{5,4},{6,5},{7,6},{9,8},{10,9},{11,10},{12... | collective-permute-start | bytes 196616 | tf_op jit(solution)/shard_map/ppermute | solution.py:33
  21.6 1.5 %copy-start.5 = (s32[16,16,128]{2,1,0:T(8,128)S(1)}, s32[16,16,128]{2,1,0:T(8,128)}, u32[]{:S(2)}) copy-start(s32[16,16,128]{2,1,0:T(8,128)} %param.7) | copy-start | bytes 393220
  21.6 1.8 %copy-start = (bf16[16,16,16,128]{3,2,1,0:T(8,128)(2,1)S(1)}, bf16[16,16,16,128]{3,2,1,0:T(8,128)(2,1)}, u32[]{:S(2)}) copy-start(bf16[16,16,16,128]{3,2,1,0:T(8,128)(2,1)} %param.4) | copy-start | bytes 3145732
  24.9 8.5 %copy-start.8 = (bf16[16,16,16,128]{3,0,2,1:T(8,128)(2,1)S(1)}, bf16[16,16,16,128]{3,0,2,1:T(8,128)(2,1)}, u32[]{:S(2)}) copy-start(bf16[16,16,16,128]{3,0,2,1:T(8,128)(2,1)} %copy-done.7) | copy-start | bytes 3145732
  26.6 9.1 %copy-start.10 = (f32[8,16,1,128]{3,2,1,0:T(1,128)S(1)}, f32[8,16,1,128]{3,2,1,0:T(1,128)}, u32[]{:S(2)}) copy-start(f32[8,16,1,128]{3,2,1,0:T(1,128)} %get-tuple-element.59) | copy-start | bytes 196612
  27.6 8.1 %collective-permute-start.2 = (bf16[16,18,1,128]{3,0,2,1:T(8,128)(2,1)S(1)}, bf16[16,18,1,128]{3,0,2,1:T(8,128)(2,1)S(1)}, u32[]{:S(2)}, u32[]{:S(2)}) collective-permute-start(bf16[16,18,1,128]{3,0,2,1:T(8,128)(2,1)S(1)} %get-tuple-element.23), channel_id=1, source_target_pairs={{0,1},{1,2},{2,3},{3,4},{4,5},{5,6},{6,7},{8,9},{9,10},{10,11},{11... | collective-permute-start | bytes 221192 | tf_op jit(solution)/shard_map/ppermute | solution.py:21
  32.1 8.7 %collective-permute-start.3 = (bf16[16,18,1,128]{3,0,2,1:T(8,128)(2,1)S(1)}, bf16[16,18,1,128]{3,0,2,1:T(8,128)(2,1)S(1)}, u32[]{:S(2)}, u32[]{:S(2)}) collective-permute-start(bf16[16,18,1,128]{3,0,2,1:T(8,128)(2,1)S(1)} %get-tuple-element.24), channel_id=1, source_target_pairs={{1,0},{2,1},{3,2},{4,3},{5,4},{6,5},{7,6},{9,8},{10,9},{11,10},{12... | collective-permute-start | bytes 221192 | tf_op jit(solution)/shard_map/ppermute | solution.py:23
  34.6 8.2 %copy-start.25 = (bf16[3,16,1,1,1]{1,4,3,2,0:T(2,128)(2,1)S(1)}, bf16[3,16,1,1,1]{1,4,3,2,0:T(2,128)(2,1)}, u32[]{:S(2)}) copy-start(bf16[3,16,1,1,1]{1,4,3,2,0:T(2,128)(2,1)} %get-tuple-element.83) | copy-start | bytes 292
  35.7 7.3 %copy-start.24 = (bf16[3,16,1,1,1]{1,4,3,2,0:T(2,128)(2,1)S(1)}, bf16[3,16,1,1,1]{1,4,3,2,0:T(2,128)(2,1)}, u32[]{:S(2)}) copy-start(bf16[3,16,1,1,1]{1,4,3,2,0:T(2,128)(2,1)} %get-tuple-element.84) | copy-start | bytes 292
  35.7 26.2 %collective-permute-start.9 = (f32[8,16,128]{2,1,0:T(8,128)S(1)}, f32[8,16,128]{2,1,0:T(8,128)S(1)}, u32[]{:S(2)}, u32[]{:S(2)}) collective-permute-start(f32[8,16,128]{2,1,0:T(8,128)S(1)} %bitcast.421), channel_id=1, source_target_pairs={{0,1},{1,2},{2,3},{3,4},{4,5},{5,6},{6,7},{8,9},{9,10},{10,11},{11... | collective-permute-start | bytes 196616 | tf_op jit(solution)/shard_map/ppermute | solution.py:33
  42.7 0.8 copy-start.23
  42.7 1.1 copy-start.22
  43.0 1.3 copy-start.21
  43.6 1.1 copy-start.13
  43.9 1.3 copy-start.12
  44.7 1.3 copy-start.20
  45.2 1.3 copy-start.19
  45.5 1.3 copy-start.18
  46.0 1.1 copy-start.17
  46.5 1.1 copy-start.16
  46.8 1.1 copy-start.15
  47.1 1.3 copy-start.14
  47.9 1.3 copy-start.32
  48.5 1.1 copy-start.31
  48.8 1.1 copy-start.27
  49.3 1.0 copy-start.6
  50.3 0.8 copy-start.30
  50.3 1.1 copy-start.29
  51.1 0.6 copy-start.26
  51.1 0.9 copy-start.28
  51.2 0.9 copy-start.33
  52.1 9.9 %copy-start.4 = (f32[8,15,16,128]{3,2,1,0:T(8,128)S(1)}, f32[8,15,16,128]{3,2,1,0:T(8,128)}, u32[]{:S(2)}) copy-start(f32[8,15,16,128]{3,2,1,0:T(8,128)} %get-tuple-element.66) | copy-start | bytes 2949124
  53.3 8.7 %copy-start.1 = (f32[8,16,15,128]{3,2,1,0:T(8,128)S(1)}, f32[8,16,15,128]{3,2,1,0:T(8,128)}, u32[]{:S(2)}) copy-start(f32[8,16,15,128]{3,2,1,0:T(8,128)} %get-tuple-element.61) | copy-start | bytes 2949124
  53.3 8.7 %copy-start.2 = (f32[8,16,15,128]{3,2,1,0:T(8,128)S(1)}, f32[8,16,15,128]{3,2,1,0:T(8,128)}, u32[]{:S(2)}) copy-start(f32[8,16,15,128]{3,2,1,0:T(8,128)} %get-tuple-element.62) | copy-start | bytes 2949124
  53.3 8.7 %copy-start.3 = (f32[8,15,16,128]{3,2,1,0:T(8,128)S(1)}, f32[8,15,16,128]{3,2,1,0:T(8,128)}, u32[]{:S(2)}) copy-start(f32[8,15,16,128]{3,2,1,0:T(8,128)} %get-tuple-element.65) | copy-start | bytes 2949124
  53.4 5.1 %copy-start.9 = (f32[3,16,16,128]{3,2,1,0:T(8,128)}, f32[3,16,16,128]{3,2,1,0:T(8,128)S(1)}, u32[]{:S(2)}) copy-start(f32[3,16,16,128]{3,2,1,0:T(8,128)S(1)} %copy.38) | copy-start | bytes 1179652
  53.4 6.4 %collective-permute-start.8 = (f32[16,128]{1,0:T(8,128)S(1)}, f32[16,128]{1,0:T(8,128)S(1)}, u32[]{:S(2)}, u32[]{:S(2)}) collective-permute-start(f32[16,128]{1,0:T(8,128)S(1)} %bitcast.430), channel_id=1, source_target_pairs={{0,1},{1,2},{2,3},{3,4},{4,5},{5,6},{6,7},{8,9},{9,10},{10,11},{11... | collective-permute-start | bytes 24584 | tf_op jit(solution)/shard_map/ppermute | solution.py:33
  59.8 2.1 %collective-permute-start.5 = (f32[16,128]{1,0:T(8,128)S(1)}, f32[16,128]{1,0:T(8,128)S(1)}, u32[]{:S(2)}, u32[]{:S(2)}) collective-permute-start(f32[16,128]{1,0:T(8,128)S(1)} %slice_bitcast_fusion.8), channel_id=1, source_target_pairs={{0,8},{8,16},{16,24},{1,9},{9,17},{17,25},{2,10},{10,18},{18,26},{... | collective-permute-start | bytes 24584 | tf_op jit(solution)/shard_map/ppermute | solution.py:33
  64.8 12.9 %collective-permute-start.10 = (f32[8,16,128]{2,1,0:T(8,128)S(1)}, f32[8,16,128]{2,1,0:T(8,128)S(1)}, u32[]{:S(2)}, u32[]{:S(2)}) collective-permute-start(f32[8,16,128]{2,1,0:T(8,128)S(1)} %get-tuple-element.52), channel_id=1, source_target_pairs={{8,0},{16,8},{24,16},{9,1},{17,9},{25,17},{10,2},{18,10},{26,18},{... | collective-permute-start | bytes 196616 | tf_op jit(solution)/shard_map/ppermute | solution.py:33
  66.1 11.6 %collective-permute-start.11 = (f32[8,16,128]{2,1,0:T(8,128)S(1)}, f32[8,16,128]{2,1,0:T(8,128)S(1)}, u32[]{:S(2)}, u32[]{:S(2)}) collective-permute-start(f32[8,16,128]{2,1,0:T(8,128)S(1)} %get-tuple-element.51), channel_id=1, source_target_pairs={{0,8},{8,16},{16,24},{1,9},{9,17},{17,25},{2,10},{10,18},{18,26},{... | collective-permute-start | bytes 196616 | tf_op jit(solution)/shard_map/ppermute | solution.py:33
  71.4 6.4 %collective-permute-start.12 = (f32[8,16,128]{2,1,0:T(8,128)S(1)}, f32[8,16,128]{2,1,0:T(8,128)S(1)}, u32[]{:S(2)}, u32[]{:S(2)}) collective-permute-start(f32[8,16,128]{2,1,0:T(8,128)S(1)} %bitcast.425), channel_id=1, source_target_pairs={{1,0},{2,1},{3,2},{4,3},{5,4},{6,5},{7,6},{9,8},{10,9},{11,10},{12... | collective-permute-start | bytes 196616 | tf_op jit(solution)/shard_map/ppermute | solution.py:33
  72.7 7.3 %collective-permute-start.13 = (f32[8,16,128]{2,1,0:T(8,128)S(1)}, f32[8,16,128]{2,1,0:T(8,128)S(1)}, u32[]{:S(2)}, u32[]{:S(2)}) collective-permute-start(f32[8,16,128]{2,1,0:T(8,128)S(1)} %bitcast.422), channel_id=1, source_target_pairs={{0,1},{1,2},{2,3},{3,4},{4,5},{5,6},{6,7},{8,9},{9,10},{10,11},{11... | collective-permute-start | bytes 196616 | tf_op jit(solution)/shard_map/ppermute | solution.py:33
  81.8 11.3 %collective-permute-start.14 = (f32[8,16,128]{2,1,0:T(8,128)S(1)}, f32[8,16,128]{2,1,0:T(8,128)S(1)}, u32[]{:S(2)}, u32[]{:S(2)}) collective-permute-start(f32[8,16,128]{2,1,0:T(8,128)S(1)} %get-tuple-element.42), channel_id=1, source_target_pairs={{8,0},{16,8},{24,16},{9,1},{17,9},{25,17},{10,2},{18,10},{26,18},{... | collective-permute-start | bytes 196616 | tf_op jit(solution)/shard_map/ppermute | solution.py:33
  83.1 10.0 %collective-permute-start.15 = (f32[8,16,128]{2,1,0:T(8,128)S(1)}, f32[8,16,128]{2,1,0:T(8,128)S(1)}, u32[]{:S(2)}, u32[]{:S(2)}) collective-permute-start(f32[8,16,128]{2,1,0:T(8,128)S(1)} %get-tuple-element.41), channel_id=1, source_target_pairs={{0,8},{8,16},{16,24},{1,9},{9,17},{17,25},{2,10},{10,18},{18,26},{... | collective-permute-start | bytes 196616 | tf_op jit(solution)/shard_map/ppermute | solution.py:33
  86.5 6.8 %collective-permute-start.16 = (f32[8,16,128]{2,1,0:T(8,128)S(1)}, f32[8,16,128]{2,1,0:T(8,128)S(1)}, u32[]{:S(2)}, u32[]{:S(2)}) collective-permute-start(f32[8,16,128]{2,1,0:T(8,128)S(1)} %bitcast.426), channel_id=1, source_target_pairs={{1,0},{2,1},{3,2},{4,3},{5,4},{6,5},{7,6},{9,8},{10,9},{11,10},{12... | collective-permute-start | bytes 196616 | tf_op jit(solution)/shard_map/ppermute | solution.py:33
  87.8 7.8 %collective-permute-start.17 = (f32[8,16,128]{2,1,0:T(8,128)S(1)}, f32[8,16,128]{2,1,0:T(8,128)S(1)}, u32[]{:S(2)}, u32[]{:S(2)}) collective-permute-start(f32[8,16,128]{2,1,0:T(8,128)S(1)} %bitcast.423), channel_id=1, source_target_pairs={{0,1},{1,2},{2,3},{3,4},{4,5},{5,6},{6,7},{8,9},{9,10},{10,11},{11... | collective-permute-start | bytes 196616 | tf_op jit(solution)/shard_map/ppermute | solution.py:33
  97.4 11.1 %collective-permute-start.18 = (f32[8,16,128]{2,1,0:T(8,128)S(1)}, f32[8,16,128]{2,1,0:T(8,128)S(1)}, u32[]{:S(2)}, u32[]{:S(2)}) collective-permute-start(f32[8,16,128]{2,1,0:T(8,128)S(1)} %get-tuple-element.32), channel_id=1, source_target_pairs={{8,0},{16,8},{24,16},{9,1},{17,9},{25,17},{10,2},{18,10},{26,18},{... | collective-permute-start | bytes 196616 | tf_op jit(solution)/shard_map/ppermute | solution.py:33
  98.7 9.8 %collective-permute-start.19 = (f32[8,16,128]{2,1,0:T(8,128)S(1)}, f32[8,16,128]{2,1,0:T(8,128)S(1)}, u32[]{:S(2)}, u32[]{:S(2)}) collective-permute-start(f32[8,16,128]{2,1,0:T(8,128)S(1)} %get-tuple-element.31), channel_id=1, source_target_pairs={{0,8},{8,16},{16,24},{1,9},{9,17},{17,25},{2,10},{10,18},{18,26},{... | collective-permute-start | bytes 196616 | tf_op jit(solution)/shard_map/ppermute | solution.py:33
  101.9 6.8 %collective-permute-start.20 = (f32[8,16,128]{2,1,0:T(8,128)S(1)}, f32[8,16,128]{2,1,0:T(8,128)S(1)}, u32[]{:S(2)}, u32[]{:S(2)}) collective-permute-start(f32[8,16,128]{2,1,0:T(8,128)S(1)} %bitcast.427), channel_id=1, source_target_pairs={{1,0},{2,1},{3,2},{4,3},{5,4},{6,5},{7,6},{9,8},{10,9},{11,10},{12... | collective-permute-start | bytes 196616 | tf_op jit(solution)/shard_map/ppermute | solution.py:33
  103.2 8.2 %collective-permute-start.21 = (f32[8,16,128]{2,1,0:T(8,128)S(1)}, f32[8,16,128]{2,1,0:T(8,128)S(1)}, u32[]{:S(2)}, u32[]{:S(2)}) collective-permute-start(f32[8,16,128]{2,1,0:T(8,128)S(1)} %bitcast.424), channel_id=1, source_target_pairs={{0,1},{1,2},{2,3},{3,4},{4,5},{5,6},{6,7},{8,9},{9,10},{10,11},{11... | collective-permute-start | bytes 196616 | tf_op jit(solution)/shard_map/ppermute | solution.py:33
  115.1 1.2 collective-permute-start.22
  116.3 3.7 %collective-permute-start.23 = (f32[9,8]{1,0:T(8,128)S(1)}, f32[9,8]{1,0:T(8,128)S(1)}, u32[]{:S(2)}, u32[]{:S(2)}) collective-permute-start(f32[9,8]{1,0:T(8,128)S(1)} %add.646), channel_id=1, source_target_pairs={{0,16},{8,24},{16,0},{24,8},{1,17},{9,25},{17,1},{25,9},{2,18},{10... | collective-permute-start | bytes 872 | tf_op jit(solution)/shard_map/ppermute | solution.py:89
  119.9 4.1 %collective-permute-start.24 = (f32[9,8]{1,0:T(8,128)S(1)}, f32[9,8]{1,0:T(8,128)S(1)}, u32[]{:S(2)}, u32[]{:S(2)}) collective-permute-start(f32[9,8]{1,0:T(8,128)S(1)} %add.647), channel_id=1, source_target_pairs={{0,1},{1,0},{2,3},{3,2},{4,5},{5,4},{6,7},{7,6},{8,9},{9,8},{10,11... | collective-permute-start | bytes 872 | tf_op jit(solution)/shard_map/ppermute | solution.py:89
  124.1 5.1 %collective-permute-start.25 = (f32[9,8]{1,0:T(8,128)S(1)}, f32[9,8]{1,0:T(8,128)S(1)}, u32[]{:S(2)}, u32[]{:S(2)}) collective-permute-start(f32[9,8]{1,0:T(8,128)S(1)} %add.648), channel_id=1, source_target_pairs={{0,2},{1,3},{2,0},{3,1},{4,6},{5,7},{6,4},{7,5},{8,10},{9,11},{10,... | collective-permute-start | bytes 872 | tf_op jit(solution)/shard_map/ppermute | solution.py:89
  129.1 5.4 %collective-permute-start.26 = (f32[9,8]{1,0:T(8,128)S(1)}, f32[9,8]{1,0:T(8,128)S(1)}, u32[]{:S(2)}, u32[]{:S(2)}) collective-permute-start(f32[9,8]{1,0:T(8,128)S(1)} %add.649), channel_id=1, source_target_pairs={{0,4},{1,5},{2,6},{3,7},{4,0},{5,1},{6,2},{7,3},{8,12},{9,13},{10,... | collective-permute-start | bytes 872 | tf_op jit(solution)/shard_map/ppermute | solution.py:89

commit v3 on v2

--- a/solution.py
+++ b/solution.py
@@ -54,28 +54,41 @@
     return summed
 
 
-def neighbours(field):
-    below_z = from_behind(field[:, -1], "gz", 1)
-    above_z = from_behind(field[:, 0], "gz", -1)
-    below_y = from_behind(field[:, :, -1], "yx", 1)
-    above_y = from_behind(field[:, :, 0], "yx", -1)
-    up_z = jnp.concatenate([field[:, 1:], above_z[:, None]], axis=1)
-    down_z = jnp.concatenate([below_z[:, None], field[:, :-1]], axis=1)
-    up_y = jnp.concatenate([field[:, :, 1:], above_y[:, :, None]], axis=2)
-    down_y = jnp.concatenate([below_y[:, :, None], field[:, :, :-1]], axis=2)
-    zero_col = jnp.zeros_like(field[..., :1])
-    up_x = jnp.concatenate([field[..., 1:], zero_col], axis=3)
-    down_x = jnp.concatenate([zero_col, field[..., :-1]], axis=3)
-    return up_z, down_z, up_y, down_y, up_x, down_x
-
-
-def operate(field, weights, seeded):
-    weight_zup, weight_zdown, weight_yup, weight_ydown, weight_xup, weight_xdown = weights
-    up_z, down_z, up_y, down_y, up_x, down_x = neighbours(field)
-    laplace = weight_zup * (field - up_z) + weight_zdown * (field - down_z)
-    laplace = laplace + weight_yup * (field - up_y) + weight_ydown * (field - down_y)
-    laplace = laplace + weight_xup * (field - up_x) + weight_xdown * (field - down_x)
-    return (1.0 - seeded) * (laplace + RIDGE_WEIGHT * field) + seeded * field
+def extend(cells, width):
+    for axis, dim in (("gz", 1), ("yx", 2)):
+        size = cells.shape[dim]
+        head = lax.slice_in_dim(cells, 0, width, axis=dim)
+        tail = lax.slice_in_dim(cells, size - width, size, axis=dim)
+        cells = jnp.concatenate(
+            [from_behind(tail, axis, 1), cells, from_behind(head, axis, -1)], axis=dim
+        )
+    return cells
+
+
+def operate_inside(field, grid, offset):
+    weight_zup, weight_yup, weight_x, seeded = grid
+    count = field.shape[1] - 2
+    inner = slice(offset, offset + count)
+    lower = slice(offset - 1, offset - 1 + count)
+    centre = field[:, 1:-1, 1:-1]
+    weight_xup = weight_x[inner, inner]
+    weight_xdown = jnp.pad(weight_xup, ((0, 0), (0, 0), (1, 0)))[:, :, :-1]
+    zero_col = jnp.zeros_like(centre[..., :1])
+    laplace = weight_zup[inner, inner] * (centre - field[:, 2:, 1:-1]) + weight_zup[lower, inner] * (
+        centre - field[:, :-2, 1:-1]
+    )
+    laplace = (
+        laplace
+        + weight_yup[inner, inner] * (centre - field[:, 1:-1, 2:])
+        + weight_yup[inner, lower] * (centre - field[:, 1:-1, :-2])
+    )
+    laplace = (
+        laplace
+        + weight_xup * (centre - jnp.concatenate([centre[..., 1:], zero_col], axis=3))
+        + weight_xdown * (centre - jnp.concatenate([zero_col, centre[..., :-1]], axis=3))
+    )
+    mask = seeded[inner, inner]
+    return (1.0 - mask) * (laplace + RIDGE_WEIGHT * centre) + mask * centre
 
 
 def all_sum(value, axes):
@@ -112,29 +125,37 @@
     affinities = jax.nn.sigmoid(
         conv_region(padded, conv_weight, depth_cells, row_cells) + bias_column
     )
-    below_plane = from_behind(affinities[0, -1], "gz", 1)
-    below_row = from_behind(affinities[1, :, -1], "yx", 1)
-    weight_zdown = jnp.concatenate([below_plane[None], affinities[0, :-1]], axis=0)
-    weight_ydown = jnp.concatenate([below_row[:, None, :], affinities[1, :, :-1]], axis=1)
-    weight_zup = affinities[0] * keep_z
-    weight_yup = affinities[1] * keep_y
-    weight_xup = affinities[2] * keep_x
-    weight_xdown = jnp.pad(weight_xup, ((0, 0), (0, 0), (1, 0)))[:, :, :-1]
-    weights = (
-        weight_zup[None],
-        weight_zdown[None],
-        weight_yup[None],
-        weight_ydown[None],
-        weight_xup[None],
-        weight_xdown[None],
-    )
-    seeded = (labels > 0).astype(jnp.float32)[None]
-    colours = jnp.arange(1, FIELDS + 1, dtype=jnp.int32)[:, None, None, None]
-    seed_field = (labels[None] == colours).astype(jnp.float32)
-
-    basis = [seed_field - operate(seed_field, weights, seeded)]
+    halo = ITERS + 1
+    stacked = jnp.concatenate([affinities, labels[None].astype(jnp.float32)], axis=0)
+    grid_cells = extend(stacked, halo)
+    cells_z = depth_cells + 2 * halo
+    cells_y = row_cells + 2 * halo
+    grid_z = lax.axis_index("gz") * depth_cells - halo + jnp.arange(cells_z, dtype=jnp.int32)
+    grid_y = lax.axis_index("yx") * row_cells - halo + jnp.arange(cells_y, dtype=jnp.int32)
+    edge_z = ((grid_z >= 0) & (grid_z < depth_cells * lax.axis_size("gz") - 1)).astype(jnp.float32)
+    edge_y = ((grid_y >= 0) & (grid_y < row_cells * lax.axis_size("yx") - 1)).astype(jnp.float32)
+    grid_labels = grid_cells[3]
+    grid = (
+        grid_cells[0] * edge_z[:, None, None],
+        grid_cells[1] * edge_y[None, :, None],
+        grid_cells[2] * keep_x,
+        (grid_labels > 0.5).astype(jnp.float32),
+    )
+    colours = jnp.arange(1, FIELDS + 1, dtype=jnp.float32)[:, None, None, None]
+    grid_seed = (grid_labels[None] == colours).astype(jnp.float32)
+    seed_field = grid_seed[:, halo:-halo, halo:-halo]
+
+    inside = grid_seed[:, 1:-1, 1:-1]
+    current = inside - operate_inside(grid_seed, grid, 1)
+    basis = [current]
     for power in range(ITERS):
-        basis.append(operate(basis[-1], weights, seeded))
+        current = operate_inside(current, grid, power + 2)
+        basis.append(current)
+    basis = [
+        vector[:, (vector.shape[1] - depth_cells) // 2 : (vector.shape[1] + depth_cells) // 2,
+               (vector.shape[2] - row_cells) // 2 : (vector.shape[2] + row_cells) // 2]
+        for vector in basis
+    ]
     size = ITERS + 1
     pairs = [(i, j) for i in range(size) for j in range(i, size) if i < size - 1]
     local = jnp.stack([field_sums(basis[i], basis[j]) for i, j in pairs])

time: 137 us -> 92.3 us (0.67)
  starting transfers between devices: 75.6 us -> 30.9 us
  local copies, waits for them, and re-layouts: 15.3 us -> 8.9 us
  waiting for transfers between devices: 17.5 us -> 22.9 us
  other arithmetic: 12.1 us -> 17 us
  matrix products: 13.7 us -> 11 us
    ppermute x18 -> x4, starting transfers between devices: 54.8 us -> 9.16 us  [from_behind(): return lax.ppermute(value, axis, pairs)]
    ppermute x2, waiting for transfers between devices: 0.01 us -> 4.68 us  [padded_2(): lax.ppermute(head, axis, [((i + 1) % count, i) for i in range(ends)])]
    slice x21 -> x13, local copies, waits for them, and re-layouts: 6.73 us -> 3.66 us  [the longest x4 2.47 us: operate_inside(): centre[..., 1:]]
    dot_general x27, matrix products: 13.7 us -> 11 us  [conv_region(): jnp.einsum('oc,czyx->ozyx', conv_weight[:, :, offset_z, offset_y, offset_...]
    add x1, other arithmetic: 1.33 us -> 3.88 us  [body(): probabilities = probabilities + coeff[:, None, None, None] * vector]
    add x3, other arithmetic: 2.19 us -> 4.44 us  [the longest x2 4.44 us: operate_inside(): return (1.0 - mask) * (laplace + RIDGE_WEIGHT * centre) + mask * centre]
    ppermute x18 -> x4, waiting for transfers between devices: 8.69 us -> 10.7 us  [from_behind(): return lax.ppermute(value, axis, pairs)]
    sub x2 -> x5, other arithmetic: 2.14 us -> 3.08 us  [the longest x1 2.58 us: body(): current = inside - operate_inside(grid_seed, grid, 1)]
  transfers between devices with their start and end apart: 27 -> 13, of which waited for: 13 -> 10; matrix products, arithmetic and copies ran while one was open for 20% -> 3% of each run, Pallas kernels for 0% -> 0%
where the time goes in v3:
time: 92.3 us; the launch traced here: 92 us
  starting transfers between devices  30.9 us (33%)
  waiting for transfers between devices  22.9 us (25%)
  other arithmetic  17 us (18%)
  matrix products  11 us (12%)
  local copies, waits for them, and re-layouts  8.9 us (10%)
  between operations  1.2 us (1%)
    dot_general x27, matrix products, conv_region(): jnp.einsum('oc,czyx->ozyx', conv_weight[:, :, offset_z, offset_y, offset_...  11 us
    ppermute x5, starting transfers between devices, all_sum(): lax.ppermute(value, axis, [(i, i ^ hop) for i in range(devices)])  11 us
    ppermute x4, waiting for transfers between devices, from_behind(): return lax.ppermute(value, axis, pairs)  10.7 us
    ppermute x4, starting transfers between devices, from_behind(): return lax.ppermute(value, axis, pairs)  9.16 us
    ppermute x2, starting transfers between devices, padded_2(): lax.ppermute(tail, axis, [(i, (i + 1) % count) for i in range(ends)])  7.94 us
    ppermute x5, waiting for transfers between devices, all_sum(): lax.ppermute(value, axis, [(i, i ^ hop) for i in range(devices)])  7.44 us
    unnamed x18, local copies, waits for them, and re-layouts  5.12 us
    ppermute x2, waiting for transfers between devices, padded_2(): lax.ppermute(head, axis, [((i + 1) % count, i) for i in range(ends)])  4.68 us
  transfers between devices with their start and end apart: 13, of which 10 were waited for; matrix products, arithmetic and copies ran while one was open for 3% of the time, Pallas kernels for 0%

profile of v3, /device:TPU:0, one launch (start us, length us, event | category | flops | bytes accessed | tf_op | source)
XLA Modules:
  0.0 92.0 jit_solution(9445929163300574516)
XLA Ops:
  0.7 2.0 %copy.13 = bf16[16,16,16,128]{3,0,2,1:T(8,128)(2,1)S(1)} copy(bf16[16,16,16,128]{3,2,1,0:T(8,128)(2,1)} %param.4) | data formatting | bytes 2097152 | tf_op args[0]
  2.7 1.3 %collective-permute-start.1 = (bf16[16,1,16,128]{3,0,2,1:T(8,128)(2,1)S(1)}, bf16[16,1,16,128]{3,0,2,1:T(8,128)(2,1)S(1)}, u32[]{:S(2)}, u32[]{:S(2)}) collective-permute-start(bf16[16,1,16,128]{3,0,2,1:T(8,128)(2,1)S(1)} %get-tuple-element.37), channel_id=1, source_target_pairs={{8,0},{16,8},{24,16},{9,1},{17,9},{25,17},{10,2},{18,10},{26,18},{... | collective-permute-start | bytes 196616 | tf_op jit(solution)/shard_map/ppermute | solution.py:23
  4.0 3.0 %collective-permute-start = (bf16[16,1,16,128]{3,0,2,1:T(8,128)(2,1)S(1)}, bf16[16,1,16,128]{3,0,2,1:T(8,128)(2,1)S(1)}, u32[]{:S(2)}, u32[]{:S(2)}) collective-permute-start(bf16[16,1,16,128]{3,0,2,1:T(8,128)(2,1)S(1)} %get-tuple-element.38), channel_id=1, source_target_pairs={{0,8},{8,16},{16,24},{1,9},{9,17},{17,25},{2,10},{10,18},{18,26},{... | collective-permute-start | bytes 196616 | tf_op jit(solution)/shard_map/ppermute | solution.py:21
  7.1 0.7 fusion.137
  7.9 0.7 constant_dynamic-update-slice_fusion.1
  8.7 4.9 %collective-permute-start.2 = (bf16[16,18,1,128]{3,0,2,1:T(8,128)(2,1)S(1)}, bf16[16,18,1,128]{3,0,2,1:T(8,128)(2,1)S(1)}, u32[]{:S(2)}, u32[]{:S(2)}) collective-permute-start(bf16[16,18,1,128]{3,0,2,1:T(8,128)(2,1)S(1)} %get-tuple-element.35), channel_id=1, source_target_pairs={{0,1},{1,2},{2,3},{3,4},{4,5},{5,6},{6,7},{8,9},{9,10},{10,11},{11... | collective-permute-start | bytes 221192 | tf_op jit(solution)/shard_map/ppermute | solution.py:21
  13.6 1.5 %collective-permute-start.3 = (bf16[16,18,1,128]{3,0,2,1:T(8,128)(2,1)S(1)}, bf16[16,18,1,128]{3,0,2,1:T(8,128)(2,1)S(1)}, u32[]{:S(2)}, u32[]{:S(2)}) collective-permute-start(bf16[16,18,1,128]{3,0,2,1:T(8,128)(2,1)S(1)} %get-tuple-element.36), channel_id=1, source_target_pairs={{1,0},{2,1},{3,2},{4,3},{5,4},{6,5},{7,6},{9,8},{10,9},{11,10},{12... | collective-permute-start | bytes 221192 | tf_op jit(solution)/shard_map/ppermute | solution.py:23
  15.1 0.3 fusion.74
  15.4 0.3 convolution_bitcast_fusion.1
  15.7 4.7 %collective-permute-done.3 = bf16[16,18,1,128]{3,0,2,1:T(8,128)(2,1)S(1)} collective-permute-done((bf16[16,18,1,128]{3,0,2,1:T(8,128)(2,1)S(1)}, bf16[16,18,1,128]{3,0,2,1:T(8,128)(2,1)S(1)}, u32[]{:S(2)}, u32[]{:S(2)}) %collective-permute-start.3) | collective-permute-done | bytes 73760 | tf_op jit(solution)/shard_map/ppermute | solution.py:23
  20.4 1.8 %fusion.5 = bf16[16,18,18,130]{3,0,2,1:T(8,128)(2,1)S(1)} fusion(bf16[16,18,1,128]{3,0,2,1:T(8,128)(2,1)S(1)} %collective-permute-done.3, bf16[16,18,16,128]{3,0,2,1:T(8,128)(2,1)S(1)} %constant_dynamic-update-slice_fusion, bf16[16,18,1,128]{3,0,2,1:T(8,128)(2,1)S(1)} %collective-permute-done.2), kind=kLoop, calls=%fused_computation.7 | loop fusion | flops 8087040 | bytes 2674944 | tf_op jit(solution)/shard_map/concatenate | solution.py:19
  22.5 0.5 convolution_bitcast_fusion.6
  23.0 0.3 convolution_bitcast_fusion.7
  23.3 0.5 convolution_bitcast_fusion.8
  23.8 0.3 convolution_bitcast_fusion.9
  24.0 0.5 convolution_bitcast_fusion.10
  24.6 0.3 convolution_bitcast_fusion.11
  24.8 0.3 fusion.104
  25.1 0.5 fusion.106
  25.6 0.3 fusion.108
  25.9 0.5 fusion.110
  26.4 0.3 fusion.112
  26.7 0.5 fusion.114
  27.2 0.3 fusion.116
  27.5 0.5 fusion.118
  28.0 0.5 convolution_bitcast_fusion.4
  28.5 0.3 fusion.121
  28.8 0.3 fusion.122
  29.1 0.3 fusion.123
  29.4 0.8 fusion.66
  30.2 0.3 convolution_bitcast_fusion.3
  30.8 0.3 convolution_bitcast_fusion.2
  31.1 1.1 %fusion.73 = f32[3,16,16,128]{3,0,2,1:T(4,128)S(1)} fusion(f32[3,16,16,128]{3,0,2,1:T(4,128)S(1)} %convolution_bitcast_fusion.4, f32[3,16,16,128]{3,0,2,1:T(4,128)S(1)} %convolution_bitcast_fusion, f32[3,16,16,128]{3,0,2,1:T(4,128)S(1)} %convolution_bitcast_fusion.5, f32[3,16,16,128]{3,0,2,1:T(4,128)S(1)} %convolution_bitcast_fusion.6, ...), kind=kOutput, calls=%fused_computation.105 | convolution fusion | flops 4816896 | bytes 8259584 | tf_op jit(solution)/shard_map/oc,czyx->ozyx/dot_general | solution.py:48
  32.3 2.0 %collective-permute-start.4 = (f32[4,4,16,128]{3,0,2,1:T(4,128)S(1)}, f32[4,4,16,128]{3,0,2,1:T(4,128)S(1)}, u32[]{:S(2)}, u32[]{:S(2)}) collective-permute-start(f32[4,4,16,128]{3,0,2,1:T(4,128)S(1)} %get-tuple-element.41), channel_id=1, source_target_pairs={{0,8},{8,16},{16,24},{1,9},{9,17},{17,25},{2,10},{10,18},{18,26},{... | collective-permute-start | bytes 393224 | tf_op jit(solution)/shard_map/ppermute | solution.py:33
  34.3 1.3 %collective-permute-start.5 = (f32[4,4,16,128]{3,0,2,1:T(4,128)S(1)}, f32[4,4,16,128]{3,0,2,1:T(4,128)S(1)}, u32[]{:S(2)}, u32[]{:S(2)}) collective-permute-start(f32[4,4,16,128]{3,0,2,1:T(4,128)S(1)} %get-tuple-element.42), channel_id=1, source_target_pairs={{8,0},{16,8},{24,16},{9,1},{17,9},{25,17},{10,2},{18,10},{26,18},{... | collective-permute-start | bytes 393224 | tf_op jit(solution)/shard_map/ppermute | solution.py:33
  35.7 4.7 %collective-permute-done.5 = f32[4,4,16,128]{3,0,2,1:T(4,128)S(1)} collective-permute-done((f32[4,4,16,128]{3,0,2,1:T(4,128)S(1)}, f32[4,4,16,128]{3,0,2,1:T(4,128)S(1)}, u32[]{:S(2)}, u32[]{:S(2)}) %collective-permute-start.5) | collective-permute-done | bytes 131104 | tf_op jit(solution)/shard_map/ppermute | solution.py:33
  40.5 4.3 %collective-permute-start.6 = (f32[4,24,4,128]{3,0,2,1:T(4,128)S(1)}, f32[4,24,4,128]{3,0,2,1:T(4,128)S(1)}, u32[]{:S(2)}, u32[]{:S(2)}) collective-permute-start(f32[4,24,4,128]{3,0,2,1:T(4,128)S(1)} %get-tuple-element.39), channel_id=1, source_target_pairs={{0,1},{1,2},{2,3},{3,4},{4,5},{5,6},{6,7},{8,9},{9,10},{10,11},{11... | collective-permute-start | bytes 589832 | tf_op jit(solution)/shard_map/ppermute | solution.py:33
  44.9 1.5 %collective-permute-start.7 = (f32[4,24,4,128]{3,0,2,1:T(4,128)S(1)}, f32[4,24,4,128]{3,0,2,1:T(4,128)S(1)}, u32[]{:S(2)}, u32[]{:S(2)}) collective-permute-start(f32[4,24,4,128]{3,0,2,1:T(4,128)S(1)} %get-tuple-element.40), channel_id=1, source_target_pairs={{1,0},{2,1},{3,2},{4,3},{5,4},{6,5},{7,6},{9,8},{10,9},{11,10},{12... | collective-permute-start | bytes 589832 | tf_op jit(solution)/shard_map/ppermute | solution.py:33
  46.4 1.6 %collective-permute-done.6 = f32[4,24,4,128]{3,0,2,1:T(4,128)S(1)} collective-permute-done((f32[4,24,4,128]{3,0,2,1:T(4,128)S(1)}, f32[4,24,4,128]{3,0,2,1:T(4,128)S(1)}, u32[]{:S(2)}, u32[]{:S(2)}) %collective-permute-start.6) | collective-permute-done | bytes 196640 | tf_op jit(solution)/shard_map/ppermute | solution.py:33
  48.0 4.4 %collective-permute-done.7 = f32[4,24,4,128]{3,0,2,1:T(4,128)S(1)} collective-permute-done((f32[4,24,4,128]{3,0,2,1:T(4,128)S(1)}, f32[4,24,4,128]{3,0,2,1:T(4,128)S(1)}, u32[]{:S(2)}, u32[]{:S(2)}) %collective-permute-start.7) | collective-permute-done | bytes 196640 | tf_op jit(solution)/shard_map/ppermute | solution.py:33
  52.4 0.4 pad_maximum_fusion.2
  52.9 0.9 fusion.215
  55.1 0.8 fusion.211
  55.9 0.7 copy-done
  56.5 2.6 %fusion.13 = f32[8,22,22,128]{3,2,1,0:T(8,128)S(1)} fusion(f32[8,24,24,128]{3,2,1,0:T(8,128)S(1)} %compare_convert_fusion, f32[8,22,22,127]{3,2,1,0:T(8,128)S(1)} %get-tuple-element.24, f32[8,22,22,127]{3,2,1,0:T(8,128)S(1)} %get-tuple-element.23, f32[22,22,128]{2,1,0:T(8,128)S(1)} %get-tuple-element.62, f32[22,22,128]{2,1,0:T(8,128)S(1)} %get-tuple-element.96, ...), kind=kLoop, calls=%fused_computation.17 | loop fusion | flops 11399168 | bytes 17811200 | tf_op jit(solution)/shard_map/sub | solution.py:149
  59.1 0.7 fusion.212
  59.9 2.3 %fusion.25 = f32[8,20,20,128]{3,2,1,0:T(8,128)S(1)} fusion(f32[8,22,22,128]{3,2,1,0:T(8,128)S(1)} %fusion.13, f32[8,20,20,127]{3,2,1,0:T(8,128)S(1)} %get-tuple-element.26, f32[8,20,20,127]{3,2,1,0:T(8,128)S(1)} %get-tuple-element.25, f32[20,20,128]{2,1,0:T(8,128)S(1)} %get-tuple-element.56, f32[20,20,128]{2,1,0:T(8,128)S(1)} %get-tuple-element.99, ...), kind=kLoop, calls=%fused_computation.33 | loop fusion | flops 9011200 | bytes 14720000 | tf_op jit(solution)/shard_map/add | solution.py:91
  62.2 0.6 fusion.213
  62.8 2.1 %fusion.37 = f32[8,18,18,128]{3,2,1,0:T(8,128)S(1)} fusion(f32[8,20,20,128]{3,2,1,0:T(8,128)S(1)} %fusion.25, f32[8,18,18,127]{3,2,1,0:T(8,128)S(1)} %get-tuple-element.28, f32[8,18,18,127]{3,2,1,0:T(8,128)S(1)} %get-tuple-element.27, f32[18,18,128]{2,1,0:T(8,128)S(1)} %get-tuple-element.50, f32[18,18,128]{2,1,0:T(8,128)S(1)} %get-tuple-element.102, ...), kind=kLoop, calls=%fused_computation.49 | loop fusion | flops 7299072 | bytes 11923200 | tf_op jit(solution)/shard_map/add | solution.py:91
  65.0 0.4 fusion.214
  65.4 0.8 copy-done.2
  66.2 2.5 %multiply_reduce_fusion.5 = (f32[8]{0:T(128)S(1)}, f32[8]{0:T(128)S(1)}, f32[8]{0:T(128)S(1)}, f32[8]{0:T(128)S(1)}, f32[8]{0:T(128)S(1)}, /*index=5*/f32[8]{0:T...) fusion(f32[8,22,22,128]{3,2,1,0:T(8,128)S(1)} %fusion.13, f32[8,20,20,128]{3,2,1,0:T(8,128)S(1)} %fusion.25, ...), kind=kLoop, calls=%fused_computation.163 | loop fusion | flops 10485688 | bytes 10469664 | tf_op jit(solution)/shard_map/reduce_sum | solution.py:108
  68.8 2.6 %collective-permute-start.8 = (f32[9,8]{1,0:T(8,128)S(1)}, f32[9,8]{1,0:T(8,128)S(1)}, u32[]{:S(2)}, u32[]{:S(2)}) collective-permute-start(f32[9,8]{1,0:T(8,128)S(1)} %stack.39), channel_id=1, source_target_pairs={{0,8},{8,0},{16,24},{24,16},{1,9},{9,1},{17,25},{25,17},{2,10},{10... | collective-permute-start | bytes 872 | tf_op jit(solution)/shard_map/ppermute | solution.py:102
  71.3 0.8 collective-permute-done.8
  72.1 1.1 %collective-permute-start.9 = (f32[9,8]{1,0:T(8,128)S(1)}, f32[9,8]{1,0:T(8,128)S(1)}, u32[]{:S(2)}, u32[]{:S(2)}) collective-permute-start(f32[9,8]{1,0:T(8,128)S(1)} %add.654), channel_id=1, source_target_pairs={{0,16},{8,24},{16,0},{24,8},{1,17},{9,25},{17,1},{25,9},{2,18},{10... | collective-permute-start | bytes 872 | tf_op jit(solution)/shard_map/ppermute | solution.py:102
  73.3 2.5 %collective-permute-done.9 = f32[9,8]{1,0:T(8,128)S(1)} collective-permute-done((f32[9,8]{1,0:T(8,128)S(1)}, f32[9,8]{1,0:T(8,128)S(1)}, u32[]{:S(2)}, u32[]{:S(2)}) %collective-permute-start.9) | collective-permute-done | bytes 320 | tf_op jit(solution)/shard_map/ppermute | solution.py:102
  75.8 2.2 %collective-permute-start.10 = (f32[9,8]{1,0:T(8,128)S(1)}, f32[9,8]{1,0:T(8,128)S(1)}, u32[]{:S(2)}, u32[]{:S(2)}) collective-permute-start(f32[9,8]{1,0:T(8,128)S(1)} %add.655), channel_id=1, source_target_pairs={{0,1},{1,0},{2,3},{3,2},{4,5},{5,4},{6,7},{7,6},{8,9},{9,8},{10,11... | collective-permute-start | bytes 872 | tf_op jit(solution)/shard_map/ppermute | solution.py:102
  78.0 1.6 %collective-permute-done.10 = f32[9,8]{1,0:T(8,128)S(1)} collective-permute-done((f32[9,8]{1,0:T(8,128)S(1)}, f32[9,8]{1,0:T(8,128)S(1)}, u32[]{:S(2)}, u32[]{:S(2)}) %collective-permute-start.10) | collective-permute-done | bytes 320 | tf_op jit(solution)/shard_map/ppermute | solution.py:102
  79.6 2.1 %collective-permute-start.11 = (f32[9,8]{1,0:T(8,128)S(1)}, f32[9,8]{1,0:T(8,128)S(1)}, u32[]{:S(2)}, u32[]{:S(2)}) collective-permute-start(f32[9,8]{1,0:T(8,128)S(1)} %add.656), channel_id=1, source_target_pairs={{0,2},{1,3},{2,0},{3,1},{4,6},{5,7},{6,4},{7,5},{8,10},{9,11},{10,... | collective-permute-start | bytes 872 | tf_op jit(solution)/shard_map/ppermute | solution.py:102
  81.7 1.6 %collective-permute-done.11 = f32[9,8]{1,0:T(8,128)S(1)} collective-permute-done((f32[9,8]{1,0:T(8,128)S(1)}, f32[9,8]{1,0:T(8,128)S(1)}, u32[]{:S(2)}, u32[]{:S(2)}) %collective-permute-start.11) | collective-permute-done | bytes 320 | tf_op jit(solution)/shard_map/ppermute | solution.py:102
  83.3 3.0 %collective-permute-start.12 = (f32[9,8]{1,0:T(8,128)S(1)}, f32[9,8]{1,0:T(8,128)S(1)}, u32[]{:S(2)}, u32[]{:S(2)}) collective-permute-start(f32[9,8]{1,0:T(8,128)S(1)} %add.657), channel_id=1, source_target_pairs={{0,4},{1,5},{2,6},{3,7},{4,0},{5,1},{6,2},{7,3},{8,12},{9,13},{10,... | collective-permute-start | bytes 872 | tf_op jit(solution)/shard_map/ppermute | solution.py:102
  86.4 0.8 copy.19
  87.1 0.8 collective-permute-done.12
  88.1 3.9 %fusion.94 = f32[8,16,16,128]{3,2,1,0:T(8,128)} fusion(f32[8,24,24,128]{3,2,1,0:T(8,128)} %copy-done, f32[8,20,20,128]{3,2,1,0:T(8,128)} %copy-done.1, f32[8,22,22,128]{3,2,1,0:T(8,128)S(1)} %fusion.13, f32[8,18,18,128]{3,2,1,0:T(8,128)} %copy-done.2, f32[8]{0:T(128)S(1)} %get-tuple-element.95, f32[8]{0:T(128)S(1)} %get-tuple-element.94, ...), kind=kLoop, calls=%fused_computation.131 | loop fusion | flops 1572864 | bytes 5242976 | tf_op jit(solution)/shard_map/add | solution.py:213
  (57 shorter events, 2.6 us)
Async XLA Ops:
  0.6 6.4 %copy-start.3 = (bf16[16,16,16,128]{3,2,1,0:T(8,128)(2,1)S(1)}, bf16[16,16,16,128]{3,2,1,0:T(8,128)(2,1)}, u32[]{:S(2)}) copy-start(bf16[16,16,16,128]{3,2,1,0:T(8,128)(2,1)} %param.4) | copy-start | bytes 3145732
  0.6 6.4 %copy-start.5 = (bf16[3,16,3,3,3]{1,4,3,2,0:T(4,128)(2,1)S(1)}, bf16[3,16,3,3,3]{1,4,3,2,0:T(4,128)(2,1)}, u32[]{:S(2)}) copy-start(bf16[3,16,3,3,3]{1,4,3,2,0:T(4,128)(2,1)} %param.5) | copy-start | bytes 7780
  0.6 7.1 %copy-start.4 = (s32[16,16,128]{2,1,0:T(8,128)S(1)}, s32[16,16,128]{2,1,0:T(8,128)}, u32[]{:S(2)}) copy-start(s32[16,16,128]{2,1,0:T(8,128)} %param.7) | copy-start | bytes 393220
  2.7 6.0 %collective-permute-start.1 = (bf16[16,1,16,128]{3,0,2,1:T(8,128)(2,1)S(1)}, bf16[16,1,16,128]{3,0,2,1:T(8,128)(2,1)S(1)}, u32[]{:S(2)}, u32[]{:S(2)}) collective-permute-start(bf16[16,1,16,128]{3,0,2,1:T(8,128)(2,1)S(1)} %get-tuple-element.37), channel_id=1, source_target_pairs={{8,0},{16,8},{24,16},{9,1},{17,9},{25,17},{10,2},{18,10},{26,18},{... | collective-permute-start | bytes 196616 | tf_op jit(solution)/shard_map/ppermute | solution.py:23
  4.0 3.9 %collective-permute-start = (bf16[16,1,16,128]{3,0,2,1:T(8,128)(2,1)S(1)}, bf16[16,1,16,128]{3,0,2,1:T(8,128)(2,1)S(1)}, u32[]{:S(2)}, u32[]{:S(2)}) collective-permute-start(bf16[16,1,16,128]{3,0,2,1:T(8,128)(2,1)S(1)} %get-tuple-element.38), channel_id=1, source_target_pairs={{0,8},{8,16},{16,24},{1,9},{9,17},{17,25},{2,10},{10,18},{18,26},{... | collective-permute-start | bytes 196616 | tf_op jit(solution)/shard_map/ppermute | solution.py:21
  8.7 7.0 %collective-permute-start.2 = (bf16[16,18,1,128]{3,0,2,1:T(8,128)(2,1)S(1)}, bf16[16,18,1,128]{3,0,2,1:T(8,128)(2,1)S(1)}, u32[]{:S(2)}, u32[]{:S(2)}) collective-permute-start(bf16[16,18,1,128]{3,0,2,1:T(8,128)(2,1)S(1)} %get-tuple-element.35), channel_id=1, source_target_pairs={{0,1},{1,2},{2,3},{3,4},{4,5},{5,6},{6,7},{8,9},{9,10},{10,11},{11... | collective-permute-start | bytes 221192 | tf_op jit(solution)/shard_map/ppermute | solution.py:21
  13.6 6.7 %collective-permute-start.3 = (bf16[16,18,1,128]{3,0,2,1:T(8,128)(2,1)S(1)}, bf16[16,18,1,128]{3,0,2,1:T(8,128)(2,1)S(1)}, u32[]{:S(2)}, u32[]{:S(2)}) collective-permute-start(bf16[16,18,1,128]{3,0,2,1:T(8,128)(2,1)S(1)} %get-tuple-element.36), channel_id=1, source_target_pairs={{1,0},{2,1},{3,2},{4,3},{5,4},{6,5},{7,6},{9,8},{10,9},{11,10},{12... | collective-permute-start | bytes 221192 | tf_op jit(solution)/shard_map/ppermute | solution.py:23
  30.5 0.7 copy-start.6
  32.3 3.4 %collective-permute-start.4 = (f32[4,4,16,128]{3,0,2,1:T(4,128)S(1)}, f32[4,4,16,128]{3,0,2,1:T(4,128)S(1)}, u32[]{:S(2)}, u32[]{:S(2)}) collective-permute-start(f32[4,4,16,128]{3,0,2,1:T(4,128)S(1)} %get-tuple-element.41), channel_id=1, source_target_pairs={{0,8},{8,16},{16,24},{1,9},{9,17},{17,25},{2,10},{10,18},{18,26},{... | collective-permute-start | bytes 393224 | tf_op jit(solution)/shard_map/ppermute | solution.py:33
  34.3 6.0 %collective-permute-start.5 = (f32[4,4,16,128]{3,0,2,1:T(4,128)S(1)}, f32[4,4,16,128]{3,0,2,1:T(4,128)S(1)}, u32[]{:S(2)}, u32[]{:S(2)}) collective-permute-start(f32[4,4,16,128]{3,0,2,1:T(4,128)S(1)} %get-tuple-element.42), channel_id=1, source_target_pairs={{8,0},{16,8},{24,16},{9,1},{17,9},{25,17},{10,2},{18,10},{26,18},{... | collective-permute-start | bytes 393224 | tf_op jit(solution)/shard_map/ppermute | solution.py:33
  40.5 7.5 %collective-permute-start.6 = (f32[4,24,4,128]{3,0,2,1:T(4,128)S(1)}, f32[4,24,4,128]{3,0,2,1:T(4,128)S(1)}, u32[]{:S(2)}, u32[]{:S(2)}) collective-permute-start(f32[4,24,4,128]{3,0,2,1:T(4,128)S(1)} %get-tuple-element.39), channel_id=1, source_target_pairs={{0,1},{1,2},{2,3},{3,4},{4,5},{5,6},{6,7},{8,9},{9,10},{10,11},{11... | collective-permute-start | bytes 589832 | tf_op jit(solution)/shard_map/ppermute | solution.py:33
  44.9 7.6 %collective-permute-start.7 = (f32[4,24,4,128]{3,0,2,1:T(4,128)S(1)}, f32[4,24,4,128]{3,0,2,1:T(4,128)S(1)}, u32[]{:S(2)}, u32[]{:S(2)}) collective-permute-start(f32[4,24,4,128]{3,0,2,1:T(4,128)S(1)} %get-tuple-element.40), channel_id=1, source_target_pairs={{1,0},{2,1},{3,2},{4,3},{5,4},{6,5},{7,6},{9,8},{10,9},{11,10},{12... | collective-permute-start | bytes 589832 | tf_op jit(solution)/shard_map/ppermute | solution.py:33
  55.1 1.4 %copy-start = (f32[8,24,24,128]{3,2,1,0:T(8,128)}, f32[8,24,24,128]{3,2,1,0:T(8,128)S(1)}, u32[]{:S(2)}) copy-start(f32[8,24,24,128]{3,2,1,0:T(8,128)S(1)} %compare_convert_fusion) | copy-start | bytes 7077892
  62.2 3.2 %copy-start.1 = (f32[8,20,20,128]{3,2,1,0:T(8,128)}, f32[8,20,20,128]{3,2,1,0:T(8,128)S(1)}, u32[]{:S(2)}) copy-start(f32[8,20,20,128]{3,2,1,0:T(8,128)S(1)} %fusion.25) | copy-start | bytes 4915204
  65.0 1.2 %copy-start.2 = (f32[8,18,18,128]{3,2,1,0:T(8,128)}, f32[8,18,18,128]{3,2,1,0:T(8,128)S(1)}, u32[]{:S(2)}) copy-start(f32[8,18,18,128]{3,2,1,0:T(8,128)S(1)} %fusion.37) | copy-start | bytes 3981316
  68.8 3.4 %collective-permute-start.8 = (f32[9,8]{1,0:T(8,128)S(1)}, f32[9,8]{1,0:T(8,128)S(1)}, u32[]{:S(2)}, u32[]{:S(2)}) collective-permute-start(f32[9,8]{1,0:T(8,128)S(1)} %stack.39), channel_id=1, source_target_pairs={{0,8},{8,0},{16,24},{24,16},{1,9},{9,1},{17,25},{25,17},{2,10},{10... | collective-permute-start | bytes 872 | tf_op jit(solution)/shard_map/ppermute | solution.py:102
  72.1 3.7 %collective-permute-start.9 = (f32[9,8]{1,0:T(8,128)S(1)}, f32[9,8]{1,0:T(8,128)S(1)}, u32[]{:S(2)}, u32[]{:S(2)}) collective-permute-start(f32[9,8]{1,0:T(8,128)S(1)} %add.654), channel_id=1, source_target_pairs={{0,16},{8,24},{16,0},{24,8},{1,17},{9,25},{17,1},{25,9},{2,18},{10... | collective-permute-start | bytes 872 | tf_op jit(solution)/shard_map/ppermute | solution.py:102
  75.8 3.8 %collective-permute-start.10 = (f32[9,8]{1,0:T(8,128)S(1)}, f32[9,8]{1,0:T(8,128)S(1)}, u32[]{:S(2)}, u32[]{:S(2)}) collective-permute-start(f32[9,8]{1,0:T(8,128)S(1)} %add.655), channel_id=1, source_target_pairs={{0,1},{1,0},{2,3},{3,2},{4,5},{5,4},{6,7},{7,6},{8,9},{9,8},{10,11... | collective-permute-start | bytes 872 | tf_op jit(solution)/shard_map/ppermute | solution.py:102
  79.6 3.7 %collective-permute-start.11 = (f32[9,8]{1,0:T(8,128)S(1)}, f32[9,8]{1,0:T(8,128)S(1)}, u32[]{:S(2)}, u32[]{:S(2)}) collective-permute-start(f32[9,8]{1,0:T(8,128)S(1)} %add.656), channel_id=1, source_target_pairs={{0,2},{1,3},{2,0},{3,1},{4,6},{5,7},{6,4},{7,5},{8,10},{9,11},{10,... | collective-permute-start | bytes 872 | tf_op jit(solution)/shard_map/ppermute | solution.py:102
  83.3 4.7 %collective-permute-start.12 = (f32[9,8]{1,0:T(8,128)S(1)}, f32[9,8]{1,0:T(8,128)S(1)}, u32[]{:S(2)}, u32[]{:S(2)}) collective-permute-start(f32[9,8]{1,0:T(8,128)S(1)} %add.657), channel_id=1, source_target_pairs={{0,4},{1,5},{2,6},{3,7},{4,0},{5,1},{6,2},{7,3},{8,12},{9,13},{10,... | collective-permute-start | bytes 872 | tf_op jit(solution)/shard_map/ppermute | solution.py:102

commit v4 on v3

--- a/solution.py
+++ b/solution.py
@@ -119,26 +119,31 @@
     keep_x = (jnp.arange(col_cells, dtype=jnp.int32) < col_cells - 1).astype(jnp.float32)[
         None, None, :
     ]
-    bias_column = conv_bias[:, None, None, None]
-    padded = padded_2(features, (("gz", 1), ("yx", 2)), 1)
-    padded = jnp.pad(padded, ((0, 0), (0, 0), (0, 0), (1, 1)))
-    affinities = jax.nn.sigmoid(
-        conv_region(padded, conv_weight, depth_cells, row_cells) + bias_column
-    )
     halo = ITERS + 1
-    stacked = jnp.concatenate([affinities, labels[None].astype(jnp.float32)], axis=0)
-    grid_cells = extend(stacked, halo)
+    stacked = jnp.concatenate([features, labels[None].astype(features.dtype)], axis=0)
+    grid_cells = extend(stacked, halo + 1)
+    channels = features.shape[0]
+    response = lax.conv_general_dilated(
+        grid_cells[None, :channels],
+        conv_weight,
+        window_strides=(1, 1, 1),
+        padding=((0, 0), (0, 0), (1, 1)),
+        dimension_numbers=("NCDHW", "OIDHW", "NCDHW"),
+        preferred_element_type=jnp.float32,
+    )[0]
+    grid_aff = jax.nn.sigmoid(response + conv_bias[:, None, None, None])
+    affinities = grid_aff[:, halo:-halo, halo:-halo]
+    grid_labels = grid_cells[channels, 1:-1, 1:-1].astype(jnp.float32)
     cells_z = depth_cells + 2 * halo
     cells_y = row_cells + 2 * halo
     grid_z = lax.axis_index("gz") * depth_cells - halo + jnp.arange(cells_z, dtype=jnp.int32)
     grid_y = lax.axis_index("yx") * row_cells - halo + jnp.arange(cells_y, dtype=jnp.int32)
     edge_z = ((grid_z >= 0) & (grid_z < depth_cells * lax.axis_size("gz") - 1)).astype(jnp.float32)
     edge_y = ((grid_y >= 0) & (grid_y < row_cells * lax.axis_size("yx") - 1)).astype(jnp.float32)
-    grid_labels = grid_cells[3]
     grid = (
-        grid_cells[0] * edge_z[:, None, None],
-        grid_cells[1] * edge_y[None, :, None],
-        grid_cells[2] * keep_x,
+        grid_aff[0] * edge_z[:, None, None],
+        grid_aff[1] * edge_y[None, :, None],
+        grid_aff[2] * keep_x,
         (grid_labels > 0.5).astype(jnp.float32),
     )
     colours = jnp.arange(1, FIELDS + 1, dtype=jnp.float32)[:, None, None, None]

time: 92.3 us -> 1530 us (16.58); the launches traced: 92 us -> 1510 us
  matrix products: 11 us -> 1320 us
  local copies, waits for them, and re-layouts: 8.9 us -> 114 us
    conv_general_dilated x0 -> x1, matrix products: none -> 1320 us  [body(): lax.conv_general_dilated(grid_cells[None, :channels], conv_weight, window...]
    conv_general_dilated x0 -> x5, local copies, waits for them, and re-layouts: none -> 98.1 us  [body(): lax.conv_general_dilated(grid_cells[None, :channels], conv_weight, window...]
    ppermute x4, waiting for transfers between devices: 10.7 us -> 26.2 us  [from_behind(): return lax.ppermute(value, axis, pairs)]
  transfers between devices with their start and end apart: 13 -> 9, of which waited for: 10 -> 7; matrix products, arithmetic and copies ran while one was open for 3% -> 0% of each run, Pallas kernels for 0% -> 0%
where the time goes in v4:
time: 1530 us; the launch traced here: 1510 us
  matrix products  1320 us (86%)
  local copies, waits for them, and re-layouts  114 us (7%)
  waiting for transfers between devices  34.8 us (2%)
  other arithmetic  24.1 us (2%)
  starting transfers between devices  21.3 us (1%)
    conv_general_dilated x1, matrix products, body(): lax.conv_general_dilated(grid_cells[None, :channels], conv_weight, window...  1320 us
    conv_general_dilated x5, local copies, waits for them, and re-layouts, body(): lax.conv_general_dilated(grid_cells[None, :channels], conv_weight, window...  98.1 us
  transfers between devices with their start and end apart: 9, of which 7 were waited for; matrix products, arithmetic and copies ran while one was open for 0% of the time, Pallas kernels for 0%

profile of v4, /device:TPU:0, one launch (start us, length us, event | category | flops | bytes accessed | tf_op | source)
XLA Modules:
  0.0 1511.8 jit_solution(11026961722489705564)
XLA Ops:
  0.7 1.0 convert_bitcast_fusion.2
  1.7 1.2 pad_maximum_fusion.7
  2.8 2.4 collective-permute-start
  5.3 1.3 collective-permute-start.1
  6.6 4.3 collective-permute-done.1
  10.9 0.2 pad_maximum_fusion.5
  11.2 0.4 fusion.102
  11.5 0.1 copy.30
  11.6 3.5 collective-permute-start.2
  15.1 1.0 copy.31
  16.1 1.3 collective-permute-start.3
  17.4 0.5 compare_convert_fusion.1
  17.9 0.5 iota_add_fusion
  18.4 0.5 and_convert_fusion.1
  19.0 0.5 and_convert_fusion
  19.5 21.9 %collective-permute-done.2 = bf16[17,26,5,128]{3,1,2,0:T(8,128)(2,1)S(1)} collective-permute-done((bf16[17,26,5,128]{3,1,2,0:T(8,128)(2,1)S(1)}, bf16[17,26,5,128]{3,1,2,0:T(8,128)(2,1)S(1)}, u32[]{:S(2)}, u32[]{:S(2)}) %collective-permute-start.2) | collective-permute-done | bytes 565792 | tf_op jit(solution)/shard_map/ppermute | solution.py:33
  41.4 0.3 copy.32
  41.7 1.7 copy.33
  43.5 4.7 fusion.12
  48.2 5.3 pad.28
  53.5 25.6 %reshape.351 = bf16[16,26,26,1,8,17]{5,4,2,1,0,3:T(8,128)(2,1)} reshape(bf16[16,26,26,1,136]{4,2,1,0,3:T(8,128)(2,1)} %pad.28) | data formatting | bytes 5883904 | tf_op jit(solution)/shard_map/conv_general_dilated | solution.py:126
  79.1 45.7 %copy.36 = bf16[16,26,26,1,8,17]{0,4,5,2,1,3:T(8,128)(2,1)} copy(bf16[16,26,26,1,8,17]{5,4,2,1,0,3:T(8,128)(2,1)} %reshape.351) | data formatting | bytes 5883904 | tf_op jit(solution)/shard_map/conv_general_dilated | solution.py:126
  124.8 2.6 slice.332
  127.4 1316.3 %fusion.9 = f32[24,24,8,17,3]{2,4,3,1,0:T(4,128)} fusion(bf16[16,26,26,1,7,2]{0,4,5,2,1,3:T(8,128)(2,1)S(1)} %slice.332, bf16[16,26,26,1,8,17]{0,4,5,2,1,3:T(8,128)(2,1)} %copy.36, pred[8,17]{0,1:T(8,128)(4,1)S(1)} %copy-done.22, bf16[3,16,3,3,3]{1,4,3,2,0:T(4,128)(2,1)S(1)} %copy-done), kind=kOutput, calls=%fused_computation.9 | convolution fusion | flops 213146112 | bytes 4187560 | tf_op jit(solution)/shard_map/conv_general_dilated | solution.py:126
  1443.7 19.2 %copy.38 = f32[24,24,8,17,3]{3,2,1,4,0:T(8,128)} copy(f32[24,24,8,17,3]{2,4,3,1,0:T(4,128)} %fusion.9) | data formatting | bytes 1880064 | tf_op jit(solution)/shard_map/conv_general_dilated | solution.py:126
  1462.9 5.0 reshape.343
  1467.9 0.3 fusion.68
  1468.3 0.1 fusion.71
  1468.5 0.1 fusion.106
  1468.5 0.1 fusion.108
  1468.7 0.1 fusion.110
  1468.9 1.0 copy-done.6
  1469.8 0.3 copy-done.8
  1470.1 0.3 copy-done.10
  1470.4 0.1 copy-done.12
  1470.4 0.1 copy-done.14
  1470.6 0.1 convert_bitcast_fusion.1
  1470.7 0.5 copy-done.17
  1471.2 0.2 compare_convert_fusion
  1471.4 0.8 fusion.99
  1472.2 0.1 broadcast_subtract_fusion
  1472.3 0.5 copy-done.2
  1472.8 2.6 fusion.20
  1475.4 0.7 fusion.100
  1476.1 0.1 broadcast_subtract_fusion.1
  1476.2 2.3 fusion.32
  1478.6 0.6 fusion.101
  1479.2 0.1 broadcast_subtract_fusion.2
  1479.4 2.1 fusion.44
  1481.5 0.4 fusion.103
  1481.9 0.1 broadcast_subtract_fusion.3
  1482.0 0.7 copy-done.4
  1482.7 2.5 multiply_reduce_fusion.5
  1485.3 4.8 collective-permute-start.4
  1490.0 0.8 collective-permute-done.4
  1490.9 3.6 collective-permute-done.5
  1494.5 2.2 collective-permute-start.6
  1496.7 1.6 collective-permute-done.6
  1498.3 2.9 collective-permute-start.7
  1501.2 1.6 collective-permute-done.7
  1502.8 3.0 collective-permute-start.8
  1505.9 0.8 copy.39
  1506.7 0.8 collective-permute-done.8
  1507.6 4.0 fusion.63
  (57 shorter events, 0.4 us)
Async XLA Ops:
  0.6 126.7 %copy-start = (bf16[3,16,3,3,3]{1,4,3,2,0:T(4,128)(2,1)S(1)}, bf16[3,16,3,3,3]{1,4,3,2,0:T(4,128)(2,1)}, u32[]{:S(2)}) copy-start(bf16[3,16,3,3,3]{1,4,3,2,0:T(4,128)(2,1)} %param.5) | copy-start | bytes 7780
  0.6 10.3 copy-start.5
  1.7 41.8 %copy-start.15 = (bf16[1,16,16,128]{3,2,1,0:T(8,128)(2,1)}, bf16[1,16,16,128]{3,2,1,0:T(8,128)(2,1)S(1)}, u32[]{:S(2)}) copy-start(bf16[1,16,16,128]{3,2,1,0:T(8,128)(2,1)S(1)} %convert_bitcast_fusion.2) | copy-start | bytes 196612
  2.8 3.7 collective-permute-start
  5.3 5.6 collective-permute-start.1
  6.6 36.9 %copy-start.11 = (bf16[17,5,16,128]{3,2,1,0:T(8,128)(2,1)}, bf16[17,5,16,128]{3,2,1,0:T(8,128)(2,1)S(1)}, u32[]{:S(2)}) copy-start(bf16[17,5,16,128]{3,2,1,0:T(8,128)(2,1)S(1)} %collective-permute-done) | copy-start | bytes 1044484
  10.9 32.6 %copy-start.13 = (bf16[17,5,16,128]{3,2,1,0:T(8,128)(2,1)}, bf16[17,5,16,128]{3,2,1,0:T(8,128)(2,1)S(1)}, u32[]{:S(2)}) copy-start(bf16[17,5,16,128]{3,2,1,0:T(8,128)(2,1)S(1)} %collective-permute-done.1) | copy-start | bytes 1044484
  11.6 29.7 %collective-permute-start.2 = (bf16[17,26,5,128]{3,1,2,0:T(8,128)(2,1)S(1)}, bf16[17,26,5,128]{3,1,2,0:T(8,128)(2,1)S(1)}, u32[]{:S(2)}, u32[]{:S(2)}) collective-permute-start(bf16[17,26,5,128]{3,1,2,0:T(8,128)(2,1)S(1)} %copy.30), channel_id=1, source_target_pairs={{0,1},{1,2},{2,3},{3,4},{4,5},{5,6},{6,7},{8,9},{9,10},{10,11},{11... | collective-permute-start | bytes 1697288 | tf_op jit(solution)/shard_map/ppermute | solution.py:33
  16.1 25.6 %collective-permute-start.3 = (bf16[17,26,5,128]{3,1,2,0:T(8,128)(2,1)}, bf16[17,26,5,128]{3,1,2,0:T(8,128)(2,1)}, u32[]{:S(2)}, u32[]{:S(2)}) collective-permute-start(bf16[17,26,5,128]{3,1,2,0:T(8,128)(2,1)} %copy.31), channel_id=1, source_target_pairs={{1,0},{2,1},{3,2},{4,3},{5,4},{6,5},{7,6},{9,8},{10,9},{11,10},{12... | collective-permute-start | bytes 1697288 | tf_op jit(solution)/shard_map/ppermute | solution.py:33
  41.7 6.5 copy-start.7
  43.5 4.7 copy-start.9
  124.8 2.6 copy-start.22
  1462.9 5.0 copy-start.21
  1462.9 5.4 copy-start.18
  1462.9 5.4 copy-start.19
  1462.9 5.4 copy-start.20
  1468.6 1.2 copy-start.6
  1468.6 1.5 copy-start.8
  1468.6 1.7 copy-start.10
  1468.6 1.8 copy-start.12
  1468.6 1.9 copy-start.14
  1468.7 1.9 copy-start.16
  1470.6 0.6 copy-start.17
  1471.4 1.4 copy-start.2
  1478.6 3.4 copy-start.3
  1481.5 1.2 copy-start.4
  1485.3 5.6 collective-permute-start.4
  1490.9 3.7 collective-permute-start.5
  1494.5 3.8 collective-permute-start.6
  1498.3 4.5 collective-permute-start.7
  1502.8 4.7 collective-permute-start.8
  1507.6 4.0 copy-start.1

commit v5 on v3

--- a/solution.py
+++ b/solution.py
@@ -35,22 +35,21 @@
 
 def conv_region(padded, conv_weight, count_z, count_y):
     col_cells = padded.shape[3] - 2
+    shifted = jnp.stack(
+        [padded[..., offset_x : offset_x + col_cells] for offset_x in range(3)], axis=1
+    )
     summed = jnp.zeros((3, count_z, count_y, col_cells), jnp.float32)
     for offset_z in range(3):
         for offset_y in range(3):
-            for offset_x in range(3):
-                window = padded[
-                    :,
-                    offset_z : offset_z + count_z,
-                    offset_y : offset_y + count_y,
-                    offset_x : offset_x + col_cells,
-                ]
-                summed = summed + jnp.einsum(
-                    "oc,czyx->ozyx",
-                    conv_weight[:, :, offset_z, offset_y, offset_x],
-                    window,
-                    preferred_element_type=jnp.float32,
-                )
+            window = shifted[
+                :, :, offset_z : offset_z + count_z, offset_y : offset_y + count_y
+            ]
+            summed = summed + jnp.einsum(
+                "oce,cezyx->ozyx",
+                conv_weight[:, :, offset_z, offset_y, :],
+                window,
+                preferred_element_type=jnp.float32,
+            )
     return summed
 
 

time: 92.3 us -> 85.9 us (0.931)
  matrix products: 11 us -> 6.24 us
  other arithmetic: 17 us -> 15.4 us
  starting transfers between devices: 30.9 us -> 29.9 us
    dot_general x27 -> x9, matrix products: 11 us -> 6.24 us  [conv_region(): jnp.einsum('oce,cezyx->ozyx', conv_weight[:, :, offset_z, offset_y, :], w...]
    ppermute x2, starting transfers between devices: 7.94 us -> 5.83 us  [padded_2(): lax.ppermute(tail, axis, [(i, (i + 1) % count) for i in range(ends)])]
    concatenate x1 -> x0, other arithmetic: 1.82 us -> none  [padded_2(): jnp.concatenate([lax.ppermute(tail, axis, [(i, (i + 1) % count) for i in...]
    ppermute x4, waiting for transfers between devices: 10.7 us -> 8.97 us  [from_behind(): return lax.ppermute(value, axis, pairs)]
    ppermute x2, waiting for transfers between devices: 4.68 us -> 6.23 us  [padded_2(): lax.ppermute(head, axis, [((i + 1) % count, i) for i in range(ends)])]
    ppermute x4, starting transfers between devices: 9.16 us -> 10.5 us  [from_behind(): return lax.ppermute(value, axis, pairs)]
    unnamed x18 -> x17, local copies, waits for them, and re-layouts: 5.12 us -> 4.27 us
  transfers between devices with their start and end apart: 13 -> 13, of which waited for: 10 -> 11; matrix products, arithmetic and copies ran while one was open for 3% -> 3% of each run, Pallas kernels for 0% -> 0%
where the time goes in v5:
time: 85.9 us; the launch traced here: 85.6 us
  starting transfers between devices  29.9 us (35%)
  waiting for transfers between devices  23.2 us (27%)
  other arithmetic  15.4 us (18%)
  local copies, waits for them, and re-layouts  9.68 us (11%)
  matrix products  6.24 us (7%)
  between operations  1.08 us (1%)
    ppermute x5, starting transfers between devices, all_sum(): lax.ppermute(value, axis, [(i, i ^ hop) for i in range(devices)])  11 us
    ppermute x4, starting transfers between devices, from_behind(): return lax.ppermute(value, axis, pairs)  10.5 us
    ppermute x4, waiting for transfers between devices, from_behind(): return lax.ppermute(value, axis, pairs)  8.97 us
    ppermute x5, waiting for transfers between devices, all_sum(): lax.ppermute(value, axis, [(i, i ^ hop) for i in range(devices)])  7.44 us
    dot_general x9, matrix products, conv_region(): jnp.einsum('oce,cezyx->ozyx', conv_weight[:, :, offset_z, offset_y, :], w...  6.24 us
    ppermute x2, waiting for transfers between devices, padded_2(): lax.ppermute(head, axis, [((i + 1) % count, i) for i in range(ends)])  6.23 us
    ppermute x2, starting transfers between devices, padded_2(): lax.ppermute(tail, axis, [(i, (i + 1) % count) for i in range(ends)])  5.83 us
    add x2, other arithmetic, operate_inside(): return (1.0 - mask) * (laplace + RIDGE_WEIGHT * centre) + mask * centre  4.43 us
  transfers between devices with their start and end apart: 13, of which 11 were waited for; matrix products, arithmetic and copies ran while one was open for 3% of the time, Pallas kernels for 0%

profile of v5, /device:TPU:0, one launch (start us, length us, event | category | flops | bytes accessed | tf_op | source)
XLA Modules:
  0.0 85.6 jit_solution(1678391301221193113)
XLA Ops:
  0.6 0.9 %fusion.97 = (bf16[16,1,16,128]{3,2,1,0:T(8,128)(2,1)S(1)}, bf16[16,1,16,128]{3,2,1,0:T(8,128)(2,1)S(1)}) fusion(bf16[16,16,16,128]{3,2,1,0:T(8,128)(2,1)} %param.4), kind=kLoop, calls=%fused_computation.192 | loop fusion | bytes 262144 | tf_op jit(solution)/shard_map/slice | solution.py:17
  1.6 2.4 %collective-permute-start = (bf16[16,1,16,128]{3,0,2,1:T(8,128)(2,1)S(1)}, bf16[16,1,16,128]{3,0,2,1:T(8,128)(2,1)S(1)}, u32[]{:S(2)}, u32[]{:S(2)}) collective-permute-start(bf16[16,1,16,128]{3,0,2,1:T(8,128)(2,1)S(1)} %copy.67), channel_id=1, source_target_pairs={{0,8},{8,16},{16,24},{1,9},{9,17},{17,25},{2,10},{10,18},{18,26},{... | collective-permute-start | bytes 196616 | tf_op jit(solution)/shard_map/ppermute | solution.py:21
  4.0 1.3 %collective-permute-start.1 = (bf16[16,1,16,128]{3,0,2,1:T(8,128)(2,1)S(1)}, bf16[16,1,16,128]{3,0,2,1:T(8,128)(2,1)S(1)}, u32[]{:S(2)}, u32[]{:S(2)}) collective-permute-start(bf16[16,1,16,128]{3,0,2,1:T(8,128)(2,1)S(1)} %copy.68), channel_id=1, source_target_pairs={{8,0},{16,8},{24,16},{9,1},{17,9},{25,17},{10,2},{18,10},{26,18},{... | collective-permute-start | bytes 196616 | tf_op jit(solution)/shard_map/ppermute | solution.py:23
  5.4 2.0 %constant_dynamic-update-slice_fusion.1 = bf16[16,18,16,128]{3,0,2,1:T(8,128)(2,1)S(1)} fusion(bf16[16,18,16,128]{3,0,2,1:T(8,128)(2,1)S(1)} %constant_dynamic-update-slice_fusion.2, bf16[16,16,16,128]{3,2,1,0:T(8,128)(2,1)} %param.4), kind=kLoop, calls=%fused_computation.127 | loop fusion | bytes 2097152
  7.3 1.9 %collective-permute-done.1 = bf16[16,1,16,128]{3,0,2,1:T(8,128)(2,1)S(1)} collective-permute-done((bf16[16,1,16,128]{3,0,2,1:T(8,128)(2,1)S(1)}, bf16[16,1,16,128]{3,0,2,1:T(8,128)(2,1)S(1)}, u32[]{:S(2)}, u32[]{:S(2)}) %collective-permute-start.1) | collective-permute-done | bytes 65568 | tf_op jit(solution)/shard_map/ppermute | solution.py:23
  9.3 3.4 %collective-permute-start.2 = (bf16[16,18,1,128]{3,0,2,1:T(8,128)(2,1)S(1)}, bf16[16,18,1,128]{3,0,2,1:T(8,128)(2,1)S(1)}, u32[]{:S(2)}, u32[]{:S(2)}) collective-permute-start(bf16[16,18,1,128]{3,0,2,1:T(8,128)(2,1)S(1)} %get-tuple-element.37), channel_id=1, source_target_pairs={{0,1},{1,2},{2,3},{3,4},{4,5},{5,6},{6,7},{8,9},{9,10},{10,11},{11... | collective-permute-start | bytes 221192 | tf_op jit(solution)/shard_map/ppermute | solution.py:21
  12.7 1.3 %collective-permute-start.3 = (bf16[16,18,1,128]{3,0,2,1:T(8,128)(2,1)S(1)}, bf16[16,18,1,128]{3,0,2,1:T(8,128)(2,1)S(1)}, u32[]{:S(2)}, u32[]{:S(2)}) collective-permute-start(bf16[16,18,1,128]{3,0,2,1:T(8,128)(2,1)S(1)} %get-tuple-element.38), channel_id=1, source_target_pairs={{1,0},{2,1},{3,2},{4,3},{5,4},{6,5},{7,6},{9,8},{10,9},{11,10},{12... | collective-permute-start | bytes 221192 | tf_op jit(solution)/shard_map/ppermute | solution.py:23
  14.1 0.6 collective-permute-done.2
  14.7 4.3 %collective-permute-done.3 = bf16[16,18,1,128]{3,0,2,1:T(8,128)(2,1)S(1)} collective-permute-done((bf16[16,18,1,128]{3,0,2,1:T(8,128)(2,1)S(1)}, bf16[16,18,1,128]{3,0,2,1:T(8,128)(2,1)S(1)}, u32[]{:S(2)}, u32[]{:S(2)}) %collective-permute-start.3) | collective-permute-done | bytes 73760 | tf_op jit(solution)/shard_map/ppermute | solution.py:23
  19.0 0.2 fusion.86
  19.2 0.8 fusion.37
  20.0 0.6 convolution_bitcast_fusion.7
  20.5 0.6 convolution_bitcast_fusion.6
  21.1 0.6 convolution_bitcast_fusion.5
  21.7 0.6 convolution_bitcast_fusion.4
  22.3 0.6 convolution_bitcast_fusion.3
  22.9 0.6 convolution_bitcast_fusion.2
  23.5 0.6 convolution_bitcast_fusion.1
  24.1 0.6 convolution_bitcast_fusion
  24.7 0.1 copy-done.5
  24.7 1.5 %fusion.52 = f32[3,16,16,128]{3,0,2,1:T(4,128)S(1)} fusion(f32[16,16,128,3]{2,3,1,0:T(4,128)S(1)} %convolution_bitcast_fusion, f32[16,16,128,3]{2,3,1,0:T(4,128)S(1)} %convolution_bitcast_fusion.1, f32[16,16,128,3]{2,3,1,0:T(4,128)S(1)} %convolution_bitcast_fusion.2, f32[16,16,128,3]{2,3,1,0:T(4,128)S(1)} %convolution_bitcast_fusion.3, ...), kind=kOutput, calls=%fused_computation.79 | convolution fusion | flops 22560768 | bytes 7520556 | tf_op jit(solution)/shard_map/oce,cezyx->ozyx/dot_general | solution.py:47
  26.3 0.1 pad_maximum_fusion.8
  26.4 3.4 %collective-permute-start.4 = (f32[4,4,16,128]{3,0,2,1:T(4,128)S(1)}, f32[4,4,16,128]{3,0,2,1:T(4,128)S(1)}, u32[]{:S(2)}, u32[]{:S(2)}) collective-permute-start(f32[4,4,16,128]{3,0,2,1:T(4,128)S(1)} %get-tuple-element.43), channel_id=1, source_target_pairs={{0,8},{8,16},{16,24},{1,9},{9,17},{17,25},{2,10},{10,18},{18,26},{... | collective-permute-start | bytes 393224 | tf_op jit(solution)/shard_map/ppermute | solution.py:33
  29.8 1.3 %collective-permute-start.5 = (f32[4,4,16,128]{3,0,2,1:T(4,128)S(1)}, f32[4,4,16,128]{3,0,2,1:T(4,128)S(1)}, u32[]{:S(2)}, u32[]{:S(2)}) collective-permute-start(f32[4,4,16,128]{3,0,2,1:T(4,128)S(1)} %get-tuple-element.44), channel_id=1, source_target_pairs={{8,0},{16,8},{24,16},{9,1},{17,9},{25,17},{10,2},{18,10},{26,18},{... | collective-permute-start | bytes 393224 | tf_op jit(solution)/shard_map/ppermute | solution.py:33
  31.2 2.9 %collective-permute-done.5 = f32[4,4,16,128]{3,0,2,1:T(4,128)S(1)} collective-permute-done((f32[4,4,16,128]{3,0,2,1:T(4,128)S(1)}, f32[4,4,16,128]{3,0,2,1:T(4,128)S(1)}, u32[]{:S(2)}, u32[]{:S(2)}) %collective-permute-start.5) | collective-permute-done | bytes 131104 | tf_op jit(solution)/shard_map/ppermute | solution.py:33
  34.1 0.1 pad_maximum_fusion.6
  34.2 4.3 %collective-permute-start.6 = (f32[4,24,4,128]{3,0,2,1:T(4,128)S(1)}, f32[4,24,4,128]{3,0,2,1:T(4,128)S(1)}, u32[]{:S(2)}, u32[]{:S(2)}) collective-permute-start(f32[4,24,4,128]{3,0,2,1:T(4,128)S(1)} %get-tuple-element.41), channel_id=1, source_target_pairs={{0,1},{1,2},{2,3},{3,4},{4,5},{5,6},{6,7},{8,9},{9,10},{10,11},{11... | collective-permute-start | bytes 589832 | tf_op jit(solution)/shard_map/ppermute | solution.py:33
  38.6 1.5 %collective-permute-start.7 = (f32[4,24,4,128]{3,0,2,1:T(4,128)S(1)}, f32[4,24,4,128]{3,0,2,1:T(4,128)S(1)}, u32[]{:S(2)}, u32[]{:S(2)}) collective-permute-start(f32[4,24,4,128]{3,0,2,1:T(4,128)S(1)} %get-tuple-element.42), channel_id=1, source_target_pairs={{1,0},{2,1},{3,2},{4,3},{5,4},{6,5},{7,6},{9,8},{10,9},{11,10},{12... | collective-permute-start | bytes 589832 | tf_op jit(solution)/shard_map/ppermute | solution.py:33
  40.1 1.6 %collective-permute-done.6 = f32[4,24,4,128]{3,0,2,1:T(4,128)S(1)} collective-permute-done((f32[4,24,4,128]{3,0,2,1:T(4,128)S(1)}, f32[4,24,4,128]{3,0,2,1:T(4,128)S(1)}, u32[]{:S(2)}, u32[]{:S(2)}) %collective-permute-start.6) | collective-permute-done | bytes 196640 | tf_op jit(solution)/shard_map/ppermute | solution.py:33
  41.7 4.4 %collective-permute-done.7 = f32[4,24,4,128]{3,0,2,1:T(4,128)S(1)} collective-permute-done((f32[4,24,4,128]{3,0,2,1:T(4,128)S(1)}, f32[4,24,4,128]{3,0,2,1:T(4,128)S(1)}, u32[]{:S(2)}, u32[]{:S(2)}) %collective-permute-start.7) | collective-permute-done | bytes 196640 | tf_op jit(solution)/shard_map/ppermute | solution.py:33
  46.1 0.4 pad_maximum_fusion.2
  46.6 0.9 %fusion.95 = (f32[1,24,24,128]{3,0,2,1:T(1,128)S(1)}, f32[1,24,24,128]{3,0,2,1:T(1,128)S(1)}, f32[1,24,24,128]{3,0,2,1:T(1,128)S(1)}, f32[1,24,24,128]{3,0,2,1:T(1,128)S(1)}) fusion(f32[4,24,24,128]{3,0,2,1:T(4,128)S(1)} %pad_maximum_fusion.2), kind=kLoop, calls=%fused_computation.190 | loop fusion | bytes 2359296 | tf_op jit(solution)/shard_map/slice | solution.py:138
  47.4 0.1 broadcast_multiply_fusion.2
  47.5 0.1 broadcast_multiply_fusion.1
  47.6 0.1 fusion.102
  47.7 0.1 fusion.104
  47.9 0.1 fusion.100
  48.1 0.1 broadcast_subtract_fusion.1
  48.2 0.1 broadcast_subtract_fusion
  48.4 0.2 compare_convert_fusion
  48.6 0.8 fusion.91
  49.4 0.7 copy-done
  50.0 2.6 %fusion.7 = f32[8,22,22,128]{3,2,1,0:T(8,128)S(1)} fusion(f32[8,24,24,128]{3,2,1,0:T(8,128)S(1)} %compare_convert_fusion, f32[8,22,22,127]{3,2,1,0:T(8,128)S(1)} %get-tuple-element.22, f32[8,22,22,127]{3,2,1,0:T(8,128)S(1)} %get-tuple-element.21, f32[22,22,128]{2,1,0:T(8,128)S(1)} %get-tuple-element.64, f32[22,22,128]{2,1,0:T(8,128)S(1)} %get-tuple-element.80, ...), kind=kLoop, calls=%fused_computation.12 | loop fusion | flops 11399168 | bytes 17811200 | tf_op jit(solution)/shard_map/sub | solution.py:148
  52.6 0.7 fusion.92
  53.3 2.3 %fusion.19 = f32[8,20,20,128]{3,2,1,0:T(8,128)S(1)} fusion(f32[8,22,22,128]{3,2,1,0:T(8,128)S(1)} %fusion.7, f32[8,20,20,127]{3,2,1,0:T(8,128)S(1)} %get-tuple-element.24, f32[8,20,20,127]{3,2,1,0:T(8,128)S(1)} %get-tuple-element.23, f32[20,20,128]{2,1,0:T(8,128)S(1)} %get-tuple-element.58, f32[20,20,128]{2,1,0:T(8,128)S(1)} %get-tuple-element.83, ...), kind=kLoop, calls=%fused_computation.28 | loop fusion | flops 9011200 | bytes 14720000 | tf_op jit(solution)/shard_map/add | solution.py:90
  55.7 0.6 fusion.93
  56.3 0.1 broadcast_subtract_fusion.2
  56.4 2.1 %fusion.31 = f32[8,18,18,128]{3,2,1,0:T(8,128)S(1)} fusion(f32[8,20,20,128]{3,2,1,0:T(8,128)S(1)} %fusion.19, f32[8,18,18,127]{3,2,1,0:T(8,128)S(1)} %get-tuple-element.26, f32[8,18,18,127]{3,2,1,0:T(8,128)S(1)} %get-tuple-element.25, f32[18,18,128]{2,1,0:T(8,128)S(1)} %get-tuple-element.52, f32[18,18,128]{2,1,0:T(8,128)S(1)} %get-tuple-element.86, ...), kind=kLoop, calls=%fused_computation.44 | loop fusion | flops 7299072 | bytes 11923200 | tf_op jit(solution)/shard_map/add | solution.py:90
  58.6 0.4 fusion.94
  58.9 0.1 broadcast_subtract_fusion.3
  59.1 0.7 copy-done.2
  59.8 2.5 %multiply_reduce_fusion.5 = (f32[8]{0:T(128)S(1)}, f32[8]{0:T(128)S(1)}, f32[8]{0:T(128)S(1)}, f32[8]{0:T(128)S(1)}, f32[8]{0:T(128)S(1)}, /*index=5*/f32[8]{0:T...) fusion(f32[8,22,22,128]{3,2,1,0:T(8,128)S(1)} %fusion.7, f32[8,20,20,128]{3,2,1,0:T(8,128)S(1)} %fusion.19, ...), kind=kLoop, calls=%fused_computation.104 | loop fusion | flops 10485688 | bytes 10469664 | tf_op jit(solution)/shard_map/reduce_sum | solution.py:107
  62.4 2.6 %collective-permute-start.8 = (f32[9,8]{1,0:T(8,128)S(1)}, f32[9,8]{1,0:T(8,128)S(1)}, u32[]{:S(2)}, u32[]{:S(2)}) collective-permute-start(f32[9,8]{1,0:T(8,128)S(1)} %stack.55), channel_id=1, source_target_pairs={{0,8},{8,0},{16,24},{24,16},{1,9},{9,1},{17,25},{25,17},{2,10},{10... | collective-permute-start | bytes 872 | tf_op jit(solution)/shard_map/ppermute | solution.py:101
  64.9 0.8 collective-permute-done.8
  65.7 1.1 %collective-permute-start.9 = (f32[9,8]{1,0:T(8,128)S(1)}, f32[9,8]{1,0:T(8,128)S(1)}, u32[]{:S(2)}, u32[]{:S(2)}) collective-permute-start(f32[9,8]{1,0:T(8,128)S(1)} %add.582), channel_id=1, source_target_pairs={{0,16},{8,24},{16,0},{24,8},{1,17},{9,25},{17,1},{25,9},{2,18},{10... | collective-permute-start | bytes 872 | tf_op jit(solution)/shard_map/ppermute | solution.py:101
  66.9 2.5 %collective-permute-done.9 = f32[9,8]{1,0:T(8,128)S(1)} collective-permute-done((f32[9,8]{1,0:T(8,128)S(1)}, f32[9,8]{1,0:T(8,128)S(1)}, u32[]{:S(2)}, u32[]{:S(2)}) %collective-permute-start.9) | collective-permute-done | bytes 320 | tf_op jit(solution)/shard_map/ppermute | solution.py:101
  69.4 2.2 %collective-permute-start.10 = (f32[9,8]{1,0:T(8,128)S(1)}, f32[9,8]{1,0:T(8,128)S(1)}, u32[]{:S(2)}, u32[]{:S(2)}) collective-permute-start(f32[9,8]{1,0:T(8,128)S(1)} %add.583), channel_id=1, source_target_pairs={{0,1},{1,0},{2,3},{3,2},{4,5},{5,4},{6,7},{7,6},{8,9},{9,8},{10,11... | collective-permute-start | bytes 872 | tf_op jit(solution)/shard_map/ppermute | solution.py:101
  71.6 1.6 %collective-permute-done.10 = f32[9,8]{1,0:T(8,128)S(1)} collective-permute-done((f32[9,8]{1,0:T(8,128)S(1)}, f32[9,8]{1,0:T(8,128)S(1)}, u32[]{:S(2)}, u32[]{:S(2)}) %collective-permute-start.10) | collective-permute-done | bytes 320 | tf_op jit(solution)/shard_map/ppermute | solution.py:101
  73.2 2.1 %collective-permute-start.11 = (f32[9,8]{1,0:T(8,128)S(1)}, f32[9,8]{1,0:T(8,128)S(1)}, u32[]{:S(2)}, u32[]{:S(2)}) collective-permute-start(f32[9,8]{1,0:T(8,128)S(1)} %add.584), channel_id=1, source_target_pairs={{0,2},{1,3},{2,0},{3,1},{4,6},{5,7},{6,4},{7,5},{8,10},{9,11},{10,... | collective-permute-start | bytes 872 | tf_op jit(solution)/shard_map/ppermute | solution.py:101
  75.3 1.6 %collective-permute-done.11 = f32[9,8]{1,0:T(8,128)S(1)} collective-permute-done((f32[9,8]{1,0:T(8,128)S(1)}, f32[9,8]{1,0:T(8,128)S(1)}, u32[]{:S(2)}, u32[]{:S(2)}) %collective-permute-start.11) | collective-permute-done | bytes 320 | tf_op jit(solution)/shard_map/ppermute | solution.py:101
  76.9 3.0 %collective-permute-start.12 = (f32[9,8]{1,0:T(8,128)S(1)}, f32[9,8]{1,0:T(8,128)S(1)}, u32[]{:S(2)}, u32[]{:S(2)}) collective-permute-start(f32[9,8]{1,0:T(8,128)S(1)} %add.585), channel_id=1, source_target_pairs={{0,4},{1,5},{2,6},{3,7},{4,0},{5,1},{6,2},{7,3},{8,12},{9,13},{10,... | collective-permute-start | bytes 872 | tf_op jit(solution)/shard_map/ppermute | solution.py:101
  80.0 0.8 copy.20
  80.7 0.8 collective-permute-done.12
  81.7 3.9 %fusion.66 = f32[8,16,16,128]{3,2,1,0:T(8,128)} fusion(f32[8,24,24,128]{3,2,1,0:T(8,128)} %copy-done, f32[8,20,20,128]{3,2,1,0:T(8,128)} %copy-done.1, f32[8,22,22,128]{3,2,1,0:T(8,128)S(1)} %fusion.7, f32[8,18,18,128]{3,2,1,0:T(8,128)} %copy-done.2, f32[8]{0:T(128)S(1)} %get-tuple-element.79, f32[8]{0:T(128)S(1)} %get-tuple-element.78, ...), kind=kLoop, calls=%fused_computation.98 | loop fusion | flops 1572864 | bytes 5242976 | tf_op jit(solution)/shard_map/add | solution.py:212
  (38 shorter events, 0.5 us)
Async XLA Ops:
  0.6 13.4 %copy-start.4 = (bf16[3,16,3,3,3]{1,4,3,2,0:T(4,128)(2,1)S(1)}, bf16[3,16,3,3,3]{1,4,3,2,0:T(4,128)(2,1)}, u32[]{:S(2)}) copy-start(bf16[3,16,3,3,3]{1,4,3,2,0:T(4,128)(2,1)} %param.5) | copy-start | bytes 7780
  0.6 13.4 %copy-start.3 = (s32[16,16,128]{2,1,0:T(8,128)S(1)}, s32[16,16,128]{2,1,0:T(8,128)}, u32[]{:S(2)}) copy-start(s32[16,16,128]{2,1,0:T(8,128)} %param.7) | copy-start | bytes 393220
  1.6 3.7 %collective-permute-start = (bf16[16,1,16,128]{3,0,2,1:T(8,128)(2,1)S(1)}, bf16[16,1,16,128]{3,0,2,1:T(8,128)(2,1)S(1)}, u32[]{:S(2)}, u32[]{:S(2)}) collective-permute-start(bf16[16,1,16,128]{3,0,2,1:T(8,128)(2,1)S(1)} %copy.67), channel_id=1, source_target_pairs={{0,8},{8,16},{16,24},{1,9},{9,17},{17,25},{2,10},{10,18},{18,26},{... | collective-permute-start | bytes 196616 | tf_op jit(solution)/shard_map/ppermute | solution.py:21
  4.0 5.2 %collective-permute-start.1 = (bf16[16,1,16,128]{3,0,2,1:T(8,128)(2,1)S(1)}, bf16[16,1,16,128]{3,0,2,1:T(8,128)(2,1)S(1)}, u32[]{:S(2)}, u32[]{:S(2)}) collective-permute-start(bf16[16,1,16,128]{3,0,2,1:T(8,128)(2,1)S(1)} %copy.68), channel_id=1, source_target_pairs={{8,0},{16,8},{24,16},{9,1},{17,9},{25,17},{10,2},{18,10},{26,18},{... | collective-permute-start | bytes 196616 | tf_op jit(solution)/shard_map/ppermute | solution.py:23
  9.3 5.4 %collective-permute-start.2 = (bf16[16,18,1,128]{3,0,2,1:T(8,128)(2,1)S(1)}, bf16[16,18,1,128]{3,0,2,1:T(8,128)(2,1)S(1)}, u32[]{:S(2)}, u32[]{:S(2)}) collective-permute-start(bf16[16,18,1,128]{3,0,2,1:T(8,128)(2,1)S(1)} %get-tuple-element.37), channel_id=1, source_target_pairs={{0,1},{1,2},{2,3},{3,4},{4,5},{5,6},{6,7},{8,9},{9,10},{10,11},{11... | collective-permute-start | bytes 221192 | tf_op jit(solution)/shard_map/ppermute | solution.py:21
  12.7 6.2 %collective-permute-start.3 = (bf16[16,18,1,128]{3,0,2,1:T(8,128)(2,1)S(1)}, bf16[16,18,1,128]{3,0,2,1:T(8,128)(2,1)S(1)}, u32[]{:S(2)}, u32[]{:S(2)}) collective-permute-start(bf16[16,18,1,128]{3,0,2,1:T(8,128)(2,1)S(1)} %get-tuple-element.38), channel_id=1, source_target_pairs={{1,0},{2,1},{3,2},{4,3},{5,4},{6,5},{7,6},{9,8},{10,9},{11,10},{12... | collective-permute-start | bytes 221192 | tf_op jit(solution)/shard_map/ppermute | solution.py:23
  24.1 0.7 copy-start.5
  26.4 4.8 %collective-permute-start.4 = (f32[4,4,16,128]{3,0,2,1:T(4,128)S(1)}, f32[4,4,16,128]{3,0,2,1:T(4,128)S(1)}, u32[]{:S(2)}, u32[]{:S(2)}) collective-permute-start(f32[4,4,16,128]{3,0,2,1:T(4,128)S(1)} %get-tuple-element.43), channel_id=1, source_target_pairs={{0,8},{8,16},{16,24},{1,9},{9,17},{17,25},{2,10},{10,18},{18,26},{... | collective-permute-start | bytes 393224 | tf_op jit(solution)/shard_map/ppermute | solution.py:33
  29.8 4.3 %collective-permute-start.5 = (f32[4,4,16,128]{3,0,2,1:T(4,128)S(1)}, f32[4,4,16,128]{3,0,2,1:T(4,128)S(1)}, u32[]{:S(2)}, u32[]{:S(2)}) collective-permute-start(f32[4,4,16,128]{3,0,2,1:T(4,128)S(1)} %get-tuple-element.44), channel_id=1, source_target_pairs={{8,0},{16,8},{24,16},{9,1},{17,9},{25,17},{10,2},{18,10},{26,18},{... | collective-permute-start | bytes 393224 | tf_op jit(solution)/shard_map/ppermute | solution.py:33
  34.2 7.5 %collective-permute-start.6 = (f32[4,24,4,128]{3,0,2,1:T(4,128)S(1)}, f32[4,24,4,128]{3,0,2,1:T(4,128)S(1)}, u32[]{:S(2)}, u32[]{:S(2)}) collective-permute-start(f32[4,24,4,128]{3,0,2,1:T(4,128)S(1)} %get-tuple-element.41), channel_id=1, source_target_pairs={{0,1},{1,2},{2,3},{3,4},{4,5},{5,6},{6,7},{8,9},{9,10},{10,11},{11... | collective-permute-start | bytes 589832 | tf_op jit(solution)/shard_map/ppermute | solution.py:33
  38.6 7.6 %collective-permute-start.7 = (f32[4,24,4,128]{3,0,2,1:T(4,128)S(1)}, f32[4,24,4,128]{3,0,2,1:T(4,128)S(1)}, u32[]{:S(2)}, u32[]{:S(2)}) collective-permute-start(f32[4,24,4,128]{3,0,2,1:T(4,128)S(1)} %get-tuple-element.42), channel_id=1, source_target_pairs={{1,0},{2,1},{3,2},{4,3},{5,4},{6,5},{7,6},{9,8},{10,9},{11,10},{12... | collective-permute-start | bytes 589832 | tf_op jit(solution)/shard_map/ppermute | solution.py:33
  48.6 1.4 %copy-start = (f32[8,24,24,128]{3,2,1,0:T(8,128)}, f32[8,24,24,128]{3,2,1,0:T(8,128)S(1)}, u32[]{:S(2)}) copy-start(f32[8,24,24,128]{3,2,1,0:T(8,128)S(1)} %compare_convert_fusion) | copy-start | bytes 7077892
  55.7 3.4 %copy-start.1 = (f32[8,20,20,128]{3,2,1,0:T(8,128)}, f32[8,20,20,128]{3,2,1,0:T(8,128)S(1)}, u32[]{:S(2)}) copy-start(f32[8,20,20,128]{3,2,1,0:T(8,128)S(1)} %fusion.19) | copy-start | bytes 4915204
  58.5 1.2 %copy-start.2 = (f32[8,18,18,128]{3,2,1,0:T(8,128)}, f32[8,18,18,128]{3,2,1,0:T(8,128)S(1)}, u32[]{:S(2)}) copy-start(f32[8,18,18,128]{3,2,1,0:T(8,128)S(1)} %fusion.31) | copy-start | bytes 3981316
  62.4 3.4 %collective-permute-start.8 = (f32[9,8]{1,0:T(8,128)S(1)}, f32[9,8]{1,0:T(8,128)S(1)}, u32[]{:S(2)}, u32[]{:S(2)}) collective-permute-start(f32[9,8]{1,0:T(8,128)S(1)} %stack.55), channel_id=1, source_target_pairs={{0,8},{8,0},{16,24},{24,16},{1,9},{9,1},{17,25},{25,17},{2,10},{10... | collective-permute-start | bytes 872 | tf_op jit(solution)/shard_map/ppermute | solution.py:101
  65.7 3.7 %collective-permute-start.9 = (f32[9,8]{1,0:T(8,128)S(1)}, f32[9,8]{1,0:T(8,128)S(1)}, u32[]{:S(2)}, u32[]{:S(2)}) collective-permute-start(f32[9,8]{1,0:T(8,128)S(1)} %add.582), channel_id=1, source_target_pairs={{0,16},{8,24},{16,0},{24,8},{1,17},{9,25},{17,1},{25,9},{2,18},{10... | collective-permute-start | bytes 872 | tf_op jit(solution)/shard_map/ppermute | solution.py:101
  69.4 3.8 %collective-permute-start.10 = (f32[9,8]{1,0:T(8,128)S(1)}, f32[9,8]{1,0:T(8,128)S(1)}, u32[]{:S(2)}, u32[]{:S(2)}) collective-permute-start(f32[9,8]{1,0:T(8,128)S(1)} %add.583), channel_id=1, source_target_pairs={{0,1},{1,0},{2,3},{3,2},{4,5},{5,4},{6,7},{7,6},{8,9},{9,8},{10,11... | collective-permute-start | bytes 872 | tf_op jit(solution)/shard_map/ppermute | solution.py:101
  73.2 3.7 %collective-permute-start.11 = (f32[9,8]{1,0:T(8,128)S(1)}, f32[9,8]{1,0:T(8,128)S(1)}, u32[]{:S(2)}, u32[]{:S(2)}) collective-permute-start(f32[9,8]{1,0:T(8,128)S(1)} %add.584), channel_id=1, source_target_pairs={{0,2},{1,3},{2,0},{3,1},{4,6},{5,7},{6,4},{7,5},{8,10},{9,11},{10,... | collective-permute-start | bytes 872 | tf_op jit(solution)/shard_map/ppermute | solution.py:101
  76.9 4.7 %collective-permute-start.12 = (f32[9,8]{1,0:T(8,128)S(1)}, f32[9,8]{1,0:T(8,128)S(1)}, u32[]{:S(2)}, u32[]{:S(2)}) collective-permute-start(f32[9,8]{1,0:T(8,128)S(1)} %add.585), channel_id=1, source_target_pairs={{0,4},{1,5},{2,6},{3,7},{4,0},{5,1},{6,2},{7,3},{8,12},{9,13},{10,... | collective-permute-start | bytes 872 | tf_op jit(solution)/shard_map/ppermute | solution.py:101

commit v6 on v5

--- a/solution.py
+++ b/solution.py
@@ -64,30 +64,45 @@
     return cells
 
 
-def operate_inside(field, grid, offset):
+def operator_cells(grid):
     weight_zup, weight_yup, weight_x, seeded = grid
-    count = field.shape[1] - 2
-    inner = slice(offset, offset + count)
-    lower = slice(offset - 1, offset - 1 + count)
-    centre = field[:, 1:-1, 1:-1]
+    inner = slice(1, weight_zup.shape[0] - 1)
+    lower = slice(0, weight_zup.shape[0] - 2)
     weight_xup = weight_x[inner, inner]
     weight_xdown = jnp.pad(weight_xup, ((0, 0), (0, 0), (1, 0)))[:, :, :-1]
+    edges = (
+        weight_zup[inner, inner],
+        weight_zup[lower, inner],
+        weight_yup[inner, inner],
+        weight_yup[inner, lower],
+        weight_xup,
+        weight_xdown,
+    )
+    mask = seeded[inner, inner]
+    free = 1.0 - mask
+    total = edges[0] + edges[1] + edges[2] + edges[3] + edges[4] + edges[5]
+    diagonal = free * (total + RIDGE_WEIGHT) + mask
+    return diagonal, tuple(free * edge for edge in edges)
+
+
+def operate_inside(field, cells, offset):
+    diagonal, edges = cells
+    count = field.shape[1] - 2
+    part = slice(offset - 1, offset - 1 + count)
+    centre = field[:, 1:-1, 1:-1]
     zero_col = jnp.zeros_like(centre[..., :1])
-    laplace = weight_zup[inner, inner] * (centre - field[:, 2:, 1:-1]) + weight_zup[lower, inner] * (
-        centre - field[:, :-2, 1:-1]
-    )
-    laplace = (
-        laplace
-        + weight_yup[inner, inner] * (centre - field[:, 1:-1, 2:])
-        + weight_yup[inner, lower] * (centre - field[:, 1:-1, :-2])
-    )
-    laplace = (
-        laplace
-        + weight_xup * (centre - jnp.concatenate([centre[..., 1:], zero_col], axis=3))
-        + weight_xdown * (centre - jnp.concatenate([zero_col, centre[..., :-1]], axis=3))
-    )
-    mask = seeded[inner, inner]
-    return (1.0 - mask) * (laplace + RIDGE_WEIGHT * centre) + mask * centre
+    near = (
+        field[:, 2:, 1:-1],
+        field[:, :-2, 1:-1],
+        field[:, 1:-1, 2:],
+        field[:, 1:-1, :-2],
+        jnp.concatenate([centre[..., 1:], zero_col], axis=3),
+        jnp.concatenate([zero_col, centre[..., :-1]], axis=3),
+    )
+    coupled = edges[0][part, part] * near[0]
+    for edge, value in zip(edges[1:], near[1:]):
+        coupled = coupled + edge[part, part] * value
+    return diagonal[part, part] * centre - coupled
 
 
 def all_sum(value, axes):
@@ -145,10 +160,11 @@
     seed_field = grid_seed[:, halo:-halo, halo:-halo]
 
     inside = grid_seed[:, 1:-1, 1:-1]
-    current = inside - operate_inside(grid_seed, grid, 1)
+    cells = operator_cells(grid)
+    current = inside - operate_inside(grid_seed, cells, 1)
     basis = [current]
     for power in range(ITERS):
-        current = operate_inside(current, grid, power + 2)
+        current = operate_inside(current, cells, power + 2)
         basis.append(current)
     basis = [
         vector[:, (vector.shape[1] - depth_cells) // 2 : (vector.shape[1] + depth_cells) // 2,

time: 85.9 us -> 84 us (0.978)
  other arithmetic: 15.4 us -> 13.3 us
    add x2 -> x1, other arithmetic: 4.43 us -> 0.21 us  [operator_cells(): diagonal = free * (total + RIDGE_WEIGHT) + mask]
    sub x5 -> x3, other arithmetic: 3.08 us -> 5.36 us  [the longest x2 3.29 us: operate_inside(): return diagonal[part, part] * centre - coupled]
where the time goes in v6:
time: 84 us; the launch traced here: 83.7 us
  starting transfers between devices  29.9 us (36%)
  waiting for transfers between devices  23.2 us (28%)
  other arithmetic  13.3 us (16%)
  local copies, waits for them, and re-layouts  9.83 us (12%)
  matrix products  6.24 us (7%)
  between operations  1.18 us (1%)
    ppermute x5, starting transfers between devices, all_sum(): lax.ppermute(value, axis, [(i, i ^ hop) for i in range(devices)])  11 us
    ppermute x4, starting transfers between devices, from_behind(): return lax.ppermute(value, axis, pairs)  10.5 us
    ppermute x4, waiting for transfers between devices, from_behind(): return lax.ppermute(value, axis, pairs)  8.97 us
    ppermute x5, waiting for transfers between devices, all_sum(): lax.ppermute(value, axis, [(i, i ^ hop) for i in range(devices)])  7.44 us
    dot_general x9, matrix products, conv_region(): jnp.einsum('oce,cezyx->ozyx', conv_weight[:, :, offset_z, offset_y, :], w...  6.24 us
    ppermute x2, waiting for transfers between devices, padded_2(): lax.ppermute(head, axis, [((i + 1) % count, i) for i in range(ends)])  6.23 us
    ppermute x2, starting transfers between devices, padded_2(): lax.ppermute(tail, axis, [(i, (i + 1) % count) for i in range(ends)])  5.83 us
    unnamed x17, local copies, waits for them, and re-layouts  4.34 us
  transfers between devices with their start and end apart: 13, of which 11 were waited for; matrix products, arithmetic and copies ran while one was open for 3% of the time, Pallas kernels for 0%

profile of v6, /device:TPU:0, one launch (start us, length us, event | category | flops | bytes accessed | tf_op | source)
XLA Modules:
  0.0 83.7 jit_solution(8790926694261720851)
XLA Ops:
  0.6 0.0 copy-start.4
  0.6 0.0 copy-start.3
  0.6 0.9 %fusion.80 = (bf16[16,1,16,128]{3,2,1,0:T(8,128)(2,1)S(1)}, bf16[16,1,16,128]{3,2,1,0:T(8,128)(2,1)S(1)}) fusion(bf16[16,16,16,128]{3,2,1,0:T(8,128)(2,1)} %param.4), kind=kLoop, calls=%fused_computation.172 | loop fusion | bytes 262144 | tf_op jit(solution)/shard_map/slice | solution.py:17
  1.6 2.4 %collective-permute-start = (bf16[16,1,16,128]{3,0,2,1:T(8,128)(2,1)S(1)}, bf16[16,1,16,128]{3,0,2,1:T(8,128)(2,1)S(1)}, u32[]{:S(2)}, u32[]{:S(2)}) collective-permute-start(bf16[16,1,16,128]{3,0,2,1:T(8,128)(2,1)S(1)} %copy.73), channel_id=1, source_target_pairs={{0,8},{8,16},{16,24},{1,9},{9,17},{17,25},{2,10},{10,18},{18,26},{... | collective-permute-start | bytes 196616 | tf_op jit(solution)/shard_map/ppermute | solution.py:21
  4.0 1.3 %collective-permute-start.1 = (bf16[16,1,16,128]{3,0,2,1:T(8,128)(2,1)S(1)}, bf16[16,1,16,128]{3,0,2,1:T(8,128)(2,1)S(1)}, u32[]{:S(2)}, u32[]{:S(2)}) collective-permute-start(bf16[16,1,16,128]{3,0,2,1:T(8,128)(2,1)S(1)} %copy.74), channel_id=1, source_target_pairs={{8,0},{16,8},{24,16},{9,1},{17,9},{25,17},{10,2},{18,10},{26,18},{... | collective-permute-start | bytes 196616 | tf_op jit(solution)/shard_map/ppermute | solution.py:23
  5.3 0.0 collective-permute-done
  5.4 2.0 %constant_dynamic-update-slice_fusion.1 = bf16[16,18,16,128]{3,0,2,1:T(8,128)(2,1)S(1)} fusion(bf16[16,18,16,128]{3,0,2,1:T(8,128)(2,1)S(1)} %constant_dynamic-update-slice_fusion.2, bf16[16,16,16,128]{3,2,1,0:T(8,128)(2,1)} %param.4), kind=kLoop, calls=%fused_computation.107 | loop fusion | bytes 2097152
  7.3 1.9 %collective-permute-done.1 = bf16[16,1,16,128]{3,0,2,1:T(8,128)(2,1)S(1)} collective-permute-done((bf16[16,1,16,128]{3,0,2,1:T(8,128)(2,1)S(1)}, bf16[16,1,16,128]{3,0,2,1:T(8,128)(2,1)S(1)}, u32[]{:S(2)}, u32[]{:S(2)}) %collective-permute-start.1) | collective-permute-done | bytes 65568 | tf_op jit(solution)/shard_map/ppermute | solution.py:23
  9.3 3.4 %collective-permute-start.2 = (bf16[16,18,1,128]{3,0,2,1:T(8,128)(2,1)S(1)}, bf16[16,18,1,128]{3,0,2,1:T(8,128)(2,1)S(1)}, u32[]{:S(2)}, u32[]{:S(2)}) collective-permute-start(bf16[16,18,1,128]{3,0,2,1:T(8,128)(2,1)S(1)} %get-tuple-element.39), channel_id=1, source_target_pairs={{0,1},{1,2},{2,3},{3,4},{4,5},{5,6},{6,7},{8,9},{9,10},{10,11},{11... | collective-permute-start | bytes 221192 | tf_op jit(solution)/shard_map/ppermute | solution.py:21
  12.7 1.3 %collective-permute-start.3 = (bf16[16,18,1,128]{3,0,2,1:T(8,128)(2,1)S(1)}, bf16[16,18,1,128]{3,0,2,1:T(8,128)(2,1)S(1)}, u32[]{:S(2)}, u32[]{:S(2)}) collective-permute-start(bf16[16,18,1,128]{3,0,2,1:T(8,128)(2,1)S(1)} %get-tuple-element.40), channel_id=1, source_target_pairs={{1,0},{2,1},{3,2},{4,3},{5,4},{6,5},{7,6},{9,8},{10,9},{11,10},{12... | collective-permute-start | bytes 221192 | tf_op jit(solution)/shard_map/ppermute | solution.py:23
  14.0 0.0 copy-done.4
  14.1 0.6 collective-permute-done.2
  14.7 4.3 %collective-permute-done.3 = bf16[16,18,1,128]{3,0,2,1:T(8,128)(2,1)S(1)} collective-permute-done((bf16[16,18,1,128]{3,0,2,1:T(8,128)(2,1)S(1)}, bf16[16,18,1,128]{3,0,2,1:T(8,128)(2,1)S(1)}, u32[]{:S(2)}, u32[]{:S(2)}) %collective-permute-start.3) | collective-permute-done | bytes 73760 | tf_op jit(solution)/shard_map/ppermute | solution.py:23
  19.0 0.2 fusion.69
  19.2 0.8 fusion.19
  20.0 0.6 convolution_bitcast_fusion.7
  20.5 0.6 convolution_bitcast_fusion.6
  21.1 0.6 convolution_bitcast_fusion.5
  21.7 0.6 convolution_bitcast_fusion.4
  22.3 0.6 convolution_bitcast_fusion.3
  22.9 0.6 convolution_bitcast_fusion.2
  23.5 0.6 convolution_bitcast_fusion.1
  24.1 0.6 convolution_bitcast_fusion
  24.7 0.1 copy-done.5
  24.7 1.5 %fusion.34 = f32[3,16,16,128]{3,0,2,1:T(4,128)S(1)} fusion(f32[16,16,128,3]{2,3,1,0:T(4,128)S(1)} %convolution_bitcast_fusion, f32[16,16,128,3]{2,3,1,0:T(4,128)S(1)} %convolution_bitcast_fusion.1, f32[16,16,128,3]{2,3,1,0:T(4,128)S(1)} %convolution_bitcast_fusion.2, f32[16,16,128,3]{2,3,1,0:T(4,128)S(1)} %convolution_bitcast_fusion.3, ...), kind=kOutput, calls=%fused_computation.63 | convolution fusion | flops 22560768 | bytes 7520556 | tf_op jit(solution)/shard_map/oce,cezyx->ozyx/dot_general | solution.py:47
  26.3 0.1 pad_maximum_fusion.8
  26.4 3.4 %collective-permute-start.4 = (f32[4,4,16,128]{3,0,2,1:T(4,128)S(1)}, f32[4,4,16,128]{3,0,2,1:T(4,128)S(1)}, u32[]{:S(2)}, u32[]{:S(2)}) collective-permute-start(f32[4,4,16,128]{3,0,2,1:T(4,128)S(1)} %get-tuple-element.45), channel_id=1, source_target_pairs={{0,8},{8,16},{16,24},{1,9},{9,17},{17,25},{2,10},{10,18},{18,26},{... | collective-permute-start | bytes 393224 | tf_op jit(solution)/shard_map/ppermute | solution.py:33
  29.8 1.3 %collective-permute-start.5 = (f32[4,4,16,128]{3,0,2,1:T(4,128)S(1)}, f32[4,4,16,128]{3,0,2,1:T(4,128)S(1)}, u32[]{:S(2)}, u32[]{:S(2)}) collective-permute-start(f32[4,4,16,128]{3,0,2,1:T(4,128)S(1)} %get-tuple-element.46), channel_id=1, source_target_pairs={{8,0},{16,8},{24,16},{9,1},{17,9},{25,17},{10,2},{18,10},{26,18},{... | collective-permute-start | bytes 393224 | tf_op jit(solution)/shard_map/ppermute | solution.py:33
  31.2 0.0 collective-permute-done.4
  31.2 2.9 %collective-permute-done.5 = f32[4,4,16,128]{3,0,2,1:T(4,128)S(1)} collective-permute-done((f32[4,4,16,128]{3,0,2,1:T(4,128)S(1)}, f32[4,4,16,128]{3,0,2,1:T(4,128)S(1)}, u32[]{:S(2)}, u32[]{:S(2)}) %collective-permute-start.5) | collective-permute-done | bytes 131104 | tf_op jit(solution)/shard_map/ppermute | solution.py:33
  34.1 0.1 pad_maximum_fusion.6
  34.2 4.3 %collective-permute-start.6 = (f32[4,24,4,128]{3,0,2,1:T(4,128)S(1)}, f32[4,24,4,128]{3,0,2,1:T(4,128)S(1)}, u32[]{:S(2)}, u32[]{:S(2)}) collective-permute-start(f32[4,24,4,128]{3,0,2,1:T(4,128)S(1)} %get-tuple-element.43), channel_id=1, source_target_pairs={{0,1},{1,2},{2,3},{3,4},{4,5},{5,6},{6,7},{8,9},{9,10},{10,11},{11... | collective-permute-start | bytes 589832 | tf_op jit(solution)/shard_map/ppermute | solution.py:33
  38.6 1.5 %collective-permute-start.7 = (f32[4,24,4,128]{3,0,2,1:T(4,128)S(1)}, f32[4,24,4,128]{3,0,2,1:T(4,128)S(1)}, u32[]{:S(2)}, u32[]{:S(2)}) collective-permute-start(f32[4,24,4,128]{3,0,2,1:T(4,128)S(1)} %get-tuple-element.44), channel_id=1, source_target_pairs={{1,0},{2,1},{3,2},{4,3},{5,4},{6,5},{7,6},{9,8},{10,9},{11,10},{12... | collective-permute-start | bytes 589832 | tf_op jit(solution)/shard_map/ppermute | solution.py:33
  40.1 1.6 %collective-permute-done.6 = f32[4,24,4,128]{3,0,2,1:T(4,128)S(1)} collective-permute-done((f32[4,24,4,128]{3,0,2,1:T(4,128)S(1)}, f32[4,24,4,128]{3,0,2,1:T(4,128)S(1)}, u32[]{:S(2)}, u32[]{:S(2)}) %collective-permute-start.6) | collective-permute-done | bytes 196640 | tf_op jit(solution)/shard_map/ppermute | solution.py:33
  41.7 4.4 %collective-permute-done.7 = f32[4,24,4,128]{3,0,2,1:T(4,128)S(1)} collective-permute-done((f32[4,24,4,128]{3,0,2,1:T(4,128)S(1)}, f32[4,24,4,128]{3,0,2,1:T(4,128)S(1)}, u32[]{:S(2)}, u32[]{:S(2)}) %collective-permute-start.7) | collective-permute-done | bytes 196640 | tf_op jit(solution)/shard_map/ppermute | solution.py:33
  46.1 0.4 pad_maximum_fusion.2
  46.6 0.9 %fusion.78 = (f32[1,24,24,128]{3,0,2,1:T(1,128)S(1)}, f32[1,24,24,128]{3,0,2,1:T(1,128)S(1)}, f32[1,24,24,128]{3,0,2,1:T(1,128)S(1)}, f32[1,24,24,128]{3,0,2,1:T(1,128)S(1)}) fusion(f32[4,24,24,128]{3,0,2,1:T(4,128)S(1)} %pad_maximum_fusion.2), kind=kLoop, calls=%fused_computation.170 | loop fusion | bytes 2359296 | tf_op jit(solution)/shard_map/slice | solution.py:153
  47.5 0.1 broadcast_multiply_fusion
  47.6 0.2 convert_add_fusion
  47.9 0.2 fusion.48
  48.5 0.2 compare_convert_fusion
  48.7 0.0 copy-start
  48.8 0.8 fusion.74
  49.5 0.6 copy-done
  50.2 2.1 %fusion.4 = f32[8,22,22,128]{3,2,1,0:T(8,128)S(1)} fusion(f32[8,24,24,128]{3,2,1,0:T(8,128)S(1)} %compare_convert_fusion, f32[8,22,22,127]{3,2,1,0:T(8,128)S(1)} %get-tuple-element.24, f32[8,22,22,127]{3,2,1,0:T(8,128)S(1)} %get-tuple-element.23, f32[22,22,128]{2,1,0:T(8,128)S(1)} %get-tuple-element.55, f32[22,22,128]{2,1,0:T(8,128)S(1)} %get-tuple-element.56, ...), kind=kLoop, calls=%fused_computation.9 | loop fusion | flops 6938624 | bytes 17563392 | tf_op jit(solution)/shard_map/sub | solution.py:164
  52.2 0.7 fusion.75
  53.0 1.8 %fusion.10 = f32[8,20,20,128]{3,2,1,0:T(8,128)S(1)} fusion(f32[8,22,22,128]{3,2,1,0:T(8,128)S(1)} %fusion.4, f32[8,20,20,127]{3,2,1,0:T(8,128)S(1)} %get-tuple-element.26, f32[8,20,20,127]{3,2,1,0:T(8,128)S(1)} %get-tuple-element.25, f32[20,20,128]{2,1,0:T(8,128)S(1)} %slice.453, f32[20,20,128]{2,1,0:T(8,128)S(1)} %slice.451, f32[20,20,128]{2,1,0:T(8,128)S(1)} %slice.449, ...), kind=kLoop, calls=%fused_computation.19 | loop fusion | flops 5324800 | bytes 14515200 | tf_op jit(solution)/shard_map/sub | solution.py:105
  54.8 0.6 fusion.76
  55.5 1.4 %fusion.16 = f32[8,18,18,128]{3,2,1,0:T(8,128)S(1)} fusion(f32[8,20,20,128]{3,2,1,0:T(8,128)S(1)} %fusion.10, f32[8,18,18,127]{3,2,1,0:T(8,128)S(1)} %get-tuple-element.28, f32[8,18,18,127]{3,2,1,0:T(8,128)S(1)} %get-tuple-element.27, f32[18,18,128]{2,1,0:T(8,128)S(1)} %slice.468, f32[18,18,128]{2,1,0:T(8,128)S(1)} %slice.466, ...), kind=kLoop, calls=%fused_computation.30 | loop fusion | flops 4313088 | bytes 11757312 | tf_op jit(solution)/shard_map/sub | solution.py:105
  56.9 0.4 fusion.77
  57.3 0.8 copy-done.2
  58.1 2.3 %multiply_reduce_fusion.5 = (f32[8]{0:T(128)S(1)}, f32[8]{0:T(128)S(1)}, f32[8]{0:T(128)S(1)}, f32[8]{0:T(128)S(1)}, f32[8]{0:T(128)S(1)}, /*index=5*/f32[8]{0:T...) fusion(f32[8,22,22,128]{3,2,1,0:T(8,128)S(1)} %fusion.4, f32[8,20,20,128]{3,2,1,0:T(8,128)S(1)} %fusion.10, ...), kind=kLoop, calls=%fused_computation.82 | loop fusion | flops 8126392 | bytes 10338592 | tf_op jit(solution)/shard_map/reduce_sum | solution.py:122
  60.5 2.6 %collective-permute-start.8 = (f32[9,8]{1,0:T(8,128)S(1)}, f32[9,8]{1,0:T(8,128)S(1)}, u32[]{:S(2)}, u32[]{:S(2)}) collective-permute-start(f32[9,8]{1,0:T(8,128)S(1)} %stack.55), channel_id=1, source_target_pairs={{0,8},{8,0},{16,24},{24,16},{1,9},{9,1},{17,25},{25,17},{2,10},{10... | collective-permute-start | bytes 872 | tf_op jit(solution)/shard_map/ppermute | solution.py:116
  63.0 0.8 collective-permute-done.8
  63.9 1.1 %collective-permute-start.9 = (f32[9,8]{1,0:T(8,128)S(1)}, f32[9,8]{1,0:T(8,128)S(1)}, u32[]{:S(2)}, u32[]{:S(2)}) collective-permute-start(f32[9,8]{1,0:T(8,128)S(1)} %add.576), channel_id=1, source_target_pairs={{0,16},{8,24},{16,0},{24,8},{1,17},{9,25},{17,1},{25,9},{2,18},{10... | collective-permute-start | bytes 872 | tf_op jit(solution)/shard_map/ppermute | solution.py:116
  65.0 2.5 %collective-permute-done.9 = f32[9,8]{1,0:T(8,128)S(1)} collective-permute-done((f32[9,8]{1,0:T(8,128)S(1)}, f32[9,8]{1,0:T(8,128)S(1)}, u32[]{:S(2)}, u32[]{:S(2)}) %collective-permute-start.9) | collective-permute-done | bytes 320 | tf_op jit(solution)/shard_map/ppermute | solution.py:116
  67.5 2.2 %collective-permute-start.10 = (f32[9,8]{1,0:T(8,128)S(1)}, f32[9,8]{1,0:T(8,128)S(1)}, u32[]{:S(2)}, u32[]{:S(2)}) collective-permute-start(f32[9,8]{1,0:T(8,128)S(1)} %add.577), channel_id=1, source_target_pairs={{0,1},{1,0},{2,3},{3,2},{4,5},{5,4},{6,7},{7,6},{8,9},{9,8},{10,11... | collective-permute-start | bytes 872 | tf_op jit(solution)/shard_map/ppermute | solution.py:116
  69.7 1.6 %collective-permute-done.10 = f32[9,8]{1,0:T(8,128)S(1)} collective-permute-done((f32[9,8]{1,0:T(8,128)S(1)}, f32[9,8]{1,0:T(8,128)S(1)}, u32[]{:S(2)}, u32[]{:S(2)}) %collective-permute-start.10) | collective-permute-done | bytes 320 | tf_op jit(solution)/shard_map/ppermute | solution.py:116
  71.3 2.1 %collective-permute-start.11 = (f32[9,8]{1,0:T(8,128)S(1)}, f32[9,8]{1,0:T(8,128)S(1)}, u32[]{:S(2)}, u32[]{:S(2)}) collective-permute-start(f32[9,8]{1,0:T(8,128)S(1)} %add.578), channel_id=1, source_target_pairs={{0,2},{1,3},{2,0},{3,1},{4,6},{5,7},{6,4},{7,5},{8,10},{9,11},{10,... | collective-permute-start | bytes 872 | tf_op jit(solution)/shard_map/ppermute | solution.py:116
  73.4 1.6 %collective-permute-done.11 = f32[9,8]{1,0:T(8,128)S(1)} collective-permute-done((f32[9,8]{1,0:T(8,128)S(1)}, f32[9,8]{1,0:T(8,128)S(1)}, u32[]{:S(2)}, u32[]{:S(2)}) %collective-permute-start.11) | collective-permute-done | bytes 320 | tf_op jit(solution)/shard_map/ppermute | solution.py:116
  75.0 3.0 %collective-permute-start.12 = (f32[9,8]{1,0:T(8,128)S(1)}, f32[9,8]{1,0:T(8,128)S(1)}, u32[]{:S(2)}, u32[]{:S(2)}) collective-permute-start(f32[9,8]{1,0:T(8,128)S(1)} %add.579), channel_id=1, source_target_pairs={{0,4},{1,5},{2,6},{3,7},{4,0},{5,1},{6,2},{7,3},{8,12},{9,13},{10,... | collective-permute-start | bytes 872 | tf_op jit(solution)/shard_map/ppermute | solution.py:116
  78.1 0.8 copy.23
  78.9 0.8 %collective-permute-done.12 = f32[9,8]{1,0:T(8,128)S(1)} collective-permute-done((f32[9,8]{1,0:T(8,128)S(1)}, f32[9,8]{1,0:T(8,128)S(1)}, u32[]{:S(2)}, u32[]{:S(2)}) %collective-permute-start.12) | collective-permute-done | bytes 320 | tf_op jit(solution)/shard_map/ppermute | solution.py:116
  79.8 3.9 %fusion.42 = f32[8,16,16,128]{3,2,1,0:T(8,128)} fusion(f32[8,24,24,128]{3,2,1,0:T(8,128)} %copy-done, f32[8,20,20,128]{3,2,1,0:T(8,128)} %copy-done.1, f32[8,22,22,128]{3,2,1,0:T(8,128)S(1)} %fusion.4, f32[8,18,18,128]{3,2,1,0:T(8,128)} %copy-done.2, f32[8]{0:T(128)S(1)} %get-tuple-element.67, f32[8]{0:T(128)S(1)} %get-tuple-element.66, ...), kind=kLoop, calls=%fused_computation.76 | loop fusion | flops 1572864 | bytes 5242976 | tf_op jit(solution)/shard_map/add | solution.py:228
  (47 shorter events, 0.7 us)
Async XLA Ops:
  0.6 13.4 %copy-start.4 = (bf16[3,16,3,3,3]{1,4,3,2,0:T(4,128)(2,1)S(1)}, bf16[3,16,3,3,3]{1,4,3,2,0:T(4,128)(2,1)}, u32[]{:S(2)}) copy-start(bf16[3,16,3,3,3]{1,4,3,2,0:T(4,128)(2,1)} %param.5) | copy-start | bytes 7780
  0.6 13.4 %copy-start.3 = (s32[16,16,128]{2,1,0:T(8,128)S(1)}, s32[16,16,128]{2,1,0:T(8,128)}, u32[]{:S(2)}) copy-start(s32[16,16,128]{2,1,0:T(8,128)} %param.7) | copy-start | bytes 393220
  1.6 3.7 %collective-permute-start = (bf16[16,1,16,128]{3,0,2,1:T(8,128)(2,1)S(1)}, bf16[16,1,16,128]{3,0,2,1:T(8,128)(2,1)S(1)}, u32[]{:S(2)}, u32[]{:S(2)}) collective-permute-start(bf16[16,1,16,128]{3,0,2,1:T(8,128)(2,1)S(1)} %copy.73), channel_id=1, source_target_pairs={{0,8},{8,16},{16,24},{1,9},{9,17},{17,25},{2,10},{10,18},{18,26},{... | collective-permute-start | bytes 196616 | tf_op jit(solution)/shard_map/ppermute | solution.py:21
  4.0 5.2 %collective-permute-start.1 = (bf16[16,1,16,128]{3,0,2,1:T(8,128)(2,1)S(1)}, bf16[16,1,16,128]{3,0,2,1:T(8,128)(2,1)S(1)}, u32[]{:S(2)}, u32[]{:S(2)}) collective-permute-start(bf16[16,1,16,128]{3,0,2,1:T(8,128)(2,1)S(1)} %copy.74), channel_id=1, source_target_pairs={{8,0},{16,8},{24,16},{9,1},{17,9},{25,17},{10,2},{18,10},{26,18},{... | collective-permute-start | bytes 196616 | tf_op jit(solution)/shard_map/ppermute | solution.py:23
  9.3 5.4 %collective-permute-start.2 = (bf16[16,18,1,128]{3,0,2,1:T(8,128)(2,1)S(1)}, bf16[16,18,1,128]{3,0,2,1:T(8,128)(2,1)S(1)}, u32[]{:S(2)}, u32[]{:S(2)}) collective-permute-start(bf16[16,18,1,128]{3,0,2,1:T(8,128)(2,1)S(1)} %get-tuple-element.39), channel_id=1, source_target_pairs={{0,1},{1,2},{2,3},{3,4},{4,5},{5,6},{6,7},{8,9},{9,10},{10,11},{11... | collective-permute-start | bytes 221192 | tf_op jit(solution)/shard_map/ppermute | solution.py:21
  12.7 6.2 %collective-permute-start.3 = (bf16[16,18,1,128]{3,0,2,1:T(8,128)(2,1)S(1)}, bf16[16,18,1,128]{3,0,2,1:T(8,128)(2,1)S(1)}, u32[]{:S(2)}, u32[]{:S(2)}) collective-permute-start(bf16[16,18,1,128]{3,0,2,1:T(8,128)(2,1)S(1)} %get-tuple-element.40), channel_id=1, source_target_pairs={{1,0},{2,1},{3,2},{4,3},{5,4},{6,5},{7,6},{9,8},{10,9},{11,10},{12... | collective-permute-start | bytes 221192 | tf_op jit(solution)/shard_map/ppermute | solution.py:23
  24.1 0.7 copy-start.5
  26.4 4.8 %collective-permute-start.4 = (f32[4,4,16,128]{3,0,2,1:T(4,128)S(1)}, f32[4,4,16,128]{3,0,2,1:T(4,128)S(1)}, u32[]{:S(2)}, u32[]{:S(2)}) collective-permute-start(f32[4,4,16,128]{3,0,2,1:T(4,128)S(1)} %get-tuple-element.45), channel_id=1, source_target_pairs={{0,8},{8,16},{16,24},{1,9},{9,17},{17,25},{2,10},{10,18},{18,26},{... | collective-permute-start | bytes 393224 | tf_op jit(solution)/shard_map/ppermute | solution.py:33
  29.8 4.3 %collective-permute-start.5 = (f32[4,4,16,128]{3,0,2,1:T(4,128)S(1)}, f32[4,4,16,128]{3,0,2,1:T(4,128)S(1)}, u32[]{:S(2)}, u32[]{:S(2)}) collective-permute-start(f32[4,4,16,128]{3,0,2,1:T(4,128)S(1)} %get-tuple-element.46), channel_id=1, source_target_pairs={{8,0},{16,8},{24,16},{9,1},{17,9},{25,17},{10,2},{18,10},{26,18},{... | collective-permute-start | bytes 393224 | tf_op jit(solution)/shard_map/ppermute | solution.py:33
  34.2 7.5 %collective-permute-start.6 = (f32[4,24,4,128]{3,0,2,1:T(4,128)S(1)}, f32[4,24,4,128]{3,0,2,1:T(4,128)S(1)}, u32[]{:S(2)}, u32[]{:S(2)}) collective-permute-start(f32[4,24,4,128]{3,0,2,1:T(4,128)S(1)} %get-tuple-element.43), channel_id=1, source_target_pairs={{0,1},{1,2},{2,3},{3,4},{4,5},{5,6},{6,7},{8,9},{9,10},{10,11},{11... | collective-permute-start | bytes 589832 | tf_op jit(solution)/shard_map/ppermute | solution.py:33
  38.6 7.6 %collective-permute-start.7 = (f32[4,24,4,128]{3,0,2,1:T(4,128)S(1)}, f32[4,24,4,128]{3,0,2,1:T(4,128)S(1)}, u32[]{:S(2)}, u32[]{:S(2)}) collective-permute-start(f32[4,24,4,128]{3,0,2,1:T(4,128)S(1)} %get-tuple-element.44), channel_id=1, source_target_pairs={{1,0},{2,1},{3,2},{4,3},{5,4},{6,5},{7,6},{9,8},{10,9},{11,10},{12... | collective-permute-start | bytes 589832 | tf_op jit(solution)/shard_map/ppermute | solution.py:33
  48.7 1.4 %copy-start = (f32[8,24,24,128]{3,2,1,0:T(8,128)}, f32[8,24,24,128]{3,2,1,0:T(8,128)S(1)}, u32[]{:S(2)}) copy-start(f32[8,24,24,128]{3,2,1,0:T(8,128)S(1)} %compare_convert_fusion) | copy-start | bytes 7077892
  54.8 2.5 %copy-start.1 = (f32[8,20,20,128]{3,2,1,0:T(8,128)}, f32[8,20,20,128]{3,2,1,0:T(8,128)S(1)}, u32[]{:S(2)}) copy-start(f32[8,20,20,128]{3,2,1,0:T(8,128)S(1)} %fusion.10) | copy-start | bytes 4915204
  56.9 1.2 %copy-start.2 = (f32[8,18,18,128]{3,2,1,0:T(8,128)}, f32[8,18,18,128]{3,2,1,0:T(8,128)S(1)}, u32[]{:S(2)}) copy-start(f32[8,18,18,128]{3,2,1,0:T(8,128)S(1)} %fusion.16) | copy-start | bytes 3981316
  60.5 3.4 %collective-permute-start.8 = (f32[9,8]{1,0:T(8,128)S(1)}, f32[9,8]{1,0:T(8,128)S(1)}, u32[]{:S(2)}, u32[]{:S(2)}) collective-permute-start(f32[9,8]{1,0:T(8,128)S(1)} %stack.55), channel_id=1, source_target_pairs={{0,8},{8,0},{16,24},{24,16},{1,9},{9,1},{17,25},{25,17},{2,10},{10... | collective-permute-start | bytes 872 | tf_op jit(solution)/shard_map/ppermute | solution.py:116
  63.9 3.7 %collective-permute-start.9 = (f32[9,8]{1,0:T(8,128)S(1)}, f32[9,8]{1,0:T(8,128)S(1)}, u32[]{:S(2)}, u32[]{:S(2)}) collective-permute-start(f32[9,8]{1,0:T(8,128)S(1)} %add.576), channel_id=1, source_target_pairs={{0,16},{8,24},{16,0},{24,8},{1,17},{9,25},{17,1},{25,9},{2,18},{10... | collective-permute-start | bytes 872 | tf_op jit(solution)/shard_map/ppermute | solution.py:116
  67.5 3.8 %collective-permute-start.10 = (f32[9,8]{1,0:T(8,128)S(1)}, f32[9,8]{1,0:T(8,128)S(1)}, u32[]{:S(2)}, u32[]{:S(2)}) collective-permute-start(f32[9,8]{1,0:T(8,128)S(1)} %add.577), channel_id=1, source_target_pairs={{0,1},{1,0},{2,3},{3,2},{4,5},{5,4},{6,7},{7,6},{8,9},{9,8},{10,11... | collective-permute-start | bytes 872 | tf_op jit(solution)/shard_map/ppermute | solution.py:116
  71.3 3.7 %collective-permute-start.11 = (f32[9,8]{1,0:T(8,128)S(1)}, f32[9,8]{1,0:T(8,128)S(1)}, u32[]{:S(2)}, u32[]{:S(2)}) collective-permute-start(f32[9,8]{1,0:T(8,128)S(1)} %add.578), channel_id=1, source_target_pairs={{0,2},{1,3},{2,0},{3,1},{4,6},{5,7},{6,4},{7,5},{8,10},{9,11},{10,... | collective-permute-start | bytes 872 | tf_op jit(solution)/shard_map/ppermute | solution.py:116
  75.0 4.7 %collective-permute-start.12 = (f32[9,8]{1,0:T(8,128)S(1)}, f32[9,8]{1,0:T(8,128)S(1)}, u32[]{:S(2)}, u32[]{:S(2)}) collective-permute-start(f32[9,8]{1,0:T(8,128)S(1)} %add.579), channel_id=1, source_target_pairs={{0,4},{1,5},{2,6},{3,7},{4,0},{5,1},{6,2},{7,3},{8,12},{9,13},{10,... | collective-permute-start | bytes 872 | tf_op jit(solution)/shard_map/ppermute | solution.py:116

commit v7 on v6

--- a/solution.py
+++ b/solution.py
@@ -133,26 +133,26 @@
     keep_x = (jnp.arange(col_cells, dtype=jnp.int32) < col_cells - 1).astype(jnp.float32)[
         None, None, :
     ]
-    bias_column = conv_bias[:, None, None, None]
-    padded = padded_2(features, (("gz", 1), ("yx", 2)), 1)
-    padded = jnp.pad(padded, ((0, 0), (0, 0), (0, 0), (1, 1)))
-    affinities = jax.nn.sigmoid(
-        conv_region(padded, conv_weight, depth_cells, row_cells) + bias_column
-    )
     halo = ITERS + 1
-    stacked = jnp.concatenate([affinities, labels[None].astype(jnp.float32)], axis=0)
-    grid_cells = extend(stacked, halo)
+    channels = features.shape[0]
+    stacked = jnp.concatenate([features, labels[None].astype(features.dtype)], axis=0)
+    grid_cells = extend(stacked, halo + 1)
+    padded = jnp.pad(grid_cells[:channels], ((0, 0), (0, 0), (0, 0), (1, 1)))
     cells_z = depth_cells + 2 * halo
     cells_y = row_cells + 2 * halo
+    grid_aff = jax.nn.sigmoid(
+        conv_region(padded, conv_weight, cells_z, cells_y) + conv_bias[:, None, None, None]
+    )
+    affinities = grid_aff[:, halo:-halo, halo:-halo]
+    grid_labels = grid_cells[channels, 1:-1, 1:-1].astype(jnp.float32)
     grid_z = lax.axis_index("gz") * depth_cells - halo + jnp.arange(cells_z, dtype=jnp.int32)
     grid_y = lax.axis_index("yx") * row_cells - halo + jnp.arange(cells_y, dtype=jnp.int32)
     edge_z = ((grid_z >= 0) & (grid_z < depth_cells * lax.axis_size("gz") - 1)).astype(jnp.float32)
     edge_y = ((grid_y >= 0) & (grid_y < row_cells * lax.axis_size("yx") - 1)).astype(jnp.float32)
-    grid_labels = grid_cells[3]
     grid = (
-        grid_cells[0] * edge_z[:, None, None],
-        grid_cells[1] * edge_y[None, :, None],
-        grid_cells[2] * keep_x,
+        grid_aff[0] * edge_z[:, None, None],
+        grid_aff[1] * edge_y[None, :, None],
+        grid_aff[2] * keep_x,
         (grid_labels > 0.5).astype(jnp.float32),
     )
     colours = jnp.arange(1, FIELDS + 1, dtype=jnp.float32)[:, None, None, None]

time: 84 us -> 106 us (1.26)
  matrix products: 6.24 us -> 19.5 us
  waiting for transfers between devices: 23.2 us -> 34.3 us
  starting transfers between devices: 29.9 us -> 22.5 us
  local copies, waits for them, and re-layouts: 9.83 us -> 13.8 us
  other arithmetic: 13.3 us -> 14.5 us
    ppermute x4, waiting for transfers between devices: 8.97 us -> 26.6 us  [from_behind(): return lax.ppermute(value, axis, pairs)]
    dot_general x9, matrix products: 6.24 us -> 19.5 us  [conv_region(): jnp.einsum('oce,cezyx->ozyx', conv_weight[:, :, offset_z, offset_y, :], w...]
    ppermute x4 -> x0, starting transfers between devices: 8.41 us -> none  [the longest x2 5.83 us: padded_2(): lax.ppermute(tail, axis, [(i, (i + 1) % count) for i in range(ends)])]
    ppermute x4 -> x0, waiting for transfers between devices: 6.83 us -> none  [the longest x2 6.23 us: padded_2(): lax.ppermute(head, axis, [((i + 1) % count, i) for i in range(ends)])]
    ppermute x0 -> x2, local copies, waits for them, and re-layouts: none -> 2.72 us  [from_behind(): return lax.ppermute(value, axis, pairs)]
    ppermute x5, starting transfers between devices: 11 us -> 13.1 us  [all_sum(): lax.ppermute(value, axis, [(i, i ^ hop) for i in range(devices)])]
    slice x3 -> x5, local copies, waits for them, and re-layouts: 1.8 us -> 3.01 us  [the longest x1 1.14 us: body(): affinities = grid_aff[:, halo:-halo, halo:-halo]]
    ppermute x4, starting transfers between devices: 10.5 us -> 9.31 us  [from_behind(): return lax.ppermute(value, axis, pairs)]
  transfers between devices with their start and end apart: 13 -> 9, of which waited for: 11 -> 7; matrix products, arithmetic and copies ran while one was open for 3% -> 4% of each run, Pallas kernels for 0% -> 0%
where the time goes in v7:
time: 106 us
  waiting for transfers between devices  34.3 us (32%)
  starting transfers between devices  22.5 us (21%)
  matrix products  19.5 us (18%)
  other arithmetic  14.5 us (14%)
  local copies, waits for them, and re-layouts  13.8 us (13%)
  between operations  1.16 us (1%)
    ppermute x4, waiting for transfers between devices, from_behind(): return lax.ppermute(value, axis, pairs)  26.6 us
    dot_general x9, matrix products, conv_region(): jnp.einsum('oce,cezyx->ozyx', conv_weight[:, :, offset_z, offset_y, :], w...  19.5 us
    ppermute x5, starting transfers between devices, all_sum(): lax.ppermute(value, axis, [(i, i ^ hop) for i in range(devices)])  13.1 us
    ppermute x4, starting transfers between devices, from_behind(): return lax.ppermute(value, axis, pairs)  9.31 us
    ppermute x5, waiting for transfers between devices, all_sum(): lax.ppermute(value, axis, [(i, i ^ hop) for i in range(devices)])  7.73 us
    sub x2, other arithmetic, operate_inside(): return diagonal[part, part] * centre - coupled  3.5 us
    add x1, other arithmetic, body(): probabilities = probabilities + coeff[:, None, None, None] * vector  3.5 us
    unnamed x17, local copies, waits for them, and re-layouts  3.38 us
  transfers between devices with their start and end apart: 9, of which 7 were waited for; matrix products, arithmetic and copies ran while one was open for 4% of the time, Pallas kernels for 0%

profile of v7, /device:TPU:0, one launch (start us, length us, event | category | flops | bytes accessed | tf_op | source)
XLA Modules:
  0.0 105.8 jit_solution(12872508214579188766)
XLA Ops:
  0.6 1.9 %copy_dynamic-update-slice_fusion = bf16[17,16,16,128]{3,0,2,1:T(8,128)(2,1)S(1)} fusion(bf16[16,16,16,128]{3,2,1,0:T(8,128)(2,1)} %param.4), kind=kLoop, calls=%fused_computation.79 | loop fusion | bytes 2097152
  2.5 0.9 convert_bitcast_fusion
  3.5 0.2 copy_dynamic-update-slice_fusion.1
  3.6 0.2 fusion.77
  3.8 2.4 %collective-permute-start = (bf16[17,5,16,128]{3,0,2,1:T(8,128)(2,1)S(1)}, bf16[17,5,16,128]{3,0,2,1:T(8,128)(2,1)S(1)}, u32[]{:S(2)}, u32[]{:S(2)}) collective-permute-start(bf16[17,5,16,128]{3,0,2,1:T(8,128)(2,1)S(1)} %get-tuple-element.39), channel_id=1, source_target_pairs={{0,8},{8,16},{16,24},{1,9},{9,17},{17,25},{2,10},{10,18},{18,26},{... | collective-permute-start | bytes 1044488 | tf_op jit(solution)/shard_map/ppermute | solution.py:33
  6.3 1.3 %collective-permute-start.1 = (bf16[17,5,16,128]{3,0,2,1:T(8,128)(2,1)S(1)}, bf16[17,5,16,128]{3,0,2,1:T(8,128)(2,1)S(1)}, u32[]{:S(2)}, u32[]{:S(2)}) collective-permute-start(bf16[17,5,16,128]{3,0,2,1:T(8,128)(2,1)S(1)} %get-tuple-element.40), channel_id=1, source_target_pairs={{8,0},{16,8},{24,16},{9,1},{17,9},{25,17},{10,2},{18,10},{26,18},{... | collective-permute-start | bytes 1044488 | tf_op jit(solution)/shard_map/ppermute | solution.py:33
  7.6 0.1 collective-permute-done
  7.7 4.4 %collective-permute-done.1 = bf16[17,5,16,128]{3,0,2,1:T(8,128)(2,1)S(1)} collective-permute-done((bf16[17,5,16,128]{3,0,2,1:T(8,128)(2,1)S(1)}, bf16[17,5,16,128]{3,0,2,1:T(8,128)(2,1)S(1)}, u32[]{:S(2)}, u32[]{:S(2)}) %collective-permute-start.1) | collective-permute-done | bytes 348192 | tf_op jit(solution)/shard_map/ppermute | solution.py:33
  12.1 0.2 pad_maximum_fusion.7
  12.3 0.0 copy-start.5
  12.3 0.1 copy.45
  12.5 4.3 %collective-permute-start.2 = (bf16[17,26,5,128]{3,1,2,0:T(8,128)(2,1)S(1)}, bf16[17,26,5,128]{3,1,2,0:T(8,128)(2,1)}, u32[]{:S(2)}, u32[]{:S(2)}) collective-permute-start(bf16[17,26,5,128]{3,1,2,0:T(8,128)(2,1)S(1)} %copy.45), channel_id=1, source_target_pairs={{0,1},{1,2},{2,3},{3,4},{4,5},{5,6},{6,7},{8,9},{9,10},{10,11},{11... | collective-permute-start | bytes 1697288 | tf_op jit(solution)/shard_map/ppermute | solution.py:33
  16.8 1.0 copy.46
  17.8 1.3 %collective-permute-start.3 = (bf16[17,26,5,128]{3,1,2,0:T(8,128)(2,1)}, bf16[17,26,5,128]{3,1,2,0:T(8,128)(2,1)}, u32[]{:S(2)}, u32[]{:S(2)}) collective-permute-start(bf16[17,26,5,128]{3,1,2,0:T(8,128)(2,1)} %copy.46), channel_id=1, source_target_pairs={{1,0},{2,1},{3,2},{4,3},{5,4},{6,5},{7,6},{9,8},{10,9},{11,10},{12... | collective-permute-start | bytes 1697288 | tf_op jit(solution)/shard_map/ppermute | solution.py:33
  19.1 0.0 copy-done.5
  19.1 22.1 %collective-permute-done.2 = bf16[17,26,5,128]{3,1,2,0:T(8,128)(2,1)} collective-permute-done((bf16[17,26,5,128]{3,1,2,0:T(8,128)(2,1)S(1)}, bf16[17,26,5,128]{3,1,2,0:T(8,128)(2,1)}, u32[]{:S(2)}, u32[]{:S(2)}) %collective-permute-start.2) | collective-permute-done | bytes 565792 | tf_op jit(solution)/shard_map/ppermute | solution.py:33
  41.2 1.4 %copy.47 = bf16[17,26,5,128]{3,0,2,1:T(8,128)(2,1)S(1)} copy(bf16[17,26,5,128]{3,1,2,0:T(8,128)(2,1)} %collective-permute-done.2) | data formatting | bytes 1131520 | tf_op jit(solution)/shard_map/ppermute | solution.py:33
  42.6 0.0 collective-permute-done.3
  42.6 1.4 %copy.48 = bf16[17,26,5,128]{3,0,2,1:T(8,128)(2,1)S(1)} copy(bf16[17,26,5,128]{3,1,2,0:T(8,128)(2,1)} %collective-permute-done.3) | data formatting | bytes 1131520 | tf_op jit(solution)/shard_map/ppermute | solution.py:33
  43.9 0.8 pad_maximum_fusion.1
  44.7 1.6 %fusion = (bf16[16,1,26,26,128]{4,0,1,3,2:T(8,128)(2,1)S(1)}, bf16[16,1,26,26,128]{4,0,1,3,2:T(8,128)(2,1)S(1)}) fusion(bf16[16,26,26,128]{3,0,2,1:T(8,128)(2,1)S(1)} %pad_maximum_fusion.1), kind=kLoop, calls=%fused_computation.3 | loop fusion | bytes 8306688 | tf_op jit(solution)/shard_map/stack | solution.py:38
  46.3 2.7 %convolution_bitcast_fusion.7 = f32[24,24,128,3]{2,3,1,0:T(4,128)S(1)} fusion(bf16[3,16,1,1,3]{1,4,3,2,0:T(4,128)(2,1)S(1)} %get-tuple-element.57, bf16[16,1,26,26,128]{4,0,1,3,2:T(8,128)(2,1)S(1)} %get-tuple-element.28, bf16[16,1,26,26,128]{4,0,1,3,2:T(8,128)(2,1)S(1)} %bitcast.249, bf16[16,1,26,26,128]{4,0,1,3,2:T(8,128)(2,1)S(1)} %get-tuple-element.27), kind=kOutput, calls=%fused_computation.50 | convolution fusion | flops 46153728 | bytes 9191712 | tf_op jit(solution)/shard_map/oce,cezyx->ozyx/dot_general | solution.py:47
  49.1 1.9 %convolution_bitcast_fusion.6 = f32[24,24,128,3]{2,3,1,0:T(4,128)S(1)} fusion(bf16[3,16,1,1,3]{1,4,3,2,0:T(4,128)(2,1)S(1)} %get-tuple-element.56, bf16[16,1,26,26,128]{4,0,1,3,2:T(8,128)(2,1)S(1)} %get-tuple-element.28, bf16[16,1,26,26,128]{4,0,1,3,2:T(8,128)(2,1)S(1)} %bitcast.250, bf16[16,1,26,26,128]{4,0,1,3,2:T(8,128)(2,1)S(1)} %get-tuple-element.27), kind=kOutput, calls=%fused_computation.49 | convolution fusion | flops 46153728 | bytes 9191712 | tf_op jit(solution)/shard_map/oce,cezyx->ozyx/dot_general | solution.py:47
  51.0 2.6 %convolution_bitcast_fusion.5 = f32[24,24,128,3]{2,3,1,0:T(4,128)S(1)} fusion(bf16[3,16,1,1,3]{1,4,3,2,0:T(4,128)(2,1)S(1)} %get-tuple-element.55, bf16[16,1,26,26,128]{4,0,1,3,2:T(8,128)(2,1)S(1)} %get-tuple-element.28, bf16[16,1,26,26,128]{4,0,1,3,2:T(8,128)(2,1)S(1)} %bitcast.251, bf16[16,1,26,26,128]{4,0,1,3,2:T(8,128)(2,1)S(1)} %get-tuple-element.27), kind=kOutput, calls=%fused_computation.48 | convolution fusion | flops 46153728 | bytes 9191712 | tf_op jit(solution)/shard_map/oce,cezyx->ozyx/dot_general | solution.py:47
  53.6 2.7 %convolution_bitcast_fusion.4 = f32[24,24,128,3]{2,3,1,0:T(4,128)S(1)} fusion(bf16[3,16,1,1,3]{1,4,3,2,0:T(4,128)(2,1)S(1)} %get-tuple-element.54, bf16[16,1,26,26,128]{4,0,1,3,2:T(8,128)(2,1)S(1)} %get-tuple-element.28, bf16[16,1,26,26,128]{4,0,1,3,2:T(8,128)(2,1)S(1)} %bitcast.252, bf16[16,1,26,26,128]{4,0,1,3,2:T(8,128)(2,1)S(1)} %get-tuple-element.27), kind=kOutput, calls=%fused_computation.47 | convolution fusion | flops 46153728 | bytes 9191712 | tf_op jit(solution)/shard_map/oce,cezyx->ozyx/dot_general | solution.py:47
  56.3 1.9 %convolution_bitcast_fusion.3 = f32[24,24,128,3]{2,3,1,0:T(4,128)S(1)} fusion(bf16[3,16,1,1,3]{1,4,3,2,0:T(4,128)(2,1)S(1)} %get-tuple-element.53, bf16[16,1,26,26,128]{4,0,1,3,2:T(8,128)(2,1)S(1)} %get-tuple-element.28, bf16[16,1,26,26,128]{4,0,1,3,2:T(8,128)(2,1)S(1)} %bitcast.253, bf16[16,1,26,26,128]{4,0,1,3,2:T(8,128)(2,1)S(1)} %get-tuple-element.27), kind=kOutput, calls=%fused_computation.46 | convolution fusion | flops 46153728 | bytes 9191712 | tf_op jit(solution)/shard_map/oce,cezyx->ozyx/dot_general | solution.py:47
  58.2 1.5 %convolution_bitcast_fusion.2 = f32[24,24,128,3]{2,3,1,0:T(4,128)S(1)} fusion(bf16[3,16,1,1,3]{1,4,3,2,0:T(4,128)(2,1)S(1)} %get-tuple-element.52, bf16[16,1,26,26,128]{4,0,1,3,2:T(8,128)(2,1)S(1)} %get-tuple-element.28, bf16[16,1,26,26,128]{4,0,1,3,2:T(8,128)(2,1)S(1)} %bitcast.254, bf16[16,1,26,26,128]{4,0,1,3,2:T(8,128)(2,1)S(1)} %get-tuple-element.27), kind=kOutput, calls=%fused_computation.45 | convolution fusion | flops 46153728 | bytes 9191712 | tf_op jit(solution)/shard_map/oce,cezyx->ozyx/dot_general | solution.py:47
  59.6 1.5 %convolution_bitcast_fusion.1 = f32[24,24,128,3]{2,3,1,0:T(4,128)S(1)} fusion(bf16[3,16,1,1,3]{1,4,3,2,0:T(4,128)(2,1)S(1)} %get-tuple-element.51, bf16[16,1,26,26,128]{4,0,1,3,2:T(8,128)(2,1)S(1)} %get-tuple-element.28, bf16[16,1,26,26,128]{4,0,1,3,2:T(8,128)(2,1)S(1)} %bitcast.255, bf16[16,1,26,26,128]{4,0,1,3,2:T(8,128)(2,1)S(1)} %get-tuple-element.27), kind=kOutput, calls=%fused_computation.44 | convolution fusion | flops 46153728 | bytes 9191712 | tf_op jit(solution)/shard_map/oce,cezyx->ozyx/dot_general | solution.py:47
  61.1 0.0 copy-start.6
  61.1 1.5 %convolution_bitcast_fusion = f32[24,24,128,3]{2,3,1,0:T(4,128)S(1)} fusion(bf16[3,16,1,1,3]{1,4,3,2,0:T(4,128)(2,1)S(1)} %get-tuple-element.58, bf16[16,1,26,26,128]{4,0,1,3,2:T(8,128)(2,1)S(1)} %get-tuple-element.28, bf16[16,1,26,26,128]{4,0,1,3,2:T(8,128)(2,1)S(1)} %bitcast.256, bf16[16,1,26,26,128]{4,0,1,3,2:T(8,128)(2,1)S(1)} %get-tuple-element.27), kind=kOutput, calls=%fused_computation.43 | convolution fusion | flops 46153728 | bytes 9191712 | tf_op jit(solution)/shard_map/oce,cezyx->ozyx/dot_general | solution.py:47
  62.6 0.0 copy-done.6
  62.6 3.3 %fusion.34 = f32[3,24,24,128]{3,0,2,1:T(4,128)S(1)} fusion(f32[24,24,128,3]{2,3,1,0:T(4,128)S(1)} %convolution_bitcast_fusion, f32[24,24,128,3]{2,3,1,0:T(4,128)S(1)} %convolution_bitcast_fusion.1, f32[24,24,128,3]{2,3,1,0:T(4,128)S(1)} %convolution_bitcast_fusion.2, f32[24,24,128,3]{2,3,1,0:T(4,128)S(1)} %convolution_bitcast_fusion.3, ...), kind=kOutput, calls=%fused_computation.65 | convolution fusion | flops 48807936 | bytes 16269612 | tf_op jit(solution)/shard_map/oce,cezyx->ozyx/dot_general | solution.py:47
  65.9 0.0 copy-start.4
  65.9 0.6 fusion.78
  66.5 0.5 broadcast_compare_fusion
  67.0 0.0 copy-done.4
  67.0 0.1 fusion.44
  67.1 0.1 broadcast_multiply_fusion
  67.2 0.2 convert_add_fusion
  68.0 0.2 compare_convert_fusion
  68.3 0.0 copy-start
  68.3 0.8 fusion.73
  69.0 0.6 copy-done
  69.7 2.0 %fusion.6 = f32[8,22,22,128]{3,2,1,0:T(8,128)S(1)} fusion(f32[8,24,24,128]{3,2,1,0:T(8,128)S(1)} %compare_convert_fusion, f32[8,22,22,127]{3,2,1,0:T(8,128)S(1)} %get-tuple-element.32, f32[8,22,22,127]{3,2,1,0:T(8,128)S(1)} %get-tuple-element.31, f32[22,22,128]{2,1,0:T(8,128)S(1)} %get-tuple-element.49, f32[22,22,128]{2,1,0:T(8,128)S(1)} %get-tuple-element.23, ...), kind=kLoop, calls=%fused_computation.15 | loop fusion | flops 6938624 | bytes 17563392 | tf_op jit(solution)/shard_map/sub | solution.py:164
  71.7 0.7 fusion.74
  72.4 2.1 %fusion.12 = f32[8,20,20,128]{3,2,1,0:T(8,128)S(1)} fusion(f32[8,22,22,128]{3,2,1,0:T(8,128)S(1)} %fusion.6, f32[8,20,20,127]{3,2,1,0:T(8,128)S(1)} %get-tuple-element.34, f32[8,20,20,127]{3,2,1,0:T(8,128)S(1)} %get-tuple-element.33, f32[20,20,128]{2,1,0:T(8,128)S(1)} %slice.442, f32[20,20,128]{2,1,0:T(8,128)S(1)} %slice.440, f32[20,20,128]{2,1,0:T(8,128)S(1)} %slice.438, ...), kind=kLoop, calls=%fused_computation.25 | loop fusion | flops 5324800 | bytes 14515200 | tf_op jit(solution)/shard_map/sub | solution.py:105
  74.5 0.6 fusion.75
  75.2 1.4 %fusion.18 = f32[8,18,18,128]{3,2,1,0:T(8,128)S(1)} fusion(f32[8,20,20,128]{3,2,1,0:T(8,128)S(1)} %fusion.12, f32[8,18,18,127]{3,2,1,0:T(8,128)S(1)} %get-tuple-element.36, f32[8,18,18,127]{3,2,1,0:T(8,128)S(1)} %get-tuple-element.35, f32[18,18,128]{2,1,0:T(8,128)S(1)} %slice.457, f32[18,18,128]{2,1,0:T(8,128)S(1)} %slice.455, ...), kind=kLoop, calls=%fused_computation.36 | loop fusion | flops 4313088 | bytes 11757312 | tf_op jit(solution)/shard_map/sub | solution.py:105
  76.6 0.4 fusion.76
  77.0 0.0 copy-done.1
  77.0 2.3 %multiply_reduce_fusion.5 = (f32[8]{0:T(128)S(1)}, f32[8]{0:T(128)S(1)}, f32[8]{0:T(128)S(1)}, f32[8]{0:T(128)S(1)}, f32[8]{0:T(128)S(1)}, /*index=5*/f32[8]{0:T...) fusion(f32[8,22,22,128]{3,2,1,0:T(8,128)S(1)} %fusion.6, f32[8,20,20,128]{3,2,1,0:T(8,128)S(1)} %fusion.12, ...), kind=kLoop, calls=%fused_computation.85 | loop fusion | flops 8126392 | bytes 10338592 | tf_op jit(solution)/shard_map/reduce_sum | solution.py:122
  79.4 5.8 %collective-permute-start.4 = (f32[9,8]{1,0:T(8,128)S(1)}, f32[9,8]{1,0:T(8,128)S(1)}, u32[]{:S(2)}, u32[]{:S(2)}) collective-permute-start(f32[9,8]{1,0:T(8,128)S(1)} %stack.55), channel_id=1, source_target_pairs={{0,8},{8,0},{16,24},{24,16},{1,9},{9,1},{17,25},{25,17},{2,10},{10... | collective-permute-start | bytes 872 | tf_op jit(solution)/shard_map/ppermute | solution.py:116
  85.2 0.8 collective-permute-done.4
  86.0 0.0 collective-permute-start.5
  86.0 3.6 %collective-permute-done.5 = f32[9,8]{1,0:T(8,128)S(1)} collective-permute-done((f32[9,8]{1,0:T(8,128)S(1)}, f32[9,8]{1,0:T(8,128)S(1)}, u32[]{:S(2)}, u32[]{:S(2)}) %collective-permute-start.5) | collective-permute-done | bytes 320 | tf_op jit(solution)/shard_map/ppermute | solution.py:116
  89.7 2.3 %collective-permute-start.6 = (f32[9,8]{1,0:T(8,128)S(1)}, f32[9,8]{1,0:T(8,128)S(1)}, u32[]{:S(2)}, u32[]{:S(2)}) collective-permute-start(f32[9,8]{1,0:T(8,128)S(1)} %add.577), channel_id=1, source_target_pairs={{0,1},{1,0},{2,3},{3,2},{4,5},{5,4},{6,7},{7,6},{8,9},{9,8},{10,11... | collective-permute-start | bytes 872 | tf_op jit(solution)/shard_map/ppermute | solution.py:116
  91.9 1.6 %collective-permute-done.6 = f32[9,8]{1,0:T(8,128)S(1)} collective-permute-done((f32[9,8]{1,0:T(8,128)S(1)}, f32[9,8]{1,0:T(8,128)S(1)}, u32[]{:S(2)}, u32[]{:S(2)}) %collective-permute-start.6) | collective-permute-done | bytes 320 | tf_op jit(solution)/shard_map/ppermute | solution.py:116
  93.6 2.0 %collective-permute-start.7 = (f32[9,8]{1,0:T(8,128)S(1)}, f32[9,8]{1,0:T(8,128)S(1)}, u32[]{:S(2)}, u32[]{:S(2)}) collective-permute-start(f32[9,8]{1,0:T(8,128)S(1)} %add.578), channel_id=1, source_target_pairs={{0,2},{1,3},{2,0},{3,1},{4,6},{5,7},{6,4},{7,5},{8,10},{9,11},{10,... | collective-permute-start | bytes 872 | tf_op jit(solution)/shard_map/ppermute | solution.py:116
  95.6 1.6 %collective-permute-done.7 = f32[9,8]{1,0:T(8,128)S(1)} collective-permute-done((f32[9,8]{1,0:T(8,128)S(1)}, f32[9,8]{1,0:T(8,128)S(1)}, u32[]{:S(2)}, u32[]{:S(2)}) %collective-permute-start.7) | collective-permute-done | bytes 320 | tf_op jit(solution)/shard_map/ppermute | solution.py:116
  97.2 3.0 %collective-permute-start.8 = (f32[9,8]{1,0:T(8,128)S(1)}, f32[9,8]{1,0:T(8,128)S(1)}, u32[]{:S(2)}, u32[]{:S(2)}) collective-permute-start(f32[9,8]{1,0:T(8,128)S(1)} %add.579), channel_id=1, source_target_pairs={{0,4},{1,5},{2,6},{3,7},{4,0},{5,1},{6,2},{7,3},{8,12},{9,13},{10,... | collective-permute-start | bytes 872 | tf_op jit(solution)/shard_map/ppermute | solution.py:116
  100.3 1.1 %slice.482 = f32[3,16,16,128]{3,0,2,1:T(4,128)S(1)} slice(f32[3,24,24,128]{3,0,2,1:T(4,128)} %copy-done.4), slice={[0:3], [4:20], [4:20], [0:128]} | slice | bytes 786432 | tf_op jit(solution)/shard_map/slice | solution.py:146
  101.4 0.8 copy.62
  102.2 0.0 collective-permute-done.8
  102.3 3.5 %fusion.42 = f32[8,16,16,128]{3,2,1,0:T(8,128)} fusion(f32[8,24,24,128]{3,2,1,0:T(8,128)} %copy-done, f32[8,20,20,128]{3,2,1,0:T(8,128)S(1)} %copy-done.2, f32[8,22,22,128]{3,2,1,0:T(8,128)S(1)} %fusion.6, f32[8,18,18,128]{3,2,1,0:T(8,128)} %copy-done.3, f32[8]{0:T(128)S(1)} %get-tuple-element.60, f32[8]{0:T(128)S(1)} %get-tuple-element.59, ...), kind=kLoop, calls=%fused_computation.78 | loop fusion | flops 1572864 | bytes 5242976 | tf_op jit(solution)/shard_map/add | solution.py:228
  (41 shorter events, 0.6 us)
Async XLA Ops:
  3.8 3.9 %collective-permute-start = (bf16[17,5,16,128]{3,0,2,1:T(8,128)(2,1)S(1)}, bf16[17,5,16,128]{3,0,2,1:T(8,128)(2,1)S(1)}, u32[]{:S(2)}, u32[]{:S(2)}) collective-permute-start(bf16[17,5,16,128]{3,0,2,1:T(8,128)(2,1)S(1)} %get-tuple-element.39), channel_id=1, source_target_pairs={{0,8},{8,16},{16,24},{1,9},{9,17},{17,25},{2,10},{10,18},{18,26},{... | collective-permute-start | bytes 1044488 | tf_op jit(solution)/shard_map/ppermute | solution.py:33
  6.3 5.8 %collective-permute-start.1 = (bf16[17,5,16,128]{3,0,2,1:T(8,128)(2,1)S(1)}, bf16[17,5,16,128]{3,0,2,1:T(8,128)(2,1)S(1)}, u32[]{:S(2)}, u32[]{:S(2)}) collective-permute-start(bf16[17,5,16,128]{3,0,2,1:T(8,128)(2,1)S(1)} %get-tuple-element.40), channel_id=1, source_target_pairs={{8,0},{16,8},{24,16},{9,1},{17,9},{25,17},{10,2},{18,10},{26,18},{... | collective-permute-start | bytes 1044488 | tf_op jit(solution)/shard_map/ppermute | solution.py:33
  12.3 6.8 %copy-start.5 = (bf16[3,16,3,3,3]{1,4,3,2,0:T(4,128)(2,1)S(1)}, bf16[3,16,3,3,3]{1,4,3,2,0:T(4,128)(2,1)}, u32[]{:S(2)}) copy-start(bf16[3,16,3,3,3]{1,4,3,2,0:T(4,128)(2,1)} %param.5) | copy-start | bytes 7780
  12.5 28.7 %collective-permute-start.2 = (bf16[17,26,5,128]{3,1,2,0:T(8,128)(2,1)S(1)}, bf16[17,26,5,128]{3,1,2,0:T(8,128)(2,1)}, u32[]{:S(2)}, u32[]{:S(2)}) collective-permute-start(bf16[17,26,5,128]{3,1,2,0:T(8,128)(2,1)S(1)} %copy.45), channel_id=1, source_target_pairs={{0,1},{1,2},{2,3},{3,4},{4,5},{5,6},{6,7},{8,9},{9,10},{10,11},{11... | collective-permute-start | bytes 1697288 | tf_op jit(solution)/shard_map/ppermute | solution.py:33
  17.8 24.8 %collective-permute-start.3 = (bf16[17,26,5,128]{3,1,2,0:T(8,128)(2,1)}, bf16[17,26,5,128]{3,1,2,0:T(8,128)(2,1)}, u32[]{:S(2)}, u32[]{:S(2)}) collective-permute-start(bf16[17,26,5,128]{3,1,2,0:T(8,128)(2,1)} %copy.46), channel_id=1, source_target_pairs={{1,0},{2,1},{3,2},{4,3},{5,4},{6,5},{7,6},{9,8},{10,9},{11,10},{12... | collective-permute-start | bytes 1697288 | tf_op jit(solution)/shard_map/ppermute | solution.py:33
  61.1 1.5 %copy-start.6 = (f32[3]{0:T(128)S(1)}, f32[3]{0:T(128)}, u32[]{:S(2)}) copy-start(f32[3]{0:T(128)} %param.6) | copy-start | bytes 40
  65.9 1.1 %copy-start.4 = (f32[3,24,24,128]{3,0,2,1:T(4,128)}, f32[3,24,24,128]{3,0,2,1:T(4,128)S(1)}, u32[]{:S(2)}) copy-start(f32[3,24,24,128]{3,0,2,1:T(4,128)S(1)} %fusion.34) | copy-start | bytes 2654212
  68.3 1.4 %copy-start = (f32[8,24,24,128]{3,2,1,0:T(8,128)}, f32[8,24,24,128]{3,2,1,0:T(8,128)S(1)}, u32[]{:S(2)}) copy-start(f32[8,24,24,128]{3,2,1,0:T(8,128)S(1)} %compare_convert_fusion) | copy-start | bytes 7077892
  74.5 2.5 %copy-start.1 = (f32[8,20,20,128]{3,2,1,0:T(8,128)}, f32[8,20,20,128]{3,2,1,0:T(8,128)S(1)}, u32[]{:S(2)}) copy-start(f32[8,20,20,128]{3,2,1,0:T(8,128)S(1)} %fusion.12) | copy-start | bytes 4915204
  76.6 2.7 %copy-start.3 = (f32[8,18,18,128]{3,2,1,0:T(8,128)}, f32[8,18,18,128]{3,2,1,0:T(8,128)S(1)}, u32[]{:S(2)}) copy-start(f32[8,18,18,128]{3,2,1,0:T(8,128)S(1)} %fusion.18) | copy-start | bytes 3981316
  79.4 22.9 %copy-start.2 = (f32[8,20,20,128]{3,2,1,0:T(8,128)S(1)}, f32[8,20,20,128]{3,2,1,0:T(8,128)}, u32[]{:S(2)}) copy-start(f32[8,20,20,128]{3,2,1,0:T(8,128)} %copy-done.1) | copy-start | bytes 4915204
  79.4 6.6 %collective-permute-start.4 = (f32[9,8]{1,0:T(8,128)S(1)}, f32[9,8]{1,0:T(8,128)S(1)}, u32[]{:S(2)}, u32[]{:S(2)}) collective-permute-start(f32[9,8]{1,0:T(8,128)S(1)} %stack.55), channel_id=1, source_target_pairs={{0,8},{8,0},{16,24},{24,16},{1,9},{9,1},{17,25},{25,17},{2,10},{10... | collective-permute-start | bytes 872 | tf_op jit(solution)/shard_map/ppermute | solution.py:116
  86.0 3.7 %collective-permute-start.5 = (f32[9,8]{1,0:T(8,128)S(1)}, f32[9,8]{1,0:T(8,128)S(1)}, u32[]{:S(2)}, u32[]{:S(2)}) collective-permute-start(f32[9,8]{1,0:T(8,128)S(1)} %add.576), channel_id=1, source_target_pairs={{0,16},{8,24},{16,0},{24,8},{1,17},{9,25},{17,1},{25,9},{2,18},{10... | collective-permute-start | bytes 872 | tf_op jit(solution)/shard_map/ppermute | solution.py:116
  89.7 3.9 %collective-permute-start.6 = (f32[9,8]{1,0:T(8,128)S(1)}, f32[9,8]{1,0:T(8,128)S(1)}, u32[]{:S(2)}, u32[]{:S(2)}) collective-permute-start(f32[9,8]{1,0:T(8,128)S(1)} %add.577), channel_id=1, source_target_pairs={{0,1},{1,0},{2,3},{3,2},{4,5},{5,4},{6,7},{7,6},{8,9},{9,8},{10,11... | collective-permute-start | bytes 872 | tf_op jit(solution)/shard_map/ppermute | solution.py:116
  93.6 3.7 %collective-permute-start.7 = (f32[9,8]{1,0:T(8,128)S(1)}, f32[9,8]{1,0:T(8,128)S(1)}, u32[]{:S(2)}, u32[]{:S(2)}) collective-permute-start(f32[9,8]{1,0:T(8,128)S(1)} %add.578), channel_id=1, source_target_pairs={{0,2},{1,3},{2,0},{3,1},{4,6},{5,7},{6,4},{7,5},{8,10},{9,11},{10,... | collective-permute-start | bytes 872 | tf_op jit(solution)/shard_map/ppermute | solution.py:116
  97.2 5.0 %collective-permute-start.8 = (f32[9,8]{1,0:T(8,128)S(1)}, f32[9,8]{1,0:T(8,128)S(1)}, u32[]{:S(2)}, u32[]{:S(2)}) collective-permute-start(f32[9,8]{1,0:T(8,128)S(1)} %add.579), channel_id=1, source_target_pairs={{0,4},{1,5},{2,6},{3,7},{4,0},{5,1},{6,2},{7,3},{8,12},{9,13},{10,... | collective-permute-start | bytes 872 | tf_op jit(solution)/shard_map/ppermute | solution.py:116

commit v8 on v6

--- a/solution.py
+++ b/solution.py
@@ -53,13 +53,21 @@
     return summed
 
 
+def from_ring(value, axis, by):
+    devices = lax.axis_size(axis)
+    moved = lax.ppermute(value, axis, [(i, (i + by) % devices) for i in range(devices)])
+    source = lax.axis_index(axis) - by
+    inside = (source >= 0) & (source < devices)
+    return jnp.where(inside, moved, jnp.zeros_like(moved))
+
+
 def extend(cells, width):
     for axis, dim in (("gz", 1), ("yx", 2)):
         size = cells.shape[dim]
         head = lax.slice_in_dim(cells, 0, width, axis=dim)
         tail = lax.slice_in_dim(cells, size - width, size, axis=dim)
         cells = jnp.concatenate(
-            [from_behind(tail, axis, 1), cells, from_behind(head, axis, -1)], axis=dim
+            [from_ring(tail, axis, 1), cells, from_ring(head, axis, -1)], axis=dim
         )
     return cells
 
@@ -134,7 +142,7 @@
         None, None, :
     ]
     bias_column = conv_bias[:, None, None, None]
-    padded = padded_2(features, (("gz", 1), ("yx", 2)), 1)
+    padded = extend(features, 1)
     padded = jnp.pad(padded, ((0, 0), (0, 0), (0, 0), (1, 1)))
     affinities = jax.nn.sigmoid(
         conv_region(padded, conv_weight, depth_cells, row_cells) + bias_column

time: 84 us -> 76.8 us (0.914)
  starting transfers between devices: 29.9 us -> 18.5 us
  waiting for transfers between devices: 23.2 us -> 28.2 us
  local copies, waits for them, and re-layouts: 9.83 us -> 8.81 us
    ppermute x5, starting transfers between devices: 11 us -> 4.09 us  [all_sum(): lax.ppermute(value, axis, [(i, i ^ hop) for i in range(devices)])]
    ppermute x8, starting transfers between devices: 18.9 us -> 14.5 us  [from_ring(): lax.ppermute(value, axis, [(i, (i + by) % devices) for i in range(devices)])]
    ppermute x5, waiting for transfers between devices: 7.44 us -> 11.9 us  [all_sum(): lax.ppermute(value, axis, [(i, i ^ hop) for i in range(devices)])]
    slice x2 -> x1, local copies, waits for them, and re-layouts: 0.94 us -> 0.01 us  [extend(): tail = lax.slice_in_dim(cells, size - width, size, axis=dim)]
    unnamed x17 -> x14, local copies, waits for them, and re-layouts: 4.34 us -> 4.27 us
  transfers between devices with their start and end apart: 13 -> 13, of which waited for: 11 -> 13; matrix products, arithmetic and copies ran while one was open for 3% -> 1% of each run, Pallas kernels for 0% -> 0%
where the time goes in v8:
time: 76.8 us; the launch traced here: 76.6 us
  waiting for transfers between devices  28.2 us (37%)
  starting transfers between devices  18.5 us (24%)
  other arithmetic  13.8 us (18%)
  local copies, waits for them, and re-layouts  8.81 us (11%)
  matrix products  6.15 us (8%)
  between operations  1.11 us (1%)
    ppermute x8, waiting for transfers between devices, from_ring(): lax.ppermute(value, axis, [(i, (i + by) % devices) for i in range(devices)])  16.4 us
    ppermute x8, starting transfers between devices, from_ring(): lax.ppermute(value, axis, [(i, (i + by) % devices) for i in range(devices)])  14.5 us
    ppermute x5, waiting for transfers between devices, all_sum(): lax.ppermute(value, axis, [(i, i ^ hop) for i in range(devices)])  11.9 us
    dot_general x9, matrix products, conv_region(): jnp.einsum('oce,cezyx->ozyx', conv_weight[:, :, offset_z, offset_y, :], w...  6.15 us
    unnamed x14, local copies, waits for them, and re-layouts  4.27 us
    ppermute x5, starting transfers between devices, all_sum(): lax.ppermute(value, axis, [(i, i ^ hop) for i in range(devices)])  4.09 us
    add x1, other arithmetic, body(): probabilities = probabilities + coeff[:, None, None, None] * vector  3.88 us
    sub x2, other arithmetic, operate_inside(): return diagonal[part, part] * centre - coupled  3.29 us
  transfers between devices with their start and end apart: 13, of which 13 were waited for; matrix products, arithmetic and copies ran while one was open for 1% of the time, Pallas kernels for 0%

profile of v8, /device:TPU:0, one launch (start us, length us, event | category | flops | bytes accessed | tf_op | source)
XLA Modules:
  0.0 76.6 jit_solution(16698082353448151539)
XLA Ops:
  0.6 0.0 copy-start.4
  0.6 0.0 copy-start.3
  0.6 1.9 %copy.6 = bf16[16,16,16,128]{3,0,2,1:T(8,128)(2,1)S(1)} copy(bf16[16,16,16,128]{3,2,1,0:T(8,128)(2,1)} %param.4) | data formatting | bytes 2097152 | tf_op args[0]
  2.6 0.5 collective-permute-start
  3.2 2.0 %collective-permute-start.1 = (bf16[16,1,16,128]{3,0,2,1:T(8,128)(2,1)S(1)}, bf16[16,1,16,128]{3,0,2,1:T(8,128)(2,1)S(1)}, u32[]{:S(2)}, u32[]{:S(2)}) collective-permute-start(bf16[16,1,16,128]{3,0,2,1:T(8,128)(2,1)S(1)} %get-tuple-element.40), channel_id=1, source_target_pairs={{0,24},{8,0},{16,8},{24,16},{1,25},{9,1},{17,9},{25,17},{2,26},{10... | collective-permute-start | bytes 196616 | tf_op jit(solution)/shard_map/ppermute | solution.py:58
  5.1 1.9 %collective-permute-done = bf16[16,1,16,128]{3,0,2,1:T(8,128)(2,1)S(1)} collective-permute-done((bf16[16,1,16,128]{3,0,2,1:T(8,128)(2,1)S(1)}, bf16[16,1,16,128]{3,0,2,1:T(8,128)(2,1)S(1)}, u32[]{:S(2)}, u32[]{:S(2)}) %collective-permute-start) | collective-permute-done | bytes 65568 | tf_op jit(solution)/shard_map/ppermute | solution.py:58
  7.0 0.5 collective-permute-done.1
  7.6 1.9 %collective-permute-start.2 = (bf16[16,18,1,128]{3,0,2,1:T(8,128)(2,1)S(1)}, bf16[16,18,1,128]{3,0,2,1:T(8,128)(2,1)S(1)}, u32[]{:S(2)}, u32[]{:S(2)}) collective-permute-start(bf16[16,18,1,128]{3,0,2,1:T(8,128)(2,1)S(1)} %get-tuple-element.37), channel_id=1, source_target_pairs={{0,1},{1,2},{2,3},{3,4},{4,5},{5,6},{6,7},{7,0},{8,9},{9,10},{10,1... | collective-permute-start | bytes 221192 | tf_op jit(solution)/shard_map/ppermute | solution.py:58
  9.5 0.0 copy-done.4
  9.5 0.0 copy-done.3
  9.5 3.1 %collective-permute-start.3 = (bf16[16,18,1,128]{3,0,2,1:T(8,128)(2,1)S(1)}, bf16[16,18,1,128]{3,0,2,1:T(8,128)(2,1)S(1)}, u32[]{:S(2)}, u32[]{:S(2)}) collective-permute-start(bf16[16,18,1,128]{3,0,2,1:T(8,128)(2,1)S(1)} %get-tuple-element.38), channel_id=1, source_target_pairs={{0,7},{1,0},{2,1},{3,2},{4,3},{5,4},{6,5},{7,6},{8,15},{9,8},{10,9... | collective-permute-start | bytes 221192 | tf_op jit(solution)/shard_map/ppermute | solution.py:58
  12.7 2.3 %collective-permute-done.2 = bf16[16,18,1,128]{3,0,2,1:T(8,128)(2,1)S(1)} collective-permute-done((bf16[16,18,1,128]{3,0,2,1:T(8,128)(2,1)S(1)}, bf16[16,18,1,128]{3,0,2,1:T(8,128)(2,1)S(1)}, u32[]{:S(2)}, u32[]{:S(2)}) %collective-permute-start.2) | collective-permute-done | bytes 73760 | tf_op jit(solution)/shard_map/ppermute | solution.py:58
  15.0 1.0 %collective-permute-done.3 = bf16[16,18,1,128]{3,0,2,1:T(8,128)(2,1)S(1)} collective-permute-done((bf16[16,18,1,128]{3,0,2,1:T(8,128)(2,1)S(1)}, bf16[16,18,1,128]{3,0,2,1:T(8,128)(2,1)S(1)}, u32[]{:S(2)}, u32[]{:S(2)}) %collective-permute-start.3) | collective-permute-done | bytes 73760 | tf_op jit(solution)/shard_map/ppermute | solution.py:58
  16.0 0.3 fusion.80
  16.3 0.3 pad_maximum_fusion.1
  16.5 0.8 fusion.19
  17.3 0.6 convolution_bitcast_fusion.7
  17.9 0.6 convolution_bitcast_fusion.6
  18.5 0.6 convolution_bitcast_fusion.5
  19.1 0.6 convolution_bitcast_fusion.4
  19.6 0.6 convolution_bitcast_fusion.3
  20.2 0.6 convolution_bitcast_fusion.2
  20.8 0.6 convolution_bitcast_fusion.1
  21.4 0.6 convolution_bitcast_fusion
  22.0 0.1 copy-done.5
  22.1 1.5 %fusion.34 = f32[3,16,16,128]{3,0,2,1:T(4,128)S(1)} fusion(f32[16,16,128,3]{2,3,1,0:T(4,128)S(1)} %convolution_bitcast_fusion, f32[16,16,128,3]{2,3,1,0:T(4,128)S(1)} %convolution_bitcast_fusion.1, f32[16,16,128,3]{2,3,1,0:T(4,128)S(1)} %convolution_bitcast_fusion.2, f32[16,16,128,3]{2,3,1,0:T(4,128)S(1)} %convolution_bitcast_fusion.3, ...), kind=kOutput, calls=%fused_computation.63 | convolution fusion | flops 22560768 | bytes 7520556 | tf_op jit(solution)/shard_map/oce,cezyx->ozyx/dot_general | solution.py:47
  23.5 0.1 pad_maximum_fusion.8
  23.7 0.2 collective-permute-start.4
  23.9 1.6 %collective-permute-start.5 = (f32[4,4,16,128]{3,0,2,1:T(4,128)S(1)}, f32[4,4,16,128]{3,0,2,1:T(4,128)S(1)}, u32[]{:S(2)}, u32[]{:S(2)}) collective-permute-start(f32[4,4,16,128]{3,0,2,1:T(4,128)S(1)} %get-tuple-element.44), channel_id=1, source_target_pairs={{0,24},{8,0},{16,8},{24,16},{1,25},{9,1},{17,9},{25,17},{2,26},{10... | collective-permute-start | bytes 393224 | tf_op jit(solution)/shard_map/ppermute | solution.py:58
  25.5 2.6 %collective-permute-done.4 = f32[4,4,16,128]{3,0,2,1:T(4,128)S(1)} collective-permute-done((f32[4,4,16,128]{3,0,2,1:T(4,128)S(1)}, f32[4,4,16,128]{3,0,2,1:T(4,128)S(1)}, u32[]{:S(2)}, u32[]{:S(2)}) %collective-permute-start.4) | collective-permute-done | bytes 131104 | tf_op jit(solution)/shard_map/ppermute | solution.py:58
  28.1 0.1 collective-permute-done.5
  28.3 0.2 pad_maximum_fusion.6
  28.4 0.9 %collective-permute-start.6 = (f32[4,24,4,128]{3,0,2,1:T(4,128)S(1)}, f32[4,24,4,128]{3,0,2,1:T(4,128)S(1)}, u32[]{:S(2)}, u32[]{:S(2)}) collective-permute-start(f32[4,24,4,128]{3,0,2,1:T(4,128)S(1)} %get-tuple-element.41), channel_id=1, source_target_pairs={{0,1},{1,2},{2,3},{3,4},{4,5},{5,6},{6,7},{7,0},{8,9},{9,10},{10,1... | collective-permute-start | bytes 589832 | tf_op jit(solution)/shard_map/ppermute | solution.py:58
  29.3 4.2 %collective-permute-start.7 = (f32[4,24,4,128]{3,0,2,1:T(4,128)S(1)}, f32[4,24,4,128]{3,0,2,1:T(4,128)S(1)}, u32[]{:S(2)}, u32[]{:S(2)}) collective-permute-start(f32[4,24,4,128]{3,0,2,1:T(4,128)S(1)} %get-tuple-element.42), channel_id=1, source_target_pairs={{0,7},{1,0},{2,1},{3,2},{4,3},{5,4},{6,5},{7,6},{8,15},{9,8},{10,9... | collective-permute-start | bytes 589832 | tf_op jit(solution)/shard_map/ppermute | solution.py:58
  33.5 5.0 %collective-permute-done.6 = f32[4,24,4,128]{3,0,2,1:T(4,128)S(1)} collective-permute-done((f32[4,24,4,128]{3,0,2,1:T(4,128)S(1)}, f32[4,24,4,128]{3,0,2,1:T(4,128)S(1)}, u32[]{:S(2)}, u32[]{:S(2)}) %collective-permute-start.6) | collective-permute-done | bytes 196640 | tf_op jit(solution)/shard_map/ppermute | solution.py:58
  38.6 2.9 %collective-permute-done.7 = f32[4,24,4,128]{3,0,2,1:T(4,128)S(1)} collective-permute-done((f32[4,24,4,128]{3,0,2,1:T(4,128)S(1)}, f32[4,24,4,128]{3,0,2,1:T(4,128)S(1)}, u32[]{:S(2)}, u32[]{:S(2)}) %collective-permute-start.7) | collective-permute-done | bytes 196640 | tf_op jit(solution)/shard_map/ppermute | solution.py:58
  41.6 0.4 pad_maximum_fusion.2
  42.0 0.9 %fusion.77 = (f32[1,24,24,128]{3,0,2,1:T(1,128)S(1)}, f32[1,24,24,128]{3,0,2,1:T(1,128)S(1)}, f32[1,24,24,128]{3,0,2,1:T(1,128)S(1)}, f32[1,24,24,128]{3,0,2,1:T(1,128)S(1)}) fusion(f32[4,24,24,128]{3,0,2,1:T(4,128)S(1)} %pad_maximum_fusion.2), kind=kLoop, calls=%fused_computation.177 | loop fusion | bytes 2359296 | tf_op jit(solution)/shard_map/slice | solution.py:161
  42.9 0.1 broadcast_multiply_fusion
  43.0 0.2 convert_add_fusion
  43.3 0.2 fusion.48
  44.0 0.2 compare_convert_fusion
  44.2 0.8 fusion.73
  45.0 0.6 copy-done
  45.6 2.1 %fusion.4 = f32[8,22,22,128]{3,2,1,0:T(8,128)S(1)} fusion(f32[8,24,24,128]{3,2,1,0:T(8,128)S(1)} %compare_convert_fusion, f32[8,22,22,127]{3,2,1,0:T(8,128)S(1)} %get-tuple-element.24, f32[8,22,22,127]{3,2,1,0:T(8,128)S(1)} %get-tuple-element.23, f32[22,22,128]{2,1,0:T(8,128)S(1)} %get-tuple-element.53, f32[22,22,128]{2,1,0:T(8,128)S(1)} %get-tuple-element.54, ...), kind=kLoop, calls=%fused_computation.9 | loop fusion | flops 6938624 | bytes 17563392 | tf_op jit(solution)/shard_map/sub | solution.py:172
  47.7 0.7 fusion.74
  48.4 1.8 %fusion.10 = f32[8,20,20,128]{3,2,1,0:T(8,128)S(1)} fusion(f32[8,22,22,128]{3,2,1,0:T(8,128)S(1)} %fusion.4, f32[8,20,20,127]{3,2,1,0:T(8,128)S(1)} %get-tuple-element.26, f32[8,20,20,127]{3,2,1,0:T(8,128)S(1)} %get-tuple-element.25, f32[20,20,128]{2,1,0:T(8,128)S(1)} %slice.451, f32[20,20,128]{2,1,0:T(8,128)S(1)} %slice.449, f32[20,20,128]{2,1,0:T(8,128)S(1)} %slice.447, ...), kind=kLoop, calls=%fused_computation.19 | loop fusion | flops 5324800 | bytes 14515200 | tf_op jit(solution)/shard_map/sub | solution.py:113
  50.3 0.6 fusion.75
  50.9 1.4 %fusion.16 = f32[8,18,18,128]{3,2,1,0:T(8,128)S(1)} fusion(f32[8,20,20,128]{3,2,1,0:T(8,128)S(1)} %fusion.10, f32[8,18,18,127]{3,2,1,0:T(8,128)S(1)} %get-tuple-element.28, f32[8,18,18,127]{3,2,1,0:T(8,128)S(1)} %get-tuple-element.27, f32[18,18,128]{2,1,0:T(8,128)S(1)} %slice.466, f32[18,18,128]{2,1,0:T(8,128)S(1)} %slice.464, ...), kind=kLoop, calls=%fused_computation.30 | loop fusion | flops 4313088 | bytes 11757312 | tf_op jit(solution)/shard_map/sub | solution.py:113
  52.3 0.4 fusion.76
  52.7 0.8 %copy-done.2 = f32[8,18,18,128]{3,2,1,0:T(8,128)} copy-done((f32[8,18,18,128]{3,2,1,0:T(8,128)}, f32[8,18,18,128]{3,2,1,0:T(8,128)S(1)}, u32[]{:S(2)}) %copy-start.2) | copy-done | bytes 1327128
  53.6 2.3 %multiply_reduce_fusion.5 = (f32[8]{0:T(128)S(1)}, f32[8]{0:T(128)S(1)}, f32[8]{0:T(128)S(1)}, f32[8]{0:T(128)S(1)}, f32[8]{0:T(128)S(1)}, /*index=5*/f32[8]{0:T...) fusion(f32[8,22,22,128]{3,2,1,0:T(8,128)S(1)} %fusion.4, f32[8,20,20,128]{3,2,1,0:T(8,128)S(1)} %fusion.10, ...), kind=kLoop, calls=%fused_computation.82 | loop fusion | flops 8126392 | bytes 10338592 | tf_op jit(solution)/shard_map/reduce_sum | solution.py:130
  55.9 0.2 collective-permute-start.8
  56.1 1.1 %collective-permute-done.8 = f32[9,8]{1,0:T(8,128)S(1)} collective-permute-done((f32[9,8]{1,0:T(8,128)S(1)}, f32[9,8]{1,0:T(8,128)S(1)}, u32[]{:S(2)}, u32[]{:S(2)}) %collective-permute-start.8) | collective-permute-done | bytes 320 | tf_op jit(solution)/shard_map/ppermute | solution.py:124
  57.1 1.1 %collective-permute-start.9 = (f32[9,8]{1,0:T(8,128)S(1)}, f32[9,8]{1,0:T(8,128)S(1)}, u32[]{:S(2)}, u32[]{:S(2)}) collective-permute-start(f32[9,8]{1,0:T(8,128)S(1)} %add.580), channel_id=1, source_target_pairs={{0,16},{8,24},{16,0},{24,8},{1,17},{9,25},{17,1},{25,9},{2,18},{10... | collective-permute-start | bytes 872 | tf_op jit(solution)/shard_map/ppermute | solution.py:124
  58.2 2.6 %collective-permute-done.9 = f32[9,8]{1,0:T(8,128)S(1)} collective-permute-done((f32[9,8]{1,0:T(8,128)S(1)}, f32[9,8]{1,0:T(8,128)S(1)}, u32[]{:S(2)}, u32[]{:S(2)}) %collective-permute-start.9) | collective-permute-done | bytes 320 | tf_op jit(solution)/shard_map/ppermute | solution.py:124
  60.8 0.0 collective-permute-start.10
  60.8 3.6 %collective-permute-done.10 = f32[9,8]{1,0:T(8,128)S(1)} collective-permute-done((f32[9,8]{1,0:T(8,128)S(1)}, f32[9,8]{1,0:T(8,128)S(1)}, u32[]{:S(2)}, u32[]{:S(2)}) %collective-permute-start.10) | collective-permute-done | bytes 320 | tf_op jit(solution)/shard_map/ppermute | solution.py:124
  64.4 0.9 %collective-permute-start.11 = (f32[9,8]{1,0:T(8,128)S(1)}, f32[9,8]{1,0:T(8,128)S(1)}, u32[]{:S(2)}, u32[]{:S(2)}) collective-permute-start(f32[9,8]{1,0:T(8,128)S(1)} %add.582), channel_id=1, source_target_pairs={{0,2},{1,3},{2,0},{3,1},{4,6},{5,7},{6,4},{7,5},{8,10},{9,11},{10,... | collective-permute-start | bytes 872 | tf_op jit(solution)/shard_map/ppermute | solution.py:124
  65.4 2.7 %collective-permute-done.11 = f32[9,8]{1,0:T(8,128)S(1)} collective-permute-done((f32[9,8]{1,0:T(8,128)S(1)}, f32[9,8]{1,0:T(8,128)S(1)}, u32[]{:S(2)}, u32[]{:S(2)}) %collective-permute-start.11) | collective-permute-done | bytes 320 | tf_op jit(solution)/shard_map/ppermute | solution.py:124
  68.1 1.9 %collective-permute-start.12 = (f32[9,8]{1,0:T(8,128)S(1)}, f32[9,8]{1,0:T(8,128)S(1)}, u32[]{:S(2)}, u32[]{:S(2)}) collective-permute-start(f32[9,8]{1,0:T(8,128)S(1)} %add.583), channel_id=1, source_target_pairs={{0,4},{1,5},{2,6},{3,7},{4,0},{5,1},{6,2},{7,3},{8,12},{9,13},{10,... | collective-permute-start | bytes 872 | tf_op jit(solution)/shard_map/ppermute | solution.py:124
  70.0 0.8 %copy.23 = f32[3,16,16,128]{3,2,1,0:T(8,128)} copy(f32[3,16,16,128]{3,0,2,1:T(4,128)S(1)} %fusion.34) | data formatting | bytes 786432
  70.8 1.8 %collective-permute-done.12 = f32[9,8]{1,0:T(8,128)S(1)} collective-permute-done((f32[9,8]{1,0:T(8,128)S(1)}, f32[9,8]{1,0:T(8,128)S(1)}, u32[]{:S(2)}, u32[]{:S(2)}) %collective-permute-start.12) | collective-permute-done | bytes 320 | tf_op jit(solution)/shard_map/ppermute | solution.py:124
  72.7 3.9 %fusion.42 = f32[8,16,16,128]{3,2,1,0:T(8,128)} fusion(f32[8,24,24,128]{3,2,1,0:T(8,128)} %copy-done, f32[8,20,20,128]{3,2,1,0:T(8,128)} %copy-done.1, f32[8,22,22,128]{3,2,1,0:T(8,128)S(1)} %fusion.4, f32[8,18,18,128]{3,2,1,0:T(8,128)} %copy-done.2, f32[8]{0:T(128)S(1)} %get-tuple-element.65, f32[8]{0:T(128)S(1)} %get-tuple-element.64, ...), kind=kLoop, calls=%fused_computation.76 | loop fusion | flops 1572864 | bytes 5242976 | tf_op jit(solution)/shard_map/add | solution.py:236
  (52 shorter events, 0.8 us)
Async XLA Ops:
  0.6 8.9 %copy-start.4 = (bf16[3,16,3,3,3]{1,4,3,2,0:T(4,128)(2,1)S(1)}, bf16[3,16,3,3,3]{1,4,3,2,0:T(4,128)(2,1)}, u32[]{:S(2)}) copy-start(bf16[3,16,3,3,3]{1,4,3,2,0:T(4,128)(2,1)} %param.5) | copy-start | bytes 7780
  0.6 8.9 %copy-start.3 = (s32[16,16,128]{2,1,0:T(8,128)S(1)}, s32[16,16,128]{2,1,0:T(8,128)}, u32[]{:S(2)}) copy-start(s32[16,16,128]{2,1,0:T(8,128)} %param.7) | copy-start | bytes 393220
  2.6 4.4 %collective-permute-start = (bf16[16,1,16,128]{3,0,2,1:T(8,128)(2,1)S(1)}, bf16[16,1,16,128]{3,0,2,1:T(8,128)(2,1)S(1)}, u32[]{:S(2)}, u32[]{:S(2)}) collective-permute-start(bf16[16,1,16,128]{3,0,2,1:T(8,128)(2,1)S(1)} %get-tuple-element.39), channel_id=1, source_target_pairs={{0,8},{8,16},{16,24},{24,0},{1,9},{9,17},{17,25},{25,1},{2,10},{10... | collective-permute-start | bytes 196616 | tf_op jit(solution)/shard_map/ppermute | solution.py:58
  3.2 4.4 %collective-permute-start.1 = (bf16[16,1,16,128]{3,0,2,1:T(8,128)(2,1)S(1)}, bf16[16,1,16,128]{3,0,2,1:T(8,128)(2,1)S(1)}, u32[]{:S(2)}, u32[]{:S(2)}) collective-permute-start(bf16[16,1,16,128]{3,0,2,1:T(8,128)(2,1)S(1)} %get-tuple-element.40), channel_id=1, source_target_pairs={{0,24},{8,0},{16,8},{24,16},{1,25},{9,1},{17,9},{25,17},{2,26},{10... | collective-permute-start | bytes 196616 | tf_op jit(solution)/shard_map/ppermute | solution.py:58
  7.6 7.4 %collective-permute-start.2 = (bf16[16,18,1,128]{3,0,2,1:T(8,128)(2,1)S(1)}, bf16[16,18,1,128]{3,0,2,1:T(8,128)(2,1)S(1)}, u32[]{:S(2)}, u32[]{:S(2)}) collective-permute-start(bf16[16,18,1,128]{3,0,2,1:T(8,128)(2,1)S(1)} %get-tuple-element.37), channel_id=1, source_target_pairs={{0,1},{1,2},{2,3},{3,4},{4,5},{5,6},{6,7},{7,0},{8,9},{9,10},{10,1... | collective-permute-start | bytes 221192 | tf_op jit(solution)/shard_map/ppermute | solution.py:58
  9.5 6.4 %collective-permute-start.3 = (bf16[16,18,1,128]{3,0,2,1:T(8,128)(2,1)S(1)}, bf16[16,18,1,128]{3,0,2,1:T(8,128)(2,1)S(1)}, u32[]{:S(2)}, u32[]{:S(2)}) collective-permute-start(bf16[16,18,1,128]{3,0,2,1:T(8,128)(2,1)S(1)} %get-tuple-element.38), channel_id=1, source_target_pairs={{0,7},{1,0},{2,1},{3,2},{4,3},{5,4},{6,5},{7,6},{8,15},{9,8},{10,9... | collective-permute-start | bytes 221192 | tf_op jit(solution)/shard_map/ppermute | solution.py:58
  21.4 0.7 copy-start.5
  23.7 4.4 %collective-permute-start.4 = (f32[4,4,16,128]{3,0,2,1:T(4,128)S(1)}, f32[4,4,16,128]{3,0,2,1:T(4,128)S(1)}, u32[]{:S(2)}, u32[]{:S(2)}) collective-permute-start(f32[4,4,16,128]{3,0,2,1:T(4,128)S(1)} %get-tuple-element.43), channel_id=1, source_target_pairs={{0,8},{8,16},{16,24},{24,0},{1,9},{9,17},{17,25},{25,1},{2,10},{10... | collective-permute-start | bytes 393224 | tf_op jit(solution)/shard_map/ppermute | solution.py:58
  23.9 4.4 %collective-permute-start.5 = (f32[4,4,16,128]{3,0,2,1:T(4,128)S(1)}, f32[4,4,16,128]{3,0,2,1:T(4,128)S(1)}, u32[]{:S(2)}, u32[]{:S(2)}) collective-permute-start(f32[4,4,16,128]{3,0,2,1:T(4,128)S(1)} %get-tuple-element.44), channel_id=1, source_target_pairs={{0,24},{8,0},{16,8},{24,16},{1,25},{9,1},{17,9},{25,17},{2,26},{10... | collective-permute-start | bytes 393224 | tf_op jit(solution)/shard_map/ppermute | solution.py:58
  28.4 10.1 %collective-permute-start.6 = (f32[4,24,4,128]{3,0,2,1:T(4,128)S(1)}, f32[4,24,4,128]{3,0,2,1:T(4,128)S(1)}, u32[]{:S(2)}, u32[]{:S(2)}) collective-permute-start(f32[4,24,4,128]{3,0,2,1:T(4,128)S(1)} %get-tuple-element.41), channel_id=1, source_target_pairs={{0,1},{1,2},{2,3},{3,4},{4,5},{5,6},{6,7},{7,0},{8,9},{9,10},{10,1... | collective-permute-start | bytes 589832 | tf_op jit(solution)/shard_map/ppermute | solution.py:58
  29.3 12.2 %collective-permute-start.7 = (f32[4,24,4,128]{3,0,2,1:T(4,128)S(1)}, f32[4,24,4,128]{3,0,2,1:T(4,128)S(1)}, u32[]{:S(2)}, u32[]{:S(2)}) collective-permute-start(f32[4,24,4,128]{3,0,2,1:T(4,128)S(1)} %get-tuple-element.42), channel_id=1, source_target_pairs={{0,7},{1,0},{2,1},{3,2},{4,3},{5,4},{6,5},{7,6},{8,15},{9,8},{10,9... | collective-permute-start | bytes 589832 | tf_op jit(solution)/shard_map/ppermute | solution.py:58
  44.2 1.4 %copy-start = (f32[8,24,24,128]{3,2,1,0:T(8,128)}, f32[8,24,24,128]{3,2,1,0:T(8,128)S(1)}, u32[]{:S(2)}) copy-start(f32[8,24,24,128]{3,2,1,0:T(8,128)S(1)} %compare_convert_fusion) | copy-start | bytes 7077892
  50.2 2.5 %copy-start.1 = (f32[8,20,20,128]{3,2,1,0:T(8,128)}, f32[8,20,20,128]{3,2,1,0:T(8,128)S(1)}, u32[]{:S(2)}) copy-start(f32[8,20,20,128]{3,2,1,0:T(8,128)S(1)} %fusion.10) | copy-start | bytes 4915204
  52.3 1.2 %copy-start.2 = (f32[8,18,18,128]{3,2,1,0:T(8,128)}, f32[8,18,18,128]{3,2,1,0:T(8,128)S(1)}, u32[]{:S(2)}) copy-start(f32[8,18,18,128]{3,2,1,0:T(8,128)S(1)} %fusion.16) | copy-start | bytes 3981316
  55.9 1.2 %collective-permute-start.8 = (f32[9,8]{1,0:T(8,128)S(1)}, f32[9,8]{1,0:T(8,128)S(1)}, u32[]{:S(2)}, u32[]{:S(2)}) collective-permute-start(f32[9,8]{1,0:T(8,128)S(1)} %stack.55), channel_id=1, source_target_pairs={{0,8},{8,0},{16,24},{24,16},{1,9},{9,1},{17,25},{25,17},{2,10},{10... | collective-permute-start | bytes 872 | tf_op jit(solution)/shard_map/ppermute | solution.py:124
  57.1 3.7 %collective-permute-start.9 = (f32[9,8]{1,0:T(8,128)S(1)}, f32[9,8]{1,0:T(8,128)S(1)}, u32[]{:S(2)}, u32[]{:S(2)}) collective-permute-start(f32[9,8]{1,0:T(8,128)S(1)} %add.580), channel_id=1, source_target_pairs={{0,16},{8,24},{16,0},{24,8},{1,17},{9,25},{17,1},{25,9},{2,18},{10... | collective-permute-start | bytes 872 | tf_op jit(solution)/shard_map/ppermute | solution.py:124
  60.8 3.7 %collective-permute-start.10 = (f32[9,8]{1,0:T(8,128)S(1)}, f32[9,8]{1,0:T(8,128)S(1)}, u32[]{:S(2)}, u32[]{:S(2)}) collective-permute-start(f32[9,8]{1,0:T(8,128)S(1)} %add.581), channel_id=1, source_target_pairs={{0,1},{1,0},{2,3},{3,2},{4,5},{5,4},{6,7},{7,6},{8,9},{9,8},{10,11... | collective-permute-start | bytes 872 | tf_op jit(solution)/shard_map/ppermute | solution.py:124
  64.4 3.7 %collective-permute-start.11 = (f32[9,8]{1,0:T(8,128)S(1)}, f32[9,8]{1,0:T(8,128)S(1)}, u32[]{:S(2)}, u32[]{:S(2)}) collective-permute-start(f32[9,8]{1,0:T(8,128)S(1)} %add.582), channel_id=1, source_target_pairs={{0,2},{1,3},{2,0},{3,1},{4,6},{5,7},{6,4},{7,5},{8,10},{9,11},{10,... | collective-permute-start | bytes 872 | tf_op jit(solution)/shard_map/ppermute | solution.py:124
  68.1 4.5 %collective-permute-start.12 = (f32[9,8]{1,0:T(8,128)S(1)}, f32[9,8]{1,0:T(8,128)S(1)}, u32[]{:S(2)}, u32[]{:S(2)}) collective-permute-start(f32[9,8]{1,0:T(8,128)S(1)} %add.583), channel_id=1, source_target_pairs={{0,4},{1,5},{2,6},{3,7},{4,0},{5,1},{6,2},{7,3},{8,12},{9,13},{10,... | collective-permute-start | bytes 872 | tf_op jit(solution)/shard_map/ppermute | solution.py:124

commit v9 on v8

--- a/solution.py
+++ b/solution.py
@@ -165,7 +165,7 @@
     )
     colours = jnp.arange(1, FIELDS + 1, dtype=jnp.float32)[:, None, None, None]
     grid_seed = (grid_labels[None] == colours).astype(jnp.float32)
-    seed_field = grid_seed[:, halo:-halo, halo:-halo]
+    seed_field = (labels[None] == jnp.arange(1, FIELDS + 1, dtype=jnp.int32)[:, None, None, None]).astype(jnp.float32)
 
     inside = grid_seed[:, 1:-1, 1:-1]
     cells = operator_cells(grid)

time: 76.8 us -> 76.3 us (level)
  waiting for transfers between devices: 28.2 us -> 29.9 us
  starting transfers between devices: 18.5 us -> 17.5 us
    ppermute x8, waiting for transfers between devices: 16.4 us -> 17.2 us  [from_ring(): lax.ppermute(value, axis, [(i, (i + by) % devices) for i in range(devices)])]
    ppermute x5, waiting for transfers between devices: 11.9 us -> 12.7 us  [all_sum(): lax.ppermute(value, axis, [(i, i ^ hop) for i in range(devices)])]
    unnamed x14 -> x12, local copies, waits for them, and re-layouts: 4.27 us -> 3.64 us
  transfers between devices with their start and end apart: 13 -> 13, of which waited for: 13 -> 12; matrix products, arithmetic and copies ran while one was open for 1% -> 1% of each run, Pallas kernels for 0% -> 0%
where the time goes in v9:
time: 76.3 us; the launch traced here: 76.1 us
  waiting for transfers between devices  29.9 us (39%)
  starting transfers between devices  17.5 us (23%)
  other arithmetic  13.3 us (17%)
  local copies, waits for them, and re-layouts  8.18 us (11%)
  matrix products  6.15 us (8%)
  between operations  1.14 us (1%)
    ppermute x8, waiting for transfers between devices, from_ring(): lax.ppermute(value, axis, [(i, (i + by) % devices) for i in range(devices)])  17.2 us
    ppermute x8, starting transfers between devices, from_ring(): lax.ppermute(value, axis, [(i, (i + by) % devices) for i in range(devices)])  14.1 us
    ppermute x5, waiting for transfers between devices, all_sum(): lax.ppermute(value, axis, [(i, i ^ hop) for i in range(devices)])  12.7 us
    dot_general x9, matrix products, conv_region(): jnp.einsum('oce,cezyx->ozyx', conv_weight[:, :, offset_z, offset_y, :], w...  6.15 us
    unnamed x12, local copies, waits for them, and re-layouts  3.64 us
    add x1, other arithmetic, body(): probabilities = probabilities + coeff[:, None, None, None] * vector  3.39 us
    ppermute x5, starting transfers between devices, all_sum(): lax.ppermute(value, axis, [(i, i ^ hop) for i in range(devices)])  3.36 us
    sub x2, other arithmetic, operate_inside(): return diagonal[part, part] * centre - coupled  3.29 us
  transfers between devices with their start and end apart: 13, of which 12 were waited for; matrix products, arithmetic and copies ran while one was open for 1% of the time, Pallas kernels for 0%

profile of v9, /device:TPU:0, one launch (start us, length us, event | category | flops | bytes accessed | tf_op | source)
XLA Modules:
  0.0 76.1 jit_solution(1420164532958503291)
XLA Ops:
  0.6 0.0 copy-start.3
  0.6 0.0 copy-start.2
  0.6 1.9 %copy.6 = bf16[16,16,16,128]{3,0,2,1:T(8,128)(2,1)S(1)} copy(bf16[16,16,16,128]{3,2,1,0:T(8,128)(2,1)} %param.4) | data formatting | bytes 2097152 | tf_op args[0]
  2.6 2.5 %collective-permute-start.1 = (bf16[16,1,16,128]{3,0,2,1:T(8,128)(2,1)S(1)}, bf16[16,1,16,128]{3,0,2,1:T(8,128)(2,1)S(1)}, u32[]{:S(2)}, u32[]{:S(2)}) collective-permute-start(bf16[16,1,16,128]{3,0,2,1:T(8,128)(2,1)S(1)} %get-tuple-element.40), channel_id=1, source_target_pairs={{0,24},{8,0},{16,8},{24,16},{1,25},{9,1},{17,9},{25,17},{2,26},{10... | collective-permute-start | bytes 196616 | tf_op jit(solution)/shard_map/ppermute | solution.py:58
  5.1 0.0 collective-permute-start
  5.1 2.4 %collective-permute-done.1 = bf16[16,1,16,128]{3,0,2,1:T(8,128)(2,1)S(1)} collective-permute-done((bf16[16,1,16,128]{3,0,2,1:T(8,128)(2,1)S(1)}, bf16[16,1,16,128]{3,0,2,1:T(8,128)(2,1)S(1)}, u32[]{:S(2)}, u32[]{:S(2)}) %collective-permute-start.1) | collective-permute-done | bytes 65568 | tf_op jit(solution)/shard_map/ppermute | solution.py:58
  7.5 1.2 %collective-permute-done = bf16[16,1,16,128]{3,0,2,1:T(8,128)(2,1)S(1)} collective-permute-done((bf16[16,1,16,128]{3,0,2,1:T(8,128)(2,1)S(1)}, bf16[16,1,16,128]{3,0,2,1:T(8,128)(2,1)S(1)}, u32[]{:S(2)}, u32[]{:S(2)}) %collective-permute-start) | collective-permute-done | bytes 65568 | tf_op jit(solution)/shard_map/ppermute | solution.py:58
  8.8 1.6 %collective-permute-start.2 = (bf16[16,18,1,128]{3,0,2,1:T(8,128)(2,1)S(1)}, bf16[16,18,1,128]{3,0,2,1:T(8,128)(2,1)S(1)}, u32[]{:S(2)}, u32[]{:S(2)}) collective-permute-start(bf16[16,18,1,128]{3,0,2,1:T(8,128)(2,1)S(1)} %get-tuple-element.37), channel_id=1, source_target_pairs={{0,1},{1,2},{2,3},{3,4},{4,5},{5,6},{6,7},{7,0},{8,9},{9,10},{10,1... | collective-permute-start | bytes 221192 | tf_op jit(solution)/shard_map/ppermute | solution.py:58
  10.4 0.0 copy-done.3
  10.4 0.0 copy-done.2
  10.4 3.3 %collective-permute-start.3 = (bf16[16,18,1,128]{3,0,2,1:T(8,128)(2,1)S(1)}, bf16[16,18,1,128]{3,0,2,1:T(8,128)(2,1)S(1)}, u32[]{:S(2)}, u32[]{:S(2)}) collective-permute-start(bf16[16,18,1,128]{3,0,2,1:T(8,128)(2,1)S(1)} %get-tuple-element.38), channel_id=1, source_target_pairs={{0,7},{1,0},{2,1},{3,2},{4,3},{5,4},{6,5},{7,6},{8,15},{9,8},{10,9... | collective-permute-start | bytes 221192 | tf_op jit(solution)/shard_map/ppermute | solution.py:58
  13.7 2.2 %collective-permute-done.2 = bf16[16,18,1,128]{3,0,2,1:T(8,128)(2,1)S(1)} collective-permute-done((bf16[16,18,1,128]{3,0,2,1:T(8,128)(2,1)S(1)}, bf16[16,18,1,128]{3,0,2,1:T(8,128)(2,1)S(1)}, u32[]{:S(2)}, u32[]{:S(2)}) %collective-permute-start.2) | collective-permute-done | bytes 73760 | tf_op jit(solution)/shard_map/ppermute | solution.py:58
  15.9 0.0 collective-permute-done.3
  16.0 0.3 pad_maximum_fusion.1
  16.2 0.3 fusion.78
  16.5 0.8 fusion.19
  17.2 0.6 convolution_bitcast_fusion.7
  17.8 0.6 convolution_bitcast_fusion.6
  18.4 0.6 convolution_bitcast_fusion.5
  19.0 0.6 convolution_bitcast_fusion.4
  19.6 0.6 convolution_bitcast_fusion.3
  20.2 0.6 convolution_bitcast_fusion.2
  20.8 0.6 convolution_bitcast_fusion.1
  21.4 0.6 convolution_bitcast_fusion
  21.9 0.1 copy-done.4
  22.0 1.5 %fusion.34 = f32[3,16,16,128]{3,0,2,1:T(4,128)S(1)} fusion(f32[16,16,128,3]{2,3,1,0:T(4,128)S(1)} %convolution_bitcast_fusion, f32[16,16,128,3]{2,3,1,0:T(4,128)S(1)} %convolution_bitcast_fusion.1, f32[16,16,128,3]{2,3,1,0:T(4,128)S(1)} %convolution_bitcast_fusion.2, f32[16,16,128,3]{2,3,1,0:T(4,128)S(1)} %convolution_bitcast_fusion.3, ...), kind=kOutput, calls=%fused_computation.63 | convolution fusion | flops 22560768 | bytes 7520556 | tf_op jit(solution)/shard_map/oce,cezyx->ozyx/dot_general | solution.py:47
  23.5 0.1 pad_maximum_fusion.8
  23.6 0.1 collective-permute-start.4
  23.7 1.8 %collective-permute-start.5 = (f32[4,4,16,128]{3,0,2,1:T(4,128)S(1)}, f32[4,4,16,128]{3,0,2,1:T(4,128)S(1)}, u32[]{:S(2)}, u32[]{:S(2)}) collective-permute-start(f32[4,4,16,128]{3,0,2,1:T(4,128)S(1)} %get-tuple-element.44), channel_id=1, source_target_pairs={{0,24},{8,0},{16,8},{24,16},{1,25},{9,1},{17,9},{25,17},{2,26},{10... | collective-permute-start | bytes 393224 | tf_op jit(solution)/shard_map/ppermute | solution.py:58
  25.5 2.6 %collective-permute-done.4 = f32[4,4,16,128]{3,0,2,1:T(4,128)S(1)} collective-permute-done((f32[4,4,16,128]{3,0,2,1:T(4,128)S(1)}, f32[4,4,16,128]{3,0,2,1:T(4,128)S(1)}, u32[]{:S(2)}, u32[]{:S(2)}) %collective-permute-start.4) | collective-permute-done | bytes 131104 | tf_op jit(solution)/shard_map/ppermute | solution.py:58
  28.1 0.7 collective-permute-done.5
  28.8 0.2 pad_maximum_fusion.6
  28.9 0.9 %collective-permute-start.6 = (f32[4,24,4,128]{3,0,2,1:T(4,128)S(1)}, f32[4,24,4,128]{3,0,2,1:T(4,128)S(1)}, u32[]{:S(2)}, u32[]{:S(2)}) collective-permute-start(f32[4,24,4,128]{3,0,2,1:T(4,128)S(1)} %get-tuple-element.41), channel_id=1, source_target_pairs={{0,1},{1,2},{2,3},{3,4},{4,5},{5,6},{6,7},{7,0},{8,9},{9,10},{10,1... | collective-permute-start | bytes 589832 | tf_op jit(solution)/shard_map/ppermute | solution.py:58
  29.8 4.1 %collective-permute-start.7 = (f32[4,24,4,128]{3,0,2,1:T(4,128)S(1)}, f32[4,24,4,128]{3,0,2,1:T(4,128)S(1)}, u32[]{:S(2)}, u32[]{:S(2)}) collective-permute-start(f32[4,24,4,128]{3,0,2,1:T(4,128)S(1)} %get-tuple-element.42), channel_id=1, source_target_pairs={{0,7},{1,0},{2,1},{3,2},{4,3},{5,4},{6,5},{7,6},{8,15},{9,8},{10,9... | collective-permute-start | bytes 589832 | tf_op jit(solution)/shard_map/ppermute | solution.py:58
  34.0 5.3 %collective-permute-done.6 = f32[4,24,4,128]{3,0,2,1:T(4,128)S(1)} collective-permute-done((f32[4,24,4,128]{3,0,2,1:T(4,128)S(1)}, f32[4,24,4,128]{3,0,2,1:T(4,128)S(1)}, u32[]{:S(2)}, u32[]{:S(2)}) %collective-permute-start.6) | collective-permute-done | bytes 196640 | tf_op jit(solution)/shard_map/ppermute | solution.py:58
  39.3 2.7 %collective-permute-done.7 = f32[4,24,4,128]{3,0,2,1:T(4,128)S(1)} collective-permute-done((f32[4,24,4,128]{3,0,2,1:T(4,128)S(1)}, f32[4,24,4,128]{3,0,2,1:T(4,128)S(1)}, u32[]{:S(2)}, u32[]{:S(2)}) %collective-permute-start.7) | collective-permute-done | bytes 196640 | tf_op jit(solution)/shard_map/ppermute | solution.py:58
  42.1 0.4 pad_maximum_fusion.2
  42.5 0.9 %fusion.75 = (f32[1,24,24,128]{3,0,2,1:T(1,128)S(1)}, f32[1,24,24,128]{3,0,2,1:T(1,128)S(1)}, f32[1,24,24,128]{3,0,2,1:T(1,128)S(1)}, f32[1,24,24,128]{3,0,2,1:T(1,128)S(1)}) fusion(f32[4,24,24,128]{3,0,2,1:T(4,128)S(1)} %pad_maximum_fusion.2), kind=kLoop, calls=%fused_computation.176 | loop fusion | bytes 2359296 | tf_op jit(solution)/shard_map/slice | solution.py:161
  43.4 0.1 broadcast_multiply_fusion
  43.6 0.2 convert_add_fusion
  43.8 0.2 fusion.46
  44.5 0.2 compare_convert_fusion
  44.7 0.8 fusion.71
  45.5 2.1 %fusion.4 = f32[8,22,22,128]{3,2,1,0:T(8,128)S(1)} fusion(f32[8,24,24,128]{3,2,1,0:T(8,128)S(1)} %compare_convert_fusion, f32[8,22,22,127]{3,2,1,0:T(8,128)S(1)} %get-tuple-element.24, f32[8,22,22,127]{3,2,1,0:T(8,128)S(1)} %get-tuple-element.23, f32[22,22,128]{2,1,0:T(8,128)S(1)} %get-tuple-element.53, f32[22,22,128]{2,1,0:T(8,128)S(1)} %get-tuple-element.54, ...), kind=kLoop, calls=%fused_computation.9 | loop fusion | flops 6938624 | bytes 17563392 | tf_op jit(solution)/shard_map/sub | solution.py:172
  47.6 0.7 fusion.72
  48.3 1.8 %fusion.10 = f32[8,20,20,128]{3,2,1,0:T(8,128)S(1)} fusion(f32[8,22,22,128]{3,2,1,0:T(8,128)S(1)} %fusion.4, f32[8,20,20,127]{3,2,1,0:T(8,128)S(1)} %get-tuple-element.26, f32[8,20,20,127]{3,2,1,0:T(8,128)S(1)} %get-tuple-element.25, f32[20,20,128]{2,1,0:T(8,128)S(1)} %slice.446, f32[20,20,128]{2,1,0:T(8,128)S(1)} %slice.444, f32[20,20,128]{2,1,0:T(8,128)S(1)} %slice.442, ...), kind=kLoop, calls=%fused_computation.19 | loop fusion | flops 5324800 | bytes 14515200 | tf_op jit(solution)/shard_map/sub | solution.py:113
  50.1 0.0 copy-start
  50.2 0.6 fusion.73
  50.8 1.4 %fusion.16 = f32[8,18,18,128]{3,2,1,0:T(8,128)S(1)} fusion(f32[8,20,20,128]{3,2,1,0:T(8,128)S(1)} %fusion.10, f32[8,18,18,127]{3,2,1,0:T(8,128)S(1)} %get-tuple-element.28, f32[8,18,18,127]{3,2,1,0:T(8,128)S(1)} %get-tuple-element.27, f32[18,18,128]{2,1,0:T(8,128)S(1)} %slice.461, f32[18,18,128]{2,1,0:T(8,128)S(1)} %slice.459, ...), kind=kLoop, calls=%fused_computation.30 | loop fusion | flops 4313088 | bytes 11757312 | tf_op jit(solution)/shard_map/sub | solution.py:113
  52.3 0.4 fusion.74
  52.6 0.8 %copy-done.1 = f32[8,18,18,128]{3,2,1,0:T(8,128)} copy-done((f32[8,18,18,128]{3,2,1,0:T(8,128)}, f32[8,18,18,128]{3,2,1,0:T(8,128)S(1)}, u32[]{:S(2)}) %copy-start.1) | copy-done | bytes 1327128
  53.5 2.3 %multiply_reduce_fusion.5 = (f32[8]{0:T(128)S(1)}, f32[8]{0:T(128)S(1)}, f32[8]{0:T(128)S(1)}, f32[8]{0:T(128)S(1)}, f32[8]{0:T(128)S(1)}, /*index=5*/f32[8]{0:T...) fusion(f32[8,22,22,128]{3,2,1,0:T(8,128)S(1)} %fusion.4, f32[8,20,20,128]{3,2,1,0:T(8,128)S(1)} %fusion.10, ...), kind=kLoop, calls=%fused_computation.80 | loop fusion | flops 8126392 | bytes 10338592 | tf_op jit(solution)/shard_map/reduce_sum | solution.py:130
  55.8 0.2 collective-permute-start.8
  56.0 1.1 %collective-permute-done.8 = f32[9,8]{1,0:T(8,128)S(1)} collective-permute-done((f32[9,8]{1,0:T(8,128)S(1)}, f32[9,8]{1,0:T(8,128)S(1)}, u32[]{:S(2)}, u32[]{:S(2)}) %collective-permute-start.8) | collective-permute-done | bytes 320 | tf_op jit(solution)/shard_map/ppermute | solution.py:124
  57.0 1.1 %collective-permute-start.9 = (f32[9,8]{1,0:T(8,128)S(1)}, f32[9,8]{1,0:T(8,128)S(1)}, u32[]{:S(2)}, u32[]{:S(2)}) collective-permute-start(f32[9,8]{1,0:T(8,128)S(1)} %add.588), channel_id=1, source_target_pairs={{0,16},{8,24},{16,0},{24,8},{1,17},{9,25},{17,1},{25,9},{2,18},{10... | collective-permute-start | bytes 872 | tf_op jit(solution)/shard_map/ppermute | solution.py:124
  58.1 2.6 %collective-permute-done.9 = f32[9,8]{1,0:T(8,128)S(1)} collective-permute-done((f32[9,8]{1,0:T(8,128)S(1)}, f32[9,8]{1,0:T(8,128)S(1)}, u32[]{:S(2)}, u32[]{:S(2)}) %collective-permute-start.9) | collective-permute-done | bytes 320 | tf_op jit(solution)/shard_map/ppermute | solution.py:124
  60.7 0.0 collective-permute-start.10
  60.7 3.6 %collective-permute-done.10 = f32[9,8]{1,0:T(8,128)S(1)} collective-permute-done((f32[9,8]{1,0:T(8,128)S(1)}, f32[9,8]{1,0:T(8,128)S(1)}, u32[]{:S(2)}, u32[]{:S(2)}) %collective-permute-start.10) | collective-permute-done | bytes 320 | tf_op jit(solution)/shard_map/ppermute | solution.py:124
  64.4 0.6 collective-permute-start.11
  64.9 3.1 %collective-permute-done.11 = f32[9,8]{1,0:T(8,128)S(1)} collective-permute-done((f32[9,8]{1,0:T(8,128)S(1)}, f32[9,8]{1,0:T(8,128)S(1)}, u32[]{:S(2)}, u32[]{:S(2)}) %collective-permute-start.11) | collective-permute-done | bytes 320 | tf_op jit(solution)/shard_map/ppermute | solution.py:124
  68.0 1.6 %collective-permute-start.12 = (f32[9,8]{1,0:T(8,128)S(1)}, f32[9,8]{1,0:T(8,128)S(1)}, u32[]{:S(2)}, u32[]{:S(2)}) collective-permute-start(f32[9,8]{1,0:T(8,128)S(1)} %add.591), channel_id=1, source_target_pairs={{0,4},{1,5},{2,6},{3,7},{4,0},{5,1},{6,2},{7,3},{8,12},{9,13},{10,... | collective-permute-start | bytes 872 | tf_op jit(solution)/shard_map/ppermute | solution.py:124
  69.6 0.8 %copy.23 = f32[3,16,16,128]{3,2,1,0:T(8,128)} copy(f32[3,16,16,128]{3,0,2,1:T(4,128)S(1)} %fusion.34) | data formatting | bytes 786432
  70.4 2.3 %collective-permute-done.12 = f32[9,8]{1,0:T(8,128)S(1)} collective-permute-done((f32[9,8]{1,0:T(8,128)S(1)}, f32[9,8]{1,0:T(8,128)S(1)}, u32[]{:S(2)}, u32[]{:S(2)}) %collective-permute-start.12) | collective-permute-done | bytes 320 | tf_op jit(solution)/shard_map/ppermute | solution.py:124
  72.7 3.4 %multiply_add_fusion = f32[8,16,16,128]{3,2,1,0:T(8,128)} fusion(f32[8,20,20,128]{3,2,1,0:T(8,128)} %copy-done, f32[8,22,22,128]{3,2,1,0:T(8,128)S(1)} %fusion.4, f32[8,18,18,128]{3,2,1,0:T(8,128)} %copy-done.1, f32[8]{0:T(128)S(1)} %get-tuple-element.65, f32[8]{0:T(128)S(1)} %get-tuple-element.64, f32[8]{0:T(128)S(1)} %get-tuple-element.13, ...), kind=kLoop, calls=%fused_computation.74 | loop fusion | flops 2097152 | bytes 4325504 | tf_op jit(solution)/shard_map/add | solution.py:236
  (51 shorter events, 0.8 us)
Async XLA Ops:
  0.6 9.7 %copy-start.3 = (bf16[3,16,3,3,3]{1,4,3,2,0:T(4,128)(2,1)S(1)}, bf16[3,16,3,3,3]{1,4,3,2,0:T(4,128)(2,1)}, u32[]{:S(2)}) copy-start(bf16[3,16,3,3,3]{1,4,3,2,0:T(4,128)(2,1)} %param.5) | copy-start | bytes 7780
  0.6 9.8 %copy-start.2 = (s32[16,16,128]{2,1,0:T(8,128)S(1)}, s32[16,16,128]{2,1,0:T(8,128)}, u32[]{:S(2)}) copy-start(s32[16,16,128]{2,1,0:T(8,128)} %param.7) | copy-start | bytes 393220
  2.6 4.9 %collective-permute-start.1 = (bf16[16,1,16,128]{3,0,2,1:T(8,128)(2,1)S(1)}, bf16[16,1,16,128]{3,0,2,1:T(8,128)(2,1)S(1)}, u32[]{:S(2)}, u32[]{:S(2)}) collective-permute-start(bf16[16,1,16,128]{3,0,2,1:T(8,128)(2,1)S(1)} %get-tuple-element.40), channel_id=1, source_target_pairs={{0,24},{8,0},{16,8},{24,16},{1,25},{9,1},{17,9},{25,17},{2,26},{10... | collective-permute-start | bytes 196616 | tf_op jit(solution)/shard_map/ppermute | solution.py:58
  5.1 3.7 %collective-permute-start = (bf16[16,1,16,128]{3,0,2,1:T(8,128)(2,1)S(1)}, bf16[16,1,16,128]{3,0,2,1:T(8,128)(2,1)S(1)}, u32[]{:S(2)}, u32[]{:S(2)}) collective-permute-start(bf16[16,1,16,128]{3,0,2,1:T(8,128)(2,1)S(1)} %get-tuple-element.39), channel_id=1, source_target_pairs={{0,8},{8,16},{16,24},{24,0},{1,9},{9,17},{17,25},{25,1},{2,10},{10... | collective-permute-start | bytes 196616 | tf_op jit(solution)/shard_map/ppermute | solution.py:58
  8.8 7.1 %collective-permute-start.2 = (bf16[16,18,1,128]{3,0,2,1:T(8,128)(2,1)S(1)}, bf16[16,18,1,128]{3,0,2,1:T(8,128)(2,1)S(1)}, u32[]{:S(2)}, u32[]{:S(2)}) collective-permute-start(bf16[16,18,1,128]{3,0,2,1:T(8,128)(2,1)S(1)} %get-tuple-element.37), channel_id=1, source_target_pairs={{0,1},{1,2},{2,3},{3,4},{4,5},{5,6},{6,7},{7,0},{8,9},{9,10},{10,1... | collective-permute-start | bytes 221192 | tf_op jit(solution)/shard_map/ppermute | solution.py:58
  10.4 5.5 %collective-permute-start.3 = (bf16[16,18,1,128]{3,0,2,1:T(8,128)(2,1)S(1)}, bf16[16,18,1,128]{3,0,2,1:T(8,128)(2,1)S(1)}, u32[]{:S(2)}, u32[]{:S(2)}) collective-permute-start(bf16[16,18,1,128]{3,0,2,1:T(8,128)(2,1)S(1)} %get-tuple-element.38), channel_id=1, source_target_pairs={{0,7},{1,0},{2,1},{3,2},{4,3},{5,4},{6,5},{7,6},{8,15},{9,8},{10,9... | collective-permute-start | bytes 221192 | tf_op jit(solution)/shard_map/ppermute | solution.py:58
  21.4 0.7 copy-start.4
  23.6 4.4 %collective-permute-start.4 = (f32[4,4,16,128]{3,0,2,1:T(4,128)S(1)}, f32[4,4,16,128]{3,0,2,1:T(4,128)S(1)}, u32[]{:S(2)}, u32[]{:S(2)}) collective-permute-start(f32[4,4,16,128]{3,0,2,1:T(4,128)S(1)} %get-tuple-element.43), channel_id=1, source_target_pairs={{0,8},{8,16},{16,24},{24,0},{1,9},{9,17},{17,25},{25,1},{2,10},{10... | collective-permute-start | bytes 393224 | tf_op jit(solution)/shard_map/ppermute | solution.py:58
  23.7 5.0 %collective-permute-start.5 = (f32[4,4,16,128]{3,0,2,1:T(4,128)S(1)}, f32[4,4,16,128]{3,0,2,1:T(4,128)S(1)}, u32[]{:S(2)}, u32[]{:S(2)}) collective-permute-start(f32[4,4,16,128]{3,0,2,1:T(4,128)S(1)} %get-tuple-element.44), channel_id=1, source_target_pairs={{0,24},{8,0},{16,8},{24,16},{1,25},{9,1},{17,9},{25,17},{2,26},{10... | collective-permute-start | bytes 393224 | tf_op jit(solution)/shard_map/ppermute | solution.py:58
  28.9 10.3 %collective-permute-start.6 = (f32[4,24,4,128]{3,0,2,1:T(4,128)S(1)}, f32[4,24,4,128]{3,0,2,1:T(4,128)S(1)}, u32[]{:S(2)}, u32[]{:S(2)}) collective-permute-start(f32[4,24,4,128]{3,0,2,1:T(4,128)S(1)} %get-tuple-element.41), channel_id=1, source_target_pairs={{0,1},{1,2},{2,3},{3,4},{4,5},{5,6},{6,7},{7,0},{8,9},{9,10},{10,1... | collective-permute-start | bytes 589832 | tf_op jit(solution)/shard_map/ppermute | solution.py:58
  29.8 12.2 %collective-permute-start.7 = (f32[4,24,4,128]{3,0,2,1:T(4,128)S(1)}, f32[4,24,4,128]{3,0,2,1:T(4,128)S(1)}, u32[]{:S(2)}, u32[]{:S(2)}) collective-permute-start(f32[4,24,4,128]{3,0,2,1:T(4,128)S(1)} %get-tuple-element.42), channel_id=1, source_target_pairs={{0,7},{1,0},{2,1},{3,2},{4,3},{5,4},{6,5},{7,6},{8,15},{9,8},{10,9... | collective-permute-start | bytes 589832 | tf_op jit(solution)/shard_map/ppermute | solution.py:58
  50.1 2.5 %copy-start = (f32[8,20,20,128]{3,2,1,0:T(8,128)}, f32[8,20,20,128]{3,2,1,0:T(8,128)S(1)}, u32[]{:S(2)}) copy-start(f32[8,20,20,128]{3,2,1,0:T(8,128)S(1)} %fusion.10) | copy-start | bytes 4915204
  52.2 1.2 %copy-start.1 = (f32[8,18,18,128]{3,2,1,0:T(8,128)}, f32[8,18,18,128]{3,2,1,0:T(8,128)S(1)}, u32[]{:S(2)}) copy-start(f32[8,18,18,128]{3,2,1,0:T(8,128)S(1)} %fusion.16) | copy-start | bytes 3981316
  55.8 1.2 %collective-permute-start.8 = (f32[9,8]{1,0:T(8,128)S(1)}, f32[9,8]{1,0:T(8,128)S(1)}, u32[]{:S(2)}, u32[]{:S(2)}) collective-permute-start(f32[9,8]{1,0:T(8,128)S(1)} %stack.55), channel_id=1, source_target_pairs={{0,8},{8,0},{16,24},{24,16},{1,9},{9,1},{17,25},{25,17},{2,10},{10... | collective-permute-start | bytes 872 | tf_op jit(solution)/shard_map/ppermute | solution.py:124
  57.0 3.7 %collective-permute-start.9 = (f32[9,8]{1,0:T(8,128)S(1)}, f32[9,8]{1,0:T(8,128)S(1)}, u32[]{:S(2)}, u32[]{:S(2)}) collective-permute-start(f32[9,8]{1,0:T(8,128)S(1)} %add.588), channel_id=1, source_target_pairs={{0,16},{8,24},{16,0},{24,8},{1,17},{9,25},{17,1},{25,9},{2,18},{10... | collective-permute-start | bytes 872 | tf_op jit(solution)/shard_map/ppermute | solution.py:124
  60.7 3.7 %collective-permute-start.10 = (f32[9,8]{1,0:T(8,128)S(1)}, f32[9,8]{1,0:T(8,128)S(1)}, u32[]{:S(2)}, u32[]{:S(2)}) collective-permute-start(f32[9,8]{1,0:T(8,128)S(1)} %add.589), channel_id=1, source_target_pairs={{0,1},{1,0},{2,3},{3,2},{4,5},{5,4},{6,7},{7,6},{8,9},{9,8},{10,11... | collective-permute-start | bytes 872 | tf_op jit(solution)/shard_map/ppermute | solution.py:124
  64.4 3.7 %collective-permute-start.11 = (f32[9,8]{1,0:T(8,128)S(1)}, f32[9,8]{1,0:T(8,128)S(1)}, u32[]{:S(2)}, u32[]{:S(2)}) collective-permute-start(f32[9,8]{1,0:T(8,128)S(1)} %add.590), channel_id=1, source_target_pairs={{0,2},{1,3},{2,0},{3,1},{4,6},{5,7},{6,4},{7,5},{8,10},{9,11},{10,... | collective-permute-start | bytes 872 | tf_op jit(solution)/shard_map/ppermute | solution.py:124
  68.0 4.6 %collective-permute-start.12 = (f32[9,8]{1,0:T(8,128)S(1)}, f32[9,8]{1,0:T(8,128)S(1)}, u32[]{:S(2)}, u32[]{:S(2)}) collective-permute-start(f32[9,8]{1,0:T(8,128)S(1)} %add.591), channel_id=1, source_target_pairs={{0,4},{1,5},{2,6},{3,7},{4,0},{5,1},{6,2},{7,3},{8,12},{9,13},{10,... | collective-permute-start | bytes 872 | tf_op jit(solution)/shard_map/ppermute | solution.py:124

commit v10 on v9

--- a/solution.py
+++ b/solution.py
@@ -167,73 +167,83 @@
     grid_seed = (grid_labels[None] == colours).astype(jnp.float32)
     seed_field = (labels[None] == jnp.arange(1, FIELDS + 1, dtype=jnp.int32)[:, None, None, None]).astype(jnp.float32)
 
-    inside = grid_seed[:, 1:-1, 1:-1]
     cells = operator_cells(grid)
-    current = inside - operate_inside(grid_seed, cells, 1)
-    basis = [current]
-    for power in range(ITERS):
-        current = operate_inside(current, cells, power + 2)
-        basis.append(current)
-    basis = [
-        vector[:, (vector.shape[1] - depth_cells) // 2 : (vector.shape[1] + depth_cells) // 2,
-               (vector.shape[2] - row_cells) // 2 : (vector.shape[2] + row_cells) // 2]
-        for vector in basis
-    ]
-    size = ITERS + 1
-    pairs = [(i, j) for i in range(size) for j in range(i, size) if i < size - 1]
-    local = jnp.stack([field_sums(basis[i], basis[j]) for i, j in pairs])
-    total = all_sum(local, ("gz", "yx"))
-    gram = {}
-    for index, (i, j) in enumerate(pairs):
-        gram[i, j] = total[index]
-        gram[j, i] = total[index]
-
-    zero = jnp.zeros((FIELDS,), jnp.float32)
-    one = jnp.ones((FIELDS,), jnp.float32)
-
-    def inner(left, right):
-        acc = zero
-        for i in range(size):
-            for j in range(size):
-                if (i, j) in gram and not (
-                    isinstance(left[i], float) or isinstance(right[j], float)
-                ):
-                    acc = acc + left[i] * gram[i, j] * right[j]
-        return acc
-
-    def shift(coeffs):
-        return [0.0] + coeffs[:-1]
-
-    def axpy(scale, left, right):
-        out = []
-        for a, b in zip(left, right):
-            if isinstance(b, float):
-                out.append(a)
-            elif isinstance(a, float):
-                out.append(scale * b)
-            else:
-                out.append(a + scale * b)
-        return out
-
-    residual = [one] + [0.0] * (size - 1)
-    direction = list(residual)
-    solution = [0.0] * size
-    norm_now = inner(residual, residual)
-    for iteration in range(ITERS):
-        applied = shift(direction)
-        step_size = norm_now / inner(direction, applied)
-        solution = axpy(step_size, solution, direction)
-        if iteration == ITERS - 1:
-            break
-        residual = axpy(-step_size, residual, applied)
-        norm_next = inner(residual, residual)
-        direction = axpy(norm_next / norm_now, residual, direction)
-        norm_now = norm_next
-
-    probabilities = seed_field
-    for coeff, vector in zip(solution, basis):
-        if not isinstance(coeff, float):
-            probabilities = probabilities + coeff[:, None, None, None] * vector
+
+    def solve(grid_seed, seed_field):
+        count = seed_field.shape[0]
+        inside = grid_seed[:, 1:-1, 1:-1]
+        current = inside - operate_inside(grid_seed, cells, 1)
+        basis = [current]
+        for power in range(ITERS):
+            current = operate_inside(current, cells, power + 2)
+            basis.append(current)
+        basis = [
+            vector[:, (vector.shape[1] - depth_cells) // 2 : (vector.shape[1] + depth_cells) // 2,
+                   (vector.shape[2] - row_cells) // 2 : (vector.shape[2] + row_cells) // 2]
+            for vector in basis
+        ]
+        size = ITERS + 1
+        pairs = [(i, j) for i in range(size) for j in range(i, size) if i < size - 1]
+        local = jnp.stack([field_sums(basis[i], basis[j]) for i, j in pairs])
+        total = all_sum(local, ("gz", "yx"))
+        gram = {}
+        for index, (i, j) in enumerate(pairs):
+            gram[i, j] = total[index]
+            gram[j, i] = total[index]
+
+        zero = jnp.zeros((count,), jnp.float32)
+        one = jnp.ones((count,), jnp.float32)
+
+        def inner(left, right):
+            acc = zero
+            for i in range(size):
+                for j in range(size):
+                    if (i, j) in gram and not (
+                        isinstance(left[i], float) or isinstance(right[j], float)
+                    ):
+                        acc = acc + left[i] * gram[i, j] * right[j]
+            return acc
+
+        def shift(coeffs):
+            return [0.0] + coeffs[:-1]
+
+        def axpy(scale, left, right):
+            out = []
+            for a, b in zip(left, right):
+                if isinstance(b, float):
+                    out.append(a)
+                elif isinstance(a, float):
+                    out.append(scale * b)
+                else:
+                    out.append(a + scale * b)
+            return out
+
+        residual = [one] + [0.0] * (size - 1)
+        direction = list(residual)
+        solution = [0.0] * size
+        norm_now = inner(residual, residual)
+        for iteration in range(ITERS):
+            applied = shift(direction)
+            step_size = norm_now / inner(direction, applied)
+            solution = axpy(step_size, solution, direction)
+            if iteration == ITERS - 1:
+                break
+            residual = axpy(-step_size, residual, applied)
+            norm_next = inner(residual, residual)
+            direction = axpy(norm_next / norm_now, residual, direction)
+            norm_now = norm_next
+
+        probabilities = seed_field
+        for coeff, vector in zip(solution, basis):
+            if not isinstance(coeff, float):
+                probabilities = probabilities + coeff[:, None, None, None] * vector
+        return probabilities
+
+    half = FIELDS // 2
+    probabilities = jnp.concatenate(
+        [solve(grid_seed[:half], seed_field[:half]), solve(grid_seed[half:], seed_field[half:])],
+        axis=0,
+    )
     return (probabilities, affinities)
 
 

time: 76.3 us -> 86.2 us (1.13)
  local copies, waits for them, and re-layouts: 8.18 us -> 15.1 us
  starting transfers between devices: 17.5 us -> 20.2 us
  waiting for transfers between devices: 29.9 us -> 27.2 us
  other arithmetic: 13.3 us -> 15.4 us
    unnamed x12 -> x116, local copies, waits for them, and re-layouts: 3.64 us -> 6.8 us
    ppermute x5 -> x10, starting transfers between devices: 3.36 us -> 6.34 us  [all_sum(): lax.ppermute(value, axis, [(i, i ^ hop) for i in range(devices)])]
    ppermute x5 -> x10, waiting for transfers between devices: 12.7 us -> 10.2 us  [all_sum(): lax.ppermute(value, axis, [(i, i ^ hop) for i in range(devices)])]
    another operation x1 -> x20, local copies, waits for them, and re-layouts: 0.04 us -> 1.86 us  [solve(): local = jnp.stack([field_sums(basis[i], basis[j]) for i, j in pairs])]
    sub x1 -> x2, other arithmetic: 2.1 us -> 3.7 us  [solve(): current = inside - operate_inside(grid_seed, cells, 1)]
    slice x4 -> x7, local copies, waits for them, and re-layouts: 2.47 us -> 3.77 us  [operate_inside(): centre[..., 1:]]
    convert_element_type x0 -> x1, other arithmetic: none -> 1.12 us  [body(): (labels[None] == jnp.arange(1, FIELDS + 1, dtype=jnp.int32)[:, None, None...]
    concatenate x0 -> x1, other arithmetic: none -> 1.04 us  [body(): jnp.concatenate([solve(grid_seed[:half], seed_field[:half]), solve(grid_s...]
  transfers between devices with their start and end apart: 13 -> 18, of which waited for: 12 -> 15; matrix products, arithmetic and copies ran while one was open for 1% -> 11% of each run, Pallas kernels for 0% -> 0%
where the time goes in v10:
time: 86.2 us; the launch traced here: 85.9 us
  waiting for transfers between devices  27.2 us (32%)
  starting transfers between devices  20.2 us (23%)
  other arithmetic  15.4 us (18%)
  local copies, waits for them, and re-layouts  15.1 us (18%)
  matrix products  6.15 us (7%)
  between operations  1.82 us (2%)
    ppermute x8, waiting for transfers between devices, from_ring(): lax.ppermute(value, axis, [(i, (i + by) % devices) for i in range(devices)])  17 us
    ppermute x8, starting transfers between devices, from_ring(): lax.ppermute(value, axis, [(i, (i + by) % devices) for i in range(devices)])  13.8 us
    ppermute x10, waiting for transfers between devices, all_sum(): lax.ppermute(value, axis, [(i, i ^ hop) for i in range(devices)])  10.2 us
    unnamed x116, local copies, waits for them, and re-layouts  6.8 us
    ppermute x10, starting transfers between devices, all_sum(): lax.ppermute(value, axis, [(i, i ^ hop) for i in range(devices)])  6.34 us
    dot_general x9, matrix products, conv_region(): jnp.einsum('oce,cezyx->ozyx', conv_weight[:, :, offset_z, offset_y, :], w...  6.15 us
    slice x7, local copies, waits for them, and re-layouts, operate_inside(): centre[..., 1:]  3.77 us
    sub x2, other arithmetic, solve(): current = inside - operate_inside(grid_seed, cells, 1)  3.7 us
  transfers between devices with their start and end apart: 18, of which 15 were waited for; matrix products, arithmetic and copies ran while one was open for 11% of the time, Pallas kernels for 0%

profile of v10, /device:TPU:0, one launch (start us, length us, event | category | flops | bytes accessed | tf_op | source)
XLA Modules:
  0.0 85.9 jit_solution(331986270199548912)
XLA Ops:
  0.6 1.9 %copy.60 = bf16[16,16,16,128]{3,0,2,1:T(8,128)(2,1)S(1)} copy(bf16[16,16,16,128]{3,2,1,0:T(8,128)(2,1)} %param.4) | data formatting | bytes 2097152 | tf_op args[0]
  2.6 2.5 %collective-permute-start.1 = (bf16[16,1,16,128]{3,0,2,1:T(8,128)(2,1)S(1)}, bf16[16,1,16,128]{3,0,2,1:T(8,128)(2,1)S(1)}, u32[]{:S(2)}, u32[]{:S(2)}) collective-permute-start(bf16[16,1,16,128]{3,0,2,1:T(8,128)(2,1)S(1)} %get-tuple-element.81), channel_id=1, source_target_pairs={{0,24},{8,0},{16,8},{24,16},{1,25},{9,1},{17,9},{25,17},{2,26},{10... | collective-permute-start | bytes 196616 | tf_op jit(solution)/shard_map/ppermute | solution.py:58
  5.2 2.3 %collective-permute-done.1 = bf16[16,1,16,128]{3,0,2,1:T(8,128)(2,1)S(1)} collective-permute-done((bf16[16,1,16,128]{3,0,2,1:T(8,128)(2,1)S(1)}, bf16[16,1,16,128]{3,0,2,1:T(8,128)(2,1)S(1)}, u32[]{:S(2)}, u32[]{:S(2)}) %collective-permute-start.1) | collective-permute-done | bytes 65568 | tf_op jit(solution)/shard_map/ppermute | solution.py:58
  7.5 1.2 %collective-permute-done = bf16[16,1,16,128]{3,0,2,1:T(8,128)(2,1)S(1)} collective-permute-done((bf16[16,1,16,128]{3,0,2,1:T(8,128)(2,1)S(1)}, bf16[16,1,16,128]{3,0,2,1:T(8,128)(2,1)S(1)}, u32[]{:S(2)}, u32[]{:S(2)}) %collective-permute-start) | collective-permute-done | bytes 65568 | tf_op jit(solution)/shard_map/ppermute | solution.py:58
  8.8 1.6 %collective-permute-start.2 = (bf16[16,18,1,128]{3,0,2,1:T(8,128)(2,1)S(1)}, bf16[16,18,1,128]{3,0,2,1:T(8,128)(2,1)S(1)}, u32[]{:S(2)}, u32[]{:S(2)}) collective-permute-start(bf16[16,18,1,128]{3,0,2,1:T(8,128)(2,1)S(1)} %get-tuple-element.72), channel_id=1, source_target_pairs={{0,1},{1,2},{2,3},{3,4},{4,5},{5,6},{6,7},{7,0},{8,9},{9,10},{10,1... | collective-permute-start | bytes 221192 | tf_op jit(solution)/shard_map/ppermute | solution.py:58
  10.4 3.2 %collective-permute-start.3 = (bf16[16,18,1,128]{3,0,2,1:T(8,128)(2,1)S(1)}, bf16[16,18,1,128]{3,0,2,1:T(8,128)(2,1)S(1)}, u32[]{:S(2)}, u32[]{:S(2)}) collective-permute-start(bf16[16,18,1,128]{3,0,2,1:T(8,128)(2,1)S(1)} %get-tuple-element.73), channel_id=1, source_target_pairs={{0,7},{1,0},{2,1},{3,2},{4,3},{5,4},{6,5},{7,6},{8,15},{9,8},{10,9... | collective-permute-start | bytes 221192 | tf_op jit(solution)/shard_map/ppermute | solution.py:58
  13.6 2.3 %collective-permute-done.2 = bf16[16,18,1,128]{3,0,2,1:T(8,128)(2,1)S(1)} collective-permute-done((bf16[16,18,1,128]{3,0,2,1:T(8,128)(2,1)S(1)}, bf16[16,18,1,128]{3,0,2,1:T(8,128)(2,1)S(1)}, u32[]{:S(2)}, u32[]{:S(2)}) %collective-permute-start.2) | collective-permute-done | bytes 73760 | tf_op jit(solution)/shard_map/ppermute | solution.py:58
  16.0 0.3 pad_maximum_fusion.1
  16.2 0.3 fusion.119
  16.5 0.8 fusion
  17.2 0.6 convolution_bitcast_fusion.7
  17.8 0.6 convolution_bitcast_fusion.6
  18.4 0.6 convolution_bitcast_fusion.5
  19.0 0.6 convolution_bitcast_fusion.4
  19.6 0.6 convolution_bitcast_fusion.3
  20.2 0.6 convolution_bitcast_fusion.2
  20.8 0.6 convolution_bitcast_fusion.1
  21.4 0.6 convolution_bitcast_fusion
  22.0 1.5 %fusion.15 = f32[3,16,16,128]{3,0,2,1:T(4,128)S(1)} fusion(f32[16,16,128,3]{2,3,1,0:T(4,128)S(1)} %convolution_bitcast_fusion, f32[16,16,128,3]{2,3,1,0:T(4,128)S(1)} %convolution_bitcast_fusion.1, f32[16,16,128,3]{2,3,1,0:T(4,128)S(1)} %convolution_bitcast_fusion.2, f32[16,16,128,3]{2,3,1,0:T(4,128)S(1)} %convolution_bitcast_fusion.3, ...), kind=kOutput, calls=%fused_computation.30 | convolution fusion | flops 22560768 | bytes 7520556 | tf_op jit(solution)/shard_map/oce,cezyx->ozyx/dot_general | solution.py:47
  23.7 1.8 %collective-permute-start.5 = (f32[4,4,16,128]{3,0,2,1:T(4,128)S(1)}, f32[4,4,16,128]{3,0,2,1:T(4,128)S(1)}, u32[]{:S(2)}, u32[]{:S(2)}) collective-permute-start(f32[4,4,16,128]{3,0,2,1:T(4,128)S(1)} %get-tuple-element.93), channel_id=1, source_target_pairs={{0,24},{8,0},{16,8},{24,16},{1,25},{9,1},{17,9},{25,17},{2,26},{10... | collective-permute-start | bytes 393224 | tf_op jit(solution)/shard_map/ppermute | solution.py:58
  25.5 2.6 %collective-permute-done.4 = f32[4,4,16,128]{3,0,2,1:T(4,128)S(1)} collective-permute-done((f32[4,4,16,128]{3,0,2,1:T(4,128)S(1)}, f32[4,4,16,128]{3,0,2,1:T(4,128)S(1)}, u32[]{:S(2)}, u32[]{:S(2)}) %collective-permute-start.4) | collective-permute-done | bytes 131104 | tf_op jit(solution)/shard_map/ppermute | solution.py:58
  28.1 0.5 collective-permute-done.5
  28.8 0.9 %collective-permute-start.6 = (f32[4,24,4,128]{3,0,2,1:T(4,128)S(1)}, f32[4,24,4,128]{3,0,2,1:T(4,128)S(1)}, u32[]{:S(2)}, u32[]{:S(2)}) collective-permute-start(f32[4,24,4,128]{3,0,2,1:T(4,128)S(1)} %get-tuple-element.86), channel_id=1, source_target_pairs={{0,1},{1,2},{2,3},{3,4},{4,5},{5,6},{6,7},{7,0},{8,9},{9,10},{10,1... | collective-permute-start | bytes 589832 | tf_op jit(solution)/shard_map/ppermute | solution.py:58
  29.7 1.1 %compare_convert_fusion.1 = f32[8,16,16,128]{3,2,1,0:T(8,128)} fusion(s32[16,16,128]{2,1,0:T(8,128)S(1)} %copy-done.54, s32[8]{0:T(128)S(1)} %iota_add_fusion.1), kind=kLoop, calls=%fused_computation.54 | loop fusion | flops 524288 | bytes 1179680 | tf_op jit(solution)/shard_map/convert_element_type | solution.py:168
  30.8 0.8 copy.95
  31.6 3.9 %collective-permute-start.7 = (f32[4,24,4,128]{3,0,2,1:T(4,128)S(1)}, f32[4,24,4,128]{3,0,2,1:T(4,128)S(1)}, u32[]{:S(2)}, u32[]{:S(2)}) collective-permute-start(f32[4,24,4,128]{3,0,2,1:T(4,128)S(1)} %get-tuple-element.87), channel_id=1, source_target_pairs={{0,7},{1,0},{2,1},{3,2},{4,3},{5,4},{6,5},{7,6},{8,15},{9,8},{10,9... | collective-permute-start | bytes 589832 | tf_op jit(solution)/shard_map/ppermute | solution.py:58
  35.5 3.7 %collective-permute-done.6 = f32[4,24,4,128]{3,0,2,1:T(4,128)S(1)} collective-permute-done((f32[4,24,4,128]{3,0,2,1:T(4,128)S(1)}, f32[4,24,4,128]{3,0,2,1:T(4,128)S(1)}, u32[]{:S(2)}, u32[]{:S(2)}) %collective-permute-start.6) | collective-permute-done | bytes 196640 | tf_op jit(solution)/shard_map/ppermute | solution.py:58
  39.2 4.4 %collective-permute-done.7 = f32[4,24,4,128]{3,0,2,1:T(4,128)S(1)} collective-permute-done((f32[4,24,4,128]{3,0,2,1:T(4,128)S(1)}, f32[4,24,4,128]{3,0,2,1:T(4,128)S(1)}, u32[]{:S(2)}, u32[]{:S(2)}) %collective-permute-start.7) | collective-permute-done | bytes 196640 | tf_op jit(solution)/shard_map/ppermute | solution.py:58
  43.6 0.4 pad_maximum_fusion.2
  44.0 0.9 %fusion.110 = (f32[1,24,24,128]{3,0,2,1:T(1,128)S(1)}, f32[1,24,24,128]{3,0,2,1:T(1,128)S(1)}, f32[1,24,24,128]{3,0,2,1:T(1,128)S(1)}, f32[1,24,24,128]{3,0,2,1:T(1,128)S(1)}) fusion(f32[4,24,24,128]{3,0,2,1:T(4,128)S(1)} %pad_maximum_fusion.2), kind=kLoop, calls=%fused_computation.263 | loop fusion | bytes 2359296 | tf_op jit(solution)/shard_map/slice | solution.py:161
  46.5 2.0 %fusion.109 = (f32[4,22,22,127]{3,2,1,0:T(8,128)}, f32[4,22,22,127]{3,2,1,0:T(8,128)S(1)}, f32[4,22,22,127]{3,2,1,0:T(8,128)S(1)}, f32[4,22,22,127]{3,2,1,0:T(8,128)}) fusion(f32[8,24,24,128]{3,2,1,0:T(8,128)S(1)} %compare_convert_fusion), kind=kLoop, calls=%fused_computation.262 | loop fusion | bytes 7867904 | tf_op jit(solution)/shard_map/slice | solution.py:107
  48.6 0.8 fusion.20
  49.4 0.3 fusion.112
  49.8 0.7 fusion.33
  50.6 0.3 fusion.115
  51.0 0.7 fusion.45
  51.9 1.0 %multiply_reduce_fusion.5 = (f32[4]{0:T(128)S(1)}, f32[4]{0:T(128)S(1)}, f32[4]{0:T(128)S(1)}, f32[4]{0:T(128)S(1)}, f32[4]{0:T(128)S(1)}, /*index=5*/f32[4]{0:T...) fusion(f32[4,22,22,128]{3,2,1,0:T(8,128)S(1)} %fusion.20, f32[4,20,20,128]{3,2,1,0:T(8,128)S(1)} %fusion.33, ...), kind=kLoop, calls=%fused_computation.131 | loop fusion | flops 4063196 | bytes 5628048 | tf_op jit(solution)/shard_map/reduce_sum | solution.py:130
  54.0 2.9 %fusion.27 = f32[4,22,22,128]{3,2,1,0:T(8,128)S(1)} fusion(f32[8,24,24,128]{3,2,1,0:T(8,128)S(1)} %compare_convert_fusion, f32[4,22,22,127]{3,2,1,0:T(8,128)} %get-tuple-element.65, f32[4,22,22,127]{3,2,1,0:T(8,128)} %get-tuple-element.62, f32[22,22,128]{2,1,0:T(8,128)} %copy-done.10, f32[22,22,128]{2,1,0:T(8,128)} %copy-done.11, ...), kind=kLoop, calls=%fused_computation.47 | loop fusion | flops 3469312 | bytes 9649024 | tf_op jit(solution)/shard_map/sub | solution.py:175
  57.0 0.4 fusion.111
  57.4 0.8 copy-done.13
  58.8 0.7 fusion.39
  59.7 0.3 fusion.114
  60.0 0.5 copy-done.27
  61.1 0.6 fusion.51
  62.0 0.8 copy-done.41
  63.3 1.0 %multiply_reduce_fusion.14 = (f32[4]{0:T(128)S(1)}, f32[4]{0:T(128)S(1)}, f32[4]{0:T(128)S(1)}, f32[4]{0:T(128)S(1)}, f32[4]{0:T(128)S(1)}, /*index=5*/f32[4]{0:...) fusion(f32[4,22,22,128]{3,2,1,0:T(8,128)S(1)} %fusion.27, f32[4,20,20,128]{3,2,1,0:T(8,128)S(1)} %fusion.39, ...), kind=kLoop, calls=%fused_computation.140 | loop fusion | flops 4063196 | bytes 5628048 | tf_op jit(solution)/shard_map/reduce_sum | solution.py:130
  65.2 0.4 collective-permute-start.8
  65.6 1.1 %collective-permute-start.14 = (f32[9,4]{0,1:T(4,128)S(1)}, f32[9,4]{0,1:T(4,128)S(1)}, u32[]{:S(2)}, u32[]{:S(2)}) collective-permute-start(f32[9,4]{0,1:T(4,128)S(1)} %add.1076), channel_id=1, source_target_pairs={{0,16},{8,24},{16,0},{24,8},{1,17},{9,25},{17,1},{25,9},{2,18},{10... | collective-permute-start | bytes 440 | tf_op jit(solution)/shard_map/ppermute | solution.py:124
  66.7 0.9 %collective-permute-start.9 = (f32[9,4]{0,1:T(4,128)S(1)}, f32[9,4]{0,1:T(4,128)S(1)}, u32[]{:S(2)}, u32[]{:S(2)}) collective-permute-start(f32[9,4]{0,1:T(4,128)S(1)} %add.1021), channel_id=1, source_target_pairs={{0,16},{8,24},{16,0},{24,8},{1,17},{9,25},{17,1},{25,9},{2,18},{10... | collective-permute-start | bytes 440 | tf_op jit(solution)/shard_map/ppermute | solution.py:124
  67.6 1.6 %collective-permute-done.14 = f32[9,4]{0,1:T(4,128)S(1)} collective-permute-done((f32[9,4]{0,1:T(4,128)S(1)}, f32[9,4]{0,1:T(4,128)S(1)}, u32[]{:S(2)}, u32[]{:S(2)}) %collective-permute-start.14) | collective-permute-done | bytes 176 | tf_op jit(solution)/shard_map/ppermute | solution.py:124
  69.2 1.1 %collective-permute-done.9 = f32[9,4]{0,1:T(4,128)S(1)} collective-permute-done((f32[9,4]{0,1:T(4,128)S(1)}, f32[9,4]{0,1:T(4,128)S(1)}, u32[]{:S(2)}, u32[]{:S(2)}) %collective-permute-start.9) | collective-permute-done | bytes 176 | tf_op jit(solution)/shard_map/ppermute | solution.py:124
  70.3 0.9 %collective-permute-start.10 = (f32[9,4]{0,1:T(4,128)S(1)}, f32[9,4]{0,1:T(4,128)S(1)}, u32[]{:S(2)}, u32[]{:S(2)}) collective-permute-start(f32[9,4]{0,1:T(4,128)S(1)} %add.1022), channel_id=1, source_target_pairs={{0,1},{1,0},{2,3},{3,2},{4,5},{5,4},{6,7},{7,6},{8,9},{9,8},{10,11... | collective-permute-start | bytes 440 | tf_op jit(solution)/shard_map/ppermute | solution.py:124
  71.2 1.6 %collective-permute-done.15 = f32[9,4]{0,1:T(4,128)S(1)} collective-permute-done((f32[9,4]{0,1:T(4,128)S(1)}, f32[9,4]{0,1:T(4,128)S(1)}, u32[]{:S(2)}, u32[]{:S(2)}) %collective-permute-start.15) | collective-permute-done | bytes 176 | tf_op jit(solution)/shard_map/ppermute | solution.py:124
  72.8 1.1 %collective-permute-done.10 = f32[9,4]{0,1:T(4,128)S(1)} collective-permute-done((f32[9,4]{0,1:T(4,128)S(1)}, f32[9,4]{0,1:T(4,128)S(1)}, u32[]{:S(2)}, u32[]{:S(2)}) %collective-permute-start.10) | collective-permute-done | bytes 176 | tf_op jit(solution)/shard_map/ppermute | solution.py:124
  73.9 0.9 %collective-permute-start.11 = (f32[9,4]{0,1:T(4,128)S(1)}, f32[9,4]{0,1:T(4,128)S(1)}, u32[]{:S(2)}, u32[]{:S(2)}) collective-permute-start(f32[9,4]{0,1:T(4,128)S(1)} %add.1023), channel_id=1, source_target_pairs={{0,2},{1,3},{2,0},{3,1},{4,6},{5,7},{6,4},{7,5},{8,10},{9,11},{10,... | collective-permute-start | bytes 440 | tf_op jit(solution)/shard_map/ppermute | solution.py:124
  74.8 1.6 %collective-permute-done.16 = f32[9,4]{0,1:T(4,128)S(1)} collective-permute-done((f32[9,4]{0,1:T(4,128)S(1)}, f32[9,4]{0,1:T(4,128)S(1)}, u32[]{:S(2)}, u32[]{:S(2)}) %collective-permute-start.16) | collective-permute-done | bytes 176 | tf_op jit(solution)/shard_map/ppermute | solution.py:124
  76.5 1.0 %collective-permute-done.11 = f32[9,4]{0,1:T(4,128)S(1)} collective-permute-done((f32[9,4]{0,1:T(4,128)S(1)}, f32[9,4]{0,1:T(4,128)S(1)}, u32[]{:S(2)}, u32[]{:S(2)}) %collective-permute-start.11) | collective-permute-done | bytes 176 | tf_op jit(solution)/shard_map/ppermute | solution.py:124
  77.5 1.8 %collective-permute-start.12 = (f32[9,4]{0,1:T(4,128)S(1)}, f32[9,4]{0,1:T(4,128)S(1)}, u32[]{:S(2)}, u32[]{:S(2)}) collective-permute-start(f32[9,4]{0,1:T(4,128)S(1)} %add.1024), channel_id=1, source_target_pairs={{0,4},{1,5},{2,6},{3,7},{4,0},{5,1},{6,2},{7,3},{8,12},{9,13},{10,... | collective-permute-start | bytes 440 | tf_op jit(solution)/shard_map/ppermute | solution.py:124
  79.3 1.6 %collective-permute-done.17 = f32[9,4]{0,1:T(4,128)S(1)} collective-permute-done((f32[9,4]{0,1:T(4,128)S(1)}, f32[9,4]{0,1:T(4,128)S(1)}, u32[]{:S(2)}, u32[]{:S(2)}) %collective-permute-start.17) | collective-permute-done | bytes 176 | tf_op jit(solution)/shard_map/ppermute | solution.py:124
  80.9 0.3 slice_reduce_fusion.2
  81.2 0.8 collective-permute-done.12
  82.0 0.3 slice_reduce_fusion.11
  82.5 2.4 %fusion.69 = (f32[4,16,16,128]{3,2,1,0:T(8,128)S(1)}, f32[4,16,16,128]{3,2,1,0:T(8,128)S(1)}) fusion(f32[8,16,16,128]{3,2,1,0:T(8,128)} %compare_convert_fusion.1, f32[4,20,20,128]{3,2,1,0:T(8,128)S(1)} %fusion.39, f32[4,22,22,128]{3,2,1,0:T(8,128)} %copy-done, f32[4,18,18,128]{3,2,1,0:T(8,128)} %copy-done.4, f32[4]{0:T(128)S(1)} %get-tuple-element.114, ...), kind=kLoop, calls=%fused_computation.125 | loop fusion | flops 1572864 | bytes 5242976 | tf_op jit(solution)/shard_map/add | solution.py:239
  84.9 1.0 %pad_maximum_fusion.3 = f32[8,16,16,128]{3,2,1,0:T(8,128)} fusion(f32[4,16,16,128]{3,2,1,0:T(8,128)S(1)} %get-tuple-element.79, f32[4,16,16,128]{3,2,1,0:T(8,128)S(1)} %get-tuple-element.78), kind=kLoop, calls=%fused_computation.53 | loop fusion | flops 262144 | bytes 2097152 | tf_op jit(solution)/shard_map/concatenate | solution.py:243
  (203 shorter events, 6.4 us)
Async XLA Ops:
  0.6 4.4 %copy-start.55 = (bf16[3,16,3,3,3]{1,4,3,2,0:T(4,128)(2,1)S(1)}, bf16[3,16,3,3,3]{1,4,3,2,0:T(4,128)(2,1)}, u32[]{:S(2)}) copy-start(bf16[3,16,3,3,3]{1,4,3,2,0:T(4,128)(2,1)} %param.5) | copy-start | bytes 7780
  0.6 4.5 %copy-start.54 = (s32[16,16,128]{2,1,0:T(8,128)S(1)}, s32[16,16,128]{2,1,0:T(8,128)}, u32[]{:S(2)}) copy-start(s32[16,16,128]{2,1,0:T(8,128)} %param.7) | copy-start | bytes 393220
  2.6 4.9 %collective-permute-start.1 = (bf16[16,1,16,128]{3,0,2,1:T(8,128)(2,1)S(1)}, bf16[16,1,16,128]{3,0,2,1:T(8,128)(2,1)S(1)}, u32[]{:S(2)}, u32[]{:S(2)}) collective-permute-start(bf16[16,1,16,128]{3,0,2,1:T(8,128)(2,1)S(1)} %get-tuple-element.81), channel_id=1, source_target_pairs={{0,24},{8,0},{16,8},{24,16},{1,25},{9,1},{17,9},{25,17},{2,26},{10... | collective-permute-start | bytes 196616 | tf_op jit(solution)/shard_map/ppermute | solution.py:58
  5.1 3.7 %collective-permute-start = (bf16[16,1,16,128]{3,0,2,1:T(8,128)(2,1)S(1)}, bf16[16,1,16,128]{3,0,2,1:T(8,128)(2,1)S(1)}, u32[]{:S(2)}, u32[]{:S(2)}) collective-permute-start(bf16[16,1,16,128]{3,0,2,1:T(8,128)(2,1)S(1)} %get-tuple-element.80), channel_id=1, source_target_pairs={{0,8},{8,16},{16,24},{24,0},{1,9},{9,17},{17,25},{25,1},{2,10},{10... | collective-permute-start | bytes 196616 | tf_op jit(solution)/shard_map/ppermute | solution.py:58
  8.8 7.1 %collective-permute-start.2 = (bf16[16,18,1,128]{3,0,2,1:T(8,128)(2,1)S(1)}, bf16[16,18,1,128]{3,0,2,1:T(8,128)(2,1)S(1)}, u32[]{:S(2)}, u32[]{:S(2)}) collective-permute-start(bf16[16,18,1,128]{3,0,2,1:T(8,128)(2,1)S(1)} %get-tuple-element.72), channel_id=1, source_target_pairs={{0,1},{1,2},{2,3},{3,4},{4,5},{5,6},{6,7},{7,0},{8,9},{9,10},{10,1... | collective-permute-start | bytes 221192 | tf_op jit(solution)/shard_map/ppermute | solution.py:58
  10.4 5.5 %collective-permute-start.3 = (bf16[16,18,1,128]{3,0,2,1:T(8,128)(2,1)S(1)}, bf16[16,18,1,128]{3,0,2,1:T(8,128)(2,1)S(1)}, u32[]{:S(2)}, u32[]{:S(2)}) collective-permute-start(bf16[16,18,1,128]{3,0,2,1:T(8,128)(2,1)S(1)} %get-tuple-element.73), channel_id=1, source_target_pairs={{0,7},{1,0},{2,1},{3,2},{4,3},{5,4},{6,5},{7,6},{8,15},{9,8},{10,9... | collective-permute-start | bytes 221192 | tf_op jit(solution)/shard_map/ppermute | solution.py:58
  23.6 4.4 %collective-permute-start.4 = (f32[4,4,16,128]{3,0,2,1:T(4,128)S(1)}, f32[4,4,16,128]{3,0,2,1:T(4,128)S(1)}, u32[]{:S(2)}, u32[]{:S(2)}) collective-permute-start(f32[4,4,16,128]{3,0,2,1:T(4,128)S(1)} %get-tuple-element.92), channel_id=1, source_target_pairs={{0,8},{8,16},{16,24},{24,0},{1,9},{9,17},{17,25},{25,1},{2,10},{10... | collective-permute-start | bytes 393224 | tf_op jit(solution)/shard_map/ppermute | solution.py:58
  23.7 4.9 %collective-permute-start.5 = (f32[4,4,16,128]{3,0,2,1:T(4,128)S(1)}, f32[4,4,16,128]{3,0,2,1:T(4,128)S(1)}, u32[]{:S(2)}, u32[]{:S(2)}) collective-permute-start(f32[4,4,16,128]{3,0,2,1:T(4,128)S(1)} %get-tuple-element.93), channel_id=1, source_target_pairs={{0,24},{8,0},{16,8},{24,16},{1,25},{9,1},{17,9},{25,17},{2,26},{10... | collective-permute-start | bytes 393224 | tf_op jit(solution)/shard_map/ppermute | solution.py:58
  28.8 10.3 %collective-permute-start.6 = (f32[4,24,4,128]{3,0,2,1:T(4,128)S(1)}, f32[4,24,4,128]{3,0,2,1:T(4,128)S(1)}, u32[]{:S(2)}, u32[]{:S(2)}) collective-permute-start(f32[4,24,4,128]{3,0,2,1:T(4,128)S(1)} %get-tuple-element.86), channel_id=1, source_target_pairs={{0,1},{1,2},{2,3},{3,4},{4,5},{5,6},{6,7},{7,0},{8,9},{9,10},{10,1... | collective-permute-start | bytes 589832 | tf_op jit(solution)/shard_map/ppermute | solution.py:58
  31.6 11.9 %collective-permute-start.7 = (f32[4,24,4,128]{3,0,2,1:T(4,128)S(1)}, f32[4,24,4,128]{3,0,2,1:T(4,128)S(1)}, u32[]{:S(2)}, u32[]{:S(2)}) collective-permute-start(f32[4,24,4,128]{3,0,2,1:T(4,128)S(1)} %get-tuple-element.87), channel_id=1, source_target_pairs={{0,7},{1,0},{2,1},{3,2},{4,3},{5,4},{6,5},{7,6},{8,15},{9,8},{10,9... | collective-permute-start | bytes 589832 | tf_op jit(solution)/shard_map/ppermute | solution.py:58
  45.3 3.3 %copy-start.5 = (f32[22,22,128]{2,1,0:T(8,128)}, f32[22,22,128]{2,1,0:T(8,128)S(1)}, u32[]{:S(2)}) copy-start(f32[22,22,128]{2,1,0:T(8,128)S(1)} %get-tuple-element.60) | copy-start | bytes 743428
  45.4 3.1 %copy-start.6 = (f32[22,22,128]{2,1,0:T(8,128)}, f32[22,22,128]{2,1,0:T(8,128)S(1)}, u32[]{:S(2)}) copy-start(f32[22,22,128]{2,1,0:T(8,128)S(1)} %get-tuple-element.94) | copy-start | bytes 743428
  45.4 3.1 %copy-start.7 = (f32[22,22,128]{2,1,0:T(8,128)}, f32[22,22,128]{2,1,0:T(8,128)S(1)}, u32[]{:S(2)}) copy-start(f32[22,22,128]{2,1,0:T(8,128)S(1)} %get-tuple-element.95) | copy-start | bytes 743428
  45.5 3.1 %copy-start.8 = (f32[22,22,128]{2,1,0:T(8,128)}, f32[22,22,128]{2,1,0:T(8,128)S(1)}, u32[]{:S(2)}) copy-start(f32[22,22,128]{2,1,0:T(8,128)S(1)} %get-tuple-element.100) | copy-start | bytes 743428
  45.5 3.1 %copy-start.9 = (f32[22,22,128]{2,1,0:T(8,128)}, f32[22,22,128]{2,1,0:T(8,128)S(1)}, u32[]{:S(2)}) copy-start(f32[22,22,128]{2,1,0:T(8,128)S(1)} %get-tuple-element.101) | copy-start | bytes 743428
  45.5 3.1 %copy-start.10 = (f32[22,22,128]{2,1,0:T(8,128)}, f32[22,22,128]{2,1,0:T(8,128)S(1)}, u32[]{:S(2)}) copy-start(f32[22,22,128]{2,1,0:T(8,128)S(1)} %get-tuple-element.102) | copy-start | bytes 743428
  45.5 3.1 %copy-start.11 = (f32[22,22,128]{2,1,0:T(8,128)}, f32[22,22,128]{2,1,0:T(8,128)S(1)}, u32[]{:S(2)}) copy-start(f32[22,22,128]{2,1,0:T(8,128)S(1)} %get-tuple-element.103) | copy-start | bytes 743428
  45.5 4.2 %copy-start.12 = (f32[20,20,128]{2,1,0:T(8,128)}, f32[20,20,128]{2,1,0:T(8,128)S(1)}, u32[]{:S(2)}) copy-start(f32[20,20,128]{2,1,0:T(8,128)S(1)} %slice.647) | copy-start | bytes 614404
  45.6 5.3 %copy-start.26 = (f32[18,18,128]{2,1,0:T(8,128)}, f32[18,18,128]{2,1,0:T(8,128)S(1)}, u32[]{:S(2)}) copy-start(f32[18,18,128]{2,1,0:T(8,128)S(1)} %slice.662) | copy-start | bytes 497668
  45.6 4.2 %copy-start.14 = (f32[20,20,128]{2,1,0:T(8,128)}, f32[20,20,128]{2,1,0:T(8,128)S(1)}, u32[]{:S(2)}) copy-start(f32[20,20,128]{2,1,0:T(8,128)S(1)} %slice.649) | copy-start | bytes 614404
  45.6 5.3 %copy-start.28 = (f32[18,18,128]{2,1,0:T(8,128)}, f32[18,18,128]{2,1,0:T(8,128)S(1)}, u32[]{:S(2)}) copy-start(f32[18,18,128]{2,1,0:T(8,128)S(1)} %slice.664) | copy-start | bytes 497668
  45.7 4.1 %copy-start.16 = (f32[20,20,128]{2,1,0:T(8,128)}, f32[20,20,128]{2,1,0:T(8,128)S(1)}, u32[]{:S(2)}) copy-start(f32[20,20,128]{2,1,0:T(8,128)S(1)} %slice.651) | copy-start | bytes 614404
  45.7 5.2 %copy-start.30 = (f32[18,18,128]{2,1,0:T(8,128)}, f32[18,18,128]{2,1,0:T(8,128)S(1)}, u32[]{:S(2)}) copy-start(f32[18,18,128]{2,1,0:T(8,128)S(1)} %slice.666) | copy-start | bytes 497668
  45.8 4.0 %copy-start.18 = (f32[20,20,128]{2,1,0:T(8,128)}, f32[20,20,128]{2,1,0:T(8,128)S(1)}, u32[]{:S(2)}) copy-start(f32[20,20,128]{2,1,0:T(8,128)S(1)} %slice.653) | copy-start | bytes 614404
  45.8 5.1 %copy-start.32 = (f32[18,18,128]{2,1,0:T(8,128)}, f32[18,18,128]{2,1,0:T(8,128)S(1)}, u32[]{:S(2)}) copy-start(f32[18,18,128]{2,1,0:T(8,128)S(1)} %slice.668) | copy-start | bytes 497668
  45.8 4.0 %copy-start.20 = (f32[20,20,128]{2,1,0:T(8,128)}, f32[20,20,128]{2,1,0:T(8,128)S(1)}, u32[]{:S(2)}) copy-start(f32[20,20,128]{2,1,0:T(8,128)S(1)} %slice.655) | copy-start | bytes 614404
  45.9 5.1 %copy-start.34 = (f32[18,18,128]{2,1,0:T(8,128)}, f32[18,18,128]{2,1,0:T(8,128)S(1)}, u32[]{:S(2)}) copy-start(f32[18,18,128]{2,1,0:T(8,128)S(1)} %slice.670) | copy-start | bytes 497668
  45.9 3.9 %copy-start.22 = (f32[20,20,128]{2,1,0:T(8,128)}, f32[20,20,128]{2,1,0:T(8,128)S(1)}, u32[]{:S(2)}) copy-start(f32[20,20,128]{2,1,0:T(8,128)S(1)} %slice.657) | copy-start | bytes 614404
  46.0 5.0 %copy-start.36 = (f32[18,18,128]{2,1,0:T(8,128)}, f32[18,18,128]{2,1,0:T(8,128)S(1)}, u32[]{:S(2)}) copy-start(f32[18,18,128]{2,1,0:T(8,128)S(1)} %slice.672) | copy-start | bytes 497668
  46.0 3.8 %copy-start.24 = (f32[20,20,128]{2,1,0:T(8,128)}, f32[20,20,128]{2,1,0:T(8,128)S(1)}, u32[]{:S(2)}) copy-start(f32[20,20,128]{2,1,0:T(8,128)S(1)} %slice.645) | copy-start | bytes 614404
  46.0 4.9 %copy-start.38 = (f32[18,18,128]{2,1,0:T(8,128)}, f32[18,18,128]{2,1,0:T(8,128)S(1)}, u32[]{:S(2)}) copy-start(f32[18,18,128]{2,1,0:T(8,128)S(1)} %slice.660) | copy-start | bytes 497668
  46.1 5.8 %copy-start.40 = (f32[16,16,128]{2,1,0:T(8,128)}, f32[16,16,128]{2,1,0:T(8,128)S(1)}, u32[]{:S(2)}) copy-start(f32[16,16,128]{2,1,0:T(8,128)S(1)} %slice.676) | copy-start | bytes 393220
  46.1 5.8 %copy-start.42 = (f32[16,16,128]{2,1,0:T(8,128)}, f32[16,16,128]{2,1,0:T(8,128)S(1)}, u32[]{:S(2)}) copy-start(f32[16,16,128]{2,1,0:T(8,128)S(1)} %slice.678) | copy-start | bytes 393220
  46.1 5.7 %copy-start.44 = (f32[16,16,128]{2,1,0:T(8,128)}, f32[16,16,128]{2,1,0:T(8,128)S(1)}, u32[]{:S(2)}) copy-start(f32[16,16,128]{2,1,0:T(8,128)S(1)} %slice.680) | copy-start | bytes 393220
  46.2 5.7 %copy-start.46 = (f32[16,16,128]{2,1,0:T(8,128)}, f32[16,16,128]{2,1,0:T(8,128)S(1)}, u32[]{:S(2)}) copy-start(f32[16,16,128]{2,1,0:T(8,128)S(1)} %slice.682) | copy-start | bytes 393220
  46.2 5.7 %copy-start.48 = (f32[16,16,128]{2,1,0:T(8,128)}, f32[16,16,128]{2,1,0:T(8,128)S(1)}, u32[]{:S(2)}) copy-start(f32[16,16,128]{2,1,0:T(8,128)S(1)} %slice.684) | copy-start | bytes 393220
  46.2 5.7 %copy-start.50 = (f32[16,16,128]{2,1,0:T(8,128)}, f32[16,16,128]{2,1,0:T(8,128)S(1)}, u32[]{:S(2)}) copy-start(f32[16,16,128]{2,1,0:T(8,128)S(1)} %slice.686) | copy-start | bytes 393220
  46.3 5.7 %copy-start.52 = (f32[16,16,128]{2,1,0:T(8,128)}, f32[16,16,128]{2,1,0:T(8,128)S(1)}, u32[]{:S(2)}) copy-start(f32[16,16,128]{2,1,0:T(8,128)S(1)} %slice.675) | copy-start | bytes 393220
  50.6 1.4 %copy-start.1 = (f32[4,20,20,128]{3,2,1,0:T(8,128)}, f32[4,20,20,128]{3,2,1,0:T(8,128)S(1)}, u32[]{:S(2)}) copy-start(f32[4,20,20,128]{3,2,1,0:T(8,128)S(1)} %fusion.33) | copy-start | bytes 2457604
  53.9 11.7 %collective-permute-start.13 = (f32[9,4]{0,1:T(4,128)S(1)}, f32[9,4]{0,1:T(4,128)S(1)}, u32[]{:S(2)}, u32[]{:S(2)}) collective-permute-start(f32[9,4]{0,1:T(4,128)S(1)} %stack.95), channel_id=1, source_target_pairs={{0,8},{8,0},{16,24},{24,16},{1,9},{9,1},{17,25},{25,17},{2,10},{10... | collective-permute-start | bytes 440 | tf_op jit(solution)/shard_map/ppermute | solution.py:124
  56.9 5.1 %copy-start = (f32[4,22,22,128]{3,2,1,0:T(8,128)}, f32[4,22,22,128]{3,2,1,0:T(8,128)S(1)}, u32[]{:S(2)}) copy-start(f32[4,22,22,128]{3,2,1,0:T(8,128)S(1)} %fusion.27) | copy-start | bytes 2973700
  56.9 1.4 %copy-start.15 = (f32[20,20,128]{2,1,0:T(8,128)S(1)}, f32[20,20,128]{2,1,0:T(8,128)}, u32[]{:S(2)}) copy-start(f32[20,20,128]{2,1,0:T(8,128)} %copy-done.14) | copy-start | bytes 614404
  57.0 1.6 %copy-start.17 = (f32[20,20,128]{2,1,0:T(8,128)S(1)}, f32[20,20,128]{2,1,0:T(8,128)}, u32[]{:S(2)}) copy-start(f32[20,20,128]{2,1,0:T(8,128)} %copy-done.16) | copy-start | bytes 614404
  57.0 1.7 %copy-start.19 = (f32[20,20,128]{2,1,0:T(8,128)S(1)}, f32[20,20,128]{2,1,0:T(8,128)}, u32[]{:S(2)}) copy-start(f32[20,20,128]{2,1,0:T(8,128)} %copy-done.18) | copy-start | bytes 614404
  57.0 1.7 %copy-start.21 = (f32[20,20,128]{2,1,0:T(8,128)S(1)}, f32[20,20,128]{2,1,0:T(8,128)}, u32[]{:S(2)}) copy-start(f32[20,20,128]{2,1,0:T(8,128)} %copy-done.20) | copy-start | bytes 614404
  57.0 1.8 %copy-start.23 = (f32[20,20,128]{2,1,0:T(8,128)S(1)}, f32[20,20,128]{2,1,0:T(8,128)}, u32[]{:S(2)}) copy-start(f32[20,20,128]{2,1,0:T(8,128)} %copy-done.22) | copy-start | bytes 614404
  57.0 1.8 %copy-start.25 = (f32[20,20,128]{2,1,0:T(8,128)S(1)}, f32[20,20,128]{2,1,0:T(8,128)}, u32[]{:S(2)}) copy-start(f32[20,20,128]{2,1,0:T(8,128)} %copy-done.24) | copy-start | bytes 614404
  59.6 1.4 %copy-start.37 = (f32[18,18,128]{2,1,0:T(8,128)S(1)}, f32[18,18,128]{2,1,0:T(8,128)}, u32[]{:S(2)}) copy-start(f32[18,18,128]{2,1,0:T(8,128)} %copy-done.36) | copy-start | bytes 497668
  59.6 1.4 %copy-start.39 = (f32[18,18,128]{2,1,0:T(8,128)S(1)}, f32[18,18,128]{2,1,0:T(8,128)}, u32[]{:S(2)}) copy-start(f32[18,18,128]{2,1,0:T(8,128)} %copy-done.38) | copy-start | bytes 497668
  61.7 2.6 %copy-start.4 = (f32[4,18,18,128]{3,2,1,0:T(8,128)}, f32[4,18,18,128]{3,2,1,0:T(8,128)S(1)}, u32[]{:S(2)}) copy-start(f32[4,18,18,128]{3,2,1,0:T(8,128)S(1)} %fusion.51) | copy-start | bytes 1990660
  61.7 1.4 %copy-start.47 = (f32[16,16,128]{2,1,0:T(8,128)S(1)}, f32[16,16,128]{2,1,0:T(8,128)}, u32[]{:S(2)}) copy-start(f32[16,16,128]{2,1,0:T(8,128)} %copy-done.46) | copy-start | bytes 393220
  61.7 1.4 %copy-start.49 = (f32[16,16,128]{2,1,0:T(8,128)S(1)}, f32[16,16,128]{2,1,0:T(8,128)}, u32[]{:S(2)}) copy-start(f32[16,16,128]{2,1,0:T(8,128)} %copy-done.48) | copy-start | bytes 393220
  61.8 1.5 %copy-start.51 = (f32[16,16,128]{2,1,0:T(8,128)S(1)}, f32[16,16,128]{2,1,0:T(8,128)}, u32[]{:S(2)}) copy-start(f32[16,16,128]{2,1,0:T(8,128)} %copy-done.50) | copy-start | bytes 393220
  61.8 1.5 %copy-start.53 = (f32[16,16,128]{2,1,0:T(8,128)S(1)}, f32[16,16,128]{2,1,0:T(8,128)}, u32[]{:S(2)}) copy-start(f32[16,16,128]{2,1,0:T(8,128)} %copy-done.52) | copy-start | bytes 393220
  63.3 19.2 %copy-start.2 = (f32[4,20,20,128]{3,2,1,0:T(8,128)S(1)}, f32[4,20,20,128]{3,2,1,0:T(8,128)}, u32[]{:S(2)}) copy-start(f32[4,20,20,128]{3,2,1,0:T(8,128)} %copy-done.1) | copy-start | bytes 2457604
  65.2 1.5 %collective-permute-start.8 = (f32[9,4]{0,1:T(4,128)S(1)}, f32[9,4]{0,1:T(4,128)S(1)}, u32[]{:S(2)}, u32[]{:S(2)}) collective-permute-start(f32[9,4]{0,1:T(4,128)S(1)} %stack.85), channel_id=1, source_target_pairs={{0,8},{8,0},{16,24},{24,16},{1,9},{9,1},{17,25},{25,17},{2,10},{10... | collective-permute-start | bytes 440 | tf_op jit(solution)/shard_map/ppermute | solution.py:124
  65.6 3.6 %collective-permute-start.14 = (f32[9,4]{0,1:T(4,128)S(1)}, f32[9,4]{0,1:T(4,128)S(1)}, u32[]{:S(2)}, u32[]{:S(2)}) collective-permute-start(f32[9,4]{0,1:T(4,128)S(1)} %add.1076), channel_id=1, source_target_pairs={{0,16},{8,24},{16,0},{24,8},{1,17},{9,25},{17,1},{25,9},{2,18},{10... | collective-permute-start | bytes 440 | tf_op jit(solution)/shard_map/ppermute | solution.py:124
  66.7 3.6 %collective-permute-start.9 = (f32[9,4]{0,1:T(4,128)S(1)}, f32[9,4]{0,1:T(4,128)S(1)}, u32[]{:S(2)}, u32[]{:S(2)}) collective-permute-start(f32[9,4]{0,1:T(4,128)S(1)} %add.1021), channel_id=1, source_target_pairs={{0,16},{8,24},{16,0},{24,8},{1,17},{9,25},{17,1},{25,9},{2,18},{10... | collective-permute-start | bytes 440 | tf_op jit(solution)/shard_map/ppermute | solution.py:124
  69.2 3.6 %collective-permute-start.15 = (f32[9,4]{0,1:T(4,128)S(1)}, f32[9,4]{0,1:T(4,128)S(1)}, u32[]{:S(2)}, u32[]{:S(2)}) collective-permute-start(f32[9,4]{0,1:T(4,128)S(1)} %add.1077), channel_id=1, source_target_pairs={{0,1},{1,0},{2,3},{3,2},{4,5},{5,4},{6,7},{7,6},{8,9},{9,8},{10,11... | collective-permute-start | bytes 440 | tf_op jit(solution)/shard_map/ppermute | solution.py:124
  70.3 3.6 %collective-permute-start.10 = (f32[9,4]{0,1:T(4,128)S(1)}, f32[9,4]{0,1:T(4,128)S(1)}, u32[]{:S(2)}, u32[]{:S(2)}) collective-permute-start(f32[9,4]{0,1:T(4,128)S(1)} %add.1022), channel_id=1, source_target_pairs={{0,1},{1,0},{2,3},{3,2},{4,5},{5,4},{6,7},{7,6},{8,9},{9,8},{10,11... | collective-permute-start | bytes 440 | tf_op jit(solution)/shard_map/ppermute | solution.py:124
  72.8 3.6 %collective-permute-start.16 = (f32[9,4]{0,1:T(4,128)S(1)}, f32[9,4]{0,1:T(4,128)S(1)}, u32[]{:S(2)}, u32[]{:S(2)}) collective-permute-start(f32[9,4]{0,1:T(4,128)S(1)} %add.1078), channel_id=1, source_target_pairs={{0,2},{1,3},{2,0},{3,1},{4,6},{5,7},{6,4},{7,5},{8,10},{9,11},{10,... | collective-permute-start | bytes 440 | tf_op jit(solution)/shard_map/ppermute | solution.py:124
  73.9 3.6 %collective-permute-start.11 = (f32[9,4]{0,1:T(4,128)S(1)}, f32[9,4]{0,1:T(4,128)S(1)}, u32[]{:S(2)}, u32[]{:S(2)}) collective-permute-start(f32[9,4]{0,1:T(4,128)S(1)} %add.1023), channel_id=1, source_target_pairs={{0,2},{1,3},{2,0},{3,1},{4,6},{5,7},{6,4},{7,5},{8,10},{9,11},{10,... | collective-permute-start | bytes 440 | tf_op jit(solution)/shard_map/ppermute | solution.py:124
  76.4 4.5 %collective-permute-start.17 = (f32[9,4]{0,1:T(4,128)S(1)}, f32[9,4]{0,1:T(4,128)S(1)}, u32[]{:S(2)}, u32[]{:S(2)}) collective-permute-start(f32[9,4]{0,1:T(4,128)S(1)} %add.1079), channel_id=1, source_target_pairs={{0,4},{1,5},{2,6},{3,7},{4,0},{5,1},{6,2},{7,3},{8,12},{9,13},{10,... | collective-permute-start | bytes 440 | tf_op jit(solution)/shard_map/ppermute | solution.py:124
  77.5 4.5 %collective-permute-start.12 = (f32[9,4]{0,1:T(4,128)S(1)}, f32[9,4]{0,1:T(4,128)S(1)}, u32[]{:S(2)}, u32[]{:S(2)}) collective-permute-start(f32[9,4]{0,1:T(4,128)S(1)} %add.1024), channel_id=1, source_target_pairs={{0,4},{1,5},{2,6},{3,7},{4,0},{5,1},{6,2},{7,3},{8,12},{9,13},{10,... | collective-permute-start | bytes 440 | tf_op jit(solution)/shard_map/ppermute | solution.py:124
  (11 other events, 12.5 us)

commit v11 on v9

--- a/solution.py
+++ b/solution.py
@@ -61,14 +61,21 @@
     return jnp.where(inside, moved, jnp.zeros_like(moved))
 
 
-def extend(cells, width):
+def extend(cells, width, corner=None):
+    corner = width if corner is None else corner
     for axis, dim in (("gz", 1), ("yx", 2)):
-        size = cells.shape[dim]
-        head = lax.slice_in_dim(cells, 0, width, axis=dim)
-        tail = lax.slice_in_dim(cells, size - width, size, axis=dim)
-        cells = jnp.concatenate(
-            [from_ring(tail, axis, 1), cells, from_ring(head, axis, -1)], axis=dim
-        )
+        source = cells
+        trim = 0
+        if dim == 2 and corner < width:
+            trim = width - corner
+            source = cells[:, trim : cells.shape[1] - trim]
+        size = source.shape[dim]
+        head = lax.slice_in_dim(source, 0, width, axis=dim)
+        tail = lax.slice_in_dim(source, size - width, size, axis=dim)
+        edges = [from_ring(tail, axis, 1), from_ring(head, axis, -1)]
+        if trim:
+            edges = [jnp.pad(edge, ((0, 0), (trim, trim), (0, 0), (0, 0))) for edge in edges]
+        cells = jnp.concatenate([edges[0], cells, edges[1]], axis=dim)
     return cells
 
 
@@ -149,7 +156,7 @@
     )
     halo = ITERS + 1
     stacked = jnp.concatenate([affinities, labels[None].astype(jnp.float32)], axis=0)
-    grid_cells = extend(stacked, halo)
+    grid_cells = extend(stacked, halo, halo - 1)
     cells_z = depth_cells + 2 * halo
     cells_y = row_cells + 2 * halo
     grid_z = lax.axis_index("gz") * depth_cells - halo + jnp.arange(cells_z, dtype=jnp.int32)

time: 76.3 us -> 75.5 us (0.990)
  no operation moved by 1% of the time
where the time goes in v11:
time: 75.5 us; the launch traced here: 75.3 us
  waiting for transfers between devices  29.2 us (39%)
  starting transfers between devices  17.5 us (23%)
  other arithmetic  13.3 us (18%)
  local copies, waits for them, and re-layouts  8.18 us (11%)
  matrix products  6.15 us (8%)
  between operations  1.14 us (2%)
    ppermute x8, waiting for transfers between devices, from_ring(): lax.ppermute(value, axis, [(i, (i + by) % devices) for i in range(devices)])  16.5 us
    ppermute x8, starting transfers between devices, from_ring(): lax.ppermute(value, axis, [(i, (i + by) % devices) for i in range(devices)])  14.1 us
    ppermute x5, waiting for transfers between devices, all_sum(): lax.ppermute(value, axis, [(i, i ^ hop) for i in range(devices)])  12.7 us
    dot_general x9, matrix products, conv_region(): jnp.einsum('oce,cezyx->ozyx', conv_weight[:, :, offset_z, offset_y, :], w...  6.15 us
    unnamed x12, local copies, waits for them, and re-layouts  3.64 us
    add x1, other arithmetic, body(): probabilities = probabilities + coeff[:, None, None, None] * vector  3.39 us
    ppermute x5, starting transfers between devices, all_sum(): lax.ppermute(value, axis, [(i, i ^ hop) for i in range(devices)])  3.35 us
    sub x2, other arithmetic, operate_inside(): return diagonal[part, part] * centre - coupled  3.29 us
  transfers between devices with their start and end apart: 13, of which 12 were waited for; matrix products, arithmetic and copies ran while one was open for 1% of the time, Pallas kernels for 0%

profile of v11, /device:TPU:0, one launch (start us, length us, event | category | flops | bytes accessed | tf_op | source)
XLA Modules:
  0.0 75.3 jit_solution(8038277972589064385)
XLA Ops:
  0.6 0.0 copy-start.3
  0.6 0.0 copy-start.2
  0.6 1.9 %copy.6 = bf16[16,16,16,128]{3,0,2,1:T(8,128)(2,1)S(1)} copy(bf16[16,16,16,128]{3,2,1,0:T(8,128)(2,1)} %param.4) | data formatting | bytes 2097152 | tf_op args[0]
  2.6 2.5 %collective-permute-start.1 = (bf16[16,1,16,128]{3,0,2,1:T(8,128)(2,1)S(1)}, bf16[16,1,16,128]{3,0,2,1:T(8,128)(2,1)S(1)}, u32[]{:S(2)}, u32[]{:S(2)}) collective-permute-start(bf16[16,1,16,128]{3,0,2,1:T(8,128)(2,1)S(1)} %get-tuple-element.40), channel_id=1, source_target_pairs={{0,24},{8,0},{16,8},{24,16},{1,25},{9,1},{17,9},{25,17},{2,26},{10... | collective-permute-start | bytes 196616 | tf_op jit(solution)/shard_map/ppermute | solution.py:58
  5.1 0.0 collective-permute-start
  5.1 2.4 %collective-permute-done.1 = bf16[16,1,16,128]{3,0,2,1:T(8,128)(2,1)S(1)} collective-permute-done((bf16[16,1,16,128]{3,0,2,1:T(8,128)(2,1)S(1)}, bf16[16,1,16,128]{3,0,2,1:T(8,128)(2,1)S(1)}, u32[]{:S(2)}, u32[]{:S(2)}) %collective-permute-start.1) | collective-permute-done | bytes 65568 | tf_op jit(solution)/shard_map/ppermute | solution.py:58
  7.5 1.2 %collective-permute-done = bf16[16,1,16,128]{3,0,2,1:T(8,128)(2,1)S(1)} collective-permute-done((bf16[16,1,16,128]{3,0,2,1:T(8,128)(2,1)S(1)}, bf16[16,1,16,128]{3,0,2,1:T(8,128)(2,1)S(1)}, u32[]{:S(2)}, u32[]{:S(2)}) %collective-permute-start) | collective-permute-done | bytes 65568 | tf_op jit(solution)/shard_map/ppermute | solution.py:58
  8.8 1.6 %collective-permute-start.2 = (bf16[16,18,1,128]{3,0,2,1:T(8,128)(2,1)S(1)}, bf16[16,18,1,128]{3,0,2,1:T(8,128)(2,1)S(1)}, u32[]{:S(2)}, u32[]{:S(2)}) collective-permute-start(bf16[16,18,1,128]{3,0,2,1:T(8,128)(2,1)S(1)} %get-tuple-element.37), channel_id=1, source_target_pairs={{0,1},{1,2},{2,3},{3,4},{4,5},{5,6},{6,7},{7,0},{8,9},{9,10},{10,1... | collective-permute-start | bytes 221192 | tf_op jit(solution)/shard_map/ppermute | solution.py:58
  10.4 0.0 copy-done.3
  10.4 0.0 copy-done.2
  10.4 3.3 %collective-permute-start.3 = (bf16[16,18,1,128]{3,0,2,1:T(8,128)(2,1)S(1)}, bf16[16,18,1,128]{3,0,2,1:T(8,128)(2,1)S(1)}, u32[]{:S(2)}, u32[]{:S(2)}) collective-permute-start(bf16[16,18,1,128]{3,0,2,1:T(8,128)(2,1)S(1)} %get-tuple-element.38), channel_id=1, source_target_pairs={{0,7},{1,0},{2,1},{3,2},{4,3},{5,4},{6,5},{7,6},{8,15},{9,8},{10,9... | collective-permute-start | bytes 221192 | tf_op jit(solution)/shard_map/ppermute | solution.py:58
  13.7 2.2 %collective-permute-done.2 = bf16[16,18,1,128]{3,0,2,1:T(8,128)(2,1)S(1)} collective-permute-done((bf16[16,18,1,128]{3,0,2,1:T(8,128)(2,1)S(1)}, bf16[16,18,1,128]{3,0,2,1:T(8,128)(2,1)S(1)}, u32[]{:S(2)}, u32[]{:S(2)}) %collective-permute-start.2) | collective-permute-done | bytes 73760 | tf_op jit(solution)/shard_map/ppermute | solution.py:58
  15.9 0.0 collective-permute-done.3
  16.0 0.3 pad_maximum_fusion.1
  16.2 0.3 fusion.78
  16.5 0.8 fusion.19
  17.2 0.6 convolution_bitcast_fusion.7
  17.8 0.6 convolution_bitcast_fusion.6
  18.4 0.6 convolution_bitcast_fusion.5
  19.0 0.6 convolution_bitcast_fusion.4
  19.6 0.6 convolution_bitcast_fusion.3
  20.2 0.6 convolution_bitcast_fusion.2
  20.8 0.6 convolution_bitcast_fusion.1
  21.4 0.6 convolution_bitcast_fusion
  21.9 0.1 copy-done.4
  22.0 1.5 %fusion.34 = f32[3,16,16,128]{3,0,2,1:T(4,128)S(1)} fusion(f32[16,16,128,3]{2,3,1,0:T(4,128)S(1)} %convolution_bitcast_fusion, f32[16,16,128,3]{2,3,1,0:T(4,128)S(1)} %convolution_bitcast_fusion.1, f32[16,16,128,3]{2,3,1,0:T(4,128)S(1)} %convolution_bitcast_fusion.2, f32[16,16,128,3]{2,3,1,0:T(4,128)S(1)} %convolution_bitcast_fusion.3, ...), kind=kOutput, calls=%fused_computation.66 | convolution fusion | flops 22560768 | bytes 7520556 | tf_op jit(solution)/shard_map/oce,cezyx->ozyx/dot_general | solution.py:47
  23.5 0.1 pad_maximum_fusion.7
  23.6 0.1 collective-permute-start.4
  23.7 1.8 %collective-permute-start.5 = (f32[4,4,16,128]{3,0,2,1:T(4,128)S(1)}, f32[4,4,16,128]{3,0,2,1:T(4,128)S(1)}, u32[]{:S(2)}, u32[]{:S(2)}) collective-permute-start(f32[4,4,16,128]{3,0,2,1:T(4,128)S(1)} %get-tuple-element.44), channel_id=1, source_target_pairs={{0,24},{8,0},{16,8},{24,16},{1,25},{9,1},{17,9},{25,17},{2,26},{10... | collective-permute-start | bytes 393224 | tf_op jit(solution)/shard_map/ppermute | solution.py:58
  25.5 2.6 %collective-permute-done.4 = f32[4,4,16,128]{3,0,2,1:T(4,128)S(1)} collective-permute-done((f32[4,4,16,128]{3,0,2,1:T(4,128)S(1)}, f32[4,4,16,128]{3,0,2,1:T(4,128)S(1)}, u32[]{:S(2)}, u32[]{:S(2)}) %collective-permute-start.4) | collective-permute-done | bytes 131104 | tf_op jit(solution)/shard_map/ppermute | solution.py:58
  28.1 0.7 collective-permute-done.5
  28.8 0.1 pad_maximum_fusion.5
  28.9 0.9 %collective-permute-start.6 = (f32[4,22,4,128]{3,0,2,1:T(4,128)S(1)}, f32[4,22,4,128]{3,0,2,1:T(4,128)S(1)}, u32[]{:S(2)}, u32[]{:S(2)}) collective-permute-start(f32[4,22,4,128]{3,0,2,1:T(4,128)S(1)} %get-tuple-element.41), channel_id=1, source_target_pairs={{0,1},{1,2},{2,3},{3,4},{4,5},{5,6},{6,7},{7,0},{8,9},{9,10},{10,1... | collective-permute-start | bytes 540680 | tf_op jit(solution)/shard_map/ppermute | solution.py:58
  29.8 4.1 %collective-permute-start.7 = (f32[4,22,4,128]{3,0,2,1:T(4,128)S(1)}, f32[4,22,4,128]{3,0,2,1:T(4,128)S(1)}, u32[]{:S(2)}, u32[]{:S(2)}) collective-permute-start(f32[4,22,4,128]{3,0,2,1:T(4,128)S(1)} %get-tuple-element.42), channel_id=1, source_target_pairs={{0,7},{1,0},{2,1},{3,2},{4,3},{5,4},{6,5},{7,6},{8,15},{9,8},{10,9... | collective-permute-start | bytes 540680 | tf_op jit(solution)/shard_map/ppermute | solution.py:58
  34.0 5.0 %collective-permute-done.6 = f32[4,22,4,128]{3,0,2,1:T(4,128)S(1)} collective-permute-done((f32[4,22,4,128]{3,0,2,1:T(4,128)S(1)}, f32[4,22,4,128]{3,0,2,1:T(4,128)S(1)}, u32[]{:S(2)}, u32[]{:S(2)}) %collective-permute-start.6) | collective-permute-done | bytes 180256 | tf_op jit(solution)/shard_map/ppermute | solution.py:58
  39.0 2.4 %collective-permute-done.7 = f32[4,22,4,128]{3,0,2,1:T(4,128)S(1)} collective-permute-done((f32[4,22,4,128]{3,0,2,1:T(4,128)S(1)}, f32[4,22,4,128]{3,0,2,1:T(4,128)S(1)}, u32[]{:S(2)}, u32[]{:S(2)}) %collective-permute-start.7) | collective-permute-done | bytes 180256 | tf_op jit(solution)/shard_map/ppermute | solution.py:58
  41.4 0.3 select_maximum_fusion
  41.7 0.9 %fusion.75 = (f32[1,24,24,128]{3,0,2,1:T(1,128)S(1)}, f32[1,24,24,128]{3,0,2,1:T(1,128)S(1)}, f32[1,24,24,128]{3,0,2,1:T(1,128)S(1)}, f32[1,24,24,128]{3,0,2,1:T(1,128)S(1)}) fusion(f32[4,24,24,128]{3,0,2,1:T(4,128)S(1)} %select_maximum_fusion), kind=kLoop, calls=%fused_computation.179 | loop fusion | bytes 2359296 | tf_op jit(solution)/shard_map/slice | solution.py:168
  42.6 0.1 broadcast_multiply_fusion
  42.8 0.2 convert_add_fusion
  43.0 0.2 fusion.46
  43.7 0.2 compare_convert_fusion
  43.9 0.8 %fusion.71 = (f32[8,22,22,127]{3,2,1,0:T(8,128)S(1)}, f32[8,22,22,127]{3,2,1,0:T(8,128)S(1)}) fusion(f32[8,24,24,128]{3,2,1,0:T(8,128)S(1)} %compare_convert_fusion), kind=kLoop, calls=%fused_computation.175 | loop fusion | bytes 7867904 | tf_op jit(solution)/shard_map/slice | solution.py:114
  44.7 2.1 %fusion.4 = f32[8,22,22,128]{3,2,1,0:T(8,128)S(1)} fusion(f32[8,24,24,128]{3,2,1,0:T(8,128)S(1)} %compare_convert_fusion, f32[8,22,22,127]{3,2,1,0:T(8,128)S(1)} %get-tuple-element.24, f32[8,22,22,127]{3,2,1,0:T(8,128)S(1)} %get-tuple-element.23, f32[22,22,128]{2,1,0:T(8,128)S(1)} %get-tuple-element.53, f32[22,22,128]{2,1,0:T(8,128)S(1)} %get-tuple-element.54, ...), kind=kLoop, calls=%fused_computation.9 | loop fusion | flops 6938624 | bytes 17563392 | tf_op jit(solution)/shard_map/sub | solution.py:179
  46.8 0.7 fusion.72
  47.5 1.8 %fusion.10 = f32[8,20,20,128]{3,2,1,0:T(8,128)S(1)} fusion(f32[8,22,22,128]{3,2,1,0:T(8,128)S(1)} %fusion.4, f32[8,20,20,127]{3,2,1,0:T(8,128)S(1)} %get-tuple-element.26, f32[8,20,20,127]{3,2,1,0:T(8,128)S(1)} %get-tuple-element.25, f32[20,20,128]{2,1,0:T(8,128)S(1)} %slice.449, f32[20,20,128]{2,1,0:T(8,128)S(1)} %slice.447, f32[20,20,128]{2,1,0:T(8,128)S(1)} %slice.445, ...), kind=kLoop, calls=%fused_computation.19 | loop fusion | flops 5324800 | bytes 14515200 | tf_op jit(solution)/shard_map/sub | solution.py:120
  49.4 0.0 copy-start
  49.4 0.6 fusion.73
  50.0 1.4 %fusion.16 = f32[8,18,18,128]{3,2,1,0:T(8,128)S(1)} fusion(f32[8,20,20,128]{3,2,1,0:T(8,128)S(1)} %fusion.10, f32[8,18,18,127]{3,2,1,0:T(8,128)S(1)} %get-tuple-element.28, f32[8,18,18,127]{3,2,1,0:T(8,128)S(1)} %get-tuple-element.27, f32[18,18,128]{2,1,0:T(8,128)S(1)} %slice.464, f32[18,18,128]{2,1,0:T(8,128)S(1)} %slice.462, ...), kind=kLoop, calls=%fused_computation.30 | loop fusion | flops 4313088 | bytes 11757312 | tf_op jit(solution)/shard_map/sub | solution.py:120
  51.5 0.4 fusion.74
  51.9 0.8 %copy-done.1 = f32[8,18,18,128]{3,2,1,0:T(8,128)} copy-done((f32[8,18,18,128]{3,2,1,0:T(8,128)}, f32[8,18,18,128]{3,2,1,0:T(8,128)S(1)}, u32[]{:S(2)}) %copy-start.1) | copy-done | bytes 1327128
  52.7 2.3 %multiply_reduce_fusion.5 = (f32[8]{0:T(128)S(1)}, f32[8]{0:T(128)S(1)}, f32[8]{0:T(128)S(1)}, f32[8]{0:T(128)S(1)}, f32[8]{0:T(128)S(1)}, /*index=5*/f32[8]{0:T...) fusion(f32[8,22,22,128]{3,2,1,0:T(8,128)S(1)} %fusion.4, f32[8,20,20,128]{3,2,1,0:T(8,128)S(1)} %fusion.10, ...), kind=kLoop, calls=%fused_computation.83 | loop fusion | flops 8126392 | bytes 10338592 | tf_op jit(solution)/shard_map/reduce_sum | solution.py:137
  55.0 0.2 collective-permute-start.8
  55.2 1.1 %collective-permute-done.8 = f32[9,8]{1,0:T(8,128)S(1)} collective-permute-done((f32[9,8]{1,0:T(8,128)S(1)}, f32[9,8]{1,0:T(8,128)S(1)}, u32[]{:S(2)}, u32[]{:S(2)}) %collective-permute-start.8) | collective-permute-done | bytes 320 | tf_op jit(solution)/shard_map/ppermute | solution.py:131
  56.3 1.1 %collective-permute-start.9 = (f32[9,8]{1,0:T(8,128)S(1)}, f32[9,8]{1,0:T(8,128)S(1)}, u32[]{:S(2)}, u32[]{:S(2)}) collective-permute-start(f32[9,8]{1,0:T(8,128)S(1)} %add.592), channel_id=1, source_target_pairs={{0,16},{8,24},{16,0},{24,8},{1,17},{9,25},{17,1},{25,9},{2,18},{10... | collective-permute-start | bytes 872 | tf_op jit(solution)/shard_map/ppermute | solution.py:131
  57.3 2.6 %collective-permute-done.9 = f32[9,8]{1,0:T(8,128)S(1)} collective-permute-done((f32[9,8]{1,0:T(8,128)S(1)}, f32[9,8]{1,0:T(8,128)S(1)}, u32[]{:S(2)}, u32[]{:S(2)}) %collective-permute-start.9) | collective-permute-done | bytes 320 | tf_op jit(solution)/shard_map/ppermute | solution.py:131
  59.9 0.0 collective-permute-start.10
  59.9 3.6 %collective-permute-done.10 = f32[9,8]{1,0:T(8,128)S(1)} collective-permute-done((f32[9,8]{1,0:T(8,128)S(1)}, f32[9,8]{1,0:T(8,128)S(1)}, u32[]{:S(2)}, u32[]{:S(2)}) %collective-permute-start.10) | collective-permute-done | bytes 320 | tf_op jit(solution)/shard_map/ppermute | solution.py:131
  63.6 0.6 collective-permute-start.11
  64.1 3.1 %collective-permute-done.11 = f32[9,8]{1,0:T(8,128)S(1)} collective-permute-done((f32[9,8]{1,0:T(8,128)S(1)}, f32[9,8]{1,0:T(8,128)S(1)}, u32[]{:S(2)}, u32[]{:S(2)}) %collective-permute-start.11) | collective-permute-done | bytes 320 | tf_op jit(solution)/shard_map/ppermute | solution.py:131
  67.2 1.6 %collective-permute-start.12 = (f32[9,8]{1,0:T(8,128)S(1)}, f32[9,8]{1,0:T(8,128)S(1)}, u32[]{:S(2)}, u32[]{:S(2)}) collective-permute-start(f32[9,8]{1,0:T(8,128)S(1)} %add.595), channel_id=1, source_target_pairs={{0,4},{1,5},{2,6},{3,7},{4,0},{5,1},{6,2},{7,3},{8,12},{9,13},{10,... | collective-permute-start | bytes 872 | tf_op jit(solution)/shard_map/ppermute | solution.py:131
  68.8 0.8 %copy.23 = f32[3,16,16,128]{3,2,1,0:T(8,128)} copy(f32[3,16,16,128]{3,0,2,1:T(4,128)S(1)} %fusion.34) | data formatting | bytes 786432
  69.6 2.3 %collective-permute-done.12 = f32[9,8]{1,0:T(8,128)S(1)} collective-permute-done((f32[9,8]{1,0:T(8,128)S(1)}, f32[9,8]{1,0:T(8,128)S(1)}, u32[]{:S(2)}, u32[]{:S(2)}) %collective-permute-start.12) | collective-permute-done | bytes 320 | tf_op jit(solution)/shard_map/ppermute | solution.py:131
  71.9 3.4 %multiply_add_fusion = f32[8,16,16,128]{3,2,1,0:T(8,128)} fusion(f32[8,20,20,128]{3,2,1,0:T(8,128)} %copy-done, f32[8,22,22,128]{3,2,1,0:T(8,128)S(1)} %fusion.4, f32[8,18,18,128]{3,2,1,0:T(8,128)} %copy-done.1, f32[8]{0:T(128)S(1)} %get-tuple-element.65, f32[8]{0:T(128)S(1)} %get-tuple-element.64, f32[8]{0:T(128)S(1)} %get-tuple-element.13, ...), kind=kLoop, calls=%fused_computation.77 | loop fusion | flops 2097152 | bytes 4325504 | tf_op jit(solution)/shard_map/add | solution.py:243
  (51 shorter events, 0.8 us)
Async XLA Ops:
  0.6 9.7 %copy-start.3 = (bf16[3,16,3,3,3]{1,4,3,2,0:T(4,128)(2,1)S(1)}, bf16[3,16,3,3,3]{1,4,3,2,0:T(4,128)(2,1)}, u32[]{:S(2)}) copy-start(bf16[3,16,3,3,3]{1,4,3,2,0:T(4,128)(2,1)} %param.5) | copy-start | bytes 7780
  0.6 9.8 %copy-start.2 = (s32[16,16,128]{2,1,0:T(8,128)S(1)}, s32[16,16,128]{2,1,0:T(8,128)}, u32[]{:S(2)}) copy-start(s32[16,16,128]{2,1,0:T(8,128)} %param.7) | copy-start | bytes 393220
  2.6 4.9 %collective-permute-start.1 = (bf16[16,1,16,128]{3,0,2,1:T(8,128)(2,1)S(1)}, bf16[16,1,16,128]{3,0,2,1:T(8,128)(2,1)S(1)}, u32[]{:S(2)}, u32[]{:S(2)}) collective-permute-start(bf16[16,1,16,128]{3,0,2,1:T(8,128)(2,1)S(1)} %get-tuple-element.40), channel_id=1, source_target_pairs={{0,24},{8,0},{16,8},{24,16},{1,25},{9,1},{17,9},{25,17},{2,26},{10... | collective-permute-start | bytes 196616 | tf_op jit(solution)/shard_map/ppermute | solution.py:58
  5.1 3.7 %collective-permute-start = (bf16[16,1,16,128]{3,0,2,1:T(8,128)(2,1)S(1)}, bf16[16,1,16,128]{3,0,2,1:T(8,128)(2,1)S(1)}, u32[]{:S(2)}, u32[]{:S(2)}) collective-permute-start(bf16[16,1,16,128]{3,0,2,1:T(8,128)(2,1)S(1)} %get-tuple-element.39), channel_id=1, source_target_pairs={{0,8},{8,16},{16,24},{24,0},{1,9},{9,17},{17,25},{25,1},{2,10},{10... | collective-permute-start | bytes 196616 | tf_op jit(solution)/shard_map/ppermute | solution.py:58
  8.8 7.1 %collective-permute-start.2 = (bf16[16,18,1,128]{3,0,2,1:T(8,128)(2,1)S(1)}, bf16[16,18,1,128]{3,0,2,1:T(8,128)(2,1)S(1)}, u32[]{:S(2)}, u32[]{:S(2)}) collective-permute-start(bf16[16,18,1,128]{3,0,2,1:T(8,128)(2,1)S(1)} %get-tuple-element.37), channel_id=1, source_target_pairs={{0,1},{1,2},{2,3},{3,4},{4,5},{5,6},{6,7},{7,0},{8,9},{9,10},{10,1... | collective-permute-start | bytes 221192 | tf_op jit(solution)/shard_map/ppermute | solution.py:58
  10.4 5.5 %collective-permute-start.3 = (bf16[16,18,1,128]{3,0,2,1:T(8,128)(2,1)S(1)}, bf16[16,18,1,128]{3,0,2,1:T(8,128)(2,1)S(1)}, u32[]{:S(2)}, u32[]{:S(2)}) collective-permute-start(bf16[16,18,1,128]{3,0,2,1:T(8,128)(2,1)S(1)} %get-tuple-element.38), channel_id=1, source_target_pairs={{0,7},{1,0},{2,1},{3,2},{4,3},{5,4},{6,5},{7,6},{8,15},{9,8},{10,9... | collective-permute-start | bytes 221192 | tf_op jit(solution)/shard_map/ppermute | solution.py:58
  21.4 0.7 copy-start.4
  23.6 4.4 %collective-permute-start.4 = (f32[4,4,16,128]{3,0,2,1:T(4,128)S(1)}, f32[4,4,16,128]{3,0,2,1:T(4,128)S(1)}, u32[]{:S(2)}, u32[]{:S(2)}) collective-permute-start(f32[4,4,16,128]{3,0,2,1:T(4,128)S(1)} %get-tuple-element.43), channel_id=1, source_target_pairs={{0,8},{8,16},{16,24},{24,0},{1,9},{9,17},{17,25},{25,1},{2,10},{10... | collective-permute-start | bytes 393224 | tf_op jit(solution)/shard_map/ppermute | solution.py:58
  23.7 5.0 %collective-permute-start.5 = (f32[4,4,16,128]{3,0,2,1:T(4,128)S(1)}, f32[4,4,16,128]{3,0,2,1:T(4,128)S(1)}, u32[]{:S(2)}, u32[]{:S(2)}) collective-permute-start(f32[4,4,16,128]{3,0,2,1:T(4,128)S(1)} %get-tuple-element.44), channel_id=1, source_target_pairs={{0,24},{8,0},{16,8},{24,16},{1,25},{9,1},{17,9},{25,17},{2,26},{10... | collective-permute-start | bytes 393224 | tf_op jit(solution)/shard_map/ppermute | solution.py:58
  28.9 10.0 %collective-permute-start.6 = (f32[4,22,4,128]{3,0,2,1:T(4,128)S(1)}, f32[4,22,4,128]{3,0,2,1:T(4,128)S(1)}, u32[]{:S(2)}, u32[]{:S(2)}) collective-permute-start(f32[4,22,4,128]{3,0,2,1:T(4,128)S(1)} %get-tuple-element.41), channel_id=1, source_target_pairs={{0,1},{1,2},{2,3},{3,4},{4,5},{5,6},{6,7},{7,0},{8,9},{9,10},{10,1... | collective-permute-start | bytes 540680 | tf_op jit(solution)/shard_map/ppermute | solution.py:58
  29.8 11.5 %collective-permute-start.7 = (f32[4,22,4,128]{3,0,2,1:T(4,128)S(1)}, f32[4,22,4,128]{3,0,2,1:T(4,128)S(1)}, u32[]{:S(2)}, u32[]{:S(2)}) collective-permute-start(f32[4,22,4,128]{3,0,2,1:T(4,128)S(1)} %get-tuple-element.42), channel_id=1, source_target_pairs={{0,7},{1,0},{2,1},{3,2},{4,3},{5,4},{6,5},{7,6},{8,15},{9,8},{10,9... | collective-permute-start | bytes 540680 | tf_op jit(solution)/shard_map/ppermute | solution.py:58
  49.4 2.5 %copy-start = (f32[8,20,20,128]{3,2,1,0:T(8,128)}, f32[8,20,20,128]{3,2,1,0:T(8,128)S(1)}, u32[]{:S(2)}) copy-start(f32[8,20,20,128]{3,2,1,0:T(8,128)S(1)} %fusion.10) | copy-start | bytes 4915204
  51.5 1.2 %copy-start.1 = (f32[8,18,18,128]{3,2,1,0:T(8,128)}, f32[8,18,18,128]{3,2,1,0:T(8,128)S(1)}, u32[]{:S(2)}) copy-start(f32[8,18,18,128]{3,2,1,0:T(8,128)S(1)} %fusion.16) | copy-start | bytes 3981316
  55.0 1.2 %collective-permute-start.8 = (f32[9,8]{1,0:T(8,128)S(1)}, f32[9,8]{1,0:T(8,128)S(1)}, u32[]{:S(2)}, u32[]{:S(2)}) collective-permute-start(f32[9,8]{1,0:T(8,128)S(1)} %stack.55), channel_id=1, source_target_pairs={{0,8},{8,0},{16,24},{24,16},{1,9},{9,1},{17,25},{25,17},{2,10},{10... | collective-permute-start | bytes 872 | tf_op jit(solution)/shard_map/ppermute | solution.py:131
  56.3 3.7 %collective-permute-start.9 = (f32[9,8]{1,0:T(8,128)S(1)}, f32[9,8]{1,0:T(8,128)S(1)}, u32[]{:S(2)}, u32[]{:S(2)}) collective-permute-start(f32[9,8]{1,0:T(8,128)S(1)} %add.592), channel_id=1, source_target_pairs={{0,16},{8,24},{16,0},{24,8},{1,17},{9,25},{17,1},{25,9},{2,18},{10... | collective-permute-start | bytes 872 | tf_op jit(solution)/shard_map/ppermute | solution.py:131
  59.9 3.7 %collective-permute-start.10 = (f32[9,8]{1,0:T(8,128)S(1)}, f32[9,8]{1,0:T(8,128)S(1)}, u32[]{:S(2)}, u32[]{:S(2)}) collective-permute-start(f32[9,8]{1,0:T(8,128)S(1)} %add.593), channel_id=1, source_target_pairs={{0,1},{1,0},{2,3},{3,2},{4,5},{5,4},{6,7},{7,6},{8,9},{9,8},{10,11... | collective-permute-start | bytes 872 | tf_op jit(solution)/shard_map/ppermute | solution.py:131
  63.6 3.7 %collective-permute-start.11 = (f32[9,8]{1,0:T(8,128)S(1)}, f32[9,8]{1,0:T(8,128)S(1)}, u32[]{:S(2)}, u32[]{:S(2)}) collective-permute-start(f32[9,8]{1,0:T(8,128)S(1)} %add.594), channel_id=1, source_target_pairs={{0,2},{1,3},{2,0},{3,1},{4,6},{5,7},{6,4},{7,5},{8,10},{9,11},{10,... | collective-permute-start | bytes 872 | tf_op jit(solution)/shard_map/ppermute | solution.py:131
  67.2 4.6 %collective-permute-start.12 = (f32[9,8]{1,0:T(8,128)S(1)}, f32[9,8]{1,0:T(8,128)S(1)}, u32[]{:S(2)}, u32[]{:S(2)}) collective-permute-start(f32[9,8]{1,0:T(8,128)S(1)} %add.595), channel_id=1, source_target_pairs={{0,4},{1,5},{2,6},{3,7},{4,0},{5,1},{6,2},{7,3},{8,12},{9,13},{10,... | collective-permute-start | bytes 872 | tf_op jit(solution)/shard_map/ppermute | solution.py:131

commit v12 on v11

--- a/solution.py
+++ b/solution.py
@@ -61,20 +61,23 @@
     return jnp.where(inside, moved, jnp.zeros_like(moved))
 
 
-def extend(cells, width, corner=None):
+def extend(cells, width, corner=None, order=(("gz", 1), ("yx", 2))):
     corner = width if corner is None else corner
-    for axis, dim in (("gz", 1), ("yx", 2)):
+    for step, (axis, dim) in enumerate(order):
         source = cells
         trim = 0
-        if dim == 2 and corner < width:
+        if step == 1 and corner < width:
             trim = width - corner
-            source = cells[:, trim : cells.shape[1] - trim]
+            other = order[0][1]
+            source = lax.slice_in_dim(cells, trim, cells.shape[other] - trim, axis=other)
         size = source.shape[dim]
         head = lax.slice_in_dim(source, 0, width, axis=dim)
         tail = lax.slice_in_dim(source, size - width, size, axis=dim)
         edges = [from_ring(tail, axis, 1), from_ring(head, axis, -1)]
         if trim:
-            edges = [jnp.pad(edge, ((0, 0), (trim, trim), (0, 0), (0, 0))) for edge in edges]
+            pads = [(0, 0)] * 4
+            pads[other] = (trim, trim)
+            edges = [jnp.pad(edge, pads) for edge in edges]
         cells = jnp.concatenate([edges[0], cells, edges[1]], axis=dim)
     return cells
 
@@ -156,7 +159,7 @@
     )
     halo = ITERS + 1
     stacked = jnp.concatenate([affinities, labels[None].astype(jnp.float32)], axis=0)
-    grid_cells = extend(stacked, halo, halo - 1)
+    grid_cells = extend(stacked, halo, halo - 1, (("yx", 2), ("gz", 1)))
     cells_z = depth_cells + 2 * halo
     cells_y = row_cells + 2 * halo
     grid_z = lax.axis_index("gz") * depth_cells - halo + jnp.arange(cells_z, dtype=jnp.int32)

time: 75.5 us -> 73.1 us (0.968)
  waiting for transfers between devices: 29.2 us -> 23.2 us
  starting transfers between devices: 17.5 us -> 21.1 us
    ppermute x5, starting transfers between devices: 3.35 us -> 6.82 us  [all_sum(): lax.ppermute(value, axis, [(i, i ^ hop) for i in range(devices)])]
    ppermute x8, waiting for transfers between devices: 16.5 us -> 13.5 us  [from_ring(): lax.ppermute(value, axis, [(i, (i + by) % devices) for i in range(devices)])]
    ppermute x5, waiting for transfers between devices: 12.7 us -> 9.69 us  [all_sum(): lax.ppermute(value, axis, [(i, i ^ hop) for i in range(devices)])]
  transfers between devices with their start and end apart: 13 -> 13, of which waited for: 12 -> 11; matrix products, arithmetic and copies ran while one was open for 1% -> 1% of each run, Pallas kernels for 0% -> 0%
where the time goes in v12:
time: 73.1 us; the launch traced here: 73 us
  waiting for transfers between devices  23.2 us (32%)
  starting transfers between devices  21.1 us (29%)
  other arithmetic  13.2 us (18%)
  local copies, waits for them, and re-layouts  8.18 us (11%)
  matrix products  6.15 us (8%)
  between operations  1.14 us (2%)
    ppermute x8, starting transfers between devices, from_ring(): lax.ppermute(value, axis, [(i, (i + by) % devices) for i in range(devices)])  14.2 us
    ppermute x8, waiting for transfers between devices, from_ring(): lax.ppermute(value, axis, [(i, (i + by) % devices) for i in range(devices)])  13.5 us
    ppermute x5, waiting for transfers between devices, all_sum(): lax.ppermute(value, axis, [(i, i ^ hop) for i in range(devices)])  9.69 us
    ppermute x5, starting transfers between devices, all_sum(): lax.ppermute(value, axis, [(i, i ^ hop) for i in range(devices)])  6.82 us
    dot_general x9, matrix products, conv_region(): jnp.einsum('oce,cezyx->ozyx', conv_weight[:, :, offset_z, offset_y, :], w...  6.15 us
    unnamed x12, local copies, waits for them, and re-layouts  3.64 us
    add x1, other arithmetic, body(): probabilities = probabilities + coeff[:, None, None, None] * vector  3.39 us
    sub x2, other arithmetic, operate_inside(): return diagonal[part, part] * centre - coupled  3.29 us
  transfers between devices with their start and end apart: 13, of which 11 were waited for; matrix products, arithmetic and copies ran while one was open for 1% of the time, Pallas kernels for 0%

profile of v12, /device:TPU:0, one launch (start us, length us, event | category | flops | bytes accessed | tf_op | source)
XLA Modules:
  0.0 73.0 jit_solution(8995675630995342129)
XLA Ops:
  0.6 0.0 copy-start.3
  0.6 1.9 %copy.6 = bf16[16,16,16,128]{3,0,2,1:T(8,128)(2,1)S(1)} copy(bf16[16,16,16,128]{3,2,1,0:T(8,128)(2,1)} %param.4) | data formatting | bytes 2097152 | tf_op args[0]
  2.6 2.5 %collective-permute-start.1 = (bf16[16,1,16,128]{3,0,2,1:T(8,128)(2,1)S(1)}, bf16[16,1,16,128]{3,0,2,1:T(8,128)(2,1)S(1)}, u32[]{:S(2)}, u32[]{:S(2)}) collective-permute-start(bf16[16,1,16,128]{3,0,2,1:T(8,128)(2,1)S(1)} %get-tuple-element.40), channel_id=1, source_target_pairs={{0,24},{8,0},{16,8},{24,16},{1,25},{9,1},{17,9},{25,17},{2,26},{10... | collective-permute-start | bytes 196616 | tf_op jit(solution)/shard_map/ppermute | solution.py:58
  5.1 0.0 collective-permute-start
  5.1 2.4 %collective-permute-done.1 = bf16[16,1,16,128]{3,0,2,1:T(8,128)(2,1)S(1)} collective-permute-done((bf16[16,1,16,128]{3,0,2,1:T(8,128)(2,1)S(1)}, bf16[16,1,16,128]{3,0,2,1:T(8,128)(2,1)S(1)}, u32[]{:S(2)}, u32[]{:S(2)}) %collective-permute-start.1) | collective-permute-done | bytes 65568 | tf_op jit(solution)/shard_map/ppermute | solution.py:58
  7.5 1.2 %collective-permute-done = bf16[16,1,16,128]{3,0,2,1:T(8,128)(2,1)S(1)} collective-permute-done((bf16[16,1,16,128]{3,0,2,1:T(8,128)(2,1)S(1)}, bf16[16,1,16,128]{3,0,2,1:T(8,128)(2,1)S(1)}, u32[]{:S(2)}, u32[]{:S(2)}) %collective-permute-start) | collective-permute-done | bytes 65568 | tf_op jit(solution)/shard_map/ppermute | solution.py:58
  8.8 1.6 %collective-permute-start.2 = (bf16[16,18,1,128]{3,0,2,1:T(8,128)(2,1)S(1)}, bf16[16,18,1,128]{3,0,2,1:T(8,128)(2,1)S(1)}, u32[]{:S(2)}, u32[]{:S(2)}) collective-permute-start(bf16[16,18,1,128]{3,0,2,1:T(8,128)(2,1)S(1)} %get-tuple-element.37), channel_id=1, source_target_pairs={{0,1},{1,2},{2,3},{3,4},{4,5},{5,6},{6,7},{7,0},{8,9},{9,10},{10,1... | collective-permute-start | bytes 221192 | tf_op jit(solution)/shard_map/ppermute | solution.py:58
  10.4 0.0 copy-done.2
  10.4 3.3 %collective-permute-start.3 = (bf16[16,18,1,128]{3,0,2,1:T(8,128)(2,1)S(1)}, bf16[16,18,1,128]{3,0,2,1:T(8,128)(2,1)S(1)}, u32[]{:S(2)}, u32[]{:S(2)}) collective-permute-start(bf16[16,18,1,128]{3,0,2,1:T(8,128)(2,1)S(1)} %get-tuple-element.38), channel_id=1, source_target_pairs={{0,7},{1,0},{2,1},{3,2},{4,3},{5,4},{6,5},{7,6},{8,15},{9,8},{10,9... | collective-permute-start | bytes 221192 | tf_op jit(solution)/shard_map/ppermute | solution.py:58
  13.7 2.2 %collective-permute-done.2 = bf16[16,18,1,128]{3,0,2,1:T(8,128)(2,1)S(1)} collective-permute-done((bf16[16,18,1,128]{3,0,2,1:T(8,128)(2,1)S(1)}, bf16[16,18,1,128]{3,0,2,1:T(8,128)(2,1)S(1)}, u32[]{:S(2)}, u32[]{:S(2)}) %collective-permute-start.2) | collective-permute-done | bytes 73760 | tf_op jit(solution)/shard_map/ppermute | solution.py:58
  15.9 0.0 collective-permute-done.3
  16.0 0.3 pad_maximum_fusion.1
  16.2 0.3 fusion.78
  16.5 0.8 %fusion.19 = (bf16[16,1,18,18,128]{4,0,1,3,2:T(8,128)(2,1)S(1)}, bf16[16,1,18,18,128]{4,0,1,3,2:T(8,128)(2,1)S(1)}) fusion(bf16[16,18,18,128]{3,0,2,1:T(8,128)(2,1)S(1)} %pad_maximum_fusion.1), kind=kLoop, calls=%fused_computation.37 | loop fusion | bytes 3981312 | tf_op jit(solution)/shard_map/stack | solution.py:38
  17.2 0.6 convolution_bitcast_fusion.7
  17.8 0.6 convolution_bitcast_fusion.6
  18.4 0.6 convolution_bitcast_fusion.5
  19.0 0.6 convolution_bitcast_fusion.4
  19.6 0.6 convolution_bitcast_fusion.3
  20.2 0.6 convolution_bitcast_fusion.2
  20.8 0.6 convolution_bitcast_fusion.1
  21.4 0.6 convolution_bitcast_fusion
  21.9 0.1 copy-done.4
  22.0 1.5 %fusion.34 = f32[3,16,16,128]{3,0,2,1:T(4,128)S(1)} fusion(f32[16,16,128,3]{2,3,1,0:T(4,128)S(1)} %convolution_bitcast_fusion, f32[16,16,128,3]{2,3,1,0:T(4,128)S(1)} %convolution_bitcast_fusion.1, f32[16,16,128,3]{2,3,1,0:T(4,128)S(1)} %convolution_bitcast_fusion.2, f32[16,16,128,3]{2,3,1,0:T(4,128)S(1)} %convolution_bitcast_fusion.3, ...), kind=kOutput, calls=%fused_computation.66 | convolution fusion | flops 22560768 | bytes 7520556 | tf_op jit(solution)/shard_map/oce,cezyx->ozyx/dot_general | solution.py:47
  23.5 0.1 pad_maximum_fusion.7
  23.6 1.4 %collective-permute-start.4 = (f32[4,16,4,128]{3,0,2,1:T(4,128)S(1)}, f32[4,16,4,128]{3,0,2,1:T(4,128)S(1)}, u32[]{:S(2)}, u32[]{:S(2)}) collective-permute-start(f32[4,16,4,128]{3,0,2,1:T(4,128)S(1)} %get-tuple-element.43), channel_id=1, source_target_pairs={{0,1},{1,2},{2,3},{3,4},{4,5},{5,6},{6,7},{7,0},{8,9},{9,10},{10,1... | collective-permute-start | bytes 393224 | tf_op jit(solution)/shard_map/ppermute | solution.py:58
  25.0 3.6 %collective-permute-start.5 = (f32[4,16,4,128]{3,0,2,1:T(4,128)S(1)}, f32[4,16,4,128]{3,0,2,1:T(4,128)S(1)}, u32[]{:S(2)}, u32[]{:S(2)}) collective-permute-start(f32[4,16,4,128]{3,0,2,1:T(4,128)S(1)} %get-tuple-element.44), channel_id=1, source_target_pairs={{0,7},{1,0},{2,1},{3,2},{4,3},{5,4},{6,5},{7,6},{8,15},{9,8},{10,9... | collective-permute-start | bytes 393224 | tf_op jit(solution)/shard_map/ppermute | solution.py:58
  28.6 2.8 %collective-permute-done.4 = f32[4,16,4,128]{3,0,2,1:T(4,128)S(1)} collective-permute-done((f32[4,16,4,128]{3,0,2,1:T(4,128)S(1)}, f32[4,16,4,128]{3,0,2,1:T(4,128)S(1)}, u32[]{:S(2)}, u32[]{:S(2)}) %collective-permute-start.4) | collective-permute-done | bytes 131104 | tf_op jit(solution)/shard_map/ppermute | solution.py:58
  31.5 0.0 collective-permute-done.5
  31.5 0.1 pad_maximum_fusion.5
  31.7 0.1 collective-permute-start.6
  31.8 2.0 %collective-permute-start.7 = (f32[4,4,22,128]{3,0,2,1:T(4,128)S(1)}, f32[4,4,22,128]{3,0,2,1:T(4,128)S(1)}, u32[]{:S(2)}, u32[]{:S(2)}) collective-permute-start(f32[4,4,22,128]{3,0,2,1:T(4,128)S(1)} %get-tuple-element.42), channel_id=1, source_target_pairs={{0,24},{8,0},{16,8},{24,16},{1,25},{9,1},{17,9},{25,17},{2,26},{10... | collective-permute-start | bytes 540680 | tf_op jit(solution)/shard_map/ppermute | solution.py:58
  33.7 2.9 %collective-permute-done.6 = f32[4,4,22,128]{3,0,2,1:T(4,128)S(1)} collective-permute-done((f32[4,4,22,128]{3,0,2,1:T(4,128)S(1)}, f32[4,4,22,128]{3,0,2,1:T(4,128)S(1)}, u32[]{:S(2)}, u32[]{:S(2)}) %collective-permute-start.6) | collective-permute-done | bytes 180256 | tf_op jit(solution)/shard_map/ppermute | solution.py:58
  36.7 1.8 %collective-permute-done.7 = f32[4,4,22,128]{3,0,2,1:T(4,128)S(1)} collective-permute-done((f32[4,4,22,128]{3,0,2,1:T(4,128)S(1)}, f32[4,4,22,128]{3,0,2,1:T(4,128)S(1)}, u32[]{:S(2)}, u32[]{:S(2)}) %collective-permute-start.7) | collective-permute-done | bytes 180256 | tf_op jit(solution)/shard_map/ppermute | solution.py:58
  38.6 0.3 select_maximum_fusion
  38.9 0.9 %fusion.75 = (f32[1,24,24,128]{3,0,2,1:T(1,128)S(1)}, f32[1,24,24,128]{3,0,2,1:T(1,128)S(1)}, f32[1,24,24,128]{3,0,2,1:T(1,128)S(1)}, f32[1,24,24,128]{3,0,2,1:T(1,128)S(1)}) fusion(f32[4,24,24,128]{3,0,2,1:T(4,128)S(1)} %select_maximum_fusion), kind=kLoop, calls=%fused_computation.179 | loop fusion | bytes 2359296 | tf_op jit(solution)/shard_map/slice | solution.py:171
  39.8 0.1 broadcast_multiply_fusion
  39.9 0.2 convert_add_fusion
  40.1 0.2 fusion.46
  40.8 0.2 compare_convert_fusion
  41.1 0.8 %fusion.71 = (f32[8,22,22,127]{3,2,1,0:T(8,128)S(1)}, f32[8,22,22,127]{3,2,1,0:T(8,128)S(1)}) fusion(f32[8,24,24,128]{3,2,1,0:T(8,128)S(1)} %compare_convert_fusion), kind=kLoop, calls=%fused_computation.175 | loop fusion | bytes 7867904 | tf_op jit(solution)/shard_map/slice | solution.py:117
  41.8 2.1 %fusion.4 = f32[8,22,22,128]{3,2,1,0:T(8,128)S(1)} fusion(f32[8,24,24,128]{3,2,1,0:T(8,128)S(1)} %compare_convert_fusion, f32[8,22,22,127]{3,2,1,0:T(8,128)S(1)} %get-tuple-element.24, f32[8,22,22,127]{3,2,1,0:T(8,128)S(1)} %get-tuple-element.23, f32[22,22,128]{2,1,0:T(8,128)S(1)} %get-tuple-element.53, f32[22,22,128]{2,1,0:T(8,128)S(1)} %get-tuple-element.54, ...), kind=kLoop, calls=%fused_computation.9 | loop fusion | flops 6938624 | bytes 17563392 | tf_op jit(solution)/shard_map/sub | solution.py:182
  43.9 0.7 fusion.72
  44.7 1.8 %fusion.10 = f32[8,20,20,128]{3,2,1,0:T(8,128)S(1)} fusion(f32[8,22,22,128]{3,2,1,0:T(8,128)S(1)} %fusion.4, f32[8,20,20,127]{3,2,1,0:T(8,128)S(1)} %get-tuple-element.26, f32[8,20,20,127]{3,2,1,0:T(8,128)S(1)} %get-tuple-element.25, f32[20,20,128]{2,1,0:T(8,128)S(1)} %slice.449, f32[20,20,128]{2,1,0:T(8,128)S(1)} %slice.447, f32[20,20,128]{2,1,0:T(8,128)S(1)} %slice.445, ...), kind=kLoop, calls=%fused_computation.19 | loop fusion | flops 5324800 | bytes 14515200 | tf_op jit(solution)/shard_map/sub | solution.py:123
  46.5 0.0 copy-start
  46.5 0.6 fusion.73
  47.2 1.4 %fusion.16 = f32[8,18,18,128]{3,2,1,0:T(8,128)S(1)} fusion(f32[8,20,20,128]{3,2,1,0:T(8,128)S(1)} %fusion.10, f32[8,18,18,127]{3,2,1,0:T(8,128)S(1)} %get-tuple-element.28, f32[8,18,18,127]{3,2,1,0:T(8,128)S(1)} %get-tuple-element.27, f32[18,18,128]{2,1,0:T(8,128)S(1)} %slice.464, f32[18,18,128]{2,1,0:T(8,128)S(1)} %slice.462, ...), kind=kLoop, calls=%fused_computation.30 | loop fusion | flops 4313088 | bytes 11757312 | tf_op jit(solution)/shard_map/sub | solution.py:123
  48.6 0.0 copy-start.1
  48.6 0.4 fusion.74
  49.0 0.0 copy-done
  49.0 0.8 %copy-done.1 = f32[8,18,18,128]{3,2,1,0:T(8,128)} copy-done((f32[8,18,18,128]{3,2,1,0:T(8,128)}, f32[8,18,18,128]{3,2,1,0:T(8,128)S(1)}, u32[]{:S(2)}) %copy-start.1) | copy-done | bytes 1327128
  49.8 2.3 %multiply_reduce_fusion.5 = (f32[8]{0:T(128)S(1)}, f32[8]{0:T(128)S(1)}, f32[8]{0:T(128)S(1)}, f32[8]{0:T(128)S(1)}, f32[8]{0:T(128)S(1)}, /*index=5*/f32[8]{0:T...) fusion(f32[8,22,22,128]{3,2,1,0:T(8,128)S(1)} %fusion.4, f32[8,20,20,128]{3,2,1,0:T(8,128)S(1)} %fusion.10, ...), kind=kLoop, calls=%fused_computation.83 | loop fusion | flops 8126392 | bytes 10338592 | tf_op jit(solution)/shard_map/reduce_sum | solution.py:140
  52.2 1.0 %collective-permute-start.8 = (f32[9,8]{1,0:T(8,128)S(1)}, f32[9,8]{1,0:T(8,128)S(1)}, u32[]{:S(2)}, u32[]{:S(2)}) collective-permute-start(f32[9,8]{1,0:T(8,128)S(1)} %stack.55), channel_id=1, source_target_pairs={{0,8},{8,0},{16,24},{24,16},{1,9},{9,1},{17,25},{25,17},{2,10},{10... | collective-permute-start | bytes 872 | tf_op jit(solution)/shard_map/ppermute | solution.py:134
  53.1 0.8 %collective-permute-done.8 = f32[9,8]{1,0:T(8,128)S(1)} collective-permute-done((f32[9,8]{1,0:T(8,128)S(1)}, f32[9,8]{1,0:T(8,128)S(1)}, u32[]{:S(2)}, u32[]{:S(2)}) %collective-permute-start.8) | collective-permute-done | bytes 320 | tf_op jit(solution)/shard_map/ppermute | solution.py:134
  54.0 1.8 %collective-permute-start.9 = (f32[9,8]{1,0:T(8,128)S(1)}, f32[9,8]{1,0:T(8,128)S(1)}, u32[]{:S(2)}, u32[]{:S(2)}) collective-permute-start(f32[9,8]{1,0:T(8,128)S(1)} %add.592), channel_id=1, source_target_pairs={{0,16},{8,24},{16,0},{24,8},{1,17},{9,25},{17,1},{25,9},{2,18},{10... | collective-permute-start | bytes 872 | tf_op jit(solution)/shard_map/ppermute | solution.py:134
  55.8 1.8 %collective-permute-done.9 = f32[9,8]{1,0:T(8,128)S(1)} collective-permute-done((f32[9,8]{1,0:T(8,128)S(1)}, f32[9,8]{1,0:T(8,128)S(1)}, u32[]{:S(2)}, u32[]{:S(2)}) %collective-permute-start.9) | collective-permute-done | bytes 320 | tf_op jit(solution)/shard_map/ppermute | solution.py:134
  57.6 0.2 collective-permute-start.10
  57.8 3.5 %collective-permute-done.10 = f32[9,8]{1,0:T(8,128)S(1)} collective-permute-done((f32[9,8]{1,0:T(8,128)S(1)}, f32[9,8]{1,0:T(8,128)S(1)}, u32[]{:S(2)}, u32[]{:S(2)}) %collective-permute-start.10) | collective-permute-done | bytes 320 | tf_op jit(solution)/shard_map/ppermute | solution.py:134
  61.3 1.4 %collective-permute-start.11 = (f32[9,8]{1,0:T(8,128)S(1)}, f32[9,8]{1,0:T(8,128)S(1)}, u32[]{:S(2)}, u32[]{:S(2)}) collective-permute-start(f32[9,8]{1,0:T(8,128)S(1)} %add.594), channel_id=1, source_target_pairs={{0,2},{1,3},{2,0},{3,1},{4,6},{5,7},{6,4},{7,5},{8,10},{9,11},{10,... | collective-permute-start | bytes 872 | tf_op jit(solution)/shard_map/ppermute | solution.py:134
  62.7 2.2 %collective-permute-done.11 = f32[9,8]{1,0:T(8,128)S(1)} collective-permute-done((f32[9,8]{1,0:T(8,128)S(1)}, f32[9,8]{1,0:T(8,128)S(1)}, u32[]{:S(2)}, u32[]{:S(2)}) %collective-permute-start.11) | collective-permute-done | bytes 320 | tf_op jit(solution)/shard_map/ppermute | solution.py:134
  64.9 2.4 %collective-permute-start.12 = (f32[9,8]{1,0:T(8,128)S(1)}, f32[9,8]{1,0:T(8,128)S(1)}, u32[]{:S(2)}, u32[]{:S(2)}) collective-permute-start(f32[9,8]{1,0:T(8,128)S(1)} %add.595), channel_id=1, source_target_pairs={{0,4},{1,5},{2,6},{3,7},{4,0},{5,1},{6,2},{7,3},{8,12},{9,13},{10,... | collective-permute-start | bytes 872 | tf_op jit(solution)/shard_map/ppermute | solution.py:134
  67.4 0.8 %copy.23 = f32[3,16,16,128]{3,2,1,0:T(8,128)} copy(f32[3,16,16,128]{3,0,2,1:T(4,128)S(1)} %fusion.34) | data formatting | bytes 786432
  68.1 1.3 %collective-permute-done.12 = f32[9,8]{1,0:T(8,128)S(1)} collective-permute-done((f32[9,8]{1,0:T(8,128)S(1)}, f32[9,8]{1,0:T(8,128)S(1)}, u32[]{:S(2)}, u32[]{:S(2)}) %collective-permute-start.12) | collective-permute-done | bytes 320 | tf_op jit(solution)/shard_map/ppermute | solution.py:134
  69.6 3.4 %multiply_add_fusion = f32[8,16,16,128]{3,2,1,0:T(8,128)} fusion(f32[8,20,20,128]{3,2,1,0:T(8,128)} %copy-done, f32[8,22,22,128]{3,2,1,0:T(8,128)S(1)} %fusion.4, f32[8,18,18,128]{3,2,1,0:T(8,128)} %copy-done.1, f32[8]{0:T(128)S(1)} %get-tuple-element.65, f32[8]{0:T(128)S(1)} %get-tuple-element.64, f32[8]{0:T(128)S(1)} %get-tuple-element.13, ...), kind=kLoop, calls=%fused_computation.77 | loop fusion | flops 2097152 | bytes 4325504 | tf_op jit(solution)/shard_map/add | solution.py:246
  (51 shorter events, 0.8 us)
Async XLA Ops:
  0.6 9.7 %copy-start.3 = (bf16[3,16,3,3,3]{1,4,3,2,0:T(4,128)(2,1)S(1)}, bf16[3,16,3,3,3]{1,4,3,2,0:T(4,128)(2,1)}, u32[]{:S(2)}) copy-start(bf16[3,16,3,3,3]{1,4,3,2,0:T(4,128)(2,1)} %param.5) | copy-start | bytes 7780
  0.6 9.8 %copy-start.2 = (s32[16,16,128]{2,1,0:T(8,128)S(1)}, s32[16,16,128]{2,1,0:T(8,128)}, u32[]{:S(2)}) copy-start(s32[16,16,128]{2,1,0:T(8,128)} %param.7) | copy-start | bytes 393220
  2.6 4.9 %collective-permute-start.1 = (bf16[16,1,16,128]{3,0,2,1:T(8,128)(2,1)S(1)}, bf16[16,1,16,128]{3,0,2,1:T(8,128)(2,1)S(1)}, u32[]{:S(2)}, u32[]{:S(2)}) collective-permute-start(bf16[16,1,16,128]{3,0,2,1:T(8,128)(2,1)S(1)} %get-tuple-element.40), channel_id=1, source_target_pairs={{0,24},{8,0},{16,8},{24,16},{1,25},{9,1},{17,9},{25,17},{2,26},{10... | collective-permute-start | bytes 196616 | tf_op jit(solution)/shard_map/ppermute | solution.py:58
  5.1 3.7 %collective-permute-start = (bf16[16,1,16,128]{3,0,2,1:T(8,128)(2,1)S(1)}, bf16[16,1,16,128]{3,0,2,1:T(8,128)(2,1)S(1)}, u32[]{:S(2)}, u32[]{:S(2)}) collective-permute-start(bf16[16,1,16,128]{3,0,2,1:T(8,128)(2,1)S(1)} %get-tuple-element.39), channel_id=1, source_target_pairs={{0,8},{8,16},{16,24},{24,0},{1,9},{9,17},{17,25},{25,1},{2,10},{10... | collective-permute-start | bytes 196616 | tf_op jit(solution)/shard_map/ppermute | solution.py:58
  8.8 7.1 %collective-permute-start.2 = (bf16[16,18,1,128]{3,0,2,1:T(8,128)(2,1)S(1)}, bf16[16,18,1,128]{3,0,2,1:T(8,128)(2,1)S(1)}, u32[]{:S(2)}, u32[]{:S(2)}) collective-permute-start(bf16[16,18,1,128]{3,0,2,1:T(8,128)(2,1)S(1)} %get-tuple-element.37), channel_id=1, source_target_pairs={{0,1},{1,2},{2,3},{3,4},{4,5},{5,6},{6,7},{7,0},{8,9},{9,10},{10,1... | collective-permute-start | bytes 221192 | tf_op jit(solution)/shard_map/ppermute | solution.py:58
  10.4 5.5 %collective-permute-start.3 = (bf16[16,18,1,128]{3,0,2,1:T(8,128)(2,1)S(1)}, bf16[16,18,1,128]{3,0,2,1:T(8,128)(2,1)S(1)}, u32[]{:S(2)}, u32[]{:S(2)}) collective-permute-start(bf16[16,18,1,128]{3,0,2,1:T(8,128)(2,1)S(1)} %get-tuple-element.38), channel_id=1, source_target_pairs={{0,7},{1,0},{2,1},{3,2},{4,3},{5,4},{6,5},{7,6},{8,15},{9,8},{10,9... | collective-permute-start | bytes 221192 | tf_op jit(solution)/shard_map/ppermute | solution.py:58
  21.4 0.7 copy-start.4
  23.6 7.8 %collective-permute-start.4 = (f32[4,16,4,128]{3,0,2,1:T(4,128)S(1)}, f32[4,16,4,128]{3,0,2,1:T(4,128)S(1)}, u32[]{:S(2)}, u32[]{:S(2)}) collective-permute-start(f32[4,16,4,128]{3,0,2,1:T(4,128)S(1)} %get-tuple-element.43), channel_id=1, source_target_pairs={{0,1},{1,2},{2,3},{3,4},{4,5},{5,6},{6,7},{7,0},{8,9},{9,10},{10,1... | collective-permute-start | bytes 393224 | tf_op jit(solution)/shard_map/ppermute | solution.py:58
  25.0 6.5 %collective-permute-start.5 = (f32[4,16,4,128]{3,0,2,1:T(4,128)S(1)}, f32[4,16,4,128]{3,0,2,1:T(4,128)S(1)}, u32[]{:S(2)}, u32[]{:S(2)}) collective-permute-start(f32[4,16,4,128]{3,0,2,1:T(4,128)S(1)} %get-tuple-element.44), channel_id=1, source_target_pairs={{0,7},{1,0},{2,1},{3,2},{4,3},{5,4},{6,5},{7,6},{8,15},{9,8},{10,9... | collective-permute-start | bytes 393224 | tf_op jit(solution)/shard_map/ppermute | solution.py:58
  31.7 5.0 %collective-permute-start.6 = (f32[4,4,22,128]{3,0,2,1:T(4,128)S(1)}, f32[4,4,22,128]{3,0,2,1:T(4,128)S(1)}, u32[]{:S(2)}, u32[]{:S(2)}) collective-permute-start(f32[4,4,22,128]{3,0,2,1:T(4,128)S(1)} %get-tuple-element.41), channel_id=1, source_target_pairs={{0,8},{8,16},{16,24},{24,0},{1,9},{9,17},{17,25},{25,1},{2,10},{10... | collective-permute-start | bytes 540680 | tf_op jit(solution)/shard_map/ppermute | solution.py:58
  31.8 6.8 %collective-permute-start.7 = (f32[4,4,22,128]{3,0,2,1:T(4,128)S(1)}, f32[4,4,22,128]{3,0,2,1:T(4,128)S(1)}, u32[]{:S(2)}, u32[]{:S(2)}) collective-permute-start(f32[4,4,22,128]{3,0,2,1:T(4,128)S(1)} %get-tuple-element.42), channel_id=1, source_target_pairs={{0,24},{8,0},{16,8},{24,16},{1,25},{9,1},{17,9},{25,17},{2,26},{10... | collective-permute-start | bytes 540680 | tf_op jit(solution)/shard_map/ppermute | solution.py:58
  46.5 2.5 %copy-start = (f32[8,20,20,128]{3,2,1,0:T(8,128)}, f32[8,20,20,128]{3,2,1,0:T(8,128)S(1)}, u32[]{:S(2)}) copy-start(f32[8,20,20,128]{3,2,1,0:T(8,128)S(1)} %fusion.10) | copy-start | bytes 4915204
  48.6 1.2 %copy-start.1 = (f32[8,18,18,128]{3,2,1,0:T(8,128)}, f32[8,18,18,128]{3,2,1,0:T(8,128)S(1)}, u32[]{:S(2)}) copy-start(f32[8,18,18,128]{3,2,1,0:T(8,128)S(1)} %fusion.16) | copy-start | bytes 3981316
  52.2 1.8 %collective-permute-start.8 = (f32[9,8]{1,0:T(8,128)S(1)}, f32[9,8]{1,0:T(8,128)S(1)}, u32[]{:S(2)}, u32[]{:S(2)}) collective-permute-start(f32[9,8]{1,0:T(8,128)S(1)} %stack.55), channel_id=1, source_target_pairs={{0,8},{8,0},{16,24},{24,16},{1,9},{9,1},{17,25},{25,17},{2,10},{10... | collective-permute-start | bytes 872 | tf_op jit(solution)/shard_map/ppermute | solution.py:134
  54.0 3.7 %collective-permute-start.9 = (f32[9,8]{1,0:T(8,128)S(1)}, f32[9,8]{1,0:T(8,128)S(1)}, u32[]{:S(2)}, u32[]{:S(2)}) collective-permute-start(f32[9,8]{1,0:T(8,128)S(1)} %add.592), channel_id=1, source_target_pairs={{0,16},{8,24},{16,0},{24,8},{1,17},{9,25},{17,1},{25,9},{2,18},{10... | collective-permute-start | bytes 872 | tf_op jit(solution)/shard_map/ppermute | solution.py:134
  57.6 3.7 %collective-permute-start.10 = (f32[9,8]{1,0:T(8,128)S(1)}, f32[9,8]{1,0:T(8,128)S(1)}, u32[]{:S(2)}, u32[]{:S(2)}) collective-permute-start(f32[9,8]{1,0:T(8,128)S(1)} %add.593), channel_id=1, source_target_pairs={{0,1},{1,0},{2,3},{3,2},{4,5},{5,4},{6,7},{7,6},{8,9},{9,8},{10,11... | collective-permute-start | bytes 872 | tf_op jit(solution)/shard_map/ppermute | solution.py:134
  61.3 3.7 %collective-permute-start.11 = (f32[9,8]{1,0:T(8,128)S(1)}, f32[9,8]{1,0:T(8,128)S(1)}, u32[]{:S(2)}, u32[]{:S(2)}) collective-permute-start(f32[9,8]{1,0:T(8,128)S(1)} %add.594), channel_id=1, source_target_pairs={{0,2},{1,3},{2,0},{3,1},{4,6},{5,7},{6,4},{7,5},{8,10},{9,11},{10,... | collective-permute-start | bytes 872 | tf_op jit(solution)/shard_map/ppermute | solution.py:134
  64.9 4.5 %collective-permute-start.12 = (f32[9,8]{1,0:T(8,128)S(1)}, f32[9,8]{1,0:T(8,128)S(1)}, u32[]{:S(2)}, u32[]{:S(2)}) collective-permute-start(f32[9,8]{1,0:T(8,128)S(1)} %add.595), channel_id=1, source_target_pairs={{0,4},{1,5},{2,6},{3,7},{4,0},{5,1},{6,2},{7,3},{8,12},{9,13},{10,... | collective-permute-start | bytes 872 | tf_op jit(solution)/shard_map/ppermute | solution.py:134

commit v13 on v12

--- a/solution.py
+++ b/solution.py
@@ -152,7 +152,7 @@
         None, None, :
     ]
     bias_column = conv_bias[:, None, None, None]
-    padded = extend(features, 1)
+    padded = extend(features, 1, order=(("yx", 2), ("gz", 1)))
     padded = jnp.pad(padded, ((0, 0), (0, 0), (0, 0), (1, 1)))
     affinities = jax.nn.sigmoid(
         conv_region(padded, conv_weight, depth_cells, row_cells) + bias_column

time: 73.1 us -> 77.1 us (1.055)
  waiting for transfers between devices: 23.2 us -> 29.7 us
  starting transfers between devices: 21.1 us -> 18.5 us
    ppermute x8, waiting for transfers between devices: 13.5 us -> 16.9 us  [from_ring(): lax.ppermute(value, axis, [(i, (i + by) % devices) for i in range(devices)])]
    ppermute x5, waiting for transfers between devices: 9.69 us -> 12.8 us  [all_sum(): lax.ppermute(value, axis, [(i, i ^ hop) for i in range(devices)])]
    ppermute x5, starting transfers between devices: 6.82 us -> 3.77 us  [all_sum(): lax.ppermute(value, axis, [(i, i ^ hop) for i in range(devices)])]
  transfers between devices with their start and end apart: 13 -> 13, of which waited for: 11 -> 12; matrix products, arithmetic and copies ran while one was open for 1% -> 1% of each run, Pallas kernels for 0% -> 0%
where the time goes in v13:
time: 77.1 us; the launch traced here: 76.9 us
  waiting for transfers between devices  29.7 us (39%)
  starting transfers between devices  18.5 us (24%)
  other arithmetic  13.2 us (17%)
  local copies, waits for them, and re-layouts  8.18 us (11%)
  matrix products  6.15 us (8%)
  between operations  1.16 us (2%)
    ppermute x8, waiting for transfers between devices, from_ring(): lax.ppermute(value, axis, [(i, (i + by) % devices) for i in range(devices)])  16.9 us
    ppermute x8, starting transfers between devices, from_ring(): lax.ppermute(value, axis, [(i, (i + by) % devices) for i in range(devices)])  14.7 us
    ppermute x5, waiting for transfers between devices, all_sum(): lax.ppermute(value, axis, [(i, i ^ hop) for i in range(devices)])  12.8 us
    dot_general x9, matrix products, conv_region(): jnp.einsum('oce,cezyx->ozyx', conv_weight[:, :, offset_z, offset_y, :], w...  6.15 us
    ppermute x5, starting transfers between devices, all_sum(): lax.ppermute(value, axis, [(i, i ^ hop) for i in range(devices)])  3.77 us
    unnamed x12, local copies, waits for them, and re-layouts  3.64 us
    add x1, other arithmetic, body(): probabilities = probabilities + coeff[:, None, None, None] * vector  3.39 us
    sub x2, other arithmetic, operate_inside(): return diagonal[part, part] * centre - coupled  3.29 us
  transfers between devices with their start and end apart: 13, of which 12 were waited for; matrix products, arithmetic and copies ran while one was open for 1% of the time, Pallas kernels for 0%

profile of v13, /device:TPU:0, one launch (start us, length us, event | category | flops | bytes accessed | tf_op | source)
XLA Modules:
  0.0 76.9 jit_solution(15105780621973648296)
XLA Ops:
  0.6 0.0 copy-start.3
  0.6 0.0 copy-start.2
  0.6 1.9 %copy.6 = bf16[16,16,16,128]{3,0,2,1:T(8,128)(2,1)S(1)} copy(bf16[16,16,16,128]{3,2,1,0:T(8,128)(2,1)} %param.4) | data formatting | bytes 2097152 | tf_op args[0]
  2.6 6.1 %collective-permute-start.1 = (bf16[16,16,1,128]{3,0,2,1:T(8,128)(2,1)S(1)}, bf16[16,16,1,128]{3,0,2,1:T(8,128)(2,1)S(1)}, u32[]{:S(2)}, u32[]{:S(2)}) collective-permute-start(bf16[16,16,1,128]{3,0,2,1:T(8,128)(2,1)S(1)} %get-tuple-element.40), channel_id=1, source_target_pairs={{0,7},{1,0},{2,1},{3,2},{4,3},{5,4},{6,5},{7,6},{8,15},{9,8},{10,9... | collective-permute-start | bytes 196616 | tf_op jit(solution)/shard_map/ppermute | solution.py:58
  8.7 0.0 collective-permute-start
  8.7 1.9 %collective-permute-done.1 = bf16[16,16,1,128]{3,0,2,1:T(8,128)(2,1)S(1)} collective-permute-done((bf16[16,16,1,128]{3,0,2,1:T(8,128)(2,1)S(1)}, bf16[16,16,1,128]{3,0,2,1:T(8,128)(2,1)S(1)}, u32[]{:S(2)}, u32[]{:S(2)}) %collective-permute-start.1) | collective-permute-done | bytes 65568 | tf_op jit(solution)/shard_map/ppermute | solution.py:58
  10.6 5.0 %collective-permute-done = bf16[16,16,1,128]{3,0,2,1:T(8,128)(2,1)S(1)} collective-permute-done((bf16[16,16,1,128]{3,0,2,1:T(8,128)(2,1)S(1)}, bf16[16,16,1,128]{3,0,2,1:T(8,128)(2,1)S(1)}, u32[]{:S(2)}, u32[]{:S(2)}) %collective-permute-start) | collective-permute-done | bytes 65568 | tf_op jit(solution)/shard_map/ppermute | solution.py:58
  15.7 0.1 collective-permute-start.2
  15.8 0.0 copy-done.3
  15.9 1.8 %collective-permute-start.3 = (bf16[16,1,18,128]{3,0,2,1:T(8,128)(2,1)S(1)}, bf16[16,1,18,128]{3,0,2,1:T(8,128)(2,1)S(1)}, u32[]{:S(2)}, u32[]{:S(2)}) collective-permute-start(bf16[16,1,18,128]{3,0,2,1:T(8,128)(2,1)S(1)} %get-tuple-element.38), channel_id=1, source_target_pairs={{0,24},{8,0},{16,8},{24,16},{1,25},{9,1},{17,9},{25,17},{2,26},{10... | collective-permute-start | bytes 221192 | tf_op jit(solution)/shard_map/ppermute | solution.py:58
  17.6 1.9 %collective-permute-done.2 = bf16[16,1,18,128]{3,0,2,1:T(8,128)(2,1)S(1)} collective-permute-done((bf16[16,1,18,128]{3,0,2,1:T(8,128)(2,1)S(1)}, bf16[16,1,18,128]{3,0,2,1:T(8,128)(2,1)S(1)}, u32[]{:S(2)}, u32[]{:S(2)}) %collective-permute-start.2) | collective-permute-done | bytes 73760 | tf_op jit(solution)/shard_map/ppermute | solution.py:58
  19.5 0.1 collective-permute-done.3
  19.6 0.3 pad_maximum_fusion.1
  19.9 0.3 fusion.78
  20.2 0.8 fusion.19
  20.9 0.6 convolution_bitcast_fusion.7
  21.5 0.6 convolution_bitcast_fusion.6
  22.1 0.6 convolution_bitcast_fusion.5
  22.7 0.6 convolution_bitcast_fusion.4
  23.3 0.6 convolution_bitcast_fusion.3
  23.8 0.6 convolution_bitcast_fusion.2
  24.4 0.6 convolution_bitcast_fusion.1
  25.0 0.6 convolution_bitcast_fusion
  25.6 0.1 copy-done.4
  25.7 1.5 %fusion.34 = f32[3,16,16,128]{3,0,2,1:T(4,128)S(1)} fusion(f32[16,16,128,3]{2,3,1,0:T(4,128)S(1)} %convolution_bitcast_fusion, f32[16,16,128,3]{2,3,1,0:T(4,128)S(1)} %convolution_bitcast_fusion.1, f32[16,16,128,3]{2,3,1,0:T(4,128)S(1)} %convolution_bitcast_fusion.2, f32[16,16,128,3]{2,3,1,0:T(4,128)S(1)} %convolution_bitcast_fusion.3, ...), kind=kOutput, calls=%fused_computation.66 | convolution fusion | flops 22560768 | bytes 7520556 | tf_op jit(solution)/shard_map/oce,cezyx->ozyx/dot_general | solution.py:47
  27.2 0.1 pad_maximum_fusion.7
  27.3 0.1 collective-permute-start.4
  27.4 4.7 %collective-permute-start.5 = (f32[4,16,4,128]{3,0,2,1:T(4,128)S(1)}, f32[4,16,4,128]{3,0,2,1:T(4,128)S(1)}, u32[]{:S(2)}, u32[]{:S(2)}) collective-permute-start(f32[4,16,4,128]{3,0,2,1:T(4,128)S(1)} %get-tuple-element.44), channel_id=1, source_target_pairs={{0,7},{1,0},{2,1},{3,2},{4,3},{5,4},{6,5},{7,6},{8,15},{9,8},{10,9... | collective-permute-start | bytes 393224 | tf_op jit(solution)/shard_map/ppermute | solution.py:58
  32.1 3.7 %collective-permute-done.4 = f32[4,16,4,128]{3,0,2,1:T(4,128)S(1)} collective-permute-done((f32[4,16,4,128]{3,0,2,1:T(4,128)S(1)}, f32[4,16,4,128]{3,0,2,1:T(4,128)S(1)}, u32[]{:S(2)}, u32[]{:S(2)}) %collective-permute-start.4) | collective-permute-done | bytes 131104 | tf_op jit(solution)/shard_map/ppermute | solution.py:58
  35.8 0.0 collective-permute-done.5
  35.9 0.1 pad_maximum_fusion.5
  36.1 0.6 collective-permute-start.6
  36.7 1.4 %collective-permute-start.7 = (f32[4,4,22,128]{3,0,2,1:T(4,128)S(1)}, f32[4,4,22,128]{3,0,2,1:T(4,128)S(1)}, u32[]{:S(2)}, u32[]{:S(2)}) collective-permute-start(f32[4,4,22,128]{3,0,2,1:T(4,128)S(1)} %get-tuple-element.42), channel_id=1, source_target_pairs={{0,24},{8,0},{16,8},{24,16},{1,25},{9,1},{17,9},{25,17},{2,26},{10... | collective-permute-start | bytes 540680 | tf_op jit(solution)/shard_map/ppermute | solution.py:58
  38.1 2.9 %collective-permute-done.6 = f32[4,4,22,128]{3,0,2,1:T(4,128)S(1)} collective-permute-done((f32[4,4,22,128]{3,0,2,1:T(4,128)S(1)}, f32[4,4,22,128]{3,0,2,1:T(4,128)S(1)}, u32[]{:S(2)}, u32[]{:S(2)}) %collective-permute-start.6) | collective-permute-done | bytes 180256 | tf_op jit(solution)/shard_map/ppermute | solution.py:58
  41.1 1.4 %collective-permute-done.7 = f32[4,4,22,128]{3,0,2,1:T(4,128)S(1)} collective-permute-done((f32[4,4,22,128]{3,0,2,1:T(4,128)S(1)}, f32[4,4,22,128]{3,0,2,1:T(4,128)S(1)}, u32[]{:S(2)}, u32[]{:S(2)}) %collective-permute-start.7) | collective-permute-done | bytes 180256 | tf_op jit(solution)/shard_map/ppermute | solution.py:58
  42.5 0.3 select_maximum_fusion
  42.8 0.9 %fusion.75 = (f32[1,24,24,128]{3,0,2,1:T(1,128)S(1)}, f32[1,24,24,128]{3,0,2,1:T(1,128)S(1)}, f32[1,24,24,128]{3,0,2,1:T(1,128)S(1)}, f32[1,24,24,128]{3,0,2,1:T(1,128)S(1)}) fusion(f32[4,24,24,128]{3,0,2,1:T(4,128)S(1)} %select_maximum_fusion), kind=kLoop, calls=%fused_computation.179 | loop fusion | bytes 2359296 | tf_op jit(solution)/shard_map/slice | solution.py:171
  43.7 0.1 broadcast_multiply_fusion
  43.8 0.2 convert_add_fusion
  44.0 0.2 fusion.46
  44.8 0.2 compare_convert_fusion
  45.0 0.8 fusion.71
  45.8 2.1 %fusion.4 = f32[8,22,22,128]{3,2,1,0:T(8,128)S(1)} fusion(f32[8,24,24,128]{3,2,1,0:T(8,128)S(1)} %compare_convert_fusion, f32[8,22,22,127]{3,2,1,0:T(8,128)S(1)} %get-tuple-element.24, f32[8,22,22,127]{3,2,1,0:T(8,128)S(1)} %get-tuple-element.23, f32[22,22,128]{2,1,0:T(8,128)S(1)} %get-tuple-element.53, f32[22,22,128]{2,1,0:T(8,128)S(1)} %get-tuple-element.54, ...), kind=kLoop, calls=%fused_computation.9 | loop fusion | flops 6938624 | bytes 17563392 | tf_op jit(solution)/shard_map/sub | solution.py:182
  47.9 0.7 fusion.72
  48.6 1.8 %fusion.10 = f32[8,20,20,128]{3,2,1,0:T(8,128)S(1)} fusion(f32[8,22,22,128]{3,2,1,0:T(8,128)S(1)} %fusion.4, f32[8,20,20,127]{3,2,1,0:T(8,128)S(1)} %get-tuple-element.26, f32[8,20,20,127]{3,2,1,0:T(8,128)S(1)} %get-tuple-element.25, f32[20,20,128]{2,1,0:T(8,128)S(1)} %slice.449, f32[20,20,128]{2,1,0:T(8,128)S(1)} %slice.447, f32[20,20,128]{2,1,0:T(8,128)S(1)} %slice.445, ...), kind=kLoop, calls=%fused_computation.19 | loop fusion | flops 5324800 | bytes 14515200 | tf_op jit(solution)/shard_map/sub | solution.py:123
  50.4 0.0 copy-start
  50.4 0.6 fusion.73
  51.1 1.4 %fusion.16 = f32[8,18,18,128]{3,2,1,0:T(8,128)S(1)} fusion(f32[8,20,20,128]{3,2,1,0:T(8,128)S(1)} %fusion.10, f32[8,18,18,127]{3,2,1,0:T(8,128)S(1)} %get-tuple-element.28, f32[8,18,18,127]{3,2,1,0:T(8,128)S(1)} %get-tuple-element.27, f32[18,18,128]{2,1,0:T(8,128)S(1)} %slice.464, f32[18,18,128]{2,1,0:T(8,128)S(1)} %slice.462, ...), kind=kLoop, calls=%fused_computation.30 | loop fusion | flops 4313088 | bytes 11757312 | tf_op jit(solution)/shard_map/sub | solution.py:123
  52.5 0.4 fusion.74
  52.9 0.0 copy-done
  52.9 0.8 %copy-done.1 = f32[8,18,18,128]{3,2,1,0:T(8,128)} copy-done((f32[8,18,18,128]{3,2,1,0:T(8,128)}, f32[8,18,18,128]{3,2,1,0:T(8,128)S(1)}, u32[]{:S(2)}) %copy-start.1) | copy-done | bytes 1327128
  53.8 2.3 %multiply_reduce_fusion.5 = (f32[8]{0:T(128)S(1)}, f32[8]{0:T(128)S(1)}, f32[8]{0:T(128)S(1)}, f32[8]{0:T(128)S(1)}, f32[8]{0:T(128)S(1)}, /*index=5*/f32[8]{0:T...) fusion(f32[8,22,22,128]{3,2,1,0:T(8,128)S(1)} %fusion.4, f32[8,20,20,128]{3,2,1,0:T(8,128)S(1)} %fusion.10, ...), kind=kLoop, calls=%fused_computation.83 | loop fusion | flops 8126392 | bytes 10338592 | tf_op jit(solution)/shard_map/reduce_sum | solution.py:140
  56.1 1.0 %collective-permute-start.8 = (f32[9,8]{1,0:T(8,128)S(1)}, f32[9,8]{1,0:T(8,128)S(1)}, u32[]{:S(2)}, u32[]{:S(2)}) collective-permute-start(f32[9,8]{1,0:T(8,128)S(1)} %stack.55), channel_id=1, source_target_pairs={{0,8},{8,0},{16,24},{24,16},{1,9},{9,1},{17,25},{25,17},{2,10},{10... | collective-permute-start | bytes 872 | tf_op jit(solution)/shard_map/ppermute | solution.py:134
  57.1 0.8 %collective-permute-done.8 = f32[9,8]{1,0:T(8,128)S(1)} collective-permute-done((f32[9,8]{1,0:T(8,128)S(1)}, f32[9,8]{1,0:T(8,128)S(1)}, u32[]{:S(2)}, u32[]{:S(2)}) %collective-permute-start.8) | collective-permute-done | bytes 320 | tf_op jit(solution)/shard_map/ppermute | solution.py:134
  57.9 1.4 %collective-permute-start.9 = (f32[9,8]{1,0:T(8,128)S(1)}, f32[9,8]{1,0:T(8,128)S(1)}, u32[]{:S(2)}, u32[]{:S(2)}) collective-permute-start(f32[9,8]{1,0:T(8,128)S(1)} %add.592), channel_id=1, source_target_pairs={{0,16},{8,24},{16,0},{24,8},{1,17},{9,25},{17,1},{25,9},{2,18},{10... | collective-permute-start | bytes 872 | tf_op jit(solution)/shard_map/ppermute | solution.py:134
  59.3 2.3 %collective-permute-done.9 = f32[9,8]{1,0:T(8,128)S(1)} collective-permute-done((f32[9,8]{1,0:T(8,128)S(1)}, f32[9,8]{1,0:T(8,128)S(1)}, u32[]{:S(2)}, u32[]{:S(2)}) %collective-permute-start.9) | collective-permute-done | bytes 320 | tf_op jit(solution)/shard_map/ppermute | solution.py:134
  61.5 0.0 collective-permute-start.10
  61.6 3.6 %collective-permute-done.10 = f32[9,8]{1,0:T(8,128)S(1)} collective-permute-done((f32[9,8]{1,0:T(8,128)S(1)}, f32[9,8]{1,0:T(8,128)S(1)}, u32[]{:S(2)}, u32[]{:S(2)}) %collective-permute-start.10) | collective-permute-done | bytes 320 | tf_op jit(solution)/shard_map/ppermute | solution.py:134
  65.2 0.0 collective-permute-start.11
  65.2 3.6 %collective-permute-done.11 = f32[9,8]{1,0:T(8,128)S(1)} collective-permute-done((f32[9,8]{1,0:T(8,128)S(1)}, f32[9,8]{1,0:T(8,128)S(1)}, u32[]{:S(2)}, u32[]{:S(2)}) %collective-permute-start.11) | collective-permute-done | bytes 320 | tf_op jit(solution)/shard_map/ppermute | solution.py:134
  68.9 1.4 %collective-permute-start.12 = (f32[9,8]{1,0:T(8,128)S(1)}, f32[9,8]{1,0:T(8,128)S(1)}, u32[]{:S(2)}, u32[]{:S(2)}) collective-permute-start(f32[9,8]{1,0:T(8,128)S(1)} %add.595), channel_id=1, source_target_pairs={{0,4},{1,5},{2,6},{3,7},{4,0},{5,1},{6,2},{7,3},{8,12},{9,13},{10,... | collective-permute-start | bytes 872 | tf_op jit(solution)/shard_map/ppermute | solution.py:134
  70.3 0.8 %copy.23 = f32[3,16,16,128]{3,2,1,0:T(8,128)} copy(f32[3,16,16,128]{3,0,2,1:T(4,128)S(1)} %fusion.34) | data formatting | bytes 786432
  71.1 2.4 %collective-permute-done.12 = f32[9,8]{1,0:T(8,128)S(1)} collective-permute-done((f32[9,8]{1,0:T(8,128)S(1)}, f32[9,8]{1,0:T(8,128)S(1)}, u32[]{:S(2)}, u32[]{:S(2)}) %collective-permute-start.12) | collective-permute-done | bytes 320 | tf_op jit(solution)/shard_map/ppermute | solution.py:134
  73.5 3.4 %multiply_add_fusion = f32[8,16,16,128]{3,2,1,0:T(8,128)} fusion(f32[8,20,20,128]{3,2,1,0:T(8,128)} %copy-done, f32[8,22,22,128]{3,2,1,0:T(8,128)S(1)} %fusion.4, f32[8,18,18,128]{3,2,1,0:T(8,128)} %copy-done.1, f32[8]{0:T(128)S(1)} %get-tuple-element.65, f32[8]{0:T(128)S(1)} %get-tuple-element.64, f32[8]{0:T(128)S(1)} %get-tuple-element.13, ...), kind=kLoop, calls=%fused_computation.77 | loop fusion | flops 2097152 | bytes 4325504 | tf_op jit(solution)/shard_map/add | solution.py:246
  (51 shorter events, 0.8 us)
Async XLA Ops:
  0.6 15.1 %copy-start.3 = (bf16[3,16,3,3,3]{1,4,3,2,0:T(4,128)(2,1)S(1)}, bf16[3,16,3,3,3]{1,4,3,2,0:T(4,128)(2,1)}, u32[]{:S(2)}) copy-start(bf16[3,16,3,3,3]{1,4,3,2,0:T(4,128)(2,1)} %param.5) | copy-start | bytes 7780
  0.6 15.2 %copy-start.2 = (s32[16,16,128]{2,1,0:T(8,128)S(1)}, s32[16,16,128]{2,1,0:T(8,128)}, u32[]{:S(2)}) copy-start(s32[16,16,128]{2,1,0:T(8,128)} %param.7) | copy-start | bytes 393220
  2.6 8.0 %collective-permute-start.1 = (bf16[16,16,1,128]{3,0,2,1:T(8,128)(2,1)S(1)}, bf16[16,16,1,128]{3,0,2,1:T(8,128)(2,1)S(1)}, u32[]{:S(2)}, u32[]{:S(2)}) collective-permute-start(bf16[16,16,1,128]{3,0,2,1:T(8,128)(2,1)S(1)} %get-tuple-element.40), channel_id=1, source_target_pairs={{0,7},{1,0},{2,1},{3,2},{4,3},{5,4},{6,5},{7,6},{8,15},{9,8},{10,9... | collective-permute-start | bytes 196616 | tf_op jit(solution)/shard_map/ppermute | solution.py:58
  8.7 7.0 %collective-permute-start = (bf16[16,16,1,128]{3,0,2,1:T(8,128)(2,1)S(1)}, bf16[16,16,1,128]{3,0,2,1:T(8,128)(2,1)S(1)}, u32[]{:S(2)}, u32[]{:S(2)}) collective-permute-start(bf16[16,16,1,128]{3,0,2,1:T(8,128)(2,1)S(1)} %get-tuple-element.39), channel_id=1, source_target_pairs={{0,1},{1,2},{2,3},{3,4},{4,5},{5,6},{6,7},{7,0},{8,9},{9,10},{10,1... | collective-permute-start | bytes 196616 | tf_op jit(solution)/shard_map/ppermute | solution.py:58
  15.7 3.8 %collective-permute-start.2 = (bf16[16,1,18,128]{3,0,2,1:T(8,128)(2,1)S(1)}, bf16[16,1,18,128]{3,0,2,1:T(8,128)(2,1)S(1)}, u32[]{:S(2)}, u32[]{:S(2)}) collective-permute-start(bf16[16,1,18,128]{3,0,2,1:T(8,128)(2,1)S(1)} %get-tuple-element.37), channel_id=1, source_target_pairs={{0,8},{8,16},{16,24},{24,0},{1,9},{9,17},{17,25},{25,1},{2,10},{10... | collective-permute-start | bytes 221192 | tf_op jit(solution)/shard_map/ppermute | solution.py:58
  15.9 3.8 %collective-permute-start.3 = (bf16[16,1,18,128]{3,0,2,1:T(8,128)(2,1)S(1)}, bf16[16,1,18,128]{3,0,2,1:T(8,128)(2,1)S(1)}, u32[]{:S(2)}, u32[]{:S(2)}) collective-permute-start(bf16[16,1,18,128]{3,0,2,1:T(8,128)(2,1)S(1)} %get-tuple-element.38), channel_id=1, source_target_pairs={{0,24},{8,0},{16,8},{24,16},{1,25},{9,1},{17,9},{25,17},{2,26},{10... | collective-permute-start | bytes 221192 | tf_op jit(solution)/shard_map/ppermute | solution.py:58
  25.0 0.7 copy-start.4
  27.3 8.5 %collective-permute-start.4 = (f32[4,16,4,128]{3,0,2,1:T(4,128)S(1)}, f32[4,16,4,128]{3,0,2,1:T(4,128)S(1)}, u32[]{:S(2)}, u32[]{:S(2)}) collective-permute-start(f32[4,16,4,128]{3,0,2,1:T(4,128)S(1)} %get-tuple-element.43), channel_id=1, source_target_pairs={{0,1},{1,2},{2,3},{3,4},{4,5},{5,6},{6,7},{7,0},{8,9},{9,10},{10,1... | collective-permute-start | bytes 393224 | tf_op jit(solution)/shard_map/ppermute | solution.py:58
  27.4 8.5 %collective-permute-start.5 = (f32[4,16,4,128]{3,0,2,1:T(4,128)S(1)}, f32[4,16,4,128]{3,0,2,1:T(4,128)S(1)}, u32[]{:S(2)}, u32[]{:S(2)}) collective-permute-start(f32[4,16,4,128]{3,0,2,1:T(4,128)S(1)} %get-tuple-element.44), channel_id=1, source_target_pairs={{0,7},{1,0},{2,1},{3,2},{4,3},{5,4},{6,5},{7,6},{8,15},{9,8},{10,9... | collective-permute-start | bytes 393224 | tf_op jit(solution)/shard_map/ppermute | solution.py:58
  36.1 5.0 %collective-permute-start.6 = (f32[4,4,22,128]{3,0,2,1:T(4,128)S(1)}, f32[4,4,22,128]{3,0,2,1:T(4,128)S(1)}, u32[]{:S(2)}, u32[]{:S(2)}) collective-permute-start(f32[4,4,22,128]{3,0,2,1:T(4,128)S(1)} %get-tuple-element.41), channel_id=1, source_target_pairs={{0,8},{8,16},{16,24},{24,0},{1,9},{9,17},{17,25},{25,1},{2,10},{10... | collective-permute-start | bytes 540680 | tf_op jit(solution)/shard_map/ppermute | solution.py:58
  36.7 5.8 %collective-permute-start.7 = (f32[4,4,22,128]{3,0,2,1:T(4,128)S(1)}, f32[4,4,22,128]{3,0,2,1:T(4,128)S(1)}, u32[]{:S(2)}, u32[]{:S(2)}) collective-permute-start(f32[4,4,22,128]{3,0,2,1:T(4,128)S(1)} %get-tuple-element.42), channel_id=1, source_target_pairs={{0,24},{8,0},{16,8},{24,16},{1,25},{9,1},{17,9},{25,17},{2,26},{10... | collective-permute-start | bytes 540680 | tf_op jit(solution)/shard_map/ppermute | solution.py:58
  50.4 2.5 %copy-start = (f32[8,20,20,128]{3,2,1,0:T(8,128)}, f32[8,20,20,128]{3,2,1,0:T(8,128)S(1)}, u32[]{:S(2)}) copy-start(f32[8,20,20,128]{3,2,1,0:T(8,128)S(1)} %fusion.10) | copy-start | bytes 4915204
  52.5 1.2 %copy-start.1 = (f32[8,18,18,128]{3,2,1,0:T(8,128)}, f32[8,18,18,128]{3,2,1,0:T(8,128)S(1)}, u32[]{:S(2)}) copy-start(f32[8,18,18,128]{3,2,1,0:T(8,128)S(1)} %fusion.16) | copy-start | bytes 3981316
  56.1 1.8 %collective-permute-start.8 = (f32[9,8]{1,0:T(8,128)S(1)}, f32[9,8]{1,0:T(8,128)S(1)}, u32[]{:S(2)}, u32[]{:S(2)}) collective-permute-start(f32[9,8]{1,0:T(8,128)S(1)} %stack.55), channel_id=1, source_target_pairs={{0,8},{8,0},{16,24},{24,16},{1,9},{9,1},{17,25},{25,17},{2,10},{10... | collective-permute-start | bytes 872 | tf_op jit(solution)/shard_map/ppermute | solution.py:134
  57.9 3.7 %collective-permute-start.9 = (f32[9,8]{1,0:T(8,128)S(1)}, f32[9,8]{1,0:T(8,128)S(1)}, u32[]{:S(2)}, u32[]{:S(2)}) collective-permute-start(f32[9,8]{1,0:T(8,128)S(1)} %add.592), channel_id=1, source_target_pairs={{0,16},{8,24},{16,0},{24,8},{1,17},{9,25},{17,1},{25,9},{2,18},{10... | collective-permute-start | bytes 872 | tf_op jit(solution)/shard_map/ppermute | solution.py:134
  61.5 3.7 %collective-permute-start.10 = (f32[9,8]{1,0:T(8,128)S(1)}, f32[9,8]{1,0:T(8,128)S(1)}, u32[]{:S(2)}, u32[]{:S(2)}) collective-permute-start(f32[9,8]{1,0:T(8,128)S(1)} %add.593), channel_id=1, source_target_pairs={{0,1},{1,0},{2,3},{3,2},{4,5},{5,4},{6,7},{7,6},{8,9},{9,8},{10,11... | collective-permute-start | bytes 872 | tf_op jit(solution)/shard_map/ppermute | solution.py:134
  65.2 3.7 %collective-permute-start.11 = (f32[9,8]{1,0:T(8,128)S(1)}, f32[9,8]{1,0:T(8,128)S(1)}, u32[]{:S(2)}, u32[]{:S(2)}) collective-permute-start(f32[9,8]{1,0:T(8,128)S(1)} %add.594), channel_id=1, source_target_pairs={{0,2},{1,3},{2,0},{3,1},{4,6},{5,7},{6,4},{7,5},{8,10},{9,11},{10,... | collective-permute-start | bytes 872 | tf_op jit(solution)/shard_map/ppermute | solution.py:134
  68.9 4.6 %collective-permute-start.12 = (f32[9,8]{1,0:T(8,128)S(1)}, f32[9,8]{1,0:T(8,128)S(1)}, u32[]{:S(2)}, u32[]{:S(2)}) collective-permute-start(f32[9,8]{1,0:T(8,128)S(1)} %add.595), channel_id=1, source_target_pairs={{0,4},{1,5},{2,6},{3,7},{4,0},{5,1},{6,2},{7,3},{8,12},{9,13},{10,... | collective-permute-start | bytes 872 | tf_op jit(solution)/shard_map/ppermute | solution.py:134

commit v14 on v12

--- a/solution.py
+++ b/solution.py
@@ -61,14 +61,14 @@
     return jnp.where(inside, moved, jnp.zeros_like(moved))
 
 
-def extend(cells, width, corner=None, order=(("gz", 1), ("yx", 2))):
+def extend(cells, width, corner=None, order=(("gz", 1), ("yx", 2)), first=0):
     corner = width if corner is None else corner
-    for step, (axis, dim) in enumerate(order):
+    for step, (axis, dim) in enumerate(order[: len(order) - first]):
         source = cells
         trim = 0
-        if step == 1 and corner < width:
+        if step + first == 1 and corner < width:
             trim = width - corner
-            other = order[0][1]
+            other = 3 - dim
             source = lax.slice_in_dim(cells, trim, cells.shape[other] - trim, axis=other)
         size = source.shape[dim]
         head = lax.slice_in_dim(source, 0, width, axis=dim)
@@ -152,14 +152,31 @@
         None, None, :
     ]
     bias_column = conv_bias[:, None, None, None]
+    halo = ITERS + 1
+    label_cells = labels[None].astype(jnp.float32)
+    label_rows = jnp.concatenate(
+        [
+            from_ring(label_cells[:, :, row_cells - halo :], "yx", 1),
+            label_cells,
+            from_ring(label_cells[:, :, :halo], "yx", -1),
+        ],
+        axis=2,
+    )
     padded = extend(features, 1)
     padded = jnp.pad(padded, ((0, 0), (0, 0), (0, 0), (1, 1)))
     affinities = jax.nn.sigmoid(
         conv_region(padded, conv_weight, depth_cells, row_cells) + bias_column
     )
-    halo = ITERS + 1
-    stacked = jnp.concatenate([affinities, labels[None].astype(jnp.float32)], axis=0)
-    grid_cells = extend(stacked, halo, halo - 1, (("yx", 2), ("gz", 1)))
+    affinity_rows = jnp.concatenate(
+        [
+            from_ring(affinities[:, :, row_cells - halo :], "yx", 1),
+            affinities,
+            from_ring(affinities[:, :, :halo], "yx", -1),
+        ],
+        axis=2,
+    )
+    stacked = jnp.concatenate([affinity_rows, label_rows], axis=0)
+    grid_cells = extend(stacked, halo, halo - 1, (("gz", 1), ("yx", 2)), first=1)
     cells_z = depth_cells + 2 * halo
     cells_y = row_cells + 2 * halo
     grid_z = lax.axis_index("gz") * depth_cells - halo + jnp.arange(cells_z, dtype=jnp.int32)

time: 73.1 us -> 74.3 us (1.016)
    ppermute x8 -> x10, starting transfers between devices: 14.2 us -> 17.2 us  [from_ring(): lax.ppermute(value, axis, [(i, (i + by) % devices) for i in range(devices)])]
    ppermute x5, waiting for transfers between devices: 9.69 us -> 12.6 us  [all_sum(): lax.ppermute(value, axis, [(i, i ^ hop) for i in range(devices)])]
    ppermute x5, starting transfers between devices: 6.82 us -> 4.28 us  [all_sum(): lax.ppermute(value, axis, [(i, i ^ hop) for i in range(devices)])]
    ppermute x8 -> x10, waiting for transfers between devices: 13.5 us -> 11.1 us  [from_ring(): lax.ppermute(value, axis, [(i, (i + by) % devices) for i in range(devices)])]
  transfers between devices with their start and end apart: 13 -> 15, of which waited for: 11 -> 11; matrix products, arithmetic and copies ran while one was open for 1% -> 11% of each run, Pallas kernels for 0% -> 0%
where the time goes in v14:
time: 74.3 us; the launch traced here: 74.1 us
  waiting for transfers between devices  23.8 us (32%)
  starting transfers between devices  21.5 us (29%)
  other arithmetic  13.3 us (18%)
  local copies, waits for them, and re-layouts  8.22 us (11%)
  matrix products  6.15 us (8%)
  between operations  1.19 us (2%)
    ppermute x10, starting transfers between devices, from_ring(): lax.ppermute(value, axis, [(i, (i + by) % devices) for i in range(devices)])  17.2 us
    ppermute x5, waiting for transfers between devices, all_sum(): lax.ppermute(value, axis, [(i, i ^ hop) for i in range(devices)])  12.6 us
    ppermute x10, waiting for transfers between devices, from_ring(): lax.ppermute(value, axis, [(i, (i + by) % devices) for i in range(devices)])  11.1 us
    dot_general x9, matrix products, conv_region(): jnp.einsum('oce,cezyx->ozyx', conv_weight[:, :, offset_z, offset_y, :], w...  6.15 us
    ppermute x5, starting transfers between devices, all_sum(): lax.ppermute(value, axis, [(i, i ^ hop) for i in range(devices)])  4.28 us
    unnamed x12, local copies, waits for them, and re-layouts  3.62 us
    add x1, other arithmetic, body(): probabilities = probabilities + coeff[:, None, None, None] * vector  3.39 us
    sub x2, other arithmetic, operate_inside(): return diagonal[part, part] * centre - coupled  3.29 us
  transfers between devices with their start and end apart: 15, of which 11 were waited for; matrix products, arithmetic and copies ran while one was open for 11% of the time, Pallas kernels for 0%

profile of v14, /device:TPU:0, one launch (start us, length us, event | category | flops | bytes accessed | tf_op | source)
XLA Modules:
  0.0 74.1 jit_solution(8132747283557345382)
XLA Ops:
  0.6 1.9 %copy.6 = bf16[16,16,16,128]{3,0,2,1:T(8,128)(2,1)S(1)} copy(bf16[16,16,16,128]{3,2,1,0:T(8,128)(2,1)} %param.4) | data formatting | bytes 2097152 | tf_op args[0]
  2.6 2.5 %collective-permute-start.1 = (bf16[16,1,16,128]{3,0,2,1:T(8,128)(2,1)S(1)}, bf16[16,1,16,128]{3,0,2,1:T(8,128)(2,1)S(1)}, u32[]{:S(2)}, u32[]{:S(2)}) collective-permute-start(bf16[16,1,16,128]{3,0,2,1:T(8,128)(2,1)S(1)} %get-tuple-element.40), channel_id=1, source_target_pairs={{0,24},{8,0},{16,8},{24,16},{1,25},{9,1},{17,9},{25,17},{2,26},{10... | collective-permute-start | bytes 196616 | tf_op jit(solution)/shard_map/ppermute | solution.py:58
  5.1 0.0 collective-permute-start
  5.1 1.6 %collective-permute-start.6 = (f32[1,16,4,128]{3,0,2,1:T(1,128)S(1)}, f32[1,16,4,128]{3,0,2,1:T(1,128)S(1)}, u32[]{:S(2)}, u32[]{:S(2)}) collective-permute-start(f32[1,16,4,128]{3,0,2,1:T(1,128)S(1)} %get-tuple-element.51), channel_id=1, source_target_pairs={{0,1},{1,2},{2,3},{3,4},{4,5},{5,6},{6,7},{7,0},{8,9},{9,10},{10,1... | collective-permute-start | bytes 98312 | tf_op jit(solution)/shard_map/ppermute | solution.py:58
  6.7 3.2 %collective-permute-start.7 = (f32[1,16,4,128]{3,0,2,1:T(1,128)S(1)}, f32[1,16,4,128]{3,0,2,1:T(1,128)S(1)}, u32[]{:S(2)}, u32[]{:S(2)}) collective-permute-start(f32[1,16,4,128]{3,0,2,1:T(1,128)S(1)} %get-tuple-element.52), channel_id=1, source_target_pairs={{0,7},{1,0},{2,1},{3,2},{4,3},{5,4},{6,5},{7,6},{8,15},{9,8},{10,9... | collective-permute-start | bytes 98312 | tf_op jit(solution)/shard_map/ppermute | solution.py:58
  9.9 0.0 copy-done.3
  10.0 0.0 collective-permute-done.1
  10.0 0.0 collective-permute-done
  10.0 0.3 collective-permute-start.2
  10.4 1.6 %collective-permute-done.6 = f32[1,16,4,128]{3,0,2,1:T(1,128)S(1)} collective-permute-done((f32[1,16,4,128]{3,0,2,1:T(1,128)S(1)}, f32[1,16,4,128]{3,0,2,1:T(1,128)S(1)}, u32[]{:S(2)}, u32[]{:S(2)}) %collective-permute-start.6) | collective-permute-done | bytes 32800 | tf_op jit(solution)/shard_map/ppermute | solution.py:58
  12.0 2.9 %collective-permute-start.3 = (bf16[16,18,1,128]{3,0,2,1:T(8,128)(2,1)S(1)}, bf16[16,18,1,128]{3,0,2,1:T(8,128)(2,1)S(1)}, u32[]{:S(2)}, u32[]{:S(2)}) collective-permute-start(bf16[16,18,1,128]{3,0,2,1:T(8,128)(2,1)S(1)} %get-tuple-element.38), channel_id=1, source_target_pairs={{0,7},{1,0},{2,1},{3,2},{4,3},{5,4},{6,5},{7,6},{8,15},{9,8},{10,9... | collective-permute-start | bytes 221192 | tf_op jit(solution)/shard_map/ppermute | solution.py:58
  14.9 2.5 %collective-permute-done.2 = bf16[16,18,1,128]{3,0,2,1:T(8,128)(2,1)S(1)} collective-permute-done((bf16[16,18,1,128]{3,0,2,1:T(8,128)(2,1)S(1)}, bf16[16,18,1,128]{3,0,2,1:T(8,128)(2,1)S(1)}, u32[]{:S(2)}, u32[]{:S(2)}) %collective-permute-start.2) | collective-permute-done | bytes 73760 | tf_op jit(solution)/shard_map/ppermute | solution.py:58
  17.4 0.6 collective-permute-done.3
  18.0 0.3 pad_maximum_fusion.1
  18.3 0.3 fusion.81
  18.6 0.8 %fusion.19 = (bf16[16,1,18,18,128]{4,0,1,3,2:T(8,128)(2,1)S(1)}, bf16[16,1,18,18,128]{4,0,1,3,2:T(8,128)(2,1)S(1)}) fusion(bf16[16,18,18,128]{3,0,2,1:T(8,128)(2,1)S(1)} %pad_maximum_fusion.1), kind=kLoop, calls=%fused_computation.37 | loop fusion | bytes 3981312 | tf_op jit(solution)/shard_map/stack | solution.py:38
  19.3 0.6 convolution_bitcast_fusion.7
  19.9 0.6 convolution_bitcast_fusion.6
  20.5 0.6 convolution_bitcast_fusion.5
  21.1 0.6 convolution_bitcast_fusion.4
  21.7 0.6 convolution_bitcast_fusion.3
  22.3 0.6 convolution_bitcast_fusion.2
  22.9 0.6 convolution_bitcast_fusion.1
  23.4 0.6 convolution_bitcast_fusion
  24.0 0.1 copy-done.4
  24.1 1.5 %fusion.34 = f32[3,16,16,128]{3,0,2,1:T(4,128)S(1)} fusion(f32[16,16,128,3]{2,3,1,0:T(4,128)S(1)} %convolution_bitcast_fusion, f32[16,16,128,3]{2,3,1,0:T(4,128)S(1)} %convolution_bitcast_fusion.1, f32[16,16,128,3]{2,3,1,0:T(4,128)S(1)} %convolution_bitcast_fusion.2, f32[16,16,128,3]{2,3,1,0:T(4,128)S(1)} %convolution_bitcast_fusion.3, ...), kind=kOutput, calls=%fused_computation.66 | convolution fusion | flops 22560768 | bytes 7520556 | tf_op jit(solution)/shard_map/oce,cezyx->ozyx/dot_general | solution.py:47
  25.6 0.1 collective-permute-start.4
  25.7 0.0 collective-permute-done.7
  25.8 4.7 %collective-permute-start.5 = (f32[3,16,4,128]{3,0,2,1:T(4,128)S(1)}, f32[3,16,4,128]{3,0,2,1:T(4,128)S(1)}, u32[]{:S(2)}, u32[]{:S(2)}) collective-permute-start(f32[3,16,4,128]{3,0,2,1:T(4,128)S(1)} %get-tuple-element.44), channel_id=1, source_target_pairs={{0,7},{1,0},{2,1},{3,2},{4,3},{5,4},{6,5},{7,6},{8,15},{9,8},{10,9... | collective-permute-start | bytes 294920 | tf_op jit(solution)/shard_map/ppermute | solution.py:58
  30.5 3.0 %collective-permute-done.4 = f32[3,16,4,128]{3,0,2,1:T(4,128)S(1)} collective-permute-done((f32[3,16,4,128]{3,0,2,1:T(4,128)S(1)}, f32[3,16,4,128]{3,0,2,1:T(4,128)S(1)}, u32[]{:S(2)}, u32[]{:S(2)}) %collective-permute-start.4) | collective-permute-done | bytes 98336 | tf_op jit(solution)/shard_map/ppermute | solution.py:58
  33.5 0.1 collective-permute-done.5
  33.6 0.2 maximum_maximum_fusion
  33.8 0.1 collective-permute-start.8
  33.9 2.0 %collective-permute-start.9 = (f32[4,4,22,128]{3,0,2,1:T(4,128)S(1)}, f32[4,4,22,128]{3,0,2,1:T(4,128)S(1)}, u32[]{:S(2)}, u32[]{:S(2)}) collective-permute-start(f32[4,4,22,128]{3,0,2,1:T(4,128)S(1)} %get-tuple-element.42), channel_id=1, source_target_pairs={{0,24},{8,0},{16,8},{24,16},{1,25},{9,1},{17,9},{25,17},{2,26},{10... | collective-permute-start | bytes 540680 | tf_op jit(solution)/shard_map/ppermute | solution.py:58
  35.8 3.3 %collective-permute-done.8 = f32[4,4,22,128]{3,0,2,1:T(4,128)S(1)} collective-permute-done((f32[4,4,22,128]{3,0,2,1:T(4,128)S(1)}, f32[4,4,22,128]{3,0,2,1:T(4,128)S(1)}, u32[]{:S(2)}, u32[]{:S(2)}) %collective-permute-start.8) | collective-permute-done | bytes 180256 | tf_op jit(solution)/shard_map/ppermute | solution.py:58
  39.2 0.0 collective-permute-done.9
  39.3 0.4 select_maximum_fusion
  39.6 0.9 %fusion.76 = (f32[1,24,24,128]{3,0,2,1:T(1,128)S(1)}, f32[1,24,24,128]{3,0,2,1:T(1,128)S(1)}, f32[1,24,24,128]{3,0,2,1:T(1,128)S(1)}, f32[1,24,24,128]{3,0,2,1:T(1,128)S(1)}) fusion(f32[4,24,24,128]{3,0,2,1:T(4,128)S(1)} %select_maximum_fusion), kind=kLoop, calls=%fused_computation.181 | loop fusion | bytes 2359296 | tf_op jit(solution)/shard_map/slice | solution.py:188
  40.5 0.1 broadcast_multiply_fusion
  40.7 0.2 convert_add_fusion
  40.9 0.2 fusion.46
  41.6 0.2 compare_convert_fusion
  41.8 0.8 %fusion.72 = (f32[8,22,22,127]{3,2,1,0:T(8,128)S(1)}, f32[8,22,22,127]{3,2,1,0:T(8,128)S(1)}) fusion(f32[8,24,24,128]{3,2,1,0:T(8,128)S(1)} %compare_convert_fusion), kind=kLoop, calls=%fused_computation.177 | loop fusion | bytes 7867904 | tf_op jit(solution)/shard_map/slice | solution.py:117
  42.6 2.1 %fusion.4 = f32[8,22,22,128]{3,2,1,0:T(8,128)S(1)} fusion(f32[8,24,24,128]{3,2,1,0:T(8,128)S(1)} %compare_convert_fusion, f32[8,22,22,127]{3,2,1,0:T(8,128)S(1)} %get-tuple-element.24, f32[8,22,22,127]{3,2,1,0:T(8,128)S(1)} %get-tuple-element.23, f32[22,22,128]{2,1,0:T(8,128)S(1)} %get-tuple-element.55, f32[22,22,128]{2,1,0:T(8,128)S(1)} %get-tuple-element.56, ...), kind=kLoop, calls=%fused_computation.9 | loop fusion | flops 6938624 | bytes 17563392 | tf_op jit(solution)/shard_map/sub | solution.py:199
  44.7 0.7 fusion.73
  45.4 1.8 %fusion.10 = f32[8,20,20,128]{3,2,1,0:T(8,128)S(1)} fusion(f32[8,22,22,128]{3,2,1,0:T(8,128)S(1)} %fusion.4, f32[8,20,20,127]{3,2,1,0:T(8,128)S(1)} %get-tuple-element.26, f32[8,20,20,127]{3,2,1,0:T(8,128)S(1)} %get-tuple-element.25, f32[20,20,128]{2,1,0:T(8,128)S(1)} %slice.461, f32[20,20,128]{2,1,0:T(8,128)S(1)} %slice.459, f32[20,20,128]{2,1,0:T(8,128)S(1)} %slice.457, ...), kind=kLoop, calls=%fused_computation.19 | loop fusion | flops 5324800 | bytes 14515200 | tf_op jit(solution)/shard_map/sub | solution.py:123
  47.3 0.0 copy-start
  47.3 0.6 fusion.74
  47.9 1.4 %fusion.16 = f32[8,18,18,128]{3,2,1,0:T(8,128)S(1)} fusion(f32[8,20,20,128]{3,2,1,0:T(8,128)S(1)} %fusion.10, f32[8,18,18,127]{3,2,1,0:T(8,128)S(1)} %get-tuple-element.28, f32[8,18,18,127]{3,2,1,0:T(8,128)S(1)} %get-tuple-element.27, f32[18,18,128]{2,1,0:T(8,128)S(1)} %slice.476, f32[18,18,128]{2,1,0:T(8,128)S(1)} %slice.474, ...), kind=kLoop, calls=%fused_computation.30 | loop fusion | flops 4313088 | bytes 11757312 | tf_op jit(solution)/shard_map/sub | solution.py:123
  49.4 0.4 fusion.75
  49.8 0.8 %copy-done.1 = f32[8,18,18,128]{3,2,1,0:T(8,128)} copy-done((f32[8,18,18,128]{3,2,1,0:T(8,128)}, f32[8,18,18,128]{3,2,1,0:T(8,128)S(1)}, u32[]{:S(2)}) %copy-start.1) | copy-done | bytes 1327128
  50.6 2.3 %multiply_reduce_fusion.5 = (f32[8]{0:T(128)S(1)}, f32[8]{0:T(128)S(1)}, f32[8]{0:T(128)S(1)}, f32[8]{0:T(128)S(1)}, f32[8]{0:T(128)S(1)}, /*index=5*/f32[8]{0:T...) fusion(f32[8,22,22,128]{3,2,1,0:T(8,128)S(1)} %fusion.4, f32[8,20,20,128]{3,2,1,0:T(8,128)S(1)} %fusion.10, ...), kind=kLoop, calls=%fused_computation.83 | loop fusion | flops 8126392 | bytes 10338592 | tf_op jit(solution)/shard_map/reduce_sum | solution.py:140
  52.9 1.3 %collective-permute-start.10 = (f32[9,8]{1,0:T(8,128)S(1)}, f32[9,8]{1,0:T(8,128)S(1)}, u32[]{:S(2)}, u32[]{:S(2)}) collective-permute-start(f32[9,8]{1,0:T(8,128)S(1)} %stack.55), channel_id=1, source_target_pairs={{0,8},{8,0},{16,24},{24,16},{1,9},{9,1},{17,25},{25,17},{2,10},{10... | collective-permute-start | bytes 872 | tf_op jit(solution)/shard_map/ppermute | solution.py:134
  54.3 0.8 %collective-permute-done.10 = f32[9,8]{1,0:T(8,128)S(1)} collective-permute-done((f32[9,8]{1,0:T(8,128)S(1)}, f32[9,8]{1,0:T(8,128)S(1)}, u32[]{:S(2)}, u32[]{:S(2)}) %collective-permute-start.10) | collective-permute-done | bytes 320 | tf_op jit(solution)/shard_map/ppermute | solution.py:134
  55.1 1.0 %collective-permute-start.11 = (f32[9,8]{1,0:T(8,128)S(1)}, f32[9,8]{1,0:T(8,128)S(1)}, u32[]{:S(2)}, u32[]{:S(2)}) collective-permute-start(f32[9,8]{1,0:T(8,128)S(1)} %add.592), channel_id=1, source_target_pairs={{0,16},{8,24},{16,0},{24,8},{1,17},{9,25},{17,1},{25,9},{2,18},{10... | collective-permute-start | bytes 872 | tf_op jit(solution)/shard_map/ppermute | solution.py:134
  56.1 2.7 %collective-permute-done.11 = f32[9,8]{1,0:T(8,128)S(1)} collective-permute-done((f32[9,8]{1,0:T(8,128)S(1)}, f32[9,8]{1,0:T(8,128)S(1)}, u32[]{:S(2)}, u32[]{:S(2)}) %collective-permute-start.11) | collective-permute-done | bytes 320 | tf_op jit(solution)/shard_map/ppermute | solution.py:134
  58.7 0.0 collective-permute-start.12
  58.7 3.6 %collective-permute-done.12 = f32[9,8]{1,0:T(8,128)S(1)} collective-permute-done((f32[9,8]{1,0:T(8,128)S(1)}, f32[9,8]{1,0:T(8,128)S(1)}, u32[]{:S(2)}, u32[]{:S(2)}) %collective-permute-start.12) | collective-permute-done | bytes 320 | tf_op jit(solution)/shard_map/ppermute | solution.py:134
  62.4 0.3 collective-permute-start.13
  62.7 3.4 %collective-permute-done.13 = f32[9,8]{1,0:T(8,128)S(1)} collective-permute-done((f32[9,8]{1,0:T(8,128)S(1)}, f32[9,8]{1,0:T(8,128)S(1)}, u32[]{:S(2)}, u32[]{:S(2)}) %collective-permute-start.13) | collective-permute-done | bytes 320 | tf_op jit(solution)/shard_map/ppermute | solution.py:134
  66.1 1.7 %collective-permute-start.14 = (f32[9,8]{1,0:T(8,128)S(1)}, f32[9,8]{1,0:T(8,128)S(1)}, u32[]{:S(2)}, u32[]{:S(2)}) collective-permute-start(f32[9,8]{1,0:T(8,128)S(1)} %add.595), channel_id=1, source_target_pairs={{0,4},{1,5},{2,6},{3,7},{4,0},{5,1},{6,2},{7,3},{8,12},{9,13},{10,... | collective-permute-start | bytes 872 | tf_op jit(solution)/shard_map/ppermute | solution.py:134
  67.7 0.8 %copy.23 = f32[3,16,16,128]{3,2,1,0:T(8,128)} copy(f32[3,16,16,128]{3,0,2,1:T(4,128)S(1)} %fusion.34) | data formatting | bytes 786432
  68.5 2.1 %collective-permute-done.14 = f32[9,8]{1,0:T(8,128)S(1)} collective-permute-done((f32[9,8]{1,0:T(8,128)S(1)}, f32[9,8]{1,0:T(8,128)S(1)}, u32[]{:S(2)}, u32[]{:S(2)}) %collective-permute-start.14) | collective-permute-done | bytes 320 | tf_op jit(solution)/shard_map/ppermute | solution.py:134
  70.7 3.4 %multiply_add_fusion = f32[8,16,16,128]{3,2,1,0:T(8,128)} fusion(f32[8,20,20,128]{3,2,1,0:T(8,128)} %copy-done, f32[8,22,22,128]{3,2,1,0:T(8,128)S(1)} %fusion.4, f32[8,18,18,128]{3,2,1,0:T(8,128)} %copy-done.1, f32[8]{0:T(128)S(1)} %get-tuple-element.67, f32[8]{0:T(128)S(1)} %get-tuple-element.66, f32[8]{0:T(128)S(1)} %get-tuple-element.13, ...), kind=kLoop, calls=%fused_computation.77 | loop fusion | flops 2097152 | bytes 4325504 | tf_op jit(solution)/shard_map/add | solution.py:263
  (58 shorter events, 1.0 us)
Async XLA Ops:
  0.6 4.4 %copy-start.2 = (s32[16,16,128]{2,1,0:T(8,128)S(1)}, s32[16,16,128]{2,1,0:T(8,128)}, u32[]{:S(2)}) copy-start(s32[16,16,128]{2,1,0:T(8,128)} %param.7) | copy-start | bytes 393220
  0.6 9.3 %copy-start.3 = (bf16[3,16,3,3,3]{1,4,3,2,0:T(4,128)(2,1)S(1)}, bf16[3,16,3,3,3]{1,4,3,2,0:T(4,128)(2,1)}, u32[]{:S(2)}) copy-start(bf16[3,16,3,3,3]{1,4,3,2,0:T(4,128)(2,1)} %param.5) | copy-start | bytes 7780
  2.6 7.3 %collective-permute-start.1 = (bf16[16,1,16,128]{3,0,2,1:T(8,128)(2,1)S(1)}, bf16[16,1,16,128]{3,0,2,1:T(8,128)(2,1)S(1)}, u32[]{:S(2)}, u32[]{:S(2)}) collective-permute-start(bf16[16,1,16,128]{3,0,2,1:T(8,128)(2,1)S(1)} %get-tuple-element.40), channel_id=1, source_target_pairs={{0,24},{8,0},{16,8},{24,16},{1,25},{9,1},{17,9},{25,17},{2,26},{10... | collective-permute-start | bytes 196616 | tf_op jit(solution)/shard_map/ppermute | solution.py:58
  5.1 4.9 %collective-permute-start = (bf16[16,1,16,128]{3,0,2,1:T(8,128)(2,1)S(1)}, bf16[16,1,16,128]{3,0,2,1:T(8,128)(2,1)S(1)}, u32[]{:S(2)}, u32[]{:S(2)}) collective-permute-start(bf16[16,1,16,128]{3,0,2,1:T(8,128)(2,1)S(1)} %get-tuple-element.39), channel_id=1, source_target_pairs={{0,8},{8,16},{16,24},{24,0},{1,9},{9,17},{17,25},{25,1},{2,10},{10... | collective-permute-start | bytes 196616 | tf_op jit(solution)/shard_map/ppermute | solution.py:58
  5.1 6.9 %collective-permute-start.6 = (f32[1,16,4,128]{3,0,2,1:T(1,128)S(1)}, f32[1,16,4,128]{3,0,2,1:T(1,128)S(1)}, u32[]{:S(2)}, u32[]{:S(2)}) collective-permute-start(f32[1,16,4,128]{3,0,2,1:T(1,128)S(1)} %get-tuple-element.51), channel_id=1, source_target_pairs={{0,1},{1,2},{2,3},{3,4},{4,5},{5,6},{6,7},{7,0},{8,9},{9,10},{10,1... | collective-permute-start | bytes 98312 | tf_op jit(solution)/shard_map/ppermute | solution.py:58
  6.7 19.0 %collective-permute-start.7 = (f32[1,16,4,128]{3,0,2,1:T(1,128)S(1)}, f32[1,16,4,128]{3,0,2,1:T(1,128)S(1)}, u32[]{:S(2)}, u32[]{:S(2)}) collective-permute-start(f32[1,16,4,128]{3,0,2,1:T(1,128)S(1)} %get-tuple-element.52), channel_id=1, source_target_pairs={{0,7},{1,0},{2,1},{3,2},{4,3},{5,4},{6,5},{7,6},{8,15},{9,8},{10,9... | collective-permute-start | bytes 98312 | tf_op jit(solution)/shard_map/ppermute | solution.py:58
  10.0 7.4 %collective-permute-start.2 = (bf16[16,18,1,128]{3,0,2,1:T(8,128)(2,1)S(1)}, bf16[16,18,1,128]{3,0,2,1:T(8,128)(2,1)S(1)}, u32[]{:S(2)}, u32[]{:S(2)}) collective-permute-start(bf16[16,18,1,128]{3,0,2,1:T(8,128)(2,1)S(1)} %get-tuple-element.37), channel_id=1, source_target_pairs={{0,1},{1,2},{2,3},{3,4},{4,5},{5,6},{6,7},{7,0},{8,9},{9,10},{10,1... | collective-permute-start | bytes 221192 | tf_op jit(solution)/shard_map/ppermute | solution.py:58
  12.0 6.0 %collective-permute-start.3 = (bf16[16,18,1,128]{3,0,2,1:T(8,128)(2,1)S(1)}, bf16[16,18,1,128]{3,0,2,1:T(8,128)(2,1)S(1)}, u32[]{:S(2)}, u32[]{:S(2)}) collective-permute-start(bf16[16,18,1,128]{3,0,2,1:T(8,128)(2,1)S(1)} %get-tuple-element.38), channel_id=1, source_target_pairs={{0,7},{1,0},{2,1},{3,2},{4,3},{5,4},{6,5},{7,6},{8,15},{9,8},{10,9... | collective-permute-start | bytes 221192 | tf_op jit(solution)/shard_map/ppermute | solution.py:58
  23.4 0.7 copy-start.4
  25.6 7.8 %collective-permute-start.4 = (f32[3,16,4,128]{3,0,2,1:T(4,128)S(1)}, f32[3,16,4,128]{3,0,2,1:T(4,128)S(1)}, u32[]{:S(2)}, u32[]{:S(2)}) collective-permute-start(f32[3,16,4,128]{3,0,2,1:T(4,128)S(1)} %get-tuple-element.43), channel_id=1, source_target_pairs={{0,1},{1,2},{2,3},{3,4},{4,5},{5,6},{6,7},{7,0},{8,9},{9,10},{10,1... | collective-permute-start | bytes 294920 | tf_op jit(solution)/shard_map/ppermute | solution.py:58
  25.8 7.8 %collective-permute-start.5 = (f32[3,16,4,128]{3,0,2,1:T(4,128)S(1)}, f32[3,16,4,128]{3,0,2,1:T(4,128)S(1)}, u32[]{:S(2)}, u32[]{:S(2)}) collective-permute-start(f32[3,16,4,128]{3,0,2,1:T(4,128)S(1)} %get-tuple-element.44), channel_id=1, source_target_pairs={{0,7},{1,0},{2,1},{3,2},{4,3},{5,4},{6,5},{7,6},{8,15},{9,8},{10,9... | collective-permute-start | bytes 294920 | tf_op jit(solution)/shard_map/ppermute | solution.py:58
  33.8 5.4 %collective-permute-start.8 = (f32[4,4,22,128]{3,0,2,1:T(4,128)S(1)}, f32[4,4,22,128]{3,0,2,1:T(4,128)S(1)}, u32[]{:S(2)}, u32[]{:S(2)}) collective-permute-start(f32[4,4,22,128]{3,0,2,1:T(4,128)S(1)} %get-tuple-element.41), channel_id=1, source_target_pairs={{0,8},{8,16},{16,24},{24,0},{1,9},{9,17},{17,25},{25,1},{2,10},{10... | collective-permute-start | bytes 540680 | tf_op jit(solution)/shard_map/ppermute | solution.py:58
  33.9 5.3 %collective-permute-start.9 = (f32[4,4,22,128]{3,0,2,1:T(4,128)S(1)}, f32[4,4,22,128]{3,0,2,1:T(4,128)S(1)}, u32[]{:S(2)}, u32[]{:S(2)}) collective-permute-start(f32[4,4,22,128]{3,0,2,1:T(4,128)S(1)} %get-tuple-element.42), channel_id=1, source_target_pairs={{0,24},{8,0},{16,8},{24,16},{1,25},{9,1},{17,9},{25,17},{2,26},{10... | collective-permute-start | bytes 540680 | tf_op jit(solution)/shard_map/ppermute | solution.py:58
  47.3 2.5 %copy-start = (f32[8,20,20,128]{3,2,1,0:T(8,128)}, f32[8,20,20,128]{3,2,1,0:T(8,128)S(1)}, u32[]{:S(2)}) copy-start(f32[8,20,20,128]{3,2,1,0:T(8,128)S(1)} %fusion.10) | copy-start | bytes 4915204
  49.4 1.2 %copy-start.1 = (f32[8,18,18,128]{3,2,1,0:T(8,128)}, f32[8,18,18,128]{3,2,1,0:T(8,128)S(1)}, u32[]{:S(2)}) copy-start(f32[8,18,18,128]{3,2,1,0:T(8,128)S(1)} %fusion.16) | copy-start | bytes 3981316
  52.9 2.2 %collective-permute-start.10 = (f32[9,8]{1,0:T(8,128)S(1)}, f32[9,8]{1,0:T(8,128)S(1)}, u32[]{:S(2)}, u32[]{:S(2)}) collective-permute-start(f32[9,8]{1,0:T(8,128)S(1)} %stack.55), channel_id=1, source_target_pairs={{0,8},{8,0},{16,24},{24,16},{1,9},{9,1},{17,25},{25,17},{2,10},{10... | collective-permute-start | bytes 872 | tf_op jit(solution)/shard_map/ppermute | solution.py:134
  55.1 3.7 %collective-permute-start.11 = (f32[9,8]{1,0:T(8,128)S(1)}, f32[9,8]{1,0:T(8,128)S(1)}, u32[]{:S(2)}, u32[]{:S(2)}) collective-permute-start(f32[9,8]{1,0:T(8,128)S(1)} %add.592), channel_id=1, source_target_pairs={{0,16},{8,24},{16,0},{24,8},{1,17},{9,25},{17,1},{25,9},{2,18},{10... | collective-permute-start | bytes 872 | tf_op jit(solution)/shard_map/ppermute | solution.py:134
  58.7 3.7 %collective-permute-start.12 = (f32[9,8]{1,0:T(8,128)S(1)}, f32[9,8]{1,0:T(8,128)S(1)}, u32[]{:S(2)}, u32[]{:S(2)}) collective-permute-start(f32[9,8]{1,0:T(8,128)S(1)} %add.593), channel_id=1, source_target_pairs={{0,1},{1,0},{2,3},{3,2},{4,5},{5,4},{6,7},{7,6},{8,9},{9,8},{10,11... | collective-permute-start | bytes 872 | tf_op jit(solution)/shard_map/ppermute | solution.py:134
  62.4 3.7 %collective-permute-start.13 = (f32[9,8]{1,0:T(8,128)S(1)}, f32[9,8]{1,0:T(8,128)S(1)}, u32[]{:S(2)}, u32[]{:S(2)}) collective-permute-start(f32[9,8]{1,0:T(8,128)S(1)} %add.594), channel_id=1, source_target_pairs={{0,2},{1,3},{2,0},{3,1},{4,6},{5,7},{6,4},{7,5},{8,10},{9,11},{10,... | collective-permute-start | bytes 872 | tf_op jit(solution)/shard_map/ppermute | solution.py:134
  66.1 4.5 %collective-permute-start.14 = (f32[9,8]{1,0:T(8,128)S(1)}, f32[9,8]{1,0:T(8,128)S(1)}, u32[]{:S(2)}, u32[]{:S(2)}) collective-permute-start(f32[9,8]{1,0:T(8,128)S(1)} %add.595), channel_id=1, source_target_pairs={{0,4},{1,5},{2,6},{3,7},{4,0},{5,1},{6,2},{7,3},{8,12},{9,13},{10,... | collective-permute-start | bytes 872 | tf_op jit(solution)/shard_map/ppermute | solution.py:134
